TPU v7x, 32 devices: a whole 2x2x4 slice. The times are simulated.
32 devices in a mesh: segment: 4 (over z), dp: 8 (over y, x, core).
Axes of the slice: x: 2, y: 2, z: 4, core: 2. Of those that a mesh axis runs over, the one named last changes fastest.
Arguments:
- x_in: bfloat16 [2, 512, 8192], P(None, 'dp'), may hold values from -6 to 6
- cotangent: bfloat16 [2, 512, 8192], P(None, 'dp'), may hold values from -6 to 6
- weights: bfloat16 [1024, 128, 128], P('segment'), may hold values from -0.375 to 0.375
- block_index: int32 [1024, 3], P('segment'), may hold values from 0 to 63, as said below
Outputs:
- weight_grad: float32 [1024, 128, 128], P(('segment', 'dp'))
Inputs may be any that keep to these rules, and one draw needn't show every extreme that they name: `block_index`: within each segment's 2 * 128 rows, layer slot j takes rows j * 128 to (j + 1) * 128 - 1. A segment holds 1 to 2 layers, the first ones; the rest have all flags 0; some segment holds 2. A held layer has 32 to 128 kept slots, flags 1 first; some layer keeps 128. The (row, column) pairs of one layer's slots are distinct. Rows and columns of empty slots are arbitrary.
All inputs are finite; a program needn't handle non-finite values.
Results may differ from a plain program's by a relative error of at most 0.013.
Values may be sent and summed in bfloat16 or wider, within the bound.
No kernel may reach another device: no remote copies, remote signals or barrier semaphores. Data moves between devices by JAX's collectives and lax.ppermute only.
A program may use at most 192 MiB of HBM per device.

v0:
```python
import functools

import jax
import jax.numpy as jnp
from jax import lax
from jax.experimental import pallas as pl
from jax.experimental.pallas import tpu as pltpu
from jax.sharding import PartitionSpec as P

BLK = 128
LSLOT = 2
KMAX = 128
CH = 512
NSUB = 16
SPLIT = 2
GROUP = 8
VMEM_LIMIT = 60 * 1024 * 1024

_SMEM = pl.BlockSpec(memory_space=pltpu.SMEM)
_VMEM = pl.BlockSpec(memory_space=pltpu.VMEM)
_ANY = pl.BlockSpec(memory_space=pl.ANY)


def shifted(value, axis, steps):
    count = lax.axis_size(axis)
    leading, last = (max(0, -steps), min(count, count - steps))
    return lax.ppermute(value, axis, [(source, source + steps) for source in range(leading, last)])


def _blk(i):
    return pl.ds(pl.multiple_of(i * BLK, BLK), BLK)


def _chunk(j):
    return pl.ds(pl.multiple_of(j * CH, CH), CH)


def _flag(idx_ref, k):
    return jnp.where(idx_ref[3 * k + 2] > 0, 1.0, 0.0).astype(jnp.float32)


class _WeightChunks:
    def __init__(self, w_hbm, base, w_vmem, sems):
        self.w_hbm, self.base, self.w_vmem, self.sems = w_hbm, base, w_vmem, sems

    def copy(self, j):
        return pltpu.make_async_copy(
            self.w_hbm.at[pl.ds(self.base + j * NSUB, NSUB)],
            self.w_vmem.at[pl.ds(j * NSUB, NSUB)],
            self.sems.at[j],
        )

    def wait_on(self, j):
        self.copy(j).wait()


def _w_copies(w_hbm, base, w_vmem, sems):
    chunks = _WeightChunks(w_hbm, base, w_vmem, sems)
    started = []
    for j in range(w_vmem.shape[0] // NSUB):
        copy = chunks.copy(j)
        copy.start()
        started.append(copy)
    return (chunks, started)


def _slot_chunks(idx_ref, base, copies, product, update):
    def chunk(j, carry):
        copies[0].wait_on(j)

        @pl.when(idx_ref[3 * (base + j * NSUB) + 2] > 0)
        def _():
            for g in range(0, NSUB, GROUP):
                ks = [j * NSUB + g + i for i in range(GROUP)]
                parts = [product(k) for k in ks]
                for k, part in zip(ks, parts):
                    update(k, part)

        return carry

    lax.fori_loop(0, len(copies[1]), chunk, 0)


def _fwd_kernel(base, layer, at_ref, idx_ref, h_ref, w_hbm, sh_in, sy_in, hout_ref, sh_ref, sy_ref, w_vmem, y_vmem, sems, io_sems):
    del sh_in, sy_in
    width = h_ref.shape[1]
    at = at_ref[0]
    copies = _w_copies(w_hbm, base, w_vmem, sems)
    save_h = pltpu.make_async_copy(h_ref, sh_ref.at[layer, at], io_sems.at[0])
    save_h.start()
    y_vmem[...] = jnp.zeros_like(y_vmem)

    def product(k):
        r = idx_ref[3 * (base + k)]
        return jnp.dot(h_ref[:, _blk(r)], w_vmem[k], preferred_element_type=jnp.float32)

    def update(k, p):
        c = idx_ref[3 * (base + k) + 1]
        y_vmem[:, _blk(c)] += p * _flag(idx_ref, base + k)

    _slot_chunks(idx_ref, base, copies, product, update)
    save_y = pltpu.make_async_copy(y_vmem, sy_ref.at[layer, at], io_sems.at[1])
    save_y.start()

    def epi(j, carry):
        y = y_vmem[:, _chunk(j)]
        h = h_ref[:, _chunk(j)].astype(jnp.float32)
        hout_ref[:, _chunk(j)] = (h + y / (1.0 + jnp.exp(-y))).astype(hout_ref.dtype)
        return carry

    lax.fori_loop(0, width // CH, epi, 0)
    save_h.wait()
    save_y.wait()


def layer_forward(h, weights, layer, block_index, at, stash_h, stash_y):
    rows, width = h.shape
    return pl.pallas_call(
        functools.partial(_fwd_kernel, layer * KMAX, layer),
        out_shape=(
            jax.ShapeDtypeStruct((rows, width), jnp.bfloat16),
            jax.ShapeDtypeStruct(stash_h.shape, stash_h.dtype),
            jax.ShapeDtypeStruct(stash_y.shape, stash_y.dtype),
        ),
        in_specs=[_SMEM, _SMEM, _VMEM, _ANY, _ANY, _ANY],
        out_specs=(_VMEM, _ANY, _ANY),
        scratch_shapes=[
            pltpu.VMEM((KMAX, BLK, BLK), weights.dtype),
            pltpu.VMEM((rows, width), jnp.float32),
            pltpu.SemaphoreType.DMA((KMAX // NSUB,)),
            pltpu.SemaphoreType.DMA((2,)),
        ],
        input_output_aliases={4: 1, 5: 2},
        compiler_params=pltpu.CompilerParams(vmem_limit_bytes=VMEM_LIMIT),
    )(at.reshape(1), block_index.reshape(-1), h, weights, stash_h, stash_y)


def _bwd_kernel(base, layer, at_ref, idx_ref, g_ref, sy_hbm, w_hbm, ss_in, gout_ref, ss_ref, y_vmem, s_vmem, sp_ref, w_vmem, sems, io_sems):
    del ss_in
    width = g_ref.shape[1]
    at = at_ref[0]
    load_y = pltpu.make_async_copy(sy_hbm.at[layer, at], y_vmem, io_sems.at[0])
    load_y.start()
    copies = _w_copies(w_hbm, base, w_vmem, sems)
    load_y.wait()

    def pre(j, carry):
        y = y_vmem[:, _chunk(j)]
        sig = 1.0 / (1.0 + jnp.exp(-y))
        g = g_ref[:, _chunk(j)].astype(jnp.float32)
        s_vmem[:, _chunk(j)] = (g * sig * (1.0 + y * (1.0 - sig))).astype(s_vmem.dtype)
        sp_ref[:, _chunk(j)] = jnp.zeros((g_ref.shape[0], CH), jnp.float32)
        return carry

    lax.fori_loop(0, width // CH, pre, 0)
    save_s = pltpu.make_async_copy(s_vmem, ss_ref.at[layer, at], io_sems.at[1])
    save_s.start()

    def product(k):
        c = idx_ref[3 * (base + k) + 1]
        return lax.dot_general(
            s_vmem[:, _blk(c)],
            w_vmem[k],
            (((1,), (1,)), ((), ())),
            preferred_element_type=jnp.float32,
        )

    def update(k, back):
        r = idx_ref[3 * (base + k)]
        sp_ref[:, _blk(r)] += back * _flag(idx_ref, base + k)

    _slot_chunks(idx_ref, base, copies, product, update)

    def epi(j, carry):
        g = g_ref[:, _chunk(j)].astype(jnp.float32)
        gout_ref[:, _chunk(j)] = (g + sp_ref[:, _chunk(j)]).astype(gout_ref.dtype)
        return carry

    lax.fori_loop(0, width // CH, epi, 0)
    save_s.wait()


def layer_backward(g, stash_y, weights, layer, block_index, at, stash_s):
    rows, width = g.shape
    return pl.pallas_call(
        functools.partial(_bwd_kernel, layer * KMAX, layer),
        out_shape=(
            jax.ShapeDtypeStruct((rows, width), jnp.bfloat16),
            jax.ShapeDtypeStruct(stash_s.shape, stash_s.dtype),
        ),
        in_specs=[_SMEM, _SMEM, _VMEM, _ANY, _ANY, _ANY],
        out_specs=(_VMEM, _ANY),
        scratch_shapes=[
            pltpu.VMEM((rows, width), jnp.float32),
            pltpu.VMEM((rows, width), jnp.bfloat16),
            pltpu.VMEM((rows, width), jnp.float32),
            pltpu.VMEM((KMAX, BLK, BLK), weights.dtype),
            pltpu.SemaphoreType.DMA((KMAX // NSUB,)),
            pltpu.SemaphoreType.DMA((2,)),
        ],
        input_output_aliases={5: 1},
        compiler_params=pltpu.CompilerParams(vmem_limit_bytes=VMEM_LIMIT),
    )(at.reshape(1), block_index.reshape(-1), g, stash_y, weights, stash_s)


def _dw_kernel(mbs, idx_ref, h_ref, s_ref, dw_ref):
    rows = h_ref.shape[1] * h_ref.shape[2]
    for j in range(dw_ref.shape[0] // NSUB):
        layer = j * NSUB // KMAX

        @pl.when(idx_ref[3 * j * NSUB + 2] > 0)
        def _():
            for k in range(j * NSUB, (j + 1) * NSUB):
                r = idx_ref[3 * k]
                c = idx_ref[3 * k + 1]
                hb = h_ref[layer, :, :, _blk(r)]
                sb = s_ref[layer, :, :, _blk(c)]
                dw_ref[k] = lax.dot_general(
                    hb.reshape(rows, BLK),
                    sb.reshape(rows, BLK),
                    (((0,), (0,)), ((), ())),
                    preferred_element_type=jnp.float32,
                ) * _flag(idx_ref, k)

        @pl.when(idx_ref[3 * j * NSUB + 2] <= 0)
        def _():
            dw_ref[pl.ds(j * NSUB, NSUB)] = jnp.zeros((NSUB, BLK, BLK), jnp.float32)


def segment_dw(stash_h, stash_s, block_index, mbs):
    return pl.pallas_call(
        functools.partial(_dw_kernel, mbs),
        out_shape=jax.ShapeDtypeStruct((block_index.shape[0], BLK, BLK), jnp.float32),
        in_specs=[_SMEM, _VMEM, _VMEM],
        out_specs=_VMEM,
        compiler_params=pltpu.CompilerParams(vmem_limit_bytes=VMEM_LIMIT),
    )(block_index.reshape(-1), stash_h, stash_s)


def _dw_half_kernel(sel_ref, idx_ref, h_ref, s_ref, out_ref):
    b0 = sel_ref[0]
    rows = h_ref.shape[1] * h_ref.shape[2]
    per = out_ref.shape[1]
    for q in range(out_ref.shape[0]):
        layer = (2 * q * per) // KMAX
        for j in range(per // NSUB):
            first = 2 * q * per + b0 * per + j * NSUB

            @pl.when(idx_ref[3 * first + 2] > 0)
            def _():
                for i in range(NSUB):
                    k = first + i
                    r = idx_ref[3 * k]
                    c = idx_ref[3 * k + 1]
                    hb = h_ref[layer, :, :, _blk(r)].reshape(rows, BLK)
                    sb = s_ref[layer, :, :, _blk(c)].reshape(rows, BLK)
                    part = lax.dot_general(
                        hb, sb, (((0,), (0,)), ((), ())), preferred_element_type=jnp.float32
                    )
                    out_ref[q, j * NSUB + i] = (part * _flag(idx_ref, k)).astype(out_ref.dtype)

            @pl.when(idx_ref[3 * first + 2] <= 0)
            def _():
                out_ref[q, pl.ds(j * NSUB, NSUB)] = jnp.zeros((NSUB, BLK, BLK), out_ref.dtype)


def dw_half(stash_h, stash_s, block_index, b0, dtype):
    per = block_index.shape[0] // 8
    return pl.pallas_call(
        _dw_half_kernel,
        out_shape=jax.ShapeDtypeStruct((4, per, BLK, BLK), dtype),
        in_specs=[_SMEM, _SMEM, _VMEM, _VMEM],
        out_specs=_VMEM,
        compiler_params=pltpu.CompilerParams(vmem_limit_bytes=VMEM_LIMIT),
    )(b0.reshape(1).astype(jnp.int32), block_index.reshape(-1), stash_h, stash_s)


def _exchange(send, pairs):
    return lax.ppermute(send.astype(jnp.bfloat16), "dp", pairs).astype(jnp.float32)


def weight_grads(stash_h, stash_s, block_index, mbs):
    n = lax.axis_size("dp")
    if n != 8:
        acc = segment_dw(stash_h, stash_s, block_index, mbs)
        return lax.psum_scatter(
            acc.astype(jnp.bfloat16), "dp", scatter_dimension=0, tiled=True
        ).astype(jnp.float32)
    d = lax.axis_index("dp")
    d0, d1, d2 = d % 2, (d // 2) % 2, d // 4
    pick = lambda a, i, axis: lax.dynamic_index_in_dim(a, i, axis, keepdims=False)
    send = dw_half(stash_h, stash_s, block_index, 1 - d0, jnp.bfloat16)
    got = lax.ppermute(send, "dp", [(i, i ^ 1) for i in range(8)])
    keep = dw_half(stash_h, stash_s, block_index, d0, jnp.float32)
    keep = keep.reshape((2, 2) + keep.shape[1:])
    got = got.reshape(keep.shape)
    core0 = d0 == 0

    def half(a, i_core0, i_core1):
        return jnp.where(core0, pick(a, i_core0, 1), pick(a, i_core1, 0)).astype(jnp.float32)

    send = half(keep, 1 - d1, 1 - d2) + half(got, 1 - d1, 1 - d2)
    got2 = _exchange(send, [(i, i ^ (2 if i % 2 == 0 else 4)) for i in range(8)])
    keep2 = half(keep, d1, d2) + half(got, d1, d2)
    rem = jnp.where(core0, d2, d1)
    send = pick(keep2, 1 - rem, 0) + pick(got2, 1 - rem, 0)
    got3 = _exchange(send, [(i, i ^ (4 if i % 2 == 0 else 2)) for i in range(8)])
    return pick(keep2, rem, 0) + pick(got2, rem, 0) + got3


def on_device(x_in, cotangent, weights, block_index):
    segments = lax.axis_size("segment")
    me_segment = lax.axis_index("segment")
    mbs, rows_dev, width = x_in.shape
    mbs, rows_dev = mbs * SPLIT, rows_dev // SPLIT
    x_in = x_in.reshape(mbs, rows_dev, width)
    cotangent = cotangent.reshape(mbs, rows_dev, width)
    idx = block_index.reshape(LSLOT, KMAX, 3)

    def tick_body(tick, carry):
        recv_f, recv_b, saved_h, saved_y, saved_s = carry
        micro_f = tick - me_segment
        live_f = (micro_f >= 0) & (micro_f < mbs)
        at_f = jnp.clip(micro_f, 0, mbs - 1)
        first = lax.dynamic_index_in_dim(x_in, at_f, 0, keepdims=False)
        start = jnp.where(me_segment == 0, first, recv_f)

        def run_f(operands):
            h, sh, sy = operands
            for layer in range(LSLOT):
                h, sh, sy = layer_forward(h, weights, layer, block_index, at_f, sh, sy)
            return (h, sh, sy)

        h_out, saved_h, saved_y = lax.cond(live_f, run_f, lambda ops: ops, (start, saved_h, saved_y))
        send_f = shifted(h_out, "segment", 1)

        micro_b = tick - (2 * segments - 2 - me_segment)
        live_b = (micro_b >= 0) & (micro_b < mbs)
        at_b = jnp.clip(micro_b, 0, mbs - 1)
        top = lax.dynamic_index_in_dim(cotangent, at_b, 0, keepdims=False)
        grad_in = jnp.where(me_segment == segments - 1, top, recv_b)
        stash_y_now = saved_y

        def run_b(operands):
            grad, ss = operands
            for layer in reversed(range(LSLOT)):
                grad, ss = layer_backward(grad, stash_y_now, weights, layer, block_index, at_b, ss)
            return (grad, ss)

        grad_out, saved_s = lax.cond(live_b, run_b, lambda ops: ops, (grad_in, saved_s))
        send_b = shifted(grad_out, "segment", -1)
        return (send_f, send_b, saved_h, saved_y, saved_s)

    stash_h = jnp.zeros((LSLOT, mbs, rows_dev, width), jnp.bfloat16)
    stash_y = jnp.zeros((LSLOT, mbs, rows_dev, width), jnp.float32)
    stash_s = jnp.zeros((LSLOT, mbs, rows_dev, width), jnp.bfloat16)
    blank = jnp.zeros((rows_dev, width), jnp.bfloat16)
    ticks = mbs + 2 * segments - 2
    carry = (blank, blank, stash_h, stash_y, stash_s)
    for tick in range(ticks):
        carry = tick_body(tick, carry)
    unused_f, unused_b, stash_h, stash_y, stash_s = carry
    return weight_grads(stash_h, stash_s, block_index, mbs)


def solution(mesh):
    return jax.shard_map(
        on_device,
        mesh=mesh,
        in_specs=(
            P(None, "dp", None),
            P(None, "dp", None),
            P("segment", None, None),
            P("segment", None),
        ),
        out_specs=P(("segment", "dp"), None, None),
        check_vma=False,
    )
```

profile of v0, /device:TPU:0, one launch (start us, length us, event | category | flops | bytes accessed | tf_op | source)
XLA Modules:
  0.0 404.8 jit_solution(13368298945979373161)
XLA Ops:
  1.1 18.3 %conditional.20 = ((bf16[32,8192]{1,0:T(8,128)(2,1)S(1)}, bf16[2,4,32,8192]{3,2,1,0:T(8,128)(2,1)}, f32[2,4,32,8192]{3,2,1,0:T(8,128)})) conditional(s32[]{:T(128)} %convert_element_type.90, bf16[32,8192]{1,0:T(8,128)(2,1)S(1)} %select_bitcast_fusion.1, (s32[]{:T(128)}, s32[256,3]{0,1:T(4,128)}, bf16[32,8192]{1,0:T(8,128)(2,1)S(1)}, ...), branch_computations={%region_0.1_spmd, %region_1.2_spmd} | conditional | bytes 12595214 | solution.py:334
  2.7 4.3 %broadcast_in_dim.7.sy_in = f32[2,4,32,8192]{3,2,1,0:T(8,128)} broadcast(f32[]{:T(128)} %constant.162.clone), dimensions={} | broadcast | bytes 8388612 | tf_op jit(solution)/shard_map/broadcast_in_dim | solution.py:355
  9.5 4.9 %branch_1_fun.48 = (bf16[32,8192]{1,0:T(8,128)(2,1)}, bf16[2,4,32,8192]{3,2,1,0:T(8,128)(2,1)}, f32[2,4,32,8192]{3,2,1,0:T(8,128)}) custom-call(s32[1]{0:T(128)} %bitcast.at_ref, s32[768]{0:T(1024)} %reshape.109.idx_ref, bf16[32,8192]{1,0:T(8,128)(2,1)S(1)} %get-tuple-element.422.h_ref, ...), custom_call_target="tpu_custom_call", output_to_operand_aliasing={{1}: (4, {}), {2}: (5, {})} | custom-call | tf_op jit(solution)/shard_map/cond/branch_1_fun/pallas_call | solution.py:118
  14.4 5.0 %branch_1_fun.49 = (bf16[32,8192]{1,0:T(8,128)(2,1)S(1)}, bf16[2,4,32,8192]{3,2,1,0:T(8,128)(2,1)}, f32[2,4,32,8192]{3,2,1,0:T(8,128)}) custom-call(s32[1]{0:T(128)} %bitcast.at_ref, s32[768]{0:T(1024)} %reshape.109.idx_ref, bf16[32,8192]{1,0:T(8,128)(2,1)} %get-tuple-element.424.h_ref, ...), custom_call_target="tpu_custom_call", output_to_operand_aliasing={{1}: (4, {}), {2}: (5, {})} | custom-call | tf_op jit(solution)/shard_map/cond/branch_1_fun/pallas_call | solution.py:118
  26.5 6.3 %collective-permute-done = bf16[32,8192]{1,0:T(8,128)(2,1)} collective-permute-done((bf16[32,8192]{1,0:T(8,128)(2,1)S(1)}, bf16[32,8192]{1,0:T(8,128)(2,1)}, u32[]{:S(2)}, u32[]{:S(2)}) %collective-permute-start) | collective-permute-done | bytes 524320 | tf_op jit(solution)/shard_map/ppermute | solution.py:27
  32.8 11.5 %conditional.21 = ((bf16[32,8192]{1,0:T(8,128)(2,1)S(1)}, bf16[2,4,32,8192]{3,2,1,0:T(8,128)(2,1)}, f32[2,4,32,8192]{3,2,1,0:T(8,128)})) conditional(s32[]{:T(128)} %convert_element_type.89, (bf16[32,8192]{1,0:T(8,128)(2,1)S(1)}, bf16[2,4,32,8192]{3,2,1,0:T(8,128)(2,1)}, f32[2,4,32,8192]{3,2,1,0:T(8,128)}) %tuple.143, (s32[]{:T(128)}, ...), branch_computations={%region_2.3_spmd, %region_3.4_spmd} | conditional | bytes 12296 | solution.py:334
  34.5 4.9 %branch_1_fun.50 = (bf16[32,8192]{1,0:T(8,128)(2,1)}, bf16[2,4,32,8192]{3,2,1,0:T(8,128)(2,1)}, f32[2,4,32,8192]{3,2,1,0:T(8,128)}) custom-call(s32[1]{0:T(128)} %bitcast.1.at_ref, s32[768]{0:T(1024)} %reshape.115.idx_ref, bf16[32,8192]{1,0:T(8,128)(2,1)S(1)} %get-tuple-element.429.h_ref, ...), custom_call_target="tpu_custom_call", output_to_operand_aliasing={{1}: (4, {}), {2}: (5, {})} | custom-call | tf_op jit(solution)/shard_map/cond/branch_1_fun/pallas_call | solution.py:118
  39.4 5.0 %branch_1_fun.51 = (bf16[32,8192]{1,0:T(8,128)(2,1)S(1)}, bf16[2,4,32,8192]{3,2,1,0:T(8,128)(2,1)}, f32[2,4,32,8192]{3,2,1,0:T(8,128)}) custom-call(s32[1]{0:T(128)} %bitcast.1.at_ref, s32[768]{0:T(1024)} %reshape.115.idx_ref, bf16[32,8192]{1,0:T(8,128)(2,1)} %get-tuple-element.433.h_ref, ...), custom_call_target="tpu_custom_call", output_to_operand_aliasing={{1}: (4, {}), {2}: (5, {})} | custom-call | tf_op jit(solution)/shard_map/cond/branch_1_fun/pallas_call | solution.py:118
  44.4 6.1 %collective-permute-start.1 = (bf16[32,8192]{1,0:T(8,128)(2,1)S(1)}, bf16[32,8192]{1,0:T(8,128)(2,1)}, u32[]{:S(2)}, u32[]{:S(2)}) collective-permute-start(bf16[32,8192]{1,0:T(8,128)(2,1)S(1)} %get-tuple-element.649), channel_id=1, source_target_pairs={{0,8},{8,16},{16,24},{1,9},{9,17},{17,25},{2,10},{10,18},{18,26},{... | collective-permute-start | bytes 1572872 | tf_op jit(solution)/shard_map/ppermute | solution.py:27
  53.0 7.8 %collective-permute-done.1 = bf16[32,8192]{1,0:T(8,128)(2,1)} collective-permute-done((bf16[32,8192]{1,0:T(8,128)(2,1)S(1)}, bf16[32,8192]{1,0:T(8,128)(2,1)}, u32[]{:S(2)}, u32[]{:S(2)}) %collective-permute-start.1) | collective-permute-done | bytes 524320 | tf_op jit(solution)/shard_map/ppermute | solution.py:27
  60.9 11.6 %conditional.22 = ((bf16[32,8192]{1,0:T(8,128)(2,1)S(1)}, bf16[2,4,32,8192]{3,2,1,0:T(8,128)(2,1)}, f32[2,4,32,8192]{3,2,1,0:T(8,128)})) conditional(s32[]{:T(128)} %convert_element_type.88, (bf16[32,8192]{1,0:T(8,128)(2,1)S(1)}, bf16[2,4,32,8192]{3,2,1,0:T(8,128)(2,1)}, f32[2,4,32,8192]{3,2,1,0:T(8,128)}) %tuple.145, (s32[]{:T(128)}, ...), branch_computations={%region_4.5_spmd, %region_5.6_spmd} | conditional | bytes 12296 | solution.py:334
  62.5 4.9 %branch_1_fun.52 = (bf16[32,8192]{1,0:T(8,128)(2,1)}, bf16[2,4,32,8192]{3,2,1,0:T(8,128)(2,1)}, f32[2,4,32,8192]{3,2,1,0:T(8,128)}) custom-call(s32[1]{0:T(128)} %bitcast.2.at_ref, s32[768]{0:T(1024)} %reshape.117.idx_ref, bf16[32,8192]{1,0:T(8,128)(2,1)S(1)} %get-tuple-element.438.h_ref, ...), custom_call_target="tpu_custom_call", output_to_operand_aliasing={{1}: (4, {}), {2}: (5, {})} | custom-call | tf_op jit(solution)/shard_map/cond/branch_1_fun/pallas_call | solution.py:118
  67.5 5.1 %branch_1_fun.53 = (bf16[32,8192]{1,0:T(8,128)(2,1)S(1)}, bf16[2,4,32,8192]{3,2,1,0:T(8,128)(2,1)}, f32[2,4,32,8192]{3,2,1,0:T(8,128)}) custom-call(s32[1]{0:T(128)} %bitcast.2.at_ref, s32[768]{0:T(1024)} %reshape.117.idx_ref, bf16[32,8192]{1,0:T(8,128)(2,1)} %get-tuple-element.442.h_ref, ...), custom_call_target="tpu_custom_call", output_to_operand_aliasing={{1}: (4, {}), {2}: (5, {})} | custom-call | tf_op jit(solution)/shard_map/cond/branch_1_fun/pallas_call | solution.py:118
  72.5 6.0 %collective-permute-start.2 = (bf16[32,8192]{1,0:T(8,128)(2,1)S(1)}, bf16[32,8192]{1,0:T(8,128)(2,1)}, u32[]{:S(2)}, u32[]{:S(2)}) collective-permute-start(bf16[32,8192]{1,0:T(8,128)(2,1)S(1)} %get-tuple-element.652), channel_id=1, source_target_pairs={{0,8},{8,16},{16,24},{1,9},{9,17},{17,25},{2,10},{10,18},{18,26},{... | collective-permute-start | bytes 1572872 | tf_op jit(solution)/shard_map/ppermute | solution.py:27
  81.1 7.0 %collective-permute-done.2 = bf16[32,8192]{1,0:T(8,128)(2,1)} collective-permute-done((bf16[32,8192]{1,0:T(8,128)(2,1)S(1)}, bf16[32,8192]{1,0:T(8,128)(2,1)}, u32[]{:S(2)}, u32[]{:S(2)}) %collective-permute-start.2) | collective-permute-done | bytes 524320 | tf_op jit(solution)/shard_map/ppermute | solution.py:27
  88.1 11.5 %conditional.23 = ((bf16[32,8192]{1,0:T(8,128)(2,1)S(1)}, bf16[2,4,32,8192]{3,2,1,0:T(8,128)(2,1)}, f32[2,4,32,8192]{3,2,1,0:T(8,128)})) conditional(s32[]{:T(128)} %convert_element_type.87, (bf16[32,8192]{1,0:T(8,128)(2,1)S(1)}, bf16[2,4,32,8192]{3,2,1,0:T(8,128)(2,1)}, f32[2,4,32,8192]{3,2,1,0:T(8,128)}) %tuple.147, (s32[]{:T(128)}, ...), branch_computations={%region_6.7_spmd, %region_7.8_spmd} | conditional | bytes 12296 | solution.py:334
  89.7 4.9 %branch_1_fun.54 = (bf16[32,8192]{1,0:T(8,128)(2,1)}, bf16[2,4,32,8192]{3,2,1,0:T(8,128)(2,1)}, f32[2,4,32,8192]{3,2,1,0:T(8,128)}) custom-call(s32[1]{0:T(128)} %bitcast.3.at_ref, s32[768]{0:T(1024)} %reshape.123.idx_ref, bf16[32,8192]{1,0:T(8,128)(2,1)S(1)} %get-tuple-element.447.h_ref, ...), custom_call_target="tpu_custom_call", output_to_operand_aliasing={{1}: (4, {}), {2}: (5, {})} | custom-call | tf_op jit(solution)/shard_map/cond/branch_1_fun/pallas_call | solution.py:118
  94.7 5.0 %branch_1_fun.55 = (bf16[32,8192]{1,0:T(8,128)(2,1)S(1)}, bf16[2,4,32,8192]{3,2,1,0:T(8,128)(2,1)}, f32[2,4,32,8192]{3,2,1,0:T(8,128)}) custom-call(s32[1]{0:T(128)} %bitcast.3.at_ref, s32[768]{0:T(1024)} %reshape.123.idx_ref, bf16[32,8192]{1,0:T(8,128)(2,1)} %get-tuple-element.451.h_ref, ...), custom_call_target="tpu_custom_call", output_to_operand_aliasing={{1}: (4, {}), {2}: (5, {})} | custom-call | tf_op jit(solution)/shard_map/cond/branch_1_fun/pallas_call | solution.py:118
  99.6 6.2 %collective-permute-start.3 = (bf16[32,8192]{1,0:T(8,128)(2,1)S(1)}, bf16[32,8192]{1,0:T(8,128)(2,1)}, u32[]{:S(2)}, u32[]{:S(2)}) collective-permute-start(bf16[32,8192]{1,0:T(8,128)(2,1)S(1)} %get-tuple-element.655), channel_id=1, source_target_pairs={{0,8},{8,16},{16,24},{1,9},{9,17},{17,25},{2,10},{10,18},{18,26},{... | collective-permute-start | bytes 1572872 | tf_op jit(solution)/shard_map/ppermute | solution.py:27
  108.4 6.0 %collective-permute-done.3 = bf16[32,8192]{1,0:T(8,128)(2,1)} collective-permute-done((bf16[32,8192]{1,0:T(8,128)(2,1)S(1)}, bf16[32,8192]{1,0:T(8,128)(2,1)}, u32[]{:S(2)}, u32[]{:S(2)}) %collective-permute-start.3) | collective-permute-done | bytes 524320 | tf_op jit(solution)/shard_map/ppermute | solution.py:27
  114.5 18.4 %collective-permute-start.4 = (bf16[32,8192]{1,0:T(8,128)(2,1)S(1)}, bf16[32,8192]{1,0:T(8,128)(2,1)}, u32[]{:S(2)}, u32[]{:S(2)}) collective-permute-start(bf16[32,8192]{1,0:T(8,128)(2,1)S(1)} %get-tuple-element.658), channel_id=1, source_target_pairs={{0,8},{8,16},{16,24},{1,9},{9,17},{17,25},{2,10},{10,18},{18,26},{... | collective-permute-start | bytes 1572872 | tf_op jit(solution)/shard_map/ppermute | solution.py:27
  135.4 5.4 %collective-permute-done.4 = bf16[32,8192]{1,0:T(8,128)(2,1)} collective-permute-done((bf16[32,8192]{1,0:T(8,128)(2,1)S(1)}, bf16[32,8192]{1,0:T(8,128)(2,1)}, u32[]{:S(2)}, u32[]{:S(2)}) %collective-permute-start.4) | collective-permute-done | bytes 524320 | tf_op jit(solution)/shard_map/ppermute | solution.py:27
  140.9 7.7 %collective-permute-start.5 = (bf16[32,8192]{1,0:T(8,128)(2,1)S(1)}, bf16[32,8192]{1,0:T(8,128)(2,1)}, u32[]{:S(2)}, u32[]{:S(2)}) collective-permute-start(bf16[32,8192]{1,0:T(8,128)(2,1)S(1)} %get-tuple-element.661), channel_id=1, source_target_pairs={{0,8},{8,16},{16,24},{1,9},{9,17},{17,25},{2,10},{10,18},{18,26},{... | collective-permute-start | bytes 1572872 | tf_op jit(solution)/shard_map/ppermute | solution.py:27
  151.4 4.3 %collective-permute-done.5 = bf16[32,8192]{1,0:T(8,128)(2,1)} collective-permute-done((bf16[32,8192]{1,0:T(8,128)(2,1)S(1)}, bf16[32,8192]{1,0:T(8,128)(2,1)}, u32[]{:S(2)}, u32[]{:S(2)}) %collective-permute-start.5) | collective-permute-done | bytes 524320 | tf_op jit(solution)/shard_map/ppermute | solution.py:27
  155.8 40.8 %collective-permute-start.6 = (bf16[32,8192]{1,0:T(8,128)(2,1)S(1)}, bf16[32,8192]{1,0:T(8,128)(2,1)}, u32[]{:S(2)}, u32[]{:S(2)}) collective-permute-start(bf16[32,8192]{1,0:T(8,128)(2,1)S(1)} %get-tuple-element.664), channel_id=1, source_target_pairs={{0,8},{8,16},{16,24},{1,9},{9,17},{17,25},{2,10},{10,18},{18,26},{... | collective-permute-start | bytes 1572872 | tf_op jit(solution)/shard_map/ppermute | solution.py:27
  196.6 6.4 %collective-permute-done.14 = bf16[32,8192]{1,0:T(8,128)(2,1)} collective-permute-done((bf16[32,8192]{1,0:T(8,128)(2,1)S(1)}, bf16[32,8192]{1,0:T(8,128)(2,1)}, u32[]{:S(2)}, u32[]{:S(2)}) %collective-permute-start.14) | collective-permute-done | bytes 524320 | tf_op jit(solution)/shard_map/ppermute | solution.py:27
  204.3 14.8 %conditional.36 = ((bf16[32,8192]{1,0:T(8,128)(2,1)S(1)}, bf16[2,4,32,8192]{3,2,1,0:T(8,128)(2,1)})) conditional(s32[]{:T(128)} %convert_element_type.94, (bf16[32,8192]{1,0:T(8,128)(2,1)S(1)}, bf16[2,4,32,8192]{3,2,1,0:T(8,128)(2,1)}) %tuple.172, (s32[]{:T(128)}, s32[256,3]{0,1:T(4,128)}, bf16[32,8192]{1,0:T(8,128)(2,1)S(1)}, ...), branch_computations={%region_32.33_spmd, %region_33.34_spmd} | conditional | bytes 12296 | solution.py:350
  206.0 7.2 %branch_1_fun.80 = (bf16[32,8192]{1,0:T(8,128)(2,1)}, bf16[2,4,32,8192]{3,2,1,0:T(8,128)(2,1)}) custom-call(s32[1]{0:T(128)} %bitcast.17.at_ref, s32[768]{0:T(1024)} %reshape.177.idx_ref, bf16[32,8192]{1,0:T(8,128)(2,1)S(1)} %get-tuple-element.561.g_ref, f32[2,4,32,8192]{3,2,1,0:T(8,128)} %get-tuple-element.562.sy_hbm, ...), custom_call_target="tpu_custom_call", output_to_operand_aliasing={{1}: (5, {})} | custom-call | tf_op jit(solution)/shard_map/cond/branch_1_fun/pallas_call | solution.py:185
  213.2 6.0 %branch_1_fun.81 = (bf16[32,8192]{1,0:T(8,128)(2,1)S(1)}, bf16[2,4,32,8192]{3,2,1,0:T(8,128)(2,1)}) custom-call(s32[1]{0:T(128)} %bitcast.17.at_ref, s32[768]{0:T(1024)} %reshape.177.idx_ref, bf16[32,8192]{1,0:T(8,128)(2,1)} %get-tuple-element.565.g_ref, f32[2,4,32,8192]{3,2,1,0:T(8,128)} %get-tuple-element.562.sy_hbm, ...), custom_call_target="tpu_custom_call", output_to_operand_aliasing={{1}: (5, {})} | custom-call | tf_op jit(solution)/shard_map/cond/branch_1_fun/pallas_call | solution.py:185
  220.5 8.0 %collective-permute-start.7 = (bf16[32,8192]{1,0:T(8,128)(2,1)S(1)}, bf16[32,8192]{1,0:T(8,128)(2,1)}, u32[]{:S(2)}, u32[]{:S(2)}) collective-permute-start(bf16[32,8192]{1,0:T(8,128)(2,1)S(1)} %get-tuple-element.667), channel_id=1, source_target_pairs={{0,8},{8,16},{16,24},{1,9},{9,17},{17,25},{2,10},{10,18},{18,26},{... | collective-permute-start | bytes 1572872 | tf_op jit(solution)/shard_map/ppermute | solution.py:27
  228.5 5.5 %collective-permute-done.15 = bf16[32,8192]{1,0:T(8,128)(2,1)} collective-permute-done((bf16[32,8192]{1,0:T(8,128)(2,1)S(1)}, bf16[32,8192]{1,0:T(8,128)(2,1)}, u32[]{:S(2)}, u32[]{:S(2)}) %collective-permute-start.15) | collective-permute-done | bytes 524320 | tf_op jit(solution)/shard_map/ppermute | solution.py:27
  236.1 15.9 %conditional.37 = ((bf16[32,8192]{1,0:T(8,128)(2,1)}, bf16[2,4,32,8192]{3,2,1,0:T(8,128)(2,1)})) conditional(s32[]{:T(128)} %convert_element_type.93, (bf16[32,8192]{1,0:T(8,128)(2,1)}, bf16[2,4,32,8192]{3,2,1,0:T(8,128)(2,1)}) %tuple.174, (s32[]{:T(128)}, s32[256,3]{0,1:T(4,128)}, bf16[32,8192]{1,0:T(8,128)(2,1)}, f32[2,4,32,8192]{3,2,1,0:T(8,128)}, ...), branch_computations={%region_34.35_spmd, %region_35.36_spmd} | conditional | bytes 12296 | solution.py:350
  237.7 7.5 %branch_1_fun.82 = (bf16[32,8192]{1,0:T(8,128)(2,1)}, bf16[2,4,32,8192]{3,2,1,0:T(8,128)(2,1)}) custom-call(s32[1]{0:T(128)} %bitcast.18.at_ref, s32[768]{0:T(1024)} %reshape.179.idx_ref, bf16[32,8192]{1,0:T(8,128)(2,1)} %get-tuple-element.569.g_ref, f32[2,4,32,8192]{3,2,1,0:T(8,128)} %get-tuple-element.570.sy_hbm, ...), custom_call_target="tpu_custom_call", output_to_operand_aliasing={{1}: (5, {})} | custom-call | tf_op jit(solution)/shard_map/cond/branch_1_fun/pallas_call | solution.py:185
  245.3 6.8 %branch_1_fun.83 = (bf16[32,8192]{1,0:T(8,128)(2,1)}, bf16[2,4,32,8192]{3,2,1,0:T(8,128)(2,1)}) custom-call(s32[1]{0:T(128)} %bitcast.18.at_ref, s32[768]{0:T(1024)} %reshape.179.idx_ref, bf16[32,8192]{1,0:T(8,128)(2,1)} %get-tuple-element.573.g_ref, f32[2,4,32,8192]{3,2,1,0:T(8,128)} %get-tuple-element.570.sy_hbm, ...), custom_call_target="tpu_custom_call", output_to_operand_aliasing={{1}: (5, {})} | custom-call | tf_op jit(solution)/shard_map/cond/branch_1_fun/pallas_call | solution.py:185
  253.5 19.0 %collective-permute-done.16 = bf16[32,8192]{1,0:T(8,128)(2,1)S(1)} collective-permute-done((bf16[32,8192]{1,0:T(8,128)(2,1)}, bf16[32,8192]{1,0:T(8,128)(2,1)S(1)}, u32[]{:S(2)}, u32[]{:S(2)}) %collective-permute-start.16) | collective-permute-done | bytes 524320 | tf_op jit(solution)/shard_map/ppermute | solution.py:27
  273.6 7.1 %collective-permute-start.8 = (bf16[32,8192]{1,0:T(8,128)(2,1)S(1)}, bf16[32,8192]{1,0:T(8,128)(2,1)}, u32[]{:S(2)}, u32[]{:S(2)}) collective-permute-start(bf16[32,8192]{1,0:T(8,128)(2,1)S(1)} %get-tuple-element.672), channel_id=1, source_target_pairs={{0,8},{8,16},{16,24},{1,9},{9,17},{17,25},{2,10},{10,18},{18,26},{... | collective-permute-start | bytes 1572872 | tf_op jit(solution)/shard_map/ppermute | solution.py:27
  280.6 14.8 %conditional.38 = ((bf16[32,8192]{1,0:T(8,128)(2,1)S(1)}, bf16[2,4,32,8192]{3,2,1,0:T(8,128)(2,1)})) conditional(s32[]{:T(128)} %convert_element_type.92, (bf16[32,8192]{1,0:T(8,128)(2,1)S(1)}, bf16[2,4,32,8192]{3,2,1,0:T(8,128)(2,1)}) %tuple.176, (s32[]{:T(128)}, s32[256,3]{0,1:T(4,128)}, bf16[32,8192]{1,0:T(8,128)(2,1)S(1)}, ...), branch_computations={%region_36.37_spmd.clone, %region_37.38_spmd.clone} | conditional | bytes 12296 | solution.py:350
  282.3 7.2 %branch_1_fun.86 = (bf16[32,8192]{1,0:T(8,128)(2,1)}, bf16[2,4,32,8192]{3,2,1,0:T(8,128)(2,1)}) custom-call(s32[1]{0:T(128)} %bitcast.55.at_ref, s32[768]{0:T(1024)} %reshape.199.idx_ref, bf16[32,8192]{1,0:T(8,128)(2,1)S(1)} %get-tuple-element.700.g_ref, f32[2,4,32,8192]{3,2,1,0:T(8,128)} %get-tuple-element.701.sy_hbm, ...), custom_call_target="tpu_custom_call", output_to_operand_aliasing={{1}: (5, {})} | custom-call | tf_op jit(solution)/shard_map/cond/branch_1_fun/pallas_call | solution.py:185
  289.4 6.0 %branch_1_fun.87 = (bf16[32,8192]{1,0:T(8,128)(2,1)S(1)}, bf16[2,4,32,8192]{3,2,1,0:T(8,128)(2,1)}) custom-call(s32[1]{0:T(128)} %bitcast.55.at_ref, s32[768]{0:T(1024)} %reshape.199.idx_ref, bf16[32,8192]{1,0:T(8,128)(2,1)} %get-tuple-element.704.g_ref, f32[2,4,32,8192]{3,2,1,0:T(8,128)} %get-tuple-element.701.sy_hbm, ...), custom_call_target="tpu_custom_call", output_to_operand_aliasing={{1}: (5, {})} | custom-call | tf_op jit(solution)/shard_map/cond/branch_1_fun/pallas_call | solution.py:185
  298.4 8.3 %collective-permute-done.17 = bf16[32,8192]{1,0:T(8,128)(2,1)} collective-permute-done((bf16[32,8192]{1,0:T(8,128)(2,1)S(1)}, bf16[32,8192]{1,0:T(8,128)(2,1)}, u32[]{:S(2)}, u32[]{:S(2)}) %collective-permute-start.17) | collective-permute-done | bytes 524320 | tf_op jit(solution)/shard_map/ppermute | solution.py:27
  306.7 17.3 %conditional.39 = (bf16[2,4,32,8192]{3,2,1,0:T(8,128)(2,1)}) conditional(s32[]{:T(128)} %convert_element_type.91, bf16[2,4,32,8192]{3,2,1,0:T(8,128)(2,1)} %get-tuple-element.690, (s32[]{:T(128)}, s32[256,3]{0,1:T(4,128)S(1)}, pred[]{:T(512)}, bf16[4,32,8192]{2,1,0:T(8,128)(2,1)}, bf16[32,8192]{1,0:T(8,128)(2,1)}, ...), branch_computations={%region_38.39_spmd, %region_39.40_spmd} | conditional | flops 262146 | bytes 1585189 | solution.py:350
  309.7 7.6 %branch_1_fun.84 = (bf16[32,8192]{1,0:T(8,128)(2,1)}, bf16[2,4,32,8192]{3,2,1,0:T(8,128)(2,1)}) custom-call(s32[1]{0:T(128)} %bitcast.19.at_ref, s32[768]{0:T(1024)} %reshape.183.idx_ref, bf16[32,8192]{1,0:T(8,128)(2,1)} %bitcast_select_fusion.1.g_ref, f32[2,4,32,8192]{3,2,1,0:T(8,128)} %get-tuple-element.592.sy_hbm, ...), custom_call_target="tpu_custom_call", output_to_operand_aliasing={{1}: (5, {})} | custom-call | tf_op jit(solution)/shard_map/cond/branch_1_fun/pallas_call | solution.py:185
  317.3 6.8 %branch_1_fun.85 = (bf16[32,8192]{1,0:T(8,128)(2,1)}, bf16[2,4,32,8192]{3,2,1,0:T(8,128)(2,1)}) custom-call(s32[1]{0:T(128)} %bitcast.19.at_ref, s32[768]{0:T(1024)} %reshape.183.idx_ref, bf16[32,8192]{1,0:T(8,128)(2,1)} %get-tuple-element.595.g_ref, f32[2,4,32,8192]{3,2,1,0:T(8,128)} %get-tuple-element.592.sy_hbm, ...), custom_call_target="tpu_custom_call", output_to_operand_aliasing={{1}: (5, {})} | custom-call | tf_op jit(solution)/shard_map/cond/branch_1_fun/pallas_call | solution.py:185
  324.1 7.8 %shard_map.47 = bf16[4,32,128,128]{3,2,1,0:T(8,128)(2,1)} custom-call(s32[1]{0:T(128)} %bitcast.45.sel_ref, s32[768]{0:T(1024)} %reshape.192.idx_ref, bf16[2,4,32,8192]{3,2,1,0:T(8,128)(2,1)} %get-tuple-element.673.h_ref, bf16[2,4,32,8192]{3,2,1,0:T(8,128)(2,1)} %get-tuple-element.946.s_ref), custom_call_target="tpu_custom_call" | custom-call | tf_op jit(solution)/shard_map/pallas_call | solution.py:269
  331.9 10.1 %shard_map.46 = f32[4,32,128,128]{3,2,1,0:T(8,128)} custom-call(s32[1]{0:T(128)} %bitcast.21.sel_ref, s32[768]{0:T(1024)} %reshape.192.idx_ref, bf16[2,4,32,8192]{3,2,1,0:T(8,128)(2,1)} %get-tuple-element.673.h_ref, bf16[2,4,32,8192]{3,2,1,0:T(8,128)(2,1)} %get-tuple-element.946.s_ref), custom_call_target="tpu_custom_call" | custom-call | tf_op jit(solution)/shard_map/pallas_call | solution.py:269
  341.9 13.6 %fusion.2 = (f32[2,32,128,128]{3,2,1,0:T(8,128)}, bf16[2,32,128,128]{3,2,1,0:T(8,128)(2,1)S(1)}) fusion(f32[2,2,32,128,128]{4,3,2,1,0:T(8,128)} %bitcast.96, s32[]{:T(128)S(6)} %select_n.237, s32[]{:T(128)S(6)} %select_n.235, bf16[2,2,32,128,128]{4,3,2,1,0:T(8,128)(2,1)} %bitcast.46, pred[]{:T(512)S(6)} %eq.8, s32[]{:T(128)S(6)} %select_n.243, s32[]{:T(128)S(6)} %select_n.242), kind=kLoop, calls=%fused_computation.6 | loop fusion | flops 9437184 | bytes 31457296 | tf_op jit(solution)/shard_map/add | solution.py:304
  355.6 26.1 %collective-permute-done.19 = bf16[2,32,128,128]{3,2,1,0:T(8,128)(2,1)} collective-permute-done((bf16[2,32,128,128]{3,2,1,0:T(8,128)(2,1)S(1)}, bf16[2,32,128,128]{3,2,1,0:T(8,128)(2,1)}, u32[]{:S(2)}, u32[]{:S(2)}) %collective-permute-start.19) | collective-permute-done | bytes 2097184 | tf_op jit(solution)/shard_map/ppermute | solution.py:279
  385.8 14.8 %collective-permute-done.20 = bf16[32,128,128]{2,1,0:T(8,128)(2,1)S(1)} collective-permute-done((bf16[32,128,128]{2,1,0:T(8,128)(2,1)S(1)}, bf16[32,128,128]{2,1,0:T(8,128)(2,1)S(1)}, u32[]{:S(2)}, u32[]{:S(2)}) %collective-permute-start.20) | collective-permute-done | bytes 1048608 | tf_op jit(solution)/shard_map/ppermute | solution.py:279
  (84 shorter events, 58.9 us)
Async XLA Ops:
  19.4 13.4 %collective-permute-start = (bf16[32,8192]{1,0:T(8,128)(2,1)S(1)}, bf16[32,8192]{1,0:T(8,128)(2,1)}, u32[]{:S(2)}, u32[]{:S(2)}) collective-permute-start(bf16[32,8192]{1,0:T(8,128)(2,1)S(1)} %get-tuple-element.646), channel_id=1, source_target_pairs={{0,8},{8,16},{16,24},{1,9},{9,17},{17,25},{2,10},{10,18},{18,26},{... | collective-permute-start | bytes 1572872 | tf_op jit(solution)/shard_map/ppermute | solution.py:27
  22.6 10.2 %copy-start.2 = (bf16[2,64,8192]{2,1,0:T(8,128)(2,1)S(1)}, bf16[2,64,8192]{2,1,0:T(8,128)(2,1)}, u32[]{:S(2)}) copy-start(bf16[2,64,8192]{2,1,0:T(8,128)(2,1)} %param.44) | copy-start | bytes 6291460
  25.1 25.4 %collective-permute-start.9 = (bf16[32,8192]{1,0:T(8,128)(2,1)S(1)}, bf16[32,8192]{1,0:T(8,128)(2,1)}, u32[]{:S(2)}, u32[]{:S(2)}) collective-permute-start(bf16[32,8192]{1,0:T(8,128)(2,1)S(1)} %get-tuple-element.674), channel_id=1, source_target_pairs={{8,0},{16,8},{24,16},{9,1},{17,9},{25,17},{10,2},{18,10},{26,18},{... | collective-permute-start | bytes 1572872 | tf_op jit(solution)/shard_map/ppermute | solution.py:27
  44.4 16.5 %collective-permute-start.1 = (bf16[32,8192]{1,0:T(8,128)(2,1)S(1)}, bf16[32,8192]{1,0:T(8,128)(2,1)}, u32[]{:S(2)}, u32[]{:S(2)}) collective-permute-start(bf16[32,8192]{1,0:T(8,128)(2,1)S(1)} %get-tuple-element.649), channel_id=1, source_target_pairs={{0,8},{8,16},{16,24},{1,9},{9,17},{17,25},{2,10},{10,18},{18,26},{... | collective-permute-start | bytes 1572872 | tf_op jit(solution)/shard_map/ppermute | solution.py:27
  51.7 26.8 %collective-permute-start.10 = (bf16[32,8192]{1,0:T(8,128)(2,1)S(1)}, bf16[32,8192]{1,0:T(8,128)(2,1)}, u32[]{:S(2)}, u32[]{:S(2)}) collective-permute-start(bf16[32,8192]{1,0:T(8,128)(2,1)S(1)} %get-tuple-element.676), channel_id=1, source_target_pairs={{8,0},{16,8},{24,16},{9,1},{17,9},{25,17},{10,2},{18,10},{26,18},{... | collective-permute-start | bytes 1572872 | tf_op jit(solution)/shard_map/ppermute | solution.py:27
  72.5 15.5 %collective-permute-start.2 = (bf16[32,8192]{1,0:T(8,128)(2,1)S(1)}, bf16[32,8192]{1,0:T(8,128)(2,1)}, u32[]{:S(2)}, u32[]{:S(2)}) collective-permute-start(bf16[32,8192]{1,0:T(8,128)(2,1)S(1)} %get-tuple-element.652), channel_id=1, source_target_pairs={{0,8},{8,16},{16,24},{1,9},{9,17},{17,25},{2,10},{10,18},{18,26},{... | collective-permute-start | bytes 1572872 | tf_op jit(solution)/shard_map/ppermute | solution.py:27
  79.8 26.0 %collective-permute-start.11 = (bf16[32,8192]{1,0:T(8,128)(2,1)S(1)}, bf16[32,8192]{1,0:T(8,128)(2,1)}, u32[]{:S(2)}, u32[]{:S(2)}) collective-permute-start(bf16[32,8192]{1,0:T(8,128)(2,1)S(1)} %get-tuple-element.678), channel_id=1, source_target_pairs={{8,0},{16,8},{24,16},{9,1},{17,9},{25,17},{10,2},{18,10},{26,18},{... | collective-permute-start | bytes 1572872 | tf_op jit(solution)/shard_map/ppermute | solution.py:27
  99.6 14.8 %collective-permute-start.3 = (bf16[32,8192]{1,0:T(8,128)(2,1)S(1)}, bf16[32,8192]{1,0:T(8,128)(2,1)}, u32[]{:S(2)}, u32[]{:S(2)}) collective-permute-start(bf16[32,8192]{1,0:T(8,128)(2,1)S(1)} %get-tuple-element.655), channel_id=1, source_target_pairs={{0,8},{8,16},{16,24},{1,9},{9,17},{17,25},{2,10},{10,18},{18,26},{... | collective-permute-start | bytes 1572872 | tf_op jit(solution)/shard_map/ppermute | solution.py:27
  107.1 25.8 %collective-permute-start.12 = (bf16[32,8192]{1,0:T(8,128)(2,1)S(1)}, bf16[32,8192]{1,0:T(8,128)(2,1)}, u32[]{:S(2)}, u32[]{:S(2)}) collective-permute-start(bf16[32,8192]{1,0:T(8,128)(2,1)S(1)} %get-tuple-element.680), channel_id=1, source_target_pairs={{8,0},{16,8},{24,16},{9,1},{17,9},{25,17},{10,2},{18,10},{26,18},{... | collective-permute-start | bytes 1572872 | tf_op jit(solution)/shard_map/ppermute | solution.py:27
  114.5 26.3 %collective-permute-start.4 = (bf16[32,8192]{1,0:T(8,128)(2,1)S(1)}, bf16[32,8192]{1,0:T(8,128)(2,1)}, u32[]{:S(2)}, u32[]{:S(2)}) collective-permute-start(bf16[32,8192]{1,0:T(8,128)(2,1)S(1)} %get-tuple-element.658), channel_id=1, source_target_pairs={{0,8},{8,16},{16,24},{1,9},{9,17},{17,25},{2,10},{10,18},{18,26},{... | collective-permute-start | bytes 1572872 | tf_op jit(solution)/shard_map/ppermute | solution.py:27
  134.1 14.5 %collective-permute-start.13 = (bf16[32,8192]{1,0:T(8,128)(2,1)S(1)}, bf16[32,8192]{1,0:T(8,128)(2,1)}, u32[]{:S(2)}, u32[]{:S(2)}) collective-permute-start(bf16[32,8192]{1,0:T(8,128)(2,1)S(1)} %get-tuple-element.682), channel_id=1, source_target_pairs={{8,0},{16,8},{24,16},{9,1},{17,9},{25,17},{10,2},{18,10},{26,18},{... | collective-permute-start | bytes 1572872 | tf_op jit(solution)/shard_map/ppermute | solution.py:27
  140.9 14.8 %collective-permute-start.5 = (bf16[32,8192]{1,0:T(8,128)(2,1)S(1)}, bf16[32,8192]{1,0:T(8,128)(2,1)}, u32[]{:S(2)}, u32[]{:S(2)}) collective-permute-start(bf16[32,8192]{1,0:T(8,128)(2,1)S(1)} %get-tuple-element.661), channel_id=1, source_target_pairs={{0,8},{8,16},{16,24},{1,9},{9,17},{17,25},{2,10},{10,18},{18,26},{... | collective-permute-start | bytes 1572872 | tf_op jit(solution)/shard_map/ppermute | solution.py:27
  150.1 53.0 %collective-permute-start.14 = (bf16[32,8192]{1,0:T(8,128)(2,1)S(1)}, bf16[32,8192]{1,0:T(8,128)(2,1)}, u32[]{:S(2)}, u32[]{:S(2)}) collective-permute-start(bf16[32,8192]{1,0:T(8,128)(2,1)S(1)} %get-tuple-element.684), channel_id=1, source_target_pairs={{8,0},{16,8},{24,16},{9,1},{17,9},{25,17},{10,2},{18,10},{26,18},{... | collective-permute-start | bytes 1572872 | tf_op jit(solution)/shard_map/ppermute | solution.py:27
  155.8 64.7 %collective-permute-start.6 = (bf16[32,8192]{1,0:T(8,128)(2,1)S(1)}, bf16[32,8192]{1,0:T(8,128)(2,1)}, u32[]{:S(2)}, u32[]{:S(2)}) collective-permute-start(bf16[32,8192]{1,0:T(8,128)(2,1)S(1)} %get-tuple-element.664), channel_id=1, source_target_pairs={{0,8},{8,16},{16,24},{1,9},{9,17},{17,25},{2,10},{10,18},{18,26},{... | collective-permute-start | bytes 1572872 | tf_op jit(solution)/shard_map/ppermute | solution.py:27
  219.1 14.9 %collective-permute-start.15 = (bf16[32,8192]{1,0:T(8,128)(2,1)S(1)}, bf16[32,8192]{1,0:T(8,128)(2,1)}, u32[]{:S(2)}, u32[]{:S(2)}) collective-permute-start(bf16[32,8192]{1,0:T(8,128)(2,1)S(1)} %get-tuple-element.686), channel_id=1, source_target_pairs={{8,0},{16,8},{24,16},{9,1},{17,9},{25,17},{10,2},{18,10},{26,18},{... | collective-permute-start | bytes 1572872 | tf_op jit(solution)/shard_map/ppermute | solution.py:27
  220.5 32.8 %collective-permute-start.7 = (bf16[32,8192]{1,0:T(8,128)(2,1)S(1)}, bf16[32,8192]{1,0:T(8,128)(2,1)}, u32[]{:S(2)}, u32[]{:S(2)}) collective-permute-start(bf16[32,8192]{1,0:T(8,128)(2,1)S(1)} %get-tuple-element.667), channel_id=1, source_target_pairs={{0,8},{8,16},{16,24},{1,9},{9,17},{17,25},{2,10},{10,18},{18,26},{... | collective-permute-start | bytes 1572872 | tf_op jit(solution)/shard_map/ppermute | solution.py:27
  252.1 20.4 %collective-permute-start.16 = (bf16[32,8192]{1,0:T(8,128)(2,1)}, bf16[32,8192]{1,0:T(8,128)(2,1)S(1)}, u32[]{:S(2)}, u32[]{:S(2)}) collective-permute-start(bf16[32,8192]{1,0:T(8,128)(2,1)} %get-tuple-element.688), channel_id=1, source_target_pairs={{8,0},{16,8},{24,16},{9,1},{17,9},{25,17},{10,2},{18,10},{26,18},{... | collective-permute-start | bytes 1572872 | tf_op jit(solution)/shard_map/ppermute | solution.py:27
  273.5 24.8 %copy-start.3 = (s32[256,3]{0,1:T(4,128)S(1)}, s32[256,3]{0,1:T(4,128)}, u32[]{:S(2)}) copy-start(s32[256,3]{0,1:T(4,128)} %param.47) | copy-start | bytes 9220
  273.6 24.8 %collective-permute-start.8 = (bf16[32,8192]{1,0:T(8,128)(2,1)S(1)}, bf16[32,8192]{1,0:T(8,128)(2,1)}, u32[]{:S(2)}, u32[]{:S(2)}) collective-permute-start(bf16[32,8192]{1,0:T(8,128)(2,1)S(1)} %get-tuple-element.672), channel_id=1, source_target_pairs={{0,8},{8,16},{16,24},{1,9},{9,17},{17,25},{2,10},{10,18},{18,26},{... | collective-permute-start | bytes 1572872 | tf_op jit(solution)/shard_map/ppermute | solution.py:27
  295.4 11.3 %collective-permute-start.17 = (bf16[32,8192]{1,0:T(8,128)(2,1)S(1)}, bf16[32,8192]{1,0:T(8,128)(2,1)}, u32[]{:S(2)}, u32[]{:S(2)}) collective-permute-start(bf16[32,8192]{1,0:T(8,128)(2,1)S(1)} %get-tuple-element.691), channel_id=1, source_target_pairs={{8,0},{16,8},{24,16},{9,1},{17,9},{25,17},{10,2},{18,10},{26,18},{... | collective-permute-start | bytes 1572872 | tf_op jit(solution)/shard_map/ppermute | solution.py:27
  331.9 10.1 %collective-permute-start.18 = (bf16[4,32,128,128]{3,2,1,0:T(8,128)(2,1)}, bf16[4,32,128,128]{3,2,1,0:T(8,128)(2,1)}, u32[]{:S(2)}, u32[]{:S(2)}) collective-permute-start(bf16[4,32,128,128]{3,2,1,0:T(8,128)(2,1)} %shard_map.47), channel_id=1, source_target_pairs={{0,1},{1,0},{2,3},{3,2},{4,5},{5,4},{6,7},{7,6},{8,9},{9,8},{10,11... | collective-permute-start | bytes 12582920 | tf_op jit(solution)/shard_map/ppermute | solution.py:293
  355.5 26.1 %collective-permute-start.19 = (bf16[2,32,128,128]{3,2,1,0:T(8,128)(2,1)S(1)}, bf16[2,32,128,128]{3,2,1,0:T(8,128)(2,1)}, u32[]{:S(2)}, u32[]{:S(2)}) collective-permute-start(bf16[2,32,128,128]{3,2,1,0:T(8,128)(2,1)S(1)} %get-tuple-element.832), channel_id=1, source_target_pairs={{0,2},{1,5},{2,0},{3,7},{4,6},{5,1},{6,4},{7,3},{8,10},{9,13},{10,... | collective-permute-start | bytes 6291464 | tf_op jit(solution)/shard_map/ppermute | solution.py:279
  355.5 28.3 %copy-start = (f32[2,32,128,128]{3,2,1,0:T(8,128)S(1)}, f32[2,32,128,128]{3,2,1,0:T(8,128)}, u32[]{:S(2)}) copy-start(f32[2,32,128,128]{3,2,1,0:T(8,128)} %get-tuple-element.831) | copy-start | bytes 12582916
  383.8 2.0 copy-start.1
  385.8 14.8 %collective-permute-start.20 = (bf16[32,128,128]{2,1,0:T(8,128)(2,1)S(1)}, bf16[32,128,128]{2,1,0:T(8,128)(2,1)S(1)}, u32[]{:S(2)}, u32[]{:S(2)}) collective-permute-start(bf16[32,128,128]{2,1,0:T(8,128)(2,1)S(1)} %fusion.3), channel_id=1, source_target_pairs={{0,4},{1,3},{2,6},{3,1},{4,0},{5,7},{6,2},{7,5},{8,12},{9,11},{10,... | collective-permute-start | bytes 3145736 | tf_op jit(solution)/shard_map/ppermute | solution.py:279
where the time goes:
time: 408 us; the launch traced here: 405 us
  waiting for transfers between devices  117 us (29%)
  starting transfers between devices  114 us (28%)
  Pallas kernels  113 us (28%)
  other arithmetic  35.6 us (9%)
  local copies, waits for them, and re-layouts  24.7 us (6%)
    ppermute x18, starting transfers between devices, shifted(): lax.ppermute(value, axis, [(source, source + steps) for source in range(l...  114 us
    ppermute x18, waiting for transfers between devices, shifted(): lax.ppermute(value, axis, [(source, source + steps) for source in range(l...  76.1 us
    pallas_call x8, Pallas kernels, layer_backward(): pl.pallas_call(functools.partial(_bwd_kernel, layer * KMAX, layer), out_s...  55 us
    ppermute x2, waiting for transfers between devices, _exchange(): lax.ppermute(send.astype(jnp.bfloat16), 'dp', pairs).astype(jnp.float32)  40.9 us
    pallas_call x8, Pallas kernels, layer_forward(): pl.pallas_call(functools.partial(_fwd_kernel, layer * KMAX, layer), out_s...  39.7 us
    pallas_call x2, Pallas kernels, dw_half(): pl.pallas_call(_dw_half_kernel, out_shape=jax.ShapeDtypeStruct((4, per, B...  17.9 us
    select_n x10, other arithmetic, tick_body(): grad_in = jnp.where(me_segment == segments - 1, top, recv_b)  13.8 us
    add x1, other arithmetic, weight_grads(): keep2 = half(keep, d1, d2) + half(got, d1, d2)  13.6 us
  transfers between devices with their start and end apart: 21, of which 12 were waited for; matrix products, arithmetic and copies ran while one was open for 6% of the time, Pallas kernels for 20%

commit v1 on v0

--- a/solution.py
+++ b/solution.py
@@ -81,11 +81,30 @@
     lax.fori_loop(0, len(copies[1]), chunk, 0)
 
 
-def _fwd_kernel(base, layer, at_ref, idx_ref, h_ref, w_hbm, sh_in, sy_in, hout_ref, sh_ref, sy_ref, w_vmem, y_vmem, sems, io_sems):
+def _pick_input(at, src_ref, local_hbm, h_ref, sem):
+    @pl.when(at[1] > 0)
+    def _():
+        pltpu.make_async_copy(local_hbm.at[at[0]], h_ref, sem).start()
+
+    @pl.when(at[1] <= 0)
+    def _():
+        pltpu.make_async_copy(src_ref, h_ref, sem).start()
+
+    pltpu.make_async_copy(src_ref, h_ref, sem).wait()
+
+
+def _fwd_kernel(base, layer, at_ref, idx_ref, h_in, w_hbm, sh_in, sy_in, *rest):
+    if layer == 0:
+        local_hbm, hout_ref, sh_ref, sy_ref, w_vmem, y_vmem, sems, io_sems, h_ref = rest
+    else:
+        hout_ref, sh_ref, sy_ref, w_vmem, y_vmem, sems, io_sems = rest
+        h_ref = h_in
     del sh_in, sy_in
     width = h_ref.shape[1]
     at = at_ref[0]
     copies = _w_copies(w_hbm, base, w_vmem, sems)
+    if layer == 0:
+        _pick_input((at, at_ref[1]), h_in, local_hbm, h_ref, io_sems.at[2])
     save_h = pltpu.make_async_copy(h_ref, sh_ref.at[layer, at], io_sems.at[0])
     save_h.start()
     y_vmem[...] = jnp.zeros_like(y_vmem)
@@ -113,8 +132,13 @@
     save_y.wait()
 
 
-def layer_forward(h, weights, layer, block_index, at, stash_h, stash_y):
+def layer_forward(h, weights, layer, block_index, at, stash_h, stash_y, local=None, use_local=None):
     rows, width = h.shape
+    extra_in, extra_args, extra_scratch = [], [], []
+    if layer == 0:
+        extra_in, extra_args = [_ANY], [local]
+        extra_scratch = [pltpu.VMEM((rows, width), h.dtype)]
+        at = jnp.stack([at, use_local.astype(jnp.int32)])
     return pl.pallas_call(
         functools.partial(_fwd_kernel, layer * KMAX, layer),
         out_shape=(
@@ -122,23 +146,31 @@
             jax.ShapeDtypeStruct(stash_h.shape, stash_h.dtype),
             jax.ShapeDtypeStruct(stash_y.shape, stash_y.dtype),
         ),
-        in_specs=[_SMEM, _SMEM, _VMEM, _ANY, _ANY, _ANY],
+        in_specs=[_SMEM, _SMEM, _VMEM, _ANY, _ANY, _ANY] + extra_in,
         out_specs=(_VMEM, _ANY, _ANY),
         scratch_shapes=[
             pltpu.VMEM((KMAX, BLK, BLK), weights.dtype),
             pltpu.VMEM((rows, width), jnp.float32),
             pltpu.SemaphoreType.DMA((KMAX // NSUB,)),
-            pltpu.SemaphoreType.DMA((2,)),
-        ],
+            pltpu.SemaphoreType.DMA((3,)),
+        ]
+        + extra_scratch,
         input_output_aliases={4: 1, 5: 2},
         compiler_params=pltpu.CompilerParams(vmem_limit_bytes=VMEM_LIMIT),
-    )(at.reshape(1), block_index.reshape(-1), h, weights, stash_h, stash_y)
-
-
-def _bwd_kernel(base, layer, at_ref, idx_ref, g_ref, sy_hbm, w_hbm, ss_in, gout_ref, ss_ref, y_vmem, s_vmem, sp_ref, w_vmem, sems, io_sems):
+    )(at.reshape(-1), block_index.reshape(-1), h, weights, stash_h, stash_y, *extra_args)
+
+
+def _bwd_kernel(base, layer, entry, at_ref, idx_ref, g_in, sy_hbm, w_hbm, ss_in, *rest):
+    if entry:
+        local_hbm, gout_ref, ss_ref, y_vmem, s_vmem, sp_ref, w_vmem, sems, io_sems, g_ref = rest
+    else:
+        gout_ref, ss_ref, y_vmem, s_vmem, sp_ref, w_vmem, sems, io_sems = rest
+        g_ref = g_in
     del ss_in
     width = g_ref.shape[1]
     at = at_ref[0]
+    if entry:
+        _pick_input((at, at_ref[1]), g_in, local_hbm, g_ref, io_sems.at[2])
     load_y = pltpu.make_async_copy(sy_hbm.at[layer, at], y_vmem, io_sems.at[0])
     load_y.start()
     copies = _w_copies(w_hbm, base, w_vmem, sems)
@@ -180,15 +212,21 @@
     save_s.wait()
 
 
-def layer_backward(g, stash_y, weights, layer, block_index, at, stash_s):
+def layer_backward(g, stash_y, weights, layer, block_index, at, stash_s, local=None, use_local=None):
     rows, width = g.shape
+    entry = local is not None
+    extra_in, extra_args, extra_scratch = [], [], []
+    if entry:
+        extra_in, extra_args = [_ANY], [local]
+        extra_scratch = [pltpu.VMEM((rows, width), g.dtype)]
+        at = jnp.stack([at, use_local.astype(jnp.int32)])
     return pl.pallas_call(
-        functools.partial(_bwd_kernel, layer * KMAX, layer),
+        functools.partial(_bwd_kernel, layer * KMAX, layer, entry),
         out_shape=(
             jax.ShapeDtypeStruct((rows, width), jnp.bfloat16),
             jax.ShapeDtypeStruct(stash_s.shape, stash_s.dtype),
         ),
-        in_specs=[_SMEM, _SMEM, _VMEM, _ANY, _ANY, _ANY],
+        in_specs=[_SMEM, _SMEM, _VMEM, _ANY, _ANY, _ANY] + extra_in,
         out_specs=(_VMEM, _ANY),
         scratch_shapes=[
             pltpu.VMEM((rows, width), jnp.float32),
@@ -196,11 +234,12 @@
             pltpu.VMEM((rows, width), jnp.float32),
             pltpu.VMEM((KMAX, BLK, BLK), weights.dtype),
             pltpu.SemaphoreType.DMA((KMAX // NSUB,)),
-            pltpu.SemaphoreType.DMA((2,)),
-        ],
+            pltpu.SemaphoreType.DMA((3,)),
+        ]
+        + extra_scratch,
         input_output_aliases={5: 1},
         compiler_params=pltpu.CompilerParams(vmem_limit_bytes=VMEM_LIMIT),
-    )(at.reshape(1), block_index.reshape(-1), g, stash_y, weights, stash_s)
+    )(at.reshape(-1), block_index.reshape(-1), g, stash_y, weights, stash_s, *extra_args)
 
 
 def _dw_kernel(mbs, idx_ref, h_ref, s_ref, dw_ref):
@@ -301,11 +340,10 @@
 
     send = half(keep, 1 - d1, 1 - d2) + half(got, 1 - d1, 1 - d2)
     got2 = _exchange(send, [(i, i ^ (2 if i % 2 == 0 else 4)) for i in range(8)])
-    keep2 = half(keep, d1, d2) + half(got, d1, d2)
+    keep2 = half(keep, d1, d2) + half(got, d1, d2) + got2
     rem = jnp.where(core0, d2, d1)
-    send = pick(keep2, 1 - rem, 0) + pick(got2, 1 - rem, 0)
-    got3 = _exchange(send, [(i, i ^ (4 if i % 2 == 0 else 2)) for i in range(8)])
-    return pick(keep2, rem, 0) + pick(got2, rem, 0) + got3
+    got3 = _exchange(pick(keep2, 1 - rem, 0), [(i, i ^ (4 if i % 2 == 0 else 2)) for i in range(8)])
+    return pick(keep2, rem, 0) + got3
 
 
 def on_device(x_in, cotangent, weights, block_index):
@@ -322,32 +360,29 @@
         micro_f = tick - me_segment
         live_f = (micro_f >= 0) & (micro_f < mbs)
         at_f = jnp.clip(micro_f, 0, mbs - 1)
-        first = lax.dynamic_index_in_dim(x_in, at_f, 0, keepdims=False)
-        start = jnp.where(me_segment == 0, first, recv_f)
-
         def run_f(operands):
             h, sh, sy = operands
             for layer in range(LSLOT):
-                h, sh, sy = layer_forward(h, weights, layer, block_index, at_f, sh, sy)
+                local = (x_in, me_segment == 0) if layer == 0 else (None, None)
+                h, sh, sy = layer_forward(h, weights, layer, block_index, at_f, sh, sy, *local)
             return (h, sh, sy)
 
-        h_out, saved_h, saved_y = lax.cond(live_f, run_f, lambda ops: ops, (start, saved_h, saved_y))
+        h_out, saved_h, saved_y = lax.cond(live_f, run_f, lambda ops: ops, (recv_f, saved_h, saved_y))
         send_f = shifted(h_out, "segment", 1)
 
         micro_b = tick - (2 * segments - 2 - me_segment)
         live_b = (micro_b >= 0) & (micro_b < mbs)
         at_b = jnp.clip(micro_b, 0, mbs - 1)
-        top = lax.dynamic_index_in_dim(cotangent, at_b, 0, keepdims=False)
-        grad_in = jnp.where(me_segment == segments - 1, top, recv_b)
         stash_y_now = saved_y
 
         def run_b(operands):
             grad, ss = operands
             for layer in reversed(range(LSLOT)):
-                grad, ss = layer_backward(grad, stash_y_now, weights, layer, block_index, at_b, ss)
+                local = (cotangent, me_segment == segments - 1) if layer == LSLOT - 1 else (None, None)
+                grad, ss = layer_backward(grad, stash_y_now, weights, layer, block_index, at_b, ss, *local)
             return (grad, ss)
 
-        grad_out, saved_s = lax.cond(live_b, run_b, lambda ops: ops, (grad_in, saved_s))
+        grad_out, saved_s = lax.cond(live_b, run_b, lambda ops: ops, (recv_b, saved_s))
         send_b = shifted(grad_out, "segment", -1)
         return (send_f, send_b, saved_h, saved_y, saved_s)
 

time: 408 us -> 380 us (0.931)
  other arithmetic: 35.6 us -> 21.1 us
  starting transfers between devices: 114 us -> 100 us
  Pallas kernels: 113 us -> 106 us
    select_n x19 -> x0, other arithmetic: 15.4 us -> none  [the longest x10 13.8 us: tick_body(): grad_in = jnp.where(me_segment == segments - 1, top, recv_b)]
    ppermute x18, starting transfers between devices: 114 us -> 100 us  [shifted(): lax.ppermute(value, axis, [(source, source + steps) for source in range(l...]
    add x2, other arithmetic: 17.8 us -> 10.1 us  [the longest x1 6.88 us: weight_grads(): keep2 = half(keep, d1, d2) + half(got, d1, d2) + got2]
    pallas_call x8, Pallas kernels: 55 us -> 49 us  [layer_backward(): pl.pallas_call(functools.partial(_bwd_kernel, layer * KMAX, layer, entry)...]
    convert_element_type x1, other arithmetic: 0.34 us -> 5.97 us  [_exchange(): send.astype(jnp.bfloat16)]
    another operation x0 -> x8, other arithmetic: none -> 4.96 us  [the longest x4 2.52 us: layer_backward(): at = jnp.stack([at, use_local.astype(jnp.int32)])]
  transfers between devices with their start and end apart: 21 -> 21, of which waited for: 12 -> 12; matrix products, arithmetic and copies ran while one was open for 6% -> 5% of each run, Pallas kernels for 20% -> 20%
where the time goes in v1:
time: 380 us; the launch traced here: 375 us
  waiting for transfers between devices  118 us (31%)
  Pallas kernels  106 us (28%)
  starting transfers between devices  100 us (26%)
  local copies, waits for them, and re-layouts  28.6 us (8%)
  other arithmetic  21.1 us (6%)
    ppermute x18, starting transfers between devices, shifted(): lax.ppermute(value, axis, [(source, source + steps) for source in range(l...  100 us
    ppermute x18, waiting for transfers between devices, shifted(): lax.ppermute(value, axis, [(source, source + steps) for source in range(l...  77.6 us
    pallas_call x8, Pallas kernels, layer_backward(): pl.pallas_call(functools.partial(_bwd_kernel, layer * KMAX, layer, entry)...  49 us
    pallas_call x8, Pallas kernels, layer_forward(): pl.pallas_call(functools.partial(_fwd_kernel, layer * KMAX, layer), out_s...  41.1 us
    ppermute x2, waiting for transfers between devices, _exchange(): lax.ppermute(send.astype(jnp.bfloat16), 'dp', pairs).astype(jnp.float32)  40.9 us
    pallas_call x2, Pallas kernels, dw_half(): pl.pallas_call(_dw_half_kernel, out_shape=jax.ShapeDtypeStruct((4, per, B...  15.5 us
    another operation x10, local copies, waits for them, and re-layouts  10.8 us
  transfers between devices with their start and end apart: 21, of which 12 were waited for; matrix products, arithmetic and copies ran while one was open for 5% of the time, Pallas kernels for 20%

profile of v1, /device:TPU:0, one launch (start us, length us, event | category | flops | bytes accessed | tf_op | source)
XLA Modules:
  0.0 374.7 jit_solution(6454752789041550006)
XLA Ops:
  0.0 20.4 %conditional.20 = ((bf16[32,8192]{1,0:T(8,128)(2,1)}, bf16[2,4,32,8192]{3,2,1,0:T(8,128)(2,1)}, f32[2,4,32,8192]{3,2,1,0:T(8,128)})) conditional(s32[]{:T(128)} %convert_element_type.111, () %tuple.135, (s32[]{:T(128)}, s32[256,3]{0,1:T(4,128)}, s32[]{:T(128)}, bf16[256,128,128]{2,1,0:T(8,128)(2,1)}, bf16[4,32,8192]{2,1,0:T(8,128)(2,1)}) %tuple.276), branch_computations={%region_0.1_spmd, %region_1.2_spmd} | conditional | flops 6 | bytes 21508194 | solution.py:370
  9.8 5.3 %branch_1_fun.42 = (bf16[32,8192]{1,0:T(8,128)(2,1)}, bf16[2,4,32,8192]{3,2,1,0:T(8,128)(2,1)}, f32[2,4,32,8192]{3,2,1,0:T(8,128)}) custom-call(s32[2]{0:T(128)} %pad_add_fusion.at_ref, s32[768]{0:T(1024)} %reshape.94.idx_ref, bf16[32,8192]{1,0:T(8,128)(2,1)} %broadcast_in_dim.14.h_in, ...), custom_call_target="tpu_custom_call", output_to_operand_aliasing={{1}: (4, {}), {2}: (5, {})} | custom-call | tf_op jit(solution)/shard_map/cond/branch_1_fun/pallas_call | solution.py:142
  15.1 5.3 %branch_1_fun.43 = (bf16[32,8192]{1,0:T(8,128)(2,1)}, bf16[2,4,32,8192]{3,2,1,0:T(8,128)(2,1)}, f32[2,4,32,8192]{3,2,1,0:T(8,128)}) custom-call(s32[1]{0:T(128)} %bitcast.at_ref, s32[768]{0:T(1024)} %reshape.94.idx_ref, bf16[32,8192]{1,0:T(8,128)(2,1)} %get-tuple-element.506.h_in, ...), custom_call_target="tpu_custom_call", output_to_operand_aliasing={{1}: (4, {}), {2}: (5, {})} | custom-call | tf_op jit(solution)/shard_map/cond/branch_1_fun/pallas_call | solution.py:142
  26.3 7.7 %collective-permute-done = bf16[32,8192]{1,0:T(8,128)(2,1)S(1)} collective-permute-done((bf16[32,8192]{1,0:T(8,128)(2,1)}, bf16[32,8192]{1,0:T(8,128)(2,1)S(1)}, u32[]{:S(2)}, u32[]{:S(2)}) %collective-permute-start) | collective-permute-done | bytes 524320 | tf_op jit(solution)/shard_map/ppermute | solution.py:27
  34.1 11.6 %conditional.21 = ((bf16[32,8192]{1,0:T(8,128)(2,1)S(1)}, bf16[2,4,32,8192]{3,2,1,0:T(8,128)(2,1)}, f32[2,4,32,8192]{3,2,1,0:T(8,128)})) conditional(s32[]{:T(128)} %convert_element_type.110, (bf16[32,8192]{1,0:T(8,128)(2,1)S(1)}, bf16[2,4,32,8192]{3,2,1,0:T(8,128)(2,1)}, f32[2,4,32,8192]{3,2,1,0:T(8,128)}) %tuple.137, (s32[]{:T(128)}, ...), branch_computations={%region_2.3_spmd, %region_3.4_spmd} | conditional | flops 6 | bytes 12350 | solution.py:370
  36.3 4.9 %branch_1_fun.44 = (bf16[32,8192]{1,0:T(8,128)(2,1)}, bf16[2,4,32,8192]{3,2,1,0:T(8,128)(2,1)}, f32[2,4,32,8192]{3,2,1,0:T(8,128)}) custom-call(s32[2]{0:T(128)} %pad_add_fusion.1.at_ref, s32[768]{0:T(1024)} %reshape.99.idx_ref, bf16[32,8192]{1,0:T(8,128)(2,1)S(1)} %get-tuple-element.512.h_in, ...), custom_call_target="tpu_custom_call", output_to_operand_aliasing={{1}: (4, {}), {2}: (5, {})} | custom-call | tf_op jit(solution)/shard_map/cond/branch_1_fun/pallas_call | solution.py:142
  41.2 4.5 %branch_1_fun.45 = (bf16[32,8192]{1,0:T(8,128)(2,1)S(1)}, bf16[2,4,32,8192]{3,2,1,0:T(8,128)(2,1)}, f32[2,4,32,8192]{3,2,1,0:T(8,128)}) custom-call(s32[1]{0:T(128)} %bitcast.2.at_ref, s32[768]{0:T(1024)} %reshape.99.idx_ref, bf16[32,8192]{1,0:T(8,128)(2,1)} %get-tuple-element.517.h_in, ...), custom_call_target="tpu_custom_call", output_to_operand_aliasing={{1}: (4, {}), {2}: (5, {})} | custom-call | tf_op jit(solution)/shard_map/cond/branch_1_fun/pallas_call | solution.py:142
  45.7 6.1 %collective-permute-start.1 = (bf16[32,8192]{1,0:T(8,128)(2,1)S(1)}, bf16[32,8192]{1,0:T(8,128)(2,1)}, u32[]{:S(2)}, u32[]{:S(2)}) collective-permute-start(bf16[32,8192]{1,0:T(8,128)(2,1)S(1)} %get-tuple-element.763), channel_id=1, source_target_pairs={{0,8},{8,16},{16,24},{1,9},{9,17},{17,25},{2,10},{10,18},{18,26},{... | collective-permute-start | bytes 1572872 | tf_op jit(solution)/shard_map/ppermute | solution.py:27
  53.1 9.1 %collective-permute-done.1 = bf16[32,8192]{1,0:T(8,128)(2,1)} collective-permute-done((bf16[32,8192]{1,0:T(8,128)(2,1)S(1)}, bf16[32,8192]{1,0:T(8,128)(2,1)}, u32[]{:S(2)}, u32[]{:S(2)}) %collective-permute-start.1) | collective-permute-done | bytes 524320 | tf_op jit(solution)/shard_map/ppermute | solution.py:27
  62.2 12.8 %conditional.22 = ((bf16[32,8192]{1,0:T(8,128)(2,1)}, bf16[2,4,32,8192]{3,2,1,0:T(8,128)(2,1)}, f32[2,4,32,8192]{3,2,1,0:T(8,128)})) conditional(s32[]{:T(128)} %convert_element_type.109, (bf16[32,8192]{1,0:T(8,128)(2,1)}, bf16[2,4,32,8192]{3,2,1,0:T(8,128)(2,1)}, f32[2,4,32,8192]{3,2,1,0:T(8,128)}) %tuple.139, (s32[]{:T(128)}, s32[256,3]{0,1:T(4,128)}, ...), branch_computations={%region_4.5_spmd, %region_5.6_spmd} | conditional | flops 6 | bytes 12350 | solution.py:370
  64.4 5.3 %branch_1_fun.46 = (bf16[32,8192]{1,0:T(8,128)(2,1)}, bf16[2,4,32,8192]{3,2,1,0:T(8,128)(2,1)}, f32[2,4,32,8192]{3,2,1,0:T(8,128)}) custom-call(s32[2]{0:T(128)} %pad_add_fusion.2.at_ref, s32[768]{0:T(1024)} %reshape.104.idx_ref, bf16[32,8192]{1,0:T(8,128)(2,1)} %get-tuple-element.523.h_in, ...), custom_call_target="tpu_custom_call", output_to_operand_aliasing={{1}: (4, {}), {2}: (5, {})} | custom-call | tf_op jit(solution)/shard_map/cond/branch_1_fun/pallas_call | solution.py:142
  69.7 5.3 %branch_1_fun.47 = (bf16[32,8192]{1,0:T(8,128)(2,1)}, bf16[2,4,32,8192]{3,2,1,0:T(8,128)(2,1)}, f32[2,4,32,8192]{3,2,1,0:T(8,128)}) custom-call(s32[1]{0:T(128)} %bitcast.4.at_ref, s32[768]{0:T(1024)} %reshape.104.idx_ref, bf16[32,8192]{1,0:T(8,128)(2,1)} %get-tuple-element.528.h_in, ...), custom_call_target="tpu_custom_call", output_to_operand_aliasing={{1}: (4, {}), {2}: (5, {})} | custom-call | tf_op jit(solution)/shard_map/cond/branch_1_fun/pallas_call | solution.py:142
  75.0 6.2 %collective-permute-start.2 = (bf16[32,8192]{1,0:T(8,128)(2,1)}, bf16[32,8192]{1,0:T(8,128)(2,1)}, u32[]{:S(2)}, u32[]{:S(2)}) collective-permute-start(bf16[32,8192]{1,0:T(8,128)(2,1)} %get-tuple-element.766), channel_id=1, source_target_pairs={{0,8},{8,16},{16,24},{1,9},{9,17},{17,25},{2,10},{10,18},{18,26},{... | collective-permute-start | bytes 1572872 | tf_op jit(solution)/shard_map/ppermute | solution.py:27
  82.5 8.5 %collective-permute-done.2 = bf16[32,8192]{1,0:T(8,128)(2,1)} collective-permute-done((bf16[32,8192]{1,0:T(8,128)(2,1)}, bf16[32,8192]{1,0:T(8,128)(2,1)}, u32[]{:S(2)}, u32[]{:S(2)}) %collective-permute-start.2) | collective-permute-done | bytes 524320 | tf_op jit(solution)/shard_map/ppermute | solution.py:27
  91.1 12.8 %conditional.23 = ((bf16[32,8192]{1,0:T(8,128)(2,1)}, bf16[2,4,32,8192]{3,2,1,0:T(8,128)(2,1)}, f32[2,4,32,8192]{3,2,1,0:T(8,128)})) conditional(s32[]{:T(128)} %convert_element_type.108, (bf16[32,8192]{1,0:T(8,128)(2,1)}, bf16[2,4,32,8192]{3,2,1,0:T(8,128)(2,1)}, f32[2,4,32,8192]{3,2,1,0:T(8,128)}) %tuple.141, (s32[]{:T(128)}, s32[256,3]{0,1:T(4,128)}, ...), branch_computations={%region_6.7_spmd, %region_7.8_spmd} | conditional | flops 6 | bytes 12350 | solution.py:370
  93.3 5.3 %branch_1_fun.48 = (bf16[32,8192]{1,0:T(8,128)(2,1)}, bf16[2,4,32,8192]{3,2,1,0:T(8,128)(2,1)}, f32[2,4,32,8192]{3,2,1,0:T(8,128)}) custom-call(s32[2]{0:T(128)} %pad_add_fusion.3.at_ref, s32[768]{0:T(1024)} %reshape.106.idx_ref, bf16[32,8192]{1,0:T(8,128)(2,1)} %get-tuple-element.534.h_in, ...), custom_call_target="tpu_custom_call", output_to_operand_aliasing={{1}: (4, {}), {2}: (5, {})} | custom-call | tf_op jit(solution)/shard_map/cond/branch_1_fun/pallas_call | solution.py:142
  98.6 5.3 %branch_1_fun.49 = (bf16[32,8192]{1,0:T(8,128)(2,1)}, bf16[2,4,32,8192]{3,2,1,0:T(8,128)(2,1)}, f32[2,4,32,8192]{3,2,1,0:T(8,128)}) custom-call(s32[1]{0:T(128)} %bitcast.6.at_ref, s32[768]{0:T(1024)} %reshape.106.idx_ref, bf16[32,8192]{1,0:T(8,128)(2,1)} %get-tuple-element.539.h_in, ...), custom_call_target="tpu_custom_call", output_to_operand_aliasing={{1}: (4, {}), {2}: (5, {})} | custom-call | tf_op jit(solution)/shard_map/cond/branch_1_fun/pallas_call | solution.py:142
  103.9 6.3 %collective-permute-start.3 = (bf16[32,8192]{1,0:T(8,128)(2,1)}, bf16[32,8192]{1,0:T(8,128)(2,1)}, u32[]{:S(2)}, u32[]{:S(2)}) collective-permute-start(bf16[32,8192]{1,0:T(8,128)(2,1)} %get-tuple-element.769), channel_id=1, source_target_pairs={{0,8},{8,16},{16,24},{1,9},{9,17},{17,25},{2,10},{10,18},{18,26},{... | collective-permute-start | bytes 1572872 | tf_op jit(solution)/shard_map/ppermute | solution.py:27
  111.5 7.6 %collective-permute-done.3 = bf16[32,8192]{1,0:T(8,128)(2,1)} collective-permute-done((bf16[32,8192]{1,0:T(8,128)(2,1)}, bf16[32,8192]{1,0:T(8,128)(2,1)}, u32[]{:S(2)}, u32[]{:S(2)}) %collective-permute-start.3) | collective-permute-done | bytes 524320 | tf_op jit(solution)/shard_map/ppermute | solution.py:27
  119.1 19.0 %collective-permute-start.4 = (bf16[32,8192]{1,0:T(8,128)(2,1)}, bf16[32,8192]{1,0:T(8,128)(2,1)}, u32[]{:S(2)}, u32[]{:S(2)}) collective-permute-start(bf16[32,8192]{1,0:T(8,128)(2,1)} %get-tuple-element.772), channel_id=1, source_target_pairs={{0,8},{8,16},{16,24},{1,9},{9,17},{17,25},{2,10},{10,18},{18,26},{... | collective-permute-start | bytes 1572872 | tf_op jit(solution)/shard_map/ppermute | solution.py:27
  139.4 6.7 %collective-permute-done.4 = bf16[32,8192]{1,0:T(8,128)(2,1)} collective-permute-done((bf16[32,8192]{1,0:T(8,128)(2,1)}, bf16[32,8192]{1,0:T(8,128)(2,1)}, u32[]{:S(2)}, u32[]{:S(2)}) %collective-permute-start.4) | collective-permute-done | bytes 524320 | tf_op jit(solution)/shard_map/ppermute | solution.py:27
  146.1 5.2 %collective-permute-start.5 = (bf16[32,8192]{1,0:T(8,128)(2,1)}, bf16[32,8192]{1,0:T(8,128)(2,1)}, u32[]{:S(2)}, u32[]{:S(2)}) collective-permute-start(bf16[32,8192]{1,0:T(8,128)(2,1)} %get-tuple-element.775), channel_id=1, source_target_pairs={{0,8},{8,16},{16,24},{1,9},{9,17},{17,25},{2,10},{10,18},{18,26},{... | collective-permute-start | bytes 1572872 | tf_op jit(solution)/shard_map/ppermute | solution.py:27
  152.6 5.8 %collective-permute-done.5 = bf16[32,8192]{1,0:T(8,128)(2,1)} collective-permute-done((bf16[32,8192]{1,0:T(8,128)(2,1)}, bf16[32,8192]{1,0:T(8,128)(2,1)}, u32[]{:S(2)}, u32[]{:S(2)}) %collective-permute-start.5) | collective-permute-done | bytes 524320 | tf_op jit(solution)/shard_map/ppermute | solution.py:27
  158.4 31.0 %collective-permute-start.6 = (bf16[32,8192]{1,0:T(8,128)(2,1)}, bf16[32,8192]{1,0:T(8,128)(2,1)}, u32[]{:S(2)}, u32[]{:S(2)}) collective-permute-start(bf16[32,8192]{1,0:T(8,128)(2,1)} %get-tuple-element.778), channel_id=1, source_target_pairs={{0,8},{8,16},{16,24},{1,9},{9,17},{17,25},{2,10},{10,18},{18,26},{... | collective-permute-start | bytes 1572872 | tf_op jit(solution)/shard_map/ppermute | solution.py:27
  189.3 7.5 %collective-permute-done.14 = bf16[32,8192]{1,0:T(8,128)(2,1)S(1)} collective-permute-done((bf16[32,8192]{1,0:T(8,128)(2,1)S(1)}, bf16[32,8192]{1,0:T(8,128)(2,1)S(1)}, u32[]{:S(2)}, u32[]{:S(2)}) %collective-permute-start.14) | collective-permute-done | bytes 524320 | tf_op jit(solution)/shard_map/ppermute | solution.py:27
  197.6 14.9 %conditional.36 = ((bf16[32,8192]{1,0:T(8,128)(2,1)}, bf16[2,4,32,8192]{3,2,1,0:T(8,128)(2,1)})) conditional(s32[]{:T(128)} %convert_element_type.115, (bf16[32,8192]{1,0:T(8,128)(2,1)}, bf16[2,4,32,8192]{3,2,1,0:T(8,128)(2,1)}) %tuple.300, (s32[]{:T(128)}, s32[256,3]{0,1:T(4,128)}, bf16[32,8192]{1,0:T(8,128)(2,1)}, f32[2,4,32,8192]{3,2,1,0:T(8,128)}, ...), branch_computations={%region_32.33_spmd, %region_33.34_spmd} | conditional | flops 6 | bytes 12350 | solution.py:385
  199.8 5.9 %branch_1_fun.74 = (bf16[32,8192]{1,0:T(8,128)(2,1)}, bf16[2,4,32,8192]{3,2,1,0:T(8,128)(2,1)}) custom-call(s32[2]{0:T(128)} %pad_add_fusion.16.at_ref, s32[768]{0:T(1024)} %reshape.149.idx_ref, bf16[32,8192]{1,0:T(8,128)(2,1)} %get-tuple-element.670.g_in, f32[2,4,32,8192]{3,2,1,0:T(8,128)} %get-tuple-element.671.sy_hbm, ...), custom_call_target="tpu_custom_call", output_to_operand_aliasing={{1}: (5, {})} | custom-call | tf_op jit(solution)/shard_map/cond/branch_1_fun/pallas_call | solution.py:223
  205.7 6.8 %branch_1_fun.75 = (bf16[32,8192]{1,0:T(8,128)(2,1)}, bf16[2,4,32,8192]{3,2,1,0:T(8,128)(2,1)}) custom-call(s32[1]{0:T(128)} %bitcast.32.at_ref, s32[768]{0:T(1024)} %reshape.149.idx_ref, bf16[32,8192]{1,0:T(8,128)(2,1)} %get-tuple-element.675.g_in, f32[2,4,32,8192]{3,2,1,0:T(8,128)} %get-tuple-element.671.sy_hbm, ...), custom_call_target="tpu_custom_call", output_to_operand_aliasing={{1}: (5, {})} | custom-call | tf_op jit(solution)/shard_map/cond/branch_1_fun/pallas_call | solution.py:223
  213.8 6.4 %collective-permute-start.7 = (bf16[32,8192]{1,0:T(8,128)(2,1)}, bf16[32,8192]{1,0:T(8,128)(2,1)S(1)}, u32[]{:S(2)}, u32[]{:S(2)}) collective-permute-start(bf16[32,8192]{1,0:T(8,128)(2,1)} %get-tuple-element.781), channel_id=1, source_target_pairs={{0,8},{8,16},{16,24},{1,9},{9,17},{17,25},{2,10},{10,18},{18,26},{... | collective-permute-start | bytes 1572872 | tf_op jit(solution)/shard_map/ppermute | solution.py:27
  220.2 7.6 %collective-permute-done.15 = bf16[32,8192]{1,0:T(8,128)(2,1)S(1)} collective-permute-done((bf16[32,8192]{1,0:T(8,128)(2,1)}, bf16[32,8192]{1,0:T(8,128)(2,1)S(1)}, u32[]{:S(2)}, u32[]{:S(2)}) %collective-permute-start.15) | collective-permute-done | bytes 524320 | tf_op jit(solution)/shard_map/ppermute | solution.py:27
  227.9 13.8 %conditional.37 = ((bf16[32,8192]{1,0:T(8,128)(2,1)S(1)}, bf16[2,4,32,8192]{3,2,1,0:T(8,128)(2,1)})) conditional(s32[]{:T(128)} %convert_element_type.114, (bf16[32,8192]{1,0:T(8,128)(2,1)S(1)}, bf16[2,4,32,8192]{3,2,1,0:T(8,128)(2,1)}) %tuple.169, (s32[]{:T(128)}, s32[256,3]{0,1:T(4,128)}, s32[]{:T(128)}, bf16[32,8192]{1,0:T(8,128)(2,1)S(1)}, ...), branch_computations={%region_34.35_spmd, %region_35.36_spmd} | conditional | flops 6 | bytes 12350 | solution.py:385
  230.2 5.5 %branch_1_fun.76 = (bf16[32,8192]{1,0:T(8,128)(2,1)}, bf16[2,4,32,8192]{3,2,1,0:T(8,128)(2,1)}) custom-call(s32[2]{0:T(128)} %pad_add_fusion.17.at_ref, s32[768]{0:T(1024)} %reshape.151.idx_ref, bf16[32,8192]{1,0:T(8,128)(2,1)S(1)} %get-tuple-element.680.g_in, f32[2,4,32,8192]{3,2,1,0:T(8,128)} %get-tuple-element.681.sy_hbm, ...), custom_call_target="tpu_custom_call", output_to_operand_aliasing={{1}: (5, {})} | custom-call | tf_op jit(solution)/shard_map/cond/branch_1_fun/pallas_call | solution.py:223
  235.7 6.0 %branch_1_fun.77 = (bf16[32,8192]{1,0:T(8,128)(2,1)S(1)}, bf16[2,4,32,8192]{3,2,1,0:T(8,128)(2,1)}) custom-call(s32[1]{0:T(128)} %bitcast.34.at_ref, s32[768]{0:T(1024)} %reshape.151.idx_ref, bf16[32,8192]{1,0:T(8,128)(2,1)} %get-tuple-element.685.g_in, f32[2,4,32,8192]{3,2,1,0:T(8,128)} %get-tuple-element.681.sy_hbm, ...), custom_call_target="tpu_custom_call", output_to_operand_aliasing={{1}: (5, {})} | custom-call | tf_op jit(solution)/shard_map/cond/branch_1_fun/pallas_call | solution.py:223
  243.8 7.4 %collective-permute-start.8 = (bf16[32,8192]{1,0:T(8,128)(2,1)}, bf16[32,8192]{1,0:T(8,128)(2,1)S(1)}, u32[]{:S(2)}, u32[]{:S(2)}) collective-permute-start(bf16[32,8192]{1,0:T(8,128)(2,1)} %get-tuple-element.786), channel_id=1, source_target_pairs={{0,8},{8,16},{16,24},{1,9},{9,17},{17,25},{2,10},{10,18},{18,26},{... | collective-permute-start | bytes 1572872 | tf_op jit(solution)/shard_map/ppermute | solution.py:27
  251.2 6.1 %collective-permute-done.16 = bf16[32,8192]{1,0:T(8,128)(2,1)} collective-permute-done((bf16[32,8192]{1,0:T(8,128)(2,1)S(1)}, bf16[32,8192]{1,0:T(8,128)(2,1)}, u32[]{:S(2)}, u32[]{:S(2)}) %collective-permute-start.16) | collective-permute-done | bytes 524320 | tf_op jit(solution)/shard_map/ppermute | solution.py:27
  257.2 15.0 %conditional.38 = ((bf16[32,8192]{1,0:T(8,128)(2,1)}, bf16[2,4,32,8192]{3,2,1,0:T(8,128)(2,1)})) conditional(s32[]{:T(128)} %convert_element_type.113, (bf16[32,8192]{1,0:T(8,128)(2,1)}, bf16[2,4,32,8192]{3,2,1,0:T(8,128)(2,1)}) %tuple.171, (s32[]{:T(128)}, s32[256,3]{0,1:T(4,128)}, s32[]{:T(128)}, bf16[32,8192]{1,0:T(8,128)(2,1)}, ...), branch_computations={%region_36.37_spmd.clone, %region_37.38_spmd.clone} | conditional | flops 6 | bytes 12350 | solution.py:385
  259.5 5.9 %branch_1_fun.80 = (bf16[32,8192]{1,0:T(8,128)(2,1)}, bf16[2,4,32,8192]{3,2,1,0:T(8,128)(2,1)}) custom-call(s32[2]{0:T(128)} %pad_add_fusion.19.at_ref, s32[768]{0:T(1024)} %reshape.171.idx_ref, bf16[32,8192]{1,0:T(8,128)(2,1)} %get-tuple-element.815.g_in, f32[2,4,32,8192]{3,2,1,0:T(8,128)} %get-tuple-element.816.sy_hbm, ...), custom_call_target="tpu_custom_call", output_to_operand_aliasing={{1}: (5, {})} | custom-call | tf_op jit(solution)/shard_map/cond/branch_1_fun/pallas_call | solution.py:223
  265.4 6.8 %branch_1_fun.81 = (bf16[32,8192]{1,0:T(8,128)(2,1)}, bf16[2,4,32,8192]{3,2,1,0:T(8,128)(2,1)}) custom-call(s32[1]{0:T(128)} %bitcast.54.at_ref, s32[768]{0:T(1024)} %reshape.171.idx_ref, bf16[32,8192]{1,0:T(8,128)(2,1)} %get-tuple-element.820.g_in, f32[2,4,32,8192]{3,2,1,0:T(8,128)} %get-tuple-element.816.sy_hbm, ...), custom_call_target="tpu_custom_call", output_to_operand_aliasing={{1}: (5, {})} | custom-call | tf_op jit(solution)/shard_map/cond/branch_1_fun/pallas_call | solution.py:223
  275.1 10.9 %collective-permute-done.17 = bf16[32,8192]{1,0:T(8,128)(2,1)S(1)} collective-permute-done((bf16[32,8192]{1,0:T(8,128)(2,1)}, bf16[32,8192]{1,0:T(8,128)(2,1)S(1)}, u32[]{:S(2)}, u32[]{:S(2)}) %collective-permute-start.17) | collective-permute-done | bytes 524320 | tf_op jit(solution)/shard_map/ppermute | solution.py:27
  286.0 13.9 %conditional.39 = (bf16[2,4,32,8192]{3,2,1,0:T(8,128)(2,1)}) conditional(s32[]{:T(128)} %convert_element_type.112, bf16[2,4,32,8192]{3,2,1,0:T(8,128)(2,1)} %get-tuple-element.804, (s32[]{:T(128)}, s32[256,3]{0,1:T(4,128)S(1)}, s32[]{:T(128)}, bf16[32,8192]{1,0:T(8,128)(2,1)S(1)}, f32[2,4,32,8192]{3,2,1,0:T(8,128)}, ...), branch_computations={%region_38.39_spmd, %region_39.40_spmd} | conditional | flops 6 | bytes 12350 | solution.py:385
  287.6 5.5 %branch_1_fun.78 = (bf16[32,8192]{1,0:T(8,128)(2,1)}, bf16[2,4,32,8192]{3,2,1,0:T(8,128)(2,1)}) custom-call(s32[2]{0:T(128)} %pad_add_fusion.18.at_ref, s32[768]{0:T(1024)} %reshape.155.idx_ref, bf16[32,8192]{1,0:T(8,128)(2,1)S(1)} %get-tuple-element.704.g_in, f32[2,4,32,8192]{3,2,1,0:T(8,128)} %get-tuple-element.705.sy_hbm, ...), custom_call_target="tpu_custom_call", output_to_operand_aliasing={{1}: (5, {})} | custom-call | tf_op jit(solution)/shard_map/cond/branch_1_fun/pallas_call | solution.py:223
  293.1 6.8 %branch_1_fun.79 = (bf16[32,8192]{1,0:T(8,128)(2,1)}, bf16[2,4,32,8192]{3,2,1,0:T(8,128)(2,1)}) custom-call(s32[1]{0:T(128)} %bitcast.36.at_ref, s32[768]{0:T(1024)} %reshape.155.idx_ref, bf16[32,8192]{1,0:T(8,128)(2,1)} %get-tuple-element.709.g_in, f32[2,4,32,8192]{3,2,1,0:T(8,128)} %get-tuple-element.705.sy_hbm, ...), custom_call_target="tpu_custom_call", output_to_operand_aliasing={{1}: (5, {})} | custom-call | tf_op jit(solution)/shard_map/cond/branch_1_fun/pallas_call | solution.py:223
  299.9 7.0 %shard_map.47 = bf16[4,32,128,128]{3,2,1,0:T(8,128)(2,1)} custom-call(s32[1]{0:T(128)} %bitcast.44.sel_ref, s32[768]{0:T(1024)} %reshape.164.idx_ref, bf16[2,4,32,8192]{3,2,1,0:T(8,128)(2,1)} %get-tuple-element.787.h_ref, bf16[2,4,32,8192]{3,2,1,0:T(8,128)(2,1)} %get-tuple-element.1093.s_ref), custom_call_target="tpu_custom_call" | custom-call | tf_op jit(solution)/shard_map/pallas_call | solution.py:308
  306.9 8.5 %shard_map.46 = f32[4,32,128,128]{3,2,1,0:T(8,128)} custom-call(s32[1]{0:T(128)} %bitcast.38.sel_ref, s32[768]{0:T(1024)} %reshape.164.idx_ref, bf16[2,4,32,8192]{3,2,1,0:T(8,128)(2,1)} %get-tuple-element.787.h_ref, bf16[2,4,32,8192]{3,2,1,0:T(8,128)(2,1)} %get-tuple-element.1093.s_ref), custom_call_target="tpu_custom_call" | custom-call | tf_op jit(solution)/shard_map/pallas_call | solution.py:308
  315.3 6.0 %fusion.1 = bf16[2,32,128,128]{3,2,1,0:T(8,128)(2,1)S(1)} fusion(f32[2,2,32,128,128]{4,3,2,1,0:T(8,128)} %bitcast.98, s32[]{:T(128)S(6)} %select_n.80, s32[]{:T(128)S(6)} %select_n.79, bf16[2,2,32,128,128]{4,3,2,1,0:T(8,128)(2,1)} %bitcast.45, pred[]{:T(512)S(6)} %eq.67), kind=kLoop, calls=%fused_computation.22 | loop fusion | flops 5242880 | bytes 14680073 | tf_op jit(solution)/shard_map/convert_element_type | solution.py:318
  321.4 26.1 %collective-permute-done.19 = bf16[2,32,128,128]{3,2,1,0:T(8,128)(2,1)} collective-permute-done((bf16[2,32,128,128]{3,2,1,0:T(8,128)(2,1)S(1)}, bf16[2,32,128,128]{3,2,1,0:T(8,128)(2,1)}, u32[]{:S(2)}, u32[]{:S(2)}) %collective-permute-start.19) | collective-permute-done | bytes 2097184 | tf_op jit(solution)/shard_map/ppermute | solution.py:318
  347.5 6.9 %fusion.3 = f32[2,32,128,128]{3,2,1,0:T(8,128)S(1)} fusion(bf16[2,32,128,128]{3,2,1,0:T(8,128)(2,1)} %collective-permute-done.19, f32[2,2,32,128,128]{4,3,2,1,0:T(8,128)} %bitcast.99, s32[]{:T(128)S(6)} %select_n.76, s32[]{:T(128)S(6)} %select_n.74, bf16[2,2,32,128,128]{4,3,2,1,0:T(8,128)(2,1)} %bitcast.45, pred[]{:T(512)S(6)} %eq.67), kind=kLoop, calls=%fused_computation.25 | loop fusion | flops 6291456 | bytes 18874376 | tf_op jit(solution)/shard_map/add | solution.py:343
  356.7 14.8 %collective-permute-done.20 = bf16[32,128,128]{2,1,0:T(8,128)(2,1)S(1)} collective-permute-done((bf16[32,128,128]{2,1,0:T(8,128)(2,1)S(1)}, bf16[32,128,128]{2,1,0:T(8,128)(2,1)S(1)}, u32[]{:S(2)}, u32[]{:S(2)}) %collective-permute-start.20) | collective-permute-done | bytes 1048608 | tf_op jit(solution)/shard_map/ppermute | solution.py:318
  (79 shorter events, 53.1 us)
Async XLA Ops:
  6.5 3.3 copy-start.1
  20.4 13.7 %collective-permute-start = (bf16[32,8192]{1,0:T(8,128)(2,1)}, bf16[32,8192]{1,0:T(8,128)(2,1)S(1)}, u32[]{:S(2)}, u32[]{:S(2)}) collective-permute-start(bf16[32,8192]{1,0:T(8,128)(2,1)} %get-tuple-element.760), channel_id=1, source_target_pairs={{0,8},{8,16},{16,24},{1,9},{9,17},{17,25},{2,10},{10,18},{18,26},{... | collective-permute-start | bytes 1572872 | tf_op jit(solution)/shard_map/ppermute | solution.py:27
  21.7 12.3 %copy-start = (bf16[2,64,8192]{2,1,0:T(8,128)(2,1)S(1)}, bf16[2,64,8192]{2,1,0:T(8,128)(2,1)}, u32[]{:S(2)}) copy-start(bf16[2,64,8192]{2,1,0:T(8,128)(2,1)} %param.44) | copy-start | bytes 6291460
  25.0 26.7 %collective-permute-start.9 = (bf16[32,8192]{1,0:T(8,128)(2,1)}, bf16[32,8192]{1,0:T(8,128)(2,1)S(1)}, u32[]{:S(2)}, u32[]{:S(2)}) collective-permute-start(bf16[32,8192]{1,0:T(8,128)(2,1)} %get-tuple-element.788), channel_id=1, source_target_pairs={{8,0},{16,8},{24,16},{9,1},{17,9},{25,17},{10,2},{18,10},{26,18},{... | collective-permute-start | bytes 1572872 | tf_op jit(solution)/shard_map/ppermute | solution.py:27
  45.7 16.5 %collective-permute-start.1 = (bf16[32,8192]{1,0:T(8,128)(2,1)S(1)}, bf16[32,8192]{1,0:T(8,128)(2,1)}, u32[]{:S(2)}, u32[]{:S(2)}) collective-permute-start(bf16[32,8192]{1,0:T(8,128)(2,1)S(1)} %get-tuple-element.763), channel_id=1, source_target_pairs={{0,8},{8,16},{16,24},{1,9},{9,17},{17,25},{2,10},{10,18},{18,26},{... | collective-permute-start | bytes 1572872 | tf_op jit(solution)/shard_map/ppermute | solution.py:27
  51.8 29.5 %collective-permute-start.10 = (bf16[32,8192]{1,0:T(8,128)(2,1)S(1)}, bf16[32,8192]{1,0:T(8,128)(2,1)}, u32[]{:S(2)}, u32[]{:S(2)}) collective-permute-start(bf16[32,8192]{1,0:T(8,128)(2,1)S(1)} %get-tuple-element.790), channel_id=1, source_target_pairs={{8,0},{16,8},{24,16},{9,1},{17,9},{25,17},{10,2},{18,10},{26,18},{... | collective-permute-start | bytes 1572872 | tf_op jit(solution)/shard_map/ppermute | solution.py:27
  75.0 16.1 %collective-permute-start.2 = (bf16[32,8192]{1,0:T(8,128)(2,1)}, bf16[32,8192]{1,0:T(8,128)(2,1)}, u32[]{:S(2)}, u32[]{:S(2)}) collective-permute-start(bf16[32,8192]{1,0:T(8,128)(2,1)} %get-tuple-element.766), channel_id=1, source_target_pairs={{0,8},{8,16},{16,24},{1,9},{9,17},{17,25},{2,10},{10,18},{18,26},{... | collective-permute-start | bytes 1572872 | tf_op jit(solution)/shard_map/ppermute | solution.py:27
  81.2 28.9 %collective-permute-start.11 = (bf16[32,8192]{1,0:T(8,128)(2,1)}, bf16[32,8192]{1,0:T(8,128)(2,1)S(1)}, u32[]{:S(2)}, u32[]{:S(2)}) collective-permute-start(bf16[32,8192]{1,0:T(8,128)(2,1)} %get-tuple-element.792), channel_id=1, source_target_pairs={{8,0},{16,8},{24,16},{9,1},{17,9},{25,17},{10,2},{18,10},{26,18},{... | collective-permute-start | bytes 1572872 | tf_op jit(solution)/shard_map/ppermute | solution.py:27
  103.9 15.2 %collective-permute-start.3 = (bf16[32,8192]{1,0:T(8,128)(2,1)}, bf16[32,8192]{1,0:T(8,128)(2,1)}, u32[]{:S(2)}, u32[]{:S(2)}) collective-permute-start(bf16[32,8192]{1,0:T(8,128)(2,1)} %get-tuple-element.769), channel_id=1, source_target_pairs={{0,8},{8,16},{16,24},{1,9},{9,17},{17,25},{2,10},{10,18},{18,26},{... | collective-permute-start | bytes 1572872 | tf_op jit(solution)/shard_map/ppermute | solution.py:27
  110.2 27.9 %collective-permute-start.12 = (bf16[32,8192]{1,0:T(8,128)(2,1)S(1)}, bf16[32,8192]{1,0:T(8,128)(2,1)S(1)}, u32[]{:S(2)}, u32[]{:S(2)}) collective-permute-start(bf16[32,8192]{1,0:T(8,128)(2,1)S(1)} %get-tuple-element.794), channel_id=1, source_target_pairs={{8,0},{16,8},{24,16},{9,1},{17,9},{25,17},{10,2},{18,10},{26,18},{... | collective-permute-start | bytes 1572872 | tf_op jit(solution)/shard_map/ppermute | solution.py:27
  119.1 27.0 %collective-permute-start.4 = (bf16[32,8192]{1,0:T(8,128)(2,1)}, bf16[32,8192]{1,0:T(8,128)(2,1)}, u32[]{:S(2)}, u32[]{:S(2)}) collective-permute-start(bf16[32,8192]{1,0:T(8,128)(2,1)} %get-tuple-element.772), channel_id=1, source_target_pairs={{0,8},{8,16},{16,24},{1,9},{9,17},{17,25},{2,10},{10,18},{18,26},{... | collective-permute-start | bytes 1572872 | tf_op jit(solution)/shard_map/ppermute | solution.py:27
  138.1 13.2 %collective-permute-start.13 = (bf16[32,8192]{1,0:T(8,128)(2,1)S(1)}, bf16[32,8192]{1,0:T(8,128)(2,1)S(1)}, u32[]{:S(2)}, u32[]{:S(2)}) collective-permute-start(bf16[32,8192]{1,0:T(8,128)(2,1)S(1)} %get-tuple-element.796), channel_id=1, source_target_pairs={{8,0},{16,8},{24,16},{9,1},{17,9},{25,17},{10,2},{18,10},{26,18},{... | collective-permute-start | bytes 1572872 | tf_op jit(solution)/shard_map/ppermute | solution.py:27
  146.1 12.3 %collective-permute-start.5 = (bf16[32,8192]{1,0:T(8,128)(2,1)}, bf16[32,8192]{1,0:T(8,128)(2,1)}, u32[]{:S(2)}, u32[]{:S(2)}) collective-permute-start(bf16[32,8192]{1,0:T(8,128)(2,1)} %get-tuple-element.775), channel_id=1, source_target_pairs={{0,8},{8,16},{16,24},{1,9},{9,17},{17,25},{2,10},{10,18},{18,26},{... | collective-permute-start | bytes 1572872 | tf_op jit(solution)/shard_map/ppermute | solution.py:27
  151.3 45.5 %collective-permute-start.14 = (bf16[32,8192]{1,0:T(8,128)(2,1)S(1)}, bf16[32,8192]{1,0:T(8,128)(2,1)S(1)}, u32[]{:S(2)}, u32[]{:S(2)}) collective-permute-start(bf16[32,8192]{1,0:T(8,128)(2,1)S(1)} %get-tuple-element.798), channel_id=1, source_target_pairs={{8,0},{16,8},{24,16},{9,1},{17,9},{25,17},{10,2},{18,10},{26,18},{... | collective-permute-start | bytes 1572872 | tf_op jit(solution)/shard_map/ppermute | solution.py:27
  158.4 55.4 %collective-permute-start.6 = (bf16[32,8192]{1,0:T(8,128)(2,1)}, bf16[32,8192]{1,0:T(8,128)(2,1)}, u32[]{:S(2)}, u32[]{:S(2)}) collective-permute-start(bf16[32,8192]{1,0:T(8,128)(2,1)} %get-tuple-element.778), channel_id=1, source_target_pairs={{0,8},{8,16},{16,24},{1,9},{9,17},{17,25},{2,10},{10,18},{18,26},{... | collective-permute-start | bytes 1572872 | tf_op jit(solution)/shard_map/ppermute | solution.py:27
  196.8 0.8 copy-start.5
  212.5 15.4 %collective-permute-start.15 = (bf16[32,8192]{1,0:T(8,128)(2,1)}, bf16[32,8192]{1,0:T(8,128)(2,1)S(1)}, u32[]{:S(2)}, u32[]{:S(2)}) collective-permute-start(bf16[32,8192]{1,0:T(8,128)(2,1)} %get-tuple-element.800), channel_id=1, source_target_pairs={{8,0},{16,8},{24,16},{9,1},{17,9},{25,17},{10,2},{18,10},{26,18},{... | collective-permute-start | bytes 1572872 | tf_op jit(solution)/shard_map/ppermute | solution.py:27
  213.8 29.2 %collective-permute-start.7 = (bf16[32,8192]{1,0:T(8,128)(2,1)}, bf16[32,8192]{1,0:T(8,128)(2,1)S(1)}, u32[]{:S(2)}, u32[]{:S(2)}) collective-permute-start(bf16[32,8192]{1,0:T(8,128)(2,1)} %get-tuple-element.781), channel_id=1, source_target_pairs={{0,8},{8,16},{16,24},{1,9},{9,17},{17,25},{2,10},{10,18},{18,26},{... | collective-permute-start | bytes 1572872 | tf_op jit(solution)/shard_map/ppermute | solution.py:27
  241.7 15.6 %collective-permute-start.16 = (bf16[32,8192]{1,0:T(8,128)(2,1)S(1)}, bf16[32,8192]{1,0:T(8,128)(2,1)}, u32[]{:S(2)}, u32[]{:S(2)}) collective-permute-start(bf16[32,8192]{1,0:T(8,128)(2,1)S(1)} %get-tuple-element.802), channel_id=1, source_target_pairs={{8,0},{16,8},{24,16},{9,1},{17,9},{25,17},{10,2},{18,10},{26,18},{... | collective-permute-start | bytes 1572872 | tf_op jit(solution)/shard_map/ppermute | solution.py:27
  243.0 0.8 copy-start.4
  243.8 31.4 %collective-permute-start.8 = (bf16[32,8192]{1,0:T(8,128)(2,1)}, bf16[32,8192]{1,0:T(8,128)(2,1)S(1)}, u32[]{:S(2)}, u32[]{:S(2)}) collective-permute-start(bf16[32,8192]{1,0:T(8,128)(2,1)} %get-tuple-element.786), channel_id=1, source_target_pairs={{0,8},{8,16},{16,24},{1,9},{9,17},{17,25},{2,10},{10,18},{18,26},{... | collective-permute-start | bytes 1572872 | tf_op jit(solution)/shard_map/ppermute | solution.py:27
  257.2 17.9 %copy-start.3 = (s32[256,3]{0,1:T(4,128)S(1)}, s32[256,3]{0,1:T(4,128)}, u32[]{:S(2)}) copy-start(s32[256,3]{0,1:T(4,128)} %param.47) | copy-start | bytes 9220
  272.2 13.8 %collective-permute-start.17 = (bf16[32,8192]{1,0:T(8,128)(2,1)}, bf16[32,8192]{1,0:T(8,128)(2,1)S(1)}, u32[]{:S(2)}, u32[]{:S(2)}) collective-permute-start(bf16[32,8192]{1,0:T(8,128)(2,1)} %get-tuple-element.805), channel_id=1, source_target_pairs={{8,0},{16,8},{24,16},{9,1},{17,9},{25,17},{10,2},{18,10},{26,18},{... | collective-permute-start | bytes 1572872 | tf_op jit(solution)/shard_map/ppermute | solution.py:27
  306.9 8.5 %collective-permute-start.18 = (bf16[4,32,128,128]{3,2,1,0:T(8,128)(2,1)}, bf16[4,32,128,128]{3,2,1,0:T(8,128)(2,1)}, u32[]{:S(2)}, u32[]{:S(2)}) collective-permute-start(bf16[4,32,128,128]{3,2,1,0:T(8,128)(2,1)} %shard_map.47), channel_id=1, source_target_pairs={{0,1},{1,0},{2,3},{3,2},{4,5},{5,4},{6,7},{7,6},{8,9},{9,8},{10,11... | collective-permute-start | bytes 12582920 | tf_op jit(solution)/shard_map/ppermute | solution.py:332
  321.3 26.2 %collective-permute-start.19 = (bf16[2,32,128,128]{3,2,1,0:T(8,128)(2,1)S(1)}, bf16[2,32,128,128]{3,2,1,0:T(8,128)(2,1)}, u32[]{:S(2)}, u32[]{:S(2)}) collective-permute-start(bf16[2,32,128,128]{3,2,1,0:T(8,128)(2,1)S(1)} %fusion.1), channel_id=1, source_target_pairs={{0,2},{1,5},{2,0},{3,7},{4,6},{5,1},{6,4},{7,3},{8,10},{9,13},{10,... | collective-permute-start | bytes 6291464 | tf_op jit(solution)/shard_map/ppermute | solution.py:318
  354.4 2.0 copy-start.2
  356.6 14.9 %collective-permute-start.20 = (bf16[32,128,128]{2,1,0:T(8,128)(2,1)S(1)}, bf16[32,128,128]{2,1,0:T(8,128)(2,1)S(1)}, u32[]{:S(2)}, u32[]{:S(2)}) collective-permute-start(bf16[32,128,128]{2,1,0:T(8,128)(2,1)S(1)} %fusion.4), channel_id=1, source_target_pairs={{0,4},{1,3},{2,6},{3,1},{4,0},{5,7},{6,2},{7,5},{8,12},{9,11},{10,... | collective-permute-start | bytes 3145736 | tf_op jit(solution)/shard_map/ppermute | solution.py:318

commit v2 on v1

--- a/solution.py
+++ b/solution.py
@@ -282,6 +282,7 @@
     per = out_ref.shape[1]
     for q in range(out_ref.shape[0]):
         layer = (2 * q * per) // KMAX
+        spot = q + b0 * ((q % 2) * 2 + q // 2 - q)
         for j in range(per // NSUB):
             first = 2 * q * per + b0 * per + j * NSUB
 
@@ -296,11 +297,11 @@
                     part = lax.dot_general(
                         hb, sb, (((0,), (0,)), ((), ())), preferred_element_type=jnp.float32
                     )
-                    out_ref[q, j * NSUB + i] = (part * _flag(idx_ref, k)).astype(out_ref.dtype)
+                    out_ref[spot, j * NSUB + i] = (part * _flag(idx_ref, k)).astype(out_ref.dtype)
 
             @pl.when(idx_ref[3 * first + 2] <= 0)
             def _():
-                out_ref[q, pl.ds(j * NSUB, NSUB)] = jnp.zeros((NSUB, BLK, BLK), out_ref.dtype)
+                out_ref[spot, pl.ds(j * NSUB, NSUB)] = jnp.zeros((NSUB, BLK, BLK), out_ref.dtype)
 
 
 def dw_half(stash_h, stash_s, block_index, b0, dtype):
@@ -332,18 +333,27 @@
     got = lax.ppermute(send, "dp", [(i, i ^ 1) for i in range(8)])
     keep = dw_half(stash_h, stash_s, block_index, d0, jnp.float32)
     keep = keep.reshape((2, 2) + keep.shape[1:])
-    got = got.reshape(keep.shape)
+    got = got.reshape(keep.shape).astype(jnp.float32)
     core0 = d0 == 0
-
-    def half(a, i_core0, i_core1):
-        return jnp.where(core0, pick(a, i_core0, 1), pick(a, i_core1, 0)).astype(jnp.float32)
-
-    send = half(keep, 1 - d1, 1 - d2) + half(got, 1 - d1, 1 - d2)
+    flip = jnp.where(core0, d1, d2)
+    send = pick(keep, 1 - flip, 1) + pick(got, 1 - flip, 1)
     got2 = _exchange(send, [(i, i ^ (2 if i % 2 == 0 else 4)) for i in range(8)])
-    keep2 = half(keep, d1, d2) + half(got, d1, d2) + got2
+    keep2 = pick(keep, flip, 1) + pick(got, flip, 1) + got2
     rem = jnp.where(core0, d2, d1)
     got3 = _exchange(pick(keep2, 1 - rem, 0), [(i, i ^ (4 if i % 2 == 0 else 2)) for i in range(8)])
     return pick(keep2, rem, 0) + got3
+
+
+def _allocate_kernel(*refs):
+    del refs
+
+
+def allocate(specs):
+    return pl.pallas_call(
+        _allocate_kernel,
+        out_shape=tuple(jax.ShapeDtypeStruct(shape, dtype) for shape, dtype in specs),
+        out_specs=tuple(_ANY for _ in specs),
+    )()
 
 
 def on_device(x_in, cotangent, weights, block_index):
@@ -386,9 +396,10 @@
         send_b = shifted(grad_out, "segment", -1)
         return (send_f, send_b, saved_h, saved_y, saved_s)
 
-    stash_h = jnp.zeros((LSLOT, mbs, rows_dev, width), jnp.bfloat16)
-    stash_y = jnp.zeros((LSLOT, mbs, rows_dev, width), jnp.float32)
-    stash_s = jnp.zeros((LSLOT, mbs, rows_dev, width), jnp.bfloat16)
+    stash_shape = (LSLOT, mbs, rows_dev, width)
+    stash_h, stash_y, stash_s = allocate(
+        [(stash_shape, jnp.bfloat16), (stash_shape, jnp.float32), (stash_shape, jnp.bfloat16)]
+    )
     blank = jnp.zeros((rows_dev, width), jnp.bfloat16)
     ticks = mbs + 2 * segments - 2
     carry = (blank, blank, stash_h, stash_y, stash_s)

time: 380 us -> 381 us (level)
  local copies, waits for them, and re-layouts: 28.6 us -> 21.1 us
  starting transfers between devices: 100 us -> 105 us
    another operation x10 -> x8, local copies, waits for them, and re-layouts: 10.8 us -> 5.89 us
    ppermute x18, starting transfers between devices: 100 us -> 105 us  [shifted(): lax.ppermute(value, axis, [(source, source + steps) for source in range(l...]
    broadcast_in_dim x1 -> x0, local copies, waits for them, and re-layouts: 4.29 us -> none  [on_device(): stash_y = jnp.zeros((LSLOT, mbs, rows_dev, width), jnp.float32)]
  transfers between devices with their start and end apart: 21 -> 21, of which waited for: 12 -> 12; matrix products, arithmetic and copies ran while one was open for 5% -> 4% of each run, Pallas kernels for 20% -> 20%
where the time goes in v2:
time: 381 us; the launch traced here: 374 us
  waiting for transfers between devices  121 us (32%)
  Pallas kernels  107 us (28%)
  starting transfers between devices  105 us (28%)
  local copies, waits for them, and re-layouts  21.1 us (6%)
  other arithmetic  18.8 us (5%)
    ppermute x18, starting transfers between devices, shifted(): lax.ppermute(value, axis, [(source, source + steps) for source in range(l...  105 us
    ppermute x18, waiting for transfers between devices, shifted(): lax.ppermute(value, axis, [(source, source + steps) for source in range(l...  80.2 us
    pallas_call x8, Pallas kernels, layer_backward(): pl.pallas_call(functools.partial(_bwd_kernel, layer * KMAX, layer, entry)...  48.9 us
    pallas_call x8, Pallas kernels, layer_forward(): pl.pallas_call(functools.partial(_fwd_kernel, layer * KMAX, layer), out_s...  42.2 us
    ppermute x2, waiting for transfers between devices, _exchange(): lax.ppermute(send.astype(jnp.bfloat16), 'dp', pairs).astype(jnp.float32)  41 us
    pallas_call x2, Pallas kernels, dw_half(): pl.pallas_call(_dw_half_kernel, out_shape=jax.ShapeDtypeStruct((4, per, B...  15.4 us
  transfers between devices with their start and end apart: 21, of which 12 were waited for; matrix products, arithmetic and copies ran while one was open for 4% of the time, Pallas kernels for 20%

profile of v2, /device:TPU:0, one launch (start us, length us, event | category | flops | bytes accessed | tf_op | source)
XLA Modules:
  0.0 373.6 jit_solution(17180089590080361297)
XLA Ops:
  0.0 14.8 %conditional.20 = ((bf16[32,8192]{1,0:T(8,128)(2,1)}, bf16[2,4,32,8192]{3,2,1,0:T(8,128)(2,1)}, f32[2,4,32,8192]{3,2,1,0:T(8,128)})) conditional(s32[]{:T(128)} %convert_element_type.114, (bf16[2,4,32,8192]{3,2,1,0:T(8,128)(2,1)}, f32[2,4,32,8192]{3,2,1,0:T(8,128)}) %tuple.135, (s32[]{:T(128)}, s32[256,3]{0,1:T(4,128)}, s32[]{:T(128)}, ...), branch_computations={%region_0.1_spmd, %region_1.2_spmd} | conditional | flops 6 | bytes 536640 | solution.py:380
  3.1 6.4 %branch_1_fun.42 = (bf16[32,8192]{1,0:T(8,128)(2,1)}, bf16[2,4,32,8192]{3,2,1,0:T(8,128)(2,1)}, f32[2,4,32,8192]{3,2,1,0:T(8,128)}) custom-call(s32[2]{0:T(128)} %pad_add_fusion.at_ref, s32[768]{0:T(1024)} %reshape.104.idx_ref, bf16[32,8192]{1,0:T(8,128)(2,1)} %broadcast_in_dim.9.h_in, ...), custom_call_target="tpu_custom_call", output_to_operand_aliasing={{1}: (4, {}), {2}: (5, {})} | custom-call | tf_op jit(solution)/shard_map/cond/branch_1_fun/pallas_call | solution.py:142
  9.5 5.3 %branch_1_fun.43 = (bf16[32,8192]{1,0:T(8,128)(2,1)}, bf16[2,4,32,8192]{3,2,1,0:T(8,128)(2,1)}, f32[2,4,32,8192]{3,2,1,0:T(8,128)}) custom-call(s32[1]{0:T(128)} %bitcast.at_ref, s32[768]{0:T(1024)} %reshape.104.idx_ref, bf16[32,8192]{1,0:T(8,128)(2,1)} %get-tuple-element.521.h_in, ...), custom_call_target="tpu_custom_call", output_to_operand_aliasing={{1}: (4, {}), {2}: (5, {})} | custom-call | tf_op jit(solution)/shard_map/cond/branch_1_fun/pallas_call | solution.py:142
  18.3 10.2 %collective-permute-done = bf16[32,8192]{1,0:T(8,128)(2,1)S(1)} collective-permute-done((bf16[32,8192]{1,0:T(8,128)(2,1)}, bf16[32,8192]{1,0:T(8,128)(2,1)S(1)}, u32[]{:S(2)}, u32[]{:S(2)}) %collective-permute-start) | collective-permute-done | bytes 524320 | tf_op jit(solution)/shard_map/ppermute | solution.py:27
  28.5 11.6 %conditional.21 = ((bf16[32,8192]{1,0:T(8,128)(2,1)S(1)}, bf16[2,4,32,8192]{3,2,1,0:T(8,128)(2,1)}, f32[2,4,32,8192]{3,2,1,0:T(8,128)})) conditional(s32[]{:T(128)} %convert_element_type.113, (bf16[32,8192]{1,0:T(8,128)(2,1)S(1)}, bf16[2,4,32,8192]{3,2,1,0:T(8,128)(2,1)}, f32[2,4,32,8192]{3,2,1,0:T(8,128)}) %tuple.137, (s32[]{:T(128)}, ...), branch_computations={%region_2.3_spmd, %region_3.4_spmd} | conditional | flops 6 | bytes 12350 | solution.py:380
  30.6 4.9 %branch_1_fun.44 = (bf16[32,8192]{1,0:T(8,128)(2,1)}, bf16[2,4,32,8192]{3,2,1,0:T(8,128)(2,1)}, f32[2,4,32,8192]{3,2,1,0:T(8,128)}) custom-call(s32[2]{0:T(128)} %pad_add_fusion.1.at_ref, s32[768]{0:T(1024)} %reshape.106.idx_ref, bf16[32,8192]{1,0:T(8,128)(2,1)S(1)} %get-tuple-element.527.h_in, ...), custom_call_target="tpu_custom_call", output_to_operand_aliasing={{1}: (4, {}), {2}: (5, {})} | custom-call | tf_op jit(solution)/shard_map/cond/branch_1_fun/pallas_call | solution.py:142
  35.6 4.5 %branch_1_fun.45 = (bf16[32,8192]{1,0:T(8,128)(2,1)S(1)}, bf16[2,4,32,8192]{3,2,1,0:T(8,128)(2,1)}, f32[2,4,32,8192]{3,2,1,0:T(8,128)}) custom-call(s32[1]{0:T(128)} %bitcast.2.at_ref, s32[768]{0:T(1024)} %reshape.106.idx_ref, bf16[32,8192]{1,0:T(8,128)(2,1)} %get-tuple-element.532.h_in, ...), custom_call_target="tpu_custom_call", output_to_operand_aliasing={{1}: (4, {}), {2}: (5, {})} | custom-call | tf_op jit(solution)/shard_map/cond/branch_1_fun/pallas_call | solution.py:142
  40.0 6.1 %collective-permute-start.1 = (bf16[32,8192]{1,0:T(8,128)(2,1)S(1)}, bf16[32,8192]{1,0:T(8,128)(2,1)}, u32[]{:S(2)}, u32[]{:S(2)}) collective-permute-start(bf16[32,8192]{1,0:T(8,128)(2,1)S(1)} %get-tuple-element.784), channel_id=1, source_target_pairs={{0,8},{8,16},{16,24},{1,9},{9,17},{17,25},{2,10},{10,18},{18,26},{... | collective-permute-start | bytes 1572872 | tf_op jit(solution)/shard_map/ppermute | solution.py:27
  47.5 9.1 %collective-permute-done.1 = bf16[32,8192]{1,0:T(8,128)(2,1)} collective-permute-done((bf16[32,8192]{1,0:T(8,128)(2,1)S(1)}, bf16[32,8192]{1,0:T(8,128)(2,1)}, u32[]{:S(2)}, u32[]{:S(2)}) %collective-permute-start.1) | collective-permute-done | bytes 524320 | tf_op jit(solution)/shard_map/ppermute | solution.py:27
  56.6 12.8 %conditional.22 = ((bf16[32,8192]{1,0:T(8,128)(2,1)}, bf16[2,4,32,8192]{3,2,1,0:T(8,128)(2,1)}, f32[2,4,32,8192]{3,2,1,0:T(8,128)})) conditional(s32[]{:T(128)} %convert_element_type.112, (bf16[32,8192]{1,0:T(8,128)(2,1)}, bf16[2,4,32,8192]{3,2,1,0:T(8,128)(2,1)}, f32[2,4,32,8192]{3,2,1,0:T(8,128)}) %tuple.139, (s32[]{:T(128)}, s32[256,3]{0,1:T(4,128)}, ...), branch_computations={%region_4.5_spmd, %region_5.6_spmd} | conditional | flops 6 | bytes 12350 | solution.py:380
  58.8 5.3 %branch_1_fun.46 = (bf16[32,8192]{1,0:T(8,128)(2,1)}, bf16[2,4,32,8192]{3,2,1,0:T(8,128)(2,1)}, f32[2,4,32,8192]{3,2,1,0:T(8,128)}) custom-call(s32[2]{0:T(128)} %pad_add_fusion.2.at_ref, s32[768]{0:T(1024)} %reshape.111.idx_ref, bf16[32,8192]{1,0:T(8,128)(2,1)} %get-tuple-element.538.h_in, ...), custom_call_target="tpu_custom_call", output_to_operand_aliasing={{1}: (4, {}), {2}: (5, {})} | custom-call | tf_op jit(solution)/shard_map/cond/branch_1_fun/pallas_call | solution.py:142
  64.0 5.3 %branch_1_fun.47 = (bf16[32,8192]{1,0:T(8,128)(2,1)}, bf16[2,4,32,8192]{3,2,1,0:T(8,128)(2,1)}, f32[2,4,32,8192]{3,2,1,0:T(8,128)}) custom-call(s32[1]{0:T(128)} %bitcast.4.at_ref, s32[768]{0:T(1024)} %reshape.111.idx_ref, bf16[32,8192]{1,0:T(8,128)(2,1)} %get-tuple-element.543.h_in, ...), custom_call_target="tpu_custom_call", output_to_operand_aliasing={{1}: (4, {}), {2}: (5, {})} | custom-call | tf_op jit(solution)/shard_map/cond/branch_1_fun/pallas_call | solution.py:142
  69.4 6.2 %collective-permute-start.2 = (bf16[32,8192]{1,0:T(8,128)(2,1)}, bf16[32,8192]{1,0:T(8,128)(2,1)}, u32[]{:S(2)}, u32[]{:S(2)}) collective-permute-start(bf16[32,8192]{1,0:T(8,128)(2,1)} %get-tuple-element.787), channel_id=1, source_target_pairs={{0,8},{8,16},{16,24},{1,9},{9,17},{17,25},{2,10},{10,18},{18,26},{... | collective-permute-start | bytes 1572872 | tf_op jit(solution)/shard_map/ppermute | solution.py:27
  76.9 8.6 %collective-permute-done.2 = bf16[32,8192]{1,0:T(8,128)(2,1)} collective-permute-done((bf16[32,8192]{1,0:T(8,128)(2,1)}, bf16[32,8192]{1,0:T(8,128)(2,1)}, u32[]{:S(2)}, u32[]{:S(2)}) %collective-permute-start.2) | collective-permute-done | bytes 524320 | tf_op jit(solution)/shard_map/ppermute | solution.py:27
  85.4 12.8 %conditional.23 = ((bf16[32,8192]{1,0:T(8,128)(2,1)}, bf16[2,4,32,8192]{3,2,1,0:T(8,128)(2,1)}, f32[2,4,32,8192]{3,2,1,0:T(8,128)})) conditional(s32[]{:T(128)} %convert_element_type.111, (bf16[32,8192]{1,0:T(8,128)(2,1)}, bf16[2,4,32,8192]{3,2,1,0:T(8,128)(2,1)}, f32[2,4,32,8192]{3,2,1,0:T(8,128)}) %tuple.141, (s32[]{:T(128)}, s32[256,3]{0,1:T(4,128)}, ...), branch_computations={%region_6.7_spmd, %region_7.8_spmd} | conditional | flops 6 | bytes 12350 | solution.py:380
  87.7 5.3 %branch_1_fun.48 = (bf16[32,8192]{1,0:T(8,128)(2,1)}, bf16[2,4,32,8192]{3,2,1,0:T(8,128)(2,1)}, f32[2,4,32,8192]{3,2,1,0:T(8,128)}) custom-call(s32[2]{0:T(128)} %pad_add_fusion.3.at_ref, s32[768]{0:T(1024)} %reshape.116.idx_ref, bf16[32,8192]{1,0:T(8,128)(2,1)} %get-tuple-element.549.h_in, ...), custom_call_target="tpu_custom_call", output_to_operand_aliasing={{1}: (4, {}), {2}: (5, {})} | custom-call | tf_op jit(solution)/shard_map/cond/branch_1_fun/pallas_call | solution.py:142
  93.0 5.3 %branch_1_fun.49 = (bf16[32,8192]{1,0:T(8,128)(2,1)}, bf16[2,4,32,8192]{3,2,1,0:T(8,128)(2,1)}, f32[2,4,32,8192]{3,2,1,0:T(8,128)}) custom-call(s32[1]{0:T(128)} %bitcast.6.at_ref, s32[768]{0:T(1024)} %reshape.116.idx_ref, bf16[32,8192]{1,0:T(8,128)(2,1)} %get-tuple-element.554.h_in, ...), custom_call_target="tpu_custom_call", output_to_operand_aliasing={{1}: (4, {}), {2}: (5, {})} | custom-call | tf_op jit(solution)/shard_map/cond/branch_1_fun/pallas_call | solution.py:142
  98.3 6.2 %collective-permute-start.3 = (bf16[32,8192]{1,0:T(8,128)(2,1)}, bf16[32,8192]{1,0:T(8,128)(2,1)}, u32[]{:S(2)}, u32[]{:S(2)}) collective-permute-start(bf16[32,8192]{1,0:T(8,128)(2,1)} %get-tuple-element.790), channel_id=1, source_target_pairs={{0,8},{8,16},{16,24},{1,9},{9,17},{17,25},{2,10},{10,18},{18,26},{... | collective-permute-start | bytes 1572872 | tf_op jit(solution)/shard_map/ppermute | solution.py:27
  105.8 7.6 %collective-permute-done.3 = bf16[32,8192]{1,0:T(8,128)(2,1)} collective-permute-done((bf16[32,8192]{1,0:T(8,128)(2,1)}, bf16[32,8192]{1,0:T(8,128)(2,1)}, u32[]{:S(2)}, u32[]{:S(2)}) %collective-permute-start.3) | collective-permute-done | bytes 524320 | tf_op jit(solution)/shard_map/ppermute | solution.py:27
  113.5 19.0 %collective-permute-start.4 = (bf16[32,8192]{1,0:T(8,128)(2,1)}, bf16[32,8192]{1,0:T(8,128)(2,1)}, u32[]{:S(2)}, u32[]{:S(2)}) collective-permute-start(bf16[32,8192]{1,0:T(8,128)(2,1)} %get-tuple-element.793), channel_id=1, source_target_pairs={{0,8},{8,16},{16,24},{1,9},{9,17},{17,25},{2,10},{10,18},{18,26},{... | collective-permute-start | bytes 1572872 | tf_op jit(solution)/shard_map/ppermute | solution.py:27
  133.8 6.7 %collective-permute-done.4 = bf16[32,8192]{1,0:T(8,128)(2,1)} collective-permute-done((bf16[32,8192]{1,0:T(8,128)(2,1)}, bf16[32,8192]{1,0:T(8,128)(2,1)}, u32[]{:S(2)}, u32[]{:S(2)}) %collective-permute-start.4) | collective-permute-done | bytes 524320 | tf_op jit(solution)/shard_map/ppermute | solution.py:27
  140.5 5.2 %collective-permute-start.5 = (bf16[32,8192]{1,0:T(8,128)(2,1)}, bf16[32,8192]{1,0:T(8,128)(2,1)}, u32[]{:S(2)}, u32[]{:S(2)}) collective-permute-start(bf16[32,8192]{1,0:T(8,128)(2,1)} %get-tuple-element.796), channel_id=1, source_target_pairs={{0,8},{8,16},{16,24},{1,9},{9,17},{17,25},{2,10},{10,18},{18,26},{... | collective-permute-start | bytes 1572872 | tf_op jit(solution)/shard_map/ppermute | solution.py:27
  147.0 5.8 %collective-permute-done.5 = bf16[32,8192]{1,0:T(8,128)(2,1)} collective-permute-done((bf16[32,8192]{1,0:T(8,128)(2,1)}, bf16[32,8192]{1,0:T(8,128)(2,1)}, u32[]{:S(2)}, u32[]{:S(2)}) %collective-permute-start.5) | collective-permute-done | bytes 524320 | tf_op jit(solution)/shard_map/ppermute | solution.py:27
  152.8 34.1 %collective-permute-start.6 = (bf16[32,8192]{1,0:T(8,128)(2,1)}, bf16[32,8192]{1,0:T(8,128)(2,1)}, u32[]{:S(2)}, u32[]{:S(2)}) collective-permute-start(bf16[32,8192]{1,0:T(8,128)(2,1)} %get-tuple-element.799), channel_id=1, source_target_pairs={{0,8},{8,16},{16,24},{1,9},{9,17},{17,25},{2,10},{10,18},{18,26},{... | collective-permute-start | bytes 1572872 | tf_op jit(solution)/shard_map/ppermute | solution.py:27
  186.9 7.3 %collective-permute-done.14 = bf16[32,8192]{1,0:T(8,128)(2,1)S(1)} collective-permute-done((bf16[32,8192]{1,0:T(8,128)(2,1)S(1)}, bf16[32,8192]{1,0:T(8,128)(2,1)S(1)}, u32[]{:S(2)}, u32[]{:S(2)}) %collective-permute-start.14) | collective-permute-done | bytes 524320 | tf_op jit(solution)/shard_map/ppermute | solution.py:27
  194.9 14.9 %conditional.36 = ((bf16[32,8192]{1,0:T(8,128)(2,1)}, bf16[2,4,32,8192]{3,2,1,0:T(8,128)(2,1)})) conditional(s32[]{:T(128)} %convert_element_type.118, (bf16[32,8192]{1,0:T(8,128)(2,1)}, bf16[2,4,32,8192]{3,2,1,0:T(8,128)(2,1)}) %tuple.299, (s32[]{:T(128)}, s32[256,3]{0,1:T(4,128)}, bf16[32,8192]{1,0:T(8,128)(2,1)}, f32[2,4,32,8192]{3,2,1,0:T(8,128)}, ...), branch_computations={%region_32.33_spmd, %region_33.34_spmd} | conditional | flops 6 | bytes 12350 | solution.py:395
  197.2 5.8 %branch_1_fun.74 = (bf16[32,8192]{1,0:T(8,128)(2,1)}, bf16[2,4,32,8192]{3,2,1,0:T(8,128)(2,1)}) custom-call(s32[2]{0:T(128)} %pad_add_fusion.16.at_ref, s32[768]{0:T(1024)} %reshape.153.idx_ref, bf16[32,8192]{1,0:T(8,128)(2,1)} %get-tuple-element.686.g_in, f32[2,4,32,8192]{3,2,1,0:T(8,128)} %get-tuple-element.687.sy_hbm, ...), custom_call_target="tpu_custom_call", output_to_operand_aliasing={{1}: (5, {})} | custom-call | tf_op jit(solution)/shard_map/cond/branch_1_fun/pallas_call | solution.py:223
  203.0 6.8 %branch_1_fun.75 = (bf16[32,8192]{1,0:T(8,128)(2,1)}, bf16[2,4,32,8192]{3,2,1,0:T(8,128)(2,1)}) custom-call(s32[1]{0:T(128)} %bitcast.32.at_ref, s32[768]{0:T(1024)} %reshape.153.idx_ref, bf16[32,8192]{1,0:T(8,128)(2,1)} %get-tuple-element.691.g_in, f32[2,4,32,8192]{3,2,1,0:T(8,128)} %get-tuple-element.687.sy_hbm, ...), custom_call_target="tpu_custom_call", output_to_operand_aliasing={{1}: (5, {})} | custom-call | tf_op jit(solution)/shard_map/cond/branch_1_fun/pallas_call | solution.py:223
  211.1 6.9 %collective-permute-start.7 = (bf16[32,8192]{1,0:T(8,128)(2,1)}, bf16[32,8192]{1,0:T(8,128)(2,1)S(1)}, u32[]{:S(2)}, u32[]{:S(2)}) collective-permute-start(bf16[32,8192]{1,0:T(8,128)(2,1)} %get-tuple-element.802), channel_id=1, source_target_pairs={{0,8},{8,16},{16,24},{1,9},{9,17},{17,25},{2,10},{10,18},{18,26},{... | collective-permute-start | bytes 1572872 | tf_op jit(solution)/shard_map/ppermute | solution.py:27
  218.0 7.6 %collective-permute-done.15 = bf16[32,8192]{1,0:T(8,128)(2,1)S(1)} collective-permute-done((bf16[32,8192]{1,0:T(8,128)(2,1)}, bf16[32,8192]{1,0:T(8,128)(2,1)S(1)}, u32[]{:S(2)}, u32[]{:S(2)}) %collective-permute-start.15) | collective-permute-done | bytes 524320 | tf_op jit(solution)/shard_map/ppermute | solution.py:27
  225.6 13.7 %conditional.37 = ((bf16[32,8192]{1,0:T(8,128)(2,1)S(1)}, bf16[2,4,32,8192]{3,2,1,0:T(8,128)(2,1)})) conditional(s32[]{:T(128)} %convert_element_type.117, (bf16[32,8192]{1,0:T(8,128)(2,1)S(1)}, bf16[2,4,32,8192]{3,2,1,0:T(8,128)(2,1)}) %tuple.168, (s32[]{:T(128)}, s32[256,3]{0,1:T(4,128)}, s32[]{:T(128)}, bf16[32,8192]{1,0:T(8,128)(2,1)S(1)}, ...), branch_computations={%region_34.35_spmd, %region_35.36_spmd} | conditional | flops 6 | bytes 12350 | solution.py:395
  227.8 5.5 %branch_1_fun.76 = (bf16[32,8192]{1,0:T(8,128)(2,1)}, bf16[2,4,32,8192]{3,2,1,0:T(8,128)(2,1)}) custom-call(s32[2]{0:T(128)} %pad_add_fusion.17.at_ref, s32[768]{0:T(1024)} %reshape.155.idx_ref, bf16[32,8192]{1,0:T(8,128)(2,1)S(1)} %get-tuple-element.696.g_in, f32[2,4,32,8192]{3,2,1,0:T(8,128)} %get-tuple-element.697.sy_hbm, ...), custom_call_target="tpu_custom_call", output_to_operand_aliasing={{1}: (5, {})} | custom-call | tf_op jit(solution)/shard_map/cond/branch_1_fun/pallas_call | solution.py:223
  233.3 6.0 %branch_1_fun.77 = (bf16[32,8192]{1,0:T(8,128)(2,1)S(1)}, bf16[2,4,32,8192]{3,2,1,0:T(8,128)(2,1)}) custom-call(s32[1]{0:T(128)} %bitcast.34.at_ref, s32[768]{0:T(1024)} %reshape.155.idx_ref, bf16[32,8192]{1,0:T(8,128)(2,1)} %get-tuple-element.701.g_in, f32[2,4,32,8192]{3,2,1,0:T(8,128)} %get-tuple-element.697.sy_hbm, ...), custom_call_target="tpu_custom_call", output_to_operand_aliasing={{1}: (5, {})} | custom-call | tf_op jit(solution)/shard_map/cond/branch_1_fun/pallas_call | solution.py:223
  241.5 8.6 %collective-permute-start.8 = (bf16[32,8192]{1,0:T(8,128)(2,1)}, bf16[32,8192]{1,0:T(8,128)(2,1)S(1)}, u32[]{:S(2)}, u32[]{:S(2)}) collective-permute-start(bf16[32,8192]{1,0:T(8,128)(2,1)} %get-tuple-element.807), channel_id=1, source_target_pairs={{0,8},{8,16},{16,24},{1,9},{9,17},{17,25},{2,10},{10,18},{18,26},{... | collective-permute-start | bytes 1572872 | tf_op jit(solution)/shard_map/ppermute | solution.py:27
  250.1 6.1 %collective-permute-done.16 = bf16[32,8192]{1,0:T(8,128)(2,1)} collective-permute-done((bf16[32,8192]{1,0:T(8,128)(2,1)S(1)}, bf16[32,8192]{1,0:T(8,128)(2,1)}, u32[]{:S(2)}, u32[]{:S(2)}) %collective-permute-start.16) | collective-permute-done | bytes 524320 | tf_op jit(solution)/shard_map/ppermute | solution.py:27
  256.1 14.9 %conditional.38 = ((bf16[32,8192]{1,0:T(8,128)(2,1)}, bf16[2,4,32,8192]{3,2,1,0:T(8,128)(2,1)})) conditional(s32[]{:T(128)} %convert_element_type.116, (bf16[32,8192]{1,0:T(8,128)(2,1)}, bf16[2,4,32,8192]{3,2,1,0:T(8,128)(2,1)}) %tuple.170, (s32[]{:T(128)}, s32[256,3]{0,1:T(4,128)}, s32[]{:T(128)}, bf16[32,8192]{1,0:T(8,128)(2,1)}, ...), branch_computations={%region_36.37_spmd.clone, %region_37.38_spmd.clone} | conditional | flops 6 | bytes 12350 | solution.py:395
  258.5 5.8 %branch_1_fun.80 = (bf16[32,8192]{1,0:T(8,128)(2,1)}, bf16[2,4,32,8192]{3,2,1,0:T(8,128)(2,1)}) custom-call(s32[2]{0:T(128)} %pad_add_fusion.19.at_ref, s32[768]{0:T(1024)} %reshape.173.idx_ref, bf16[32,8192]{1,0:T(8,128)(2,1)} %get-tuple-element.837.g_in, f32[2,4,32,8192]{3,2,1,0:T(8,128)} %get-tuple-element.838.sy_hbm, ...), custom_call_target="tpu_custom_call", output_to_operand_aliasing={{1}: (5, {})} | custom-call | tf_op jit(solution)/shard_map/cond/branch_1_fun/pallas_call | solution.py:223
  264.3 6.8 %branch_1_fun.81 = (bf16[32,8192]{1,0:T(8,128)(2,1)}, bf16[2,4,32,8192]{3,2,1,0:T(8,128)(2,1)}) custom-call(s32[1]{0:T(128)} %bitcast.49.at_ref, s32[768]{0:T(1024)} %reshape.173.idx_ref, bf16[32,8192]{1,0:T(8,128)(2,1)} %get-tuple-element.842.g_in, f32[2,4,32,8192]{3,2,1,0:T(8,128)} %get-tuple-element.838.sy_hbm, ...), custom_call_target="tpu_custom_call", output_to_operand_aliasing={{1}: (5, {})} | custom-call | tf_op jit(solution)/shard_map/cond/branch_1_fun/pallas_call | solution.py:223
  274.0 11.3 %collective-permute-done.17 = bf16[32,8192]{1,0:T(8,128)(2,1)S(1)} collective-permute-done((bf16[32,8192]{1,0:T(8,128)(2,1)}, bf16[32,8192]{1,0:T(8,128)(2,1)S(1)}, u32[]{:S(2)}, u32[]{:S(2)}) %collective-permute-start.17) | collective-permute-done | bytes 524320 | tf_op jit(solution)/shard_map/ppermute | solution.py:27
  285.3 13.8 %conditional.39 = (bf16[2,4,32,8192]{3,2,1,0:T(8,128)(2,1)}) conditional(s32[]{:T(128)} %convert_element_type.115, bf16[2,4,32,8192]{3,2,1,0:T(8,128)(2,1)} %get-tuple-element.826, (s32[]{:T(128)}, s32[256,3]{0,1:T(4,128)S(1)}, s32[]{:T(128)}, bf16[32,8192]{1,0:T(8,128)(2,1)S(1)}, f32[2,4,32,8192]{3,2,1,0:T(8,128)}, ...), branch_computations={%region_38.39_spmd, %region_39.40_spmd} | conditional | flops 6 | bytes 12350 | solution.py:395
  286.9 5.5 %branch_1_fun.78 = (bf16[32,8192]{1,0:T(8,128)(2,1)}, bf16[2,4,32,8192]{3,2,1,0:T(8,128)(2,1)}) custom-call(s32[2]{0:T(128)} %pad_add_fusion.18.at_ref, s32[768]{0:T(1024)} %reshape.159.idx_ref, bf16[32,8192]{1,0:T(8,128)(2,1)S(1)} %get-tuple-element.720.g_in, f32[2,4,32,8192]{3,2,1,0:T(8,128)} %get-tuple-element.721.sy_hbm, ...), custom_call_target="tpu_custom_call", output_to_operand_aliasing={{1}: (5, {})} | custom-call | tf_op jit(solution)/shard_map/cond/branch_1_fun/pallas_call | solution.py:223
  292.4 6.8 %branch_1_fun.79 = (bf16[32,8192]{1,0:T(8,128)(2,1)}, bf16[2,4,32,8192]{3,2,1,0:T(8,128)(2,1)}) custom-call(s32[1]{0:T(128)} %bitcast.36.at_ref, s32[768]{0:T(1024)} %reshape.159.idx_ref, bf16[32,8192]{1,0:T(8,128)(2,1)} %get-tuple-element.725.g_in, f32[2,4,32,8192]{3,2,1,0:T(8,128)} %get-tuple-element.721.sy_hbm, ...), custom_call_target="tpu_custom_call", output_to_operand_aliasing={{1}: (5, {})} | custom-call | tf_op jit(solution)/shard_map/cond/branch_1_fun/pallas_call | solution.py:223
  299.1 7.0 %shard_map.48 = bf16[4,32,128,128]{3,2,1,0:T(8,128)(2,1)} custom-call(s32[1]{0:T(128)} %bitcast.42.sel_ref, s32[768]{0:T(1024)} %reshape.167.idx_ref, bf16[2,4,32,8192]{3,2,1,0:T(8,128)(2,1)} %get-tuple-element.808.h_ref, bf16[2,4,32,8192]{3,2,1,0:T(8,128)(2,1)} %get-tuple-element.1118.s_ref), custom_call_target="tpu_custom_call" | custom-call | tf_op jit(solution)/shard_map/pallas_call | solution.py:309
  306.1 8.5 %shard_map.47 = f32[4,32,128,128]{3,2,1,0:T(8,128)} custom-call(s32[1]{0:T(128)} %bitcast.38.sel_ref, s32[768]{0:T(1024)} %reshape.167.idx_ref, bf16[2,4,32,8192]{3,2,1,0:T(8,128)(2,1)} %get-tuple-element.808.h_ref, bf16[2,4,32,8192]{3,2,1,0:T(8,128)(2,1)} %get-tuple-element.1118.s_ref), custom_call_target="tpu_custom_call" | custom-call | tf_op jit(solution)/shard_map/pallas_call | solution.py:309
  314.6 3.4 convert.21
  322.0 26.2 %collective-permute-done.19 = bf16[2,32,128,128]{3,2,1,0:T(8,128)(2,1)S(1)} collective-permute-done((bf16[2,32,128,128]{3,2,1,0:T(8,128)(2,1)}, bf16[2,32,128,128]{3,2,1,0:T(8,128)(2,1)S(1)}, u32[]{:S(2)}, u32[]{:S(2)}) %collective-permute-start.19) | collective-permute-done | bytes 2097184 | tf_op jit(solution)/shard_map/ppermute | solution.py:319
  348.3 5.0 %fusion.2 = f32[2,32,128,128]{3,2,1,0:T(8,128)S(1)} fusion(bf16[2,32,128,128]{3,2,1,0:T(8,128)(2,1)S(1)} %collective-permute-done.19, f32[2,2,32,128,128]{4,3,2,1,0:T(8,128)} %copy-done.1, s32[]{:T(128)S(6)} %select_n.45, f32[2,2,32,128,128]{4,3,2,1,0:T(8,128)} %bitcast.95), kind=kLoop, calls=%fused_computation.24 | loop fusion | flops 3145728 | bytes 14680068 | tf_op jit(solution)/shard_map/add | solution.py:341
  355.5 14.8 %collective-permute-done.20 = bf16[32,128,128]{2,1,0:T(8,128)(2,1)S(1)} collective-permute-done((bf16[32,128,128]{2,1,0:T(8,128)(2,1)S(1)}, bf16[32,128,128]{2,1,0:T(8,128)(2,1)S(1)}, u32[]{:S(2)}, u32[]{:S(2)}) %collective-permute-start.20) | collective-permute-done | bytes 1048608 | tf_op jit(solution)/shard_map/ppermute | solution.py:319
  (80 shorter events, 45.3 us)
Async XLA Ops:
  14.8 13.7 %collective-permute-start = (bf16[32,8192]{1,0:T(8,128)(2,1)}, bf16[32,8192]{1,0:T(8,128)(2,1)S(1)}, u32[]{:S(2)}, u32[]{:S(2)}) collective-permute-start(bf16[32,8192]{1,0:T(8,128)(2,1)} %get-tuple-element.781), channel_id=1, source_target_pairs={{0,8},{8,16},{16,24},{1,9},{9,17},{17,25},{2,10},{10,18},{18,26},{... | collective-permute-start | bytes 1572872 | tf_op jit(solution)/shard_map/ppermute | solution.py:27
  16.1 12.3 %copy-start = (bf16[2,64,8192]{2,1,0:T(8,128)(2,1)S(1)}, bf16[2,64,8192]{2,1,0:T(8,128)(2,1)}, u32[]{:S(2)}) copy-start(bf16[2,64,8192]{2,1,0:T(8,128)(2,1)} %param.44) | copy-start | bytes 6291460
  17.0 29.2 %collective-permute-start.9 = (bf16[32,8192]{1,0:T(8,128)(2,1)}, bf16[32,8192]{1,0:T(8,128)(2,1)S(1)}, u32[]{:S(2)}, u32[]{:S(2)}) collective-permute-start(bf16[32,8192]{1,0:T(8,128)(2,1)} %get-tuple-element.810), channel_id=1, source_target_pairs={{8,0},{16,8},{24,16},{9,1},{17,9},{25,17},{10,2},{18,10},{26,18},{... | collective-permute-start | bytes 1572872 | tf_op jit(solution)/shard_map/ppermute | solution.py:27
  40.0 16.5 %collective-permute-start.1 = (bf16[32,8192]{1,0:T(8,128)(2,1)S(1)}, bf16[32,8192]{1,0:T(8,128)(2,1)}, u32[]{:S(2)}, u32[]{:S(2)}) collective-permute-start(bf16[32,8192]{1,0:T(8,128)(2,1)S(1)} %get-tuple-element.784), channel_id=1, source_target_pairs={{0,8},{8,16},{16,24},{1,9},{9,17},{17,25},{2,10},{10,18},{18,26},{... | collective-permute-start | bytes 1572872 | tf_op jit(solution)/shard_map/ppermute | solution.py:27
  46.2 29.4 %collective-permute-start.10 = (bf16[32,8192]{1,0:T(8,128)(2,1)S(1)}, bf16[32,8192]{1,0:T(8,128)(2,1)}, u32[]{:S(2)}, u32[]{:S(2)}) collective-permute-start(bf16[32,8192]{1,0:T(8,128)(2,1)S(1)} %get-tuple-element.812), channel_id=1, source_target_pairs={{8,0},{16,8},{24,16},{9,1},{17,9},{25,17},{10,2},{18,10},{26,18},{... | collective-permute-start | bytes 1572872 | tf_op jit(solution)/shard_map/ppermute | solution.py:27
  69.4 16.1 %collective-permute-start.2 = (bf16[32,8192]{1,0:T(8,128)(2,1)}, bf16[32,8192]{1,0:T(8,128)(2,1)}, u32[]{:S(2)}, u32[]{:S(2)}) collective-permute-start(bf16[32,8192]{1,0:T(8,128)(2,1)} %get-tuple-element.787), channel_id=1, source_target_pairs={{0,8},{8,16},{16,24},{1,9},{9,17},{17,25},{2,10},{10,18},{18,26},{... | collective-permute-start | bytes 1572872 | tf_op jit(solution)/shard_map/ppermute | solution.py:27
  75.6 28.9 %collective-permute-start.11 = (bf16[32,8192]{1,0:T(8,128)(2,1)}, bf16[32,8192]{1,0:T(8,128)(2,1)S(1)}, u32[]{:S(2)}, u32[]{:S(2)}) collective-permute-start(bf16[32,8192]{1,0:T(8,128)(2,1)} %get-tuple-element.814), channel_id=1, source_target_pairs={{8,0},{16,8},{24,16},{9,1},{17,9},{25,17},{10,2},{18,10},{26,18},{... | collective-permute-start | bytes 1572872 | tf_op jit(solution)/shard_map/ppermute | solution.py:27
  98.3 15.2 %collective-permute-start.3 = (bf16[32,8192]{1,0:T(8,128)(2,1)}, bf16[32,8192]{1,0:T(8,128)(2,1)}, u32[]{:S(2)}, u32[]{:S(2)}) collective-permute-start(bf16[32,8192]{1,0:T(8,128)(2,1)} %get-tuple-element.790), channel_id=1, source_target_pairs={{0,8},{8,16},{16,24},{1,9},{9,17},{17,25},{2,10},{10,18},{18,26},{... | collective-permute-start | bytes 1572872 | tf_op jit(solution)/shard_map/ppermute | solution.py:27
  104.5 28.0 %collective-permute-start.12 = (bf16[32,8192]{1,0:T(8,128)(2,1)S(1)}, bf16[32,8192]{1,0:T(8,128)(2,1)S(1)}, u32[]{:S(2)}, u32[]{:S(2)}) collective-permute-start(bf16[32,8192]{1,0:T(8,128)(2,1)S(1)} %get-tuple-element.816), channel_id=1, source_target_pairs={{8,0},{16,8},{24,16},{9,1},{17,9},{25,17},{10,2},{18,10},{26,18},{... | collective-permute-start | bytes 1572872 | tf_op jit(solution)/shard_map/ppermute | solution.py:27
  113.5 27.1 %collective-permute-start.4 = (bf16[32,8192]{1,0:T(8,128)(2,1)}, bf16[32,8192]{1,0:T(8,128)(2,1)}, u32[]{:S(2)}, u32[]{:S(2)}) collective-permute-start(bf16[32,8192]{1,0:T(8,128)(2,1)} %get-tuple-element.793), channel_id=1, source_target_pairs={{0,8},{8,16},{16,24},{1,9},{9,17},{17,25},{2,10},{10,18},{18,26},{... | collective-permute-start | bytes 1572872 | tf_op jit(solution)/shard_map/ppermute | solution.py:27
  132.5 13.2 %collective-permute-start.13 = (bf16[32,8192]{1,0:T(8,128)(2,1)S(1)}, bf16[32,8192]{1,0:T(8,128)(2,1)S(1)}, u32[]{:S(2)}, u32[]{:S(2)}) collective-permute-start(bf16[32,8192]{1,0:T(8,128)(2,1)S(1)} %get-tuple-element.818), channel_id=1, source_target_pairs={{8,0},{16,8},{24,16},{9,1},{17,9},{25,17},{10,2},{18,10},{26,18},{... | collective-permute-start | bytes 1572872 | tf_op jit(solution)/shard_map/ppermute | solution.py:27
  140.5 12.3 %collective-permute-start.5 = (bf16[32,8192]{1,0:T(8,128)(2,1)}, bf16[32,8192]{1,0:T(8,128)(2,1)}, u32[]{:S(2)}, u32[]{:S(2)}) collective-permute-start(bf16[32,8192]{1,0:T(8,128)(2,1)} %get-tuple-element.796), channel_id=1, source_target_pairs={{0,8},{8,16},{16,24},{1,9},{9,17},{17,25},{2,10},{10,18},{18,26},{... | collective-permute-start | bytes 1572872 | tf_op jit(solution)/shard_map/ppermute | solution.py:27
  145.7 48.4 %collective-permute-start.14 = (bf16[32,8192]{1,0:T(8,128)(2,1)S(1)}, bf16[32,8192]{1,0:T(8,128)(2,1)S(1)}, u32[]{:S(2)}, u32[]{:S(2)}) collective-permute-start(bf16[32,8192]{1,0:T(8,128)(2,1)S(1)} %get-tuple-element.820), channel_id=1, source_target_pairs={{8,0},{16,8},{24,16},{9,1},{17,9},{25,17},{10,2},{18,10},{26,18},{... | collective-permute-start | bytes 1572872 | tf_op jit(solution)/shard_map/ppermute | solution.py:27
  152.8 58.3 %collective-permute-start.6 = (bf16[32,8192]{1,0:T(8,128)(2,1)}, bf16[32,8192]{1,0:T(8,128)(2,1)}, u32[]{:S(2)}, u32[]{:S(2)}) collective-permute-start(bf16[32,8192]{1,0:T(8,128)(2,1)} %get-tuple-element.799), channel_id=1, source_target_pairs={{0,8},{8,16},{16,24},{1,9},{9,17},{17,25},{2,10},{10,18},{18,26},{... | collective-permute-start | bytes 1572872 | tf_op jit(solution)/shard_map/ppermute | solution.py:27
  194.1 0.8 copy-start.6
  209.8 15.8 %collective-permute-start.15 = (bf16[32,8192]{1,0:T(8,128)(2,1)}, bf16[32,8192]{1,0:T(8,128)(2,1)S(1)}, u32[]{:S(2)}, u32[]{:S(2)}) collective-permute-start(bf16[32,8192]{1,0:T(8,128)(2,1)} %get-tuple-element.822), channel_id=1, source_target_pairs={{8,0},{16,8},{24,16},{9,1},{17,9},{25,17},{10,2},{18,10},{26,18},{... | collective-permute-start | bytes 1572872 | tf_op jit(solution)/shard_map/ppermute | solution.py:27
  211.1 29.5 %collective-permute-start.7 = (bf16[32,8192]{1,0:T(8,128)(2,1)}, bf16[32,8192]{1,0:T(8,128)(2,1)S(1)}, u32[]{:S(2)}, u32[]{:S(2)}) collective-permute-start(bf16[32,8192]{1,0:T(8,128)(2,1)} %get-tuple-element.802), channel_id=1, source_target_pairs={{0,8},{8,16},{16,24},{1,9},{9,17},{17,25},{2,10},{10,18},{18,26},{... | collective-permute-start | bytes 1572872 | tf_op jit(solution)/shard_map/ppermute | solution.py:27
  239.3 16.8 %collective-permute-start.16 = (bf16[32,8192]{1,0:T(8,128)(2,1)S(1)}, bf16[32,8192]{1,0:T(8,128)(2,1)}, u32[]{:S(2)}, u32[]{:S(2)}) collective-permute-start(bf16[32,8192]{1,0:T(8,128)(2,1)S(1)} %get-tuple-element.824), channel_id=1, source_target_pairs={{8,0},{16,8},{24,16},{9,1},{17,9},{25,17},{10,2},{18,10},{26,18},{... | collective-permute-start | bytes 1572872 | tf_op jit(solution)/shard_map/ppermute | solution.py:27
  240.7 0.8 copy-start.5
  241.5 32.6 %collective-permute-start.8 = (bf16[32,8192]{1,0:T(8,128)(2,1)}, bf16[32,8192]{1,0:T(8,128)(2,1)S(1)}, u32[]{:S(2)}, u32[]{:S(2)}) collective-permute-start(bf16[32,8192]{1,0:T(8,128)(2,1)} %get-tuple-element.807), channel_id=1, source_target_pairs={{0,8},{8,16},{16,24},{1,9},{9,17},{17,25},{2,10},{10,18},{18,26},{... | collective-permute-start | bytes 1572872 | tf_op jit(solution)/shard_map/ppermute | solution.py:27
  256.1 17.9 %copy-start.4 = (s32[256,3]{0,1:T(4,128)S(1)}, s32[256,3]{0,1:T(4,128)}, u32[]{:S(2)}) copy-start(s32[256,3]{0,1:T(4,128)} %param.47) | copy-start | bytes 9220
  271.1 14.2 %collective-permute-start.17 = (bf16[32,8192]{1,0:T(8,128)(2,1)}, bf16[32,8192]{1,0:T(8,128)(2,1)S(1)}, u32[]{:S(2)}, u32[]{:S(2)}) collective-permute-start(bf16[32,8192]{1,0:T(8,128)(2,1)} %get-tuple-element.827), channel_id=1, source_target_pairs={{8,0},{16,8},{24,16},{9,1},{17,9},{25,17},{10,2},{18,10},{26,18},{... | collective-permute-start | bytes 1572872 | tf_op jit(solution)/shard_map/ppermute | solution.py:27
  306.1 8.5 %collective-permute-start.18 = (bf16[4,32,128,128]{3,2,1,0:T(8,128)(2,1)}, bf16[4,32,128,128]{3,2,1,0:T(8,128)(2,1)}, u32[]{:S(2)}, u32[]{:S(2)}) collective-permute-start(bf16[4,32,128,128]{3,2,1,0:T(8,128)(2,1)} %shard_map.48), channel_id=1, source_target_pairs={{0,1},{1,0},{2,3},{3,2},{4,5},{5,4},{6,7},{7,6},{8,9},{9,8},{10,11... | collective-permute-start | bytes 12582920 | tf_op jit(solution)/shard_map/ppermute | solution.py:333
  314.6 5.2 %copy-start.2 = (f32[4,32,128,128]{3,2,1,0:T(8,128)S(1)}, f32[4,32,128,128]{3,2,1,0:T(8,128)}, u32[]{:S(2)}) copy-start(f32[4,32,128,128]{3,2,1,0:T(8,128)} %shard_map.47) | copy-start | bytes 25165828
  318.0 4.0 %copy-start.1 = (f32[2,2,32,128,128]{4,3,2,1,0:T(8,128)}, f32[2,2,32,128,128]{4,3,2,1,0:T(8,128)S(1)}, u32[]{:S(2)}) copy-start(f32[2,2,32,128,128]{4,3,2,1,0:T(8,128)S(1)} %convert.21) | copy-start | bytes 25165828
  322.0 26.2 %collective-permute-start.19 = (bf16[2,32,128,128]{3,2,1,0:T(8,128)(2,1)}, bf16[2,32,128,128]{3,2,1,0:T(8,128)(2,1)S(1)}, u32[]{:S(2)}, u32[]{:S(2)}) collective-permute-start(bf16[2,32,128,128]{3,2,1,0:T(8,128)(2,1)} %fusion.3), channel_id=1, source_target_pairs={{0,2},{1,5},{2,0},{3,7},{4,6},{5,1},{6,4},{7,3},{8,10},{9,13},{10,... | collective-permute-start | bytes 6291464 | tf_op jit(solution)/shard_map/ppermute | solution.py:319
  353.3 2.0 copy-start.3
  355.4 14.9 %collective-permute-start.20 = (bf16[32,128,128]{2,1,0:T(8,128)(2,1)S(1)}, bf16[32,128,128]{2,1,0:T(8,128)(2,1)S(1)}, u32[]{:S(2)}, u32[]{:S(2)}) collective-permute-start(bf16[32,128,128]{2,1,0:T(8,128)(2,1)S(1)} %fusion.4), channel_id=1, source_target_pairs={{0,4},{1,3},{2,6},{3,1},{4,0},{5,7},{6,2},{7,5},{8,12},{9,11},{10,... | collective-permute-start | bytes 3145736 | tf_op jit(solution)/shard_map/ppermute | solution.py:319

commit v3 on v2

--- a/solution.py
+++ b/solution.py
@@ -333,15 +333,21 @@
     got = lax.ppermute(send, "dp", [(i, i ^ 1) for i in range(8)])
     keep = dw_half(stash_h, stash_s, block_index, d0, jnp.float32)
     keep = keep.reshape((2, 2) + keep.shape[1:])
-    got = got.reshape(keep.shape).astype(jnp.float32)
+    got = got.reshape(keep.shape)
     core0 = d0 == 0
     flip = jnp.where(core0, d1, d2)
-    send = pick(keep, 1 - flip, 1) + pick(got, 1 - flip, 1)
-    got2 = _exchange(send, [(i, i ^ (2 if i % 2 == 0 else 4)) for i in range(8)])
-    keep2 = pick(keep, flip, 1) + pick(got, flip, 1) + got2
     rem = jnp.where(core0, d2, d1)
-    got3 = _exchange(pick(keep2, 1 - rem, 0), [(i, i ^ (4 if i % 2 == 0 else 2)) for i in range(8)])
-    return pick(keep2, rem, 0) + got3
+
+    def summed(a, b, i):
+        return pick(a, i, 1) + pick(b, i, 1).astype(jnp.float32)
+
+    got2 = _exchange(summed(keep, got, 1 - flip), [(i, i ^ (2 if i % 2 == 0 else 4)) for i in range(8)])
+
+    def part(i):
+        return pick(pick(keep, flip, 1), i, 0) + pick(pick(got, flip, 1), i, 0).astype(jnp.float32) + pick(got2, i, 0)
+
+    got3 = _exchange(part(1 - rem), [(i, i ^ (4 if i % 2 == 0 else 2)) for i in range(8)])
+    return part(rem) + got3
 
 
 def _allocate_kernel(*refs):

time: 381 us -> 377 us (0.990); the launches traced: 374 us -> 380 us
  Pallas kernels: 107 us -> 118 us
    pallas_call x8, Pallas kernels: 48.9 us -> 55.2 us  [layer_backward(): pl.pallas_call(functools.partial(_bwd_kernel, layer * KMAX, layer, entry)...]
    convert_element_type x1 -> x2, other arithmetic: 2.26 us -> 7.37 us  [_exchange(): send.astype(jnp.bfloat16)]
    pallas_call x8, Pallas kernels: 42.2 us -> 46.3 us  [layer_forward(): pl.pallas_call(functools.partial(_fwd_kernel, layer * KMAX, layer), out_s...]
    add x2 -> x1, other arithmetic: 8.25 us -> 4.49 us  [weight_grads(): return part(rem) + got3]
  transfers between devices with their start and end apart: 21 -> 21, of which waited for: 12 -> 12; matrix products, arithmetic and copies ran while one was open for 4% -> 4% of each run, Pallas kernels for 20% -> 22%
where the time goes in v3:
time: 377 us; the launch traced here: 380 us
  waiting for transfers between devices  120 us (32%)
  Pallas kernels  118 us (31%)
  starting transfers between devices  105 us (28%)
  local copies, waits for them, and re-layouts  19.2 us (5%)
  other arithmetic  17.2 us (5%)
    ppermute x18, starting transfers between devices, shifted(): lax.ppermute(value, axis, [(source, source + steps) for source in range(l...  105 us
    ppermute x18, waiting for transfers between devices, shifted(): lax.ppermute(value, axis, [(source, source + steps) for source in range(l...  78.6 us
    pallas_call x8, Pallas kernels, layer_backward(): pl.pallas_call(functools.partial(_bwd_kernel, layer * KMAX, layer, entry)...  55.2 us
    pallas_call x8, Pallas kernels, layer_forward(): pl.pallas_call(functools.partial(_fwd_kernel, layer * KMAX, layer), out_s...  46.3 us
    ppermute x2, waiting for transfers between devices, _exchange(): lax.ppermute(send.astype(jnp.bfloat16), 'dp', pairs).astype(jnp.float32)  41 us
    pallas_call x2, Pallas kernels, dw_half(): pl.pallas_call(_dw_half_kernel, out_shape=jax.ShapeDtypeStruct((4, per, B...  17 us
  transfers between devices with their start and end apart: 21, of which 12 were waited for; matrix products, arithmetic and copies ran while one was open for 4% of the time, Pallas kernels for 22%

profile of v3, /device:TPU:0, one launch (start us, length us, event | category | flops | bytes accessed | tf_op | source)
XLA Modules:
  0.0 380.4 jit_solution(9284362523270717331)
XLA Ops:
  0.0 15.7 %conditional.20 = ((bf16[32,8192]{1,0:T(8,128)(2,1)}, bf16[2,4,32,8192]{3,2,1,0:T(8,128)(2,1)}, f32[2,4,32,8192]{3,2,1,0:T(8,128)})) conditional(s32[]{:T(128)} %convert_element_type.117, (bf16[2,4,32,8192]{3,2,1,0:T(8,128)(2,1)}, f32[2,4,32,8192]{3,2,1,0:T(8,128)}) %tuple.135, (s32[]{:T(128)}, s32[256,3]{0,1:T(4,128)}, s32[]{:T(128)}, ...), branch_computations={%region_0.1_spmd, %region_1.2_spmd} | conditional | flops 6 | bytes 536640 | solution.py:386
  3.0 7.4 %branch_1_fun.42 = (bf16[32,8192]{1,0:T(8,128)(2,1)}, bf16[2,4,32,8192]{3,2,1,0:T(8,128)(2,1)}, f32[2,4,32,8192]{3,2,1,0:T(8,128)}) custom-call(s32[2]{0:T(128)} %pad_add_fusion.at_ref, s32[768]{0:T(1024)} %reshape.123.idx_ref, bf16[32,8192]{1,0:T(8,128)(2,1)} %broadcast_in_dim.9.h_in, ...), custom_call_target="tpu_custom_call", output_to_operand_aliasing={{1}: (4, {}), {2}: (5, {})} | custom-call | tf_op jit(solution)/shard_map/cond/branch_1_fun/pallas_call | solution.py:142
  10.4 5.3 %branch_1_fun.43 = (bf16[32,8192]{1,0:T(8,128)(2,1)}, bf16[2,4,32,8192]{3,2,1,0:T(8,128)(2,1)}, f32[2,4,32,8192]{3,2,1,0:T(8,128)}) custom-call(s32[1]{0:T(128)} %bitcast.at_ref, s32[768]{0:T(1024)} %reshape.123.idx_ref, bf16[32,8192]{1,0:T(8,128)(2,1)} %get-tuple-element.521.h_in, ...), custom_call_target="tpu_custom_call", output_to_operand_aliasing={{1}: (4, {}), {2}: (5, {})} | custom-call | tf_op jit(solution)/shard_map/cond/branch_1_fun/pallas_call | solution.py:142
  19.2 10.2 %collective-permute-done = bf16[32,8192]{1,0:T(8,128)(2,1)S(1)} collective-permute-done((bf16[32,8192]{1,0:T(8,128)(2,1)}, bf16[32,8192]{1,0:T(8,128)(2,1)S(1)}, u32[]{:S(2)}, u32[]{:S(2)}) %collective-permute-start) | collective-permute-done | bytes 524320 | tf_op jit(solution)/shard_map/ppermute | solution.py:27
  29.4 12.6 %conditional.21 = ((bf16[32,8192]{1,0:T(8,128)(2,1)S(1)}, bf16[2,4,32,8192]{3,2,1,0:T(8,128)(2,1)}, f32[2,4,32,8192]{3,2,1,0:T(8,128)})) conditional(s32[]{:T(128)} %convert_element_type.116, (bf16[32,8192]{1,0:T(8,128)(2,1)S(1)}, bf16[2,4,32,8192]{3,2,1,0:T(8,128)(2,1)}, f32[2,4,32,8192]{3,2,1,0:T(8,128)}) %tuple.137, (s32[]{:T(128)}, ...), branch_computations={%region_2.3_spmd, %region_3.4_spmd} | conditional | flops 6 | bytes 12350 | solution.py:386
  31.6 5.9 %branch_1_fun.44 = (bf16[32,8192]{1,0:T(8,128)(2,1)}, bf16[2,4,32,8192]{3,2,1,0:T(8,128)(2,1)}, f32[2,4,32,8192]{3,2,1,0:T(8,128)}) custom-call(s32[2]{0:T(128)} %pad_add_fusion.1.at_ref, s32[768]{0:T(1024)} %reshape.125.idx_ref, bf16[32,8192]{1,0:T(8,128)(2,1)S(1)} %get-tuple-element.527.h_in, ...), custom_call_target="tpu_custom_call", output_to_operand_aliasing={{1}: (4, {}), {2}: (5, {})} | custom-call | tf_op jit(solution)/shard_map/cond/branch_1_fun/pallas_call | solution.py:142
  37.6 4.5 %branch_1_fun.45 = (bf16[32,8192]{1,0:T(8,128)(2,1)S(1)}, bf16[2,4,32,8192]{3,2,1,0:T(8,128)(2,1)}, f32[2,4,32,8192]{3,2,1,0:T(8,128)}) custom-call(s32[1]{0:T(128)} %bitcast.2.at_ref, s32[768]{0:T(1024)} %reshape.125.idx_ref, bf16[32,8192]{1,0:T(8,128)(2,1)} %get-tuple-element.532.h_in, ...), custom_call_target="tpu_custom_call", output_to_operand_aliasing={{1}: (4, {}), {2}: (5, {})} | custom-call | tf_op jit(solution)/shard_map/cond/branch_1_fun/pallas_call | solution.py:142
  42.0 5.1 %collective-permute-start.1 = (bf16[32,8192]{1,0:T(8,128)(2,1)S(1)}, bf16[32,8192]{1,0:T(8,128)(2,1)}, u32[]{:S(2)}, u32[]{:S(2)}) collective-permute-start(bf16[32,8192]{1,0:T(8,128)(2,1)S(1)} %get-tuple-element.784), channel_id=1, source_target_pairs={{0,8},{8,16},{16,24},{1,9},{9,17},{17,25},{2,10},{10,18},{18,26},{... | collective-permute-start | bytes 1572872 | tf_op jit(solution)/shard_map/ppermute | solution.py:27
  48.5 9.1 %collective-permute-done.1 = bf16[32,8192]{1,0:T(8,128)(2,1)} collective-permute-done((bf16[32,8192]{1,0:T(8,128)(2,1)S(1)}, bf16[32,8192]{1,0:T(8,128)(2,1)}, u32[]{:S(2)}, u32[]{:S(2)}) %collective-permute-start.1) | collective-permute-done | bytes 524320 | tf_op jit(solution)/shard_map/ppermute | solution.py:27
  57.6 13.8 %conditional.22 = ((bf16[32,8192]{1,0:T(8,128)(2,1)}, bf16[2,4,32,8192]{3,2,1,0:T(8,128)(2,1)}, f32[2,4,32,8192]{3,2,1,0:T(8,128)})) conditional(s32[]{:T(128)} %convert_element_type.115, (bf16[32,8192]{1,0:T(8,128)(2,1)}, bf16[2,4,32,8192]{3,2,1,0:T(8,128)(2,1)}, f32[2,4,32,8192]{3,2,1,0:T(8,128)}) %tuple.139, (s32[]{:T(128)}, s32[256,3]{0,1:T(4,128)}, ...), branch_computations={%region_4.5_spmd, %region_5.6_spmd} | conditional | flops 6 | bytes 12350 | solution.py:386
  59.8 6.3 %branch_1_fun.46 = (bf16[32,8192]{1,0:T(8,128)(2,1)}, bf16[2,4,32,8192]{3,2,1,0:T(8,128)(2,1)}, f32[2,4,32,8192]{3,2,1,0:T(8,128)}) custom-call(s32[2]{0:T(128)} %pad_add_fusion.2.at_ref, s32[768]{0:T(1024)} %reshape.127.idx_ref, bf16[32,8192]{1,0:T(8,128)(2,1)} %get-tuple-element.538.h_in, ...), custom_call_target="tpu_custom_call", output_to_operand_aliasing={{1}: (4, {}), {2}: (5, {})} | custom-call | tf_op jit(solution)/shard_map/cond/branch_1_fun/pallas_call | solution.py:142
  66.0 5.3 %branch_1_fun.47 = (bf16[32,8192]{1,0:T(8,128)(2,1)}, bf16[2,4,32,8192]{3,2,1,0:T(8,128)(2,1)}, f32[2,4,32,8192]{3,2,1,0:T(8,128)}) custom-call(s32[1]{0:T(128)} %bitcast.4.at_ref, s32[768]{0:T(1024)} %reshape.127.idx_ref, bf16[32,8192]{1,0:T(8,128)(2,1)} %get-tuple-element.543.h_in, ...), custom_call_target="tpu_custom_call", output_to_operand_aliasing={{1}: (4, {}), {2}: (5, {})} | custom-call | tf_op jit(solution)/shard_map/cond/branch_1_fun/pallas_call | solution.py:142
  71.4 5.2 %collective-permute-start.2 = (bf16[32,8192]{1,0:T(8,128)(2,1)}, bf16[32,8192]{1,0:T(8,128)(2,1)}, u32[]{:S(2)}, u32[]{:S(2)}) collective-permute-start(bf16[32,8192]{1,0:T(8,128)(2,1)} %get-tuple-element.787), channel_id=1, source_target_pairs={{0,8},{8,16},{16,24},{1,9},{9,17},{17,25},{2,10},{10,18},{18,26},{... | collective-permute-start | bytes 1572872 | tf_op jit(solution)/shard_map/ppermute | solution.py:27
  78.0 8.5 %collective-permute-done.2 = bf16[32,8192]{1,0:T(8,128)(2,1)} collective-permute-done((bf16[32,8192]{1,0:T(8,128)(2,1)}, bf16[32,8192]{1,0:T(8,128)(2,1)}, u32[]{:S(2)}, u32[]{:S(2)}) %collective-permute-start.2) | collective-permute-done | bytes 524320 | tf_op jit(solution)/shard_map/ppermute | solution.py:27
  86.5 13.7 %conditional.23 = ((bf16[32,8192]{1,0:T(8,128)(2,1)}, bf16[2,4,32,8192]{3,2,1,0:T(8,128)(2,1)}, f32[2,4,32,8192]{3,2,1,0:T(8,128)})) conditional(s32[]{:T(128)} %convert_element_type.114, (bf16[32,8192]{1,0:T(8,128)(2,1)}, bf16[2,4,32,8192]{3,2,1,0:T(8,128)(2,1)}, f32[2,4,32,8192]{3,2,1,0:T(8,128)}) %tuple.141, (s32[]{:T(128)}, s32[256,3]{0,1:T(4,128)}, ...), branch_computations={%region_6.7_spmd, %region_7.8_spmd} | conditional | flops 6 | bytes 12350 | solution.py:386
  88.7 6.3 %branch_1_fun.48 = (bf16[32,8192]{1,0:T(8,128)(2,1)}, bf16[2,4,32,8192]{3,2,1,0:T(8,128)(2,1)}, f32[2,4,32,8192]{3,2,1,0:T(8,128)}) custom-call(s32[2]{0:T(128)} %pad_add_fusion.3.at_ref, s32[768]{0:T(1024)} %reshape.137.idx_ref, bf16[32,8192]{1,0:T(8,128)(2,1)} %get-tuple-element.549.h_in, ...), custom_call_target="tpu_custom_call", output_to_operand_aliasing={{1}: (4, {}), {2}: (5, {})} | custom-call | tf_op jit(solution)/shard_map/cond/branch_1_fun/pallas_call | solution.py:142
  95.0 5.3 %branch_1_fun.49 = (bf16[32,8192]{1,0:T(8,128)(2,1)}, bf16[2,4,32,8192]{3,2,1,0:T(8,128)(2,1)}, f32[2,4,32,8192]{3,2,1,0:T(8,128)}) custom-call(s32[1]{0:T(128)} %bitcast.6.at_ref, s32[768]{0:T(1024)} %reshape.137.idx_ref, bf16[32,8192]{1,0:T(8,128)(2,1)} %get-tuple-element.554.h_in, ...), custom_call_target="tpu_custom_call", output_to_operand_aliasing={{1}: (4, {}), {2}: (5, {})} | custom-call | tf_op jit(solution)/shard_map/cond/branch_1_fun/pallas_call | solution.py:142
  100.3 5.3 %collective-permute-start.3 = (bf16[32,8192]{1,0:T(8,128)(2,1)}, bf16[32,8192]{1,0:T(8,128)(2,1)}, u32[]{:S(2)}, u32[]{:S(2)}) collective-permute-start(bf16[32,8192]{1,0:T(8,128)(2,1)} %get-tuple-element.790), channel_id=1, source_target_pairs={{0,8},{8,16},{16,24},{1,9},{9,17},{17,25},{2,10},{10,18},{18,26},{... | collective-permute-start | bytes 1572872 | tf_op jit(solution)/shard_map/ppermute | solution.py:27
  106.8 7.6 %collective-permute-done.3 = bf16[32,8192]{1,0:T(8,128)(2,1)} collective-permute-done((bf16[32,8192]{1,0:T(8,128)(2,1)}, bf16[32,8192]{1,0:T(8,128)(2,1)}, u32[]{:S(2)}, u32[]{:S(2)}) %collective-permute-start.3) | collective-permute-done | bytes 524320 | tf_op jit(solution)/shard_map/ppermute | solution.py:27
  114.4 19.0 %collective-permute-start.4 = (bf16[32,8192]{1,0:T(8,128)(2,1)}, bf16[32,8192]{1,0:T(8,128)(2,1)}, u32[]{:S(2)}, u32[]{:S(2)}) collective-permute-start(bf16[32,8192]{1,0:T(8,128)(2,1)} %get-tuple-element.793), channel_id=1, source_target_pairs={{0,8},{8,16},{16,24},{1,9},{9,17},{17,25},{2,10},{10,18},{18,26},{... | collective-permute-start | bytes 1572872 | tf_op jit(solution)/shard_map/ppermute | solution.py:27
  134.7 6.7 %collective-permute-done.4 = bf16[32,8192]{1,0:T(8,128)(2,1)} collective-permute-done((bf16[32,8192]{1,0:T(8,128)(2,1)}, bf16[32,8192]{1,0:T(8,128)(2,1)}, u32[]{:S(2)}, u32[]{:S(2)}) %collective-permute-start.4) | collective-permute-done | bytes 524320 | tf_op jit(solution)/shard_map/ppermute | solution.py:27
  141.4 5.2 %collective-permute-start.5 = (bf16[32,8192]{1,0:T(8,128)(2,1)}, bf16[32,8192]{1,0:T(8,128)(2,1)}, u32[]{:S(2)}, u32[]{:S(2)}) collective-permute-start(bf16[32,8192]{1,0:T(8,128)(2,1)} %get-tuple-element.796), channel_id=1, source_target_pairs={{0,8},{8,16},{16,24},{1,9},{9,17},{17,25},{2,10},{10,18},{18,26},{... | collective-permute-start | bytes 1572872 | tf_op jit(solution)/shard_map/ppermute | solution.py:27
  147.9 5.8 %collective-permute-done.5 = bf16[32,8192]{1,0:T(8,128)(2,1)} collective-permute-done((bf16[32,8192]{1,0:T(8,128)(2,1)}, bf16[32,8192]{1,0:T(8,128)(2,1)}, u32[]{:S(2)}, u32[]{:S(2)}) %collective-permute-start.5) | collective-permute-done | bytes 524320 | tf_op jit(solution)/shard_map/ppermute | solution.py:27
  153.7 37.1 %collective-permute-start.6 = (bf16[32,8192]{1,0:T(8,128)(2,1)}, bf16[32,8192]{1,0:T(8,128)(2,1)}, u32[]{:S(2)}, u32[]{:S(2)}) collective-permute-start(bf16[32,8192]{1,0:T(8,128)(2,1)} %get-tuple-element.799), channel_id=1, source_target_pairs={{0,8},{8,16},{16,24},{1,9},{9,17},{17,25},{2,10},{10,18},{18,26},{... | collective-permute-start | bytes 1572872 | tf_op jit(solution)/shard_map/ppermute | solution.py:27
  190.8 7.3 %collective-permute-done.14 = bf16[32,8192]{1,0:T(8,128)(2,1)S(1)} collective-permute-done((bf16[32,8192]{1,0:T(8,128)(2,1)S(1)}, bf16[32,8192]{1,0:T(8,128)(2,1)S(1)}, u32[]{:S(2)}, u32[]{:S(2)}) %collective-permute-start.14) | collective-permute-done | bytes 524320 | tf_op jit(solution)/shard_map/ppermute | solution.py:27
  198.9 16.4 %conditional.36 = ((bf16[32,8192]{1,0:T(8,128)(2,1)}, bf16[2,4,32,8192]{3,2,1,0:T(8,128)(2,1)})) conditional(s32[]{:T(128)} %convert_element_type.121, (bf16[32,8192]{1,0:T(8,128)(2,1)}, bf16[2,4,32,8192]{3,2,1,0:T(8,128)(2,1)}) %tuple.299, (s32[]{:T(128)}, s32[256,3]{0,1:T(4,128)}, bf16[32,8192]{1,0:T(8,128)(2,1)}, f32[2,4,32,8192]{3,2,1,0:T(8,128)}, ...), branch_computations={%region_32.33_spmd, %region_33.34_spmd} | conditional | flops 6 | bytes 12350 | solution.py:401
  201.1 5.8 %branch_1_fun.74 = (bf16[32,8192]{1,0:T(8,128)(2,1)}, bf16[2,4,32,8192]{3,2,1,0:T(8,128)(2,1)}) custom-call(s32[2]{0:T(128)} %pad_add_fusion.16.at_ref, s32[768]{0:T(1024)} %reshape.163.idx_ref, bf16[32,8192]{1,0:T(8,128)(2,1)} %get-tuple-element.686.g_in, f32[2,4,32,8192]{3,2,1,0:T(8,128)} %get-tuple-element.687.sy_hbm, ...), custom_call_target="tpu_custom_call", output_to_operand_aliasing={{1}: (5, {})} | custom-call | tf_op jit(solution)/shard_map/cond/branch_1_fun/pallas_call | solution.py:223
  207.0 8.3 %branch_1_fun.75 = (bf16[32,8192]{1,0:T(8,128)(2,1)}, bf16[2,4,32,8192]{3,2,1,0:T(8,128)(2,1)}) custom-call(s32[1]{0:T(128)} %bitcast.32.at_ref, s32[768]{0:T(1024)} %reshape.163.idx_ref, bf16[32,8192]{1,0:T(8,128)(2,1)} %get-tuple-element.691.g_in, f32[2,4,32,8192]{3,2,1,0:T(8,128)} %get-tuple-element.687.sy_hbm, ...), custom_call_target="tpu_custom_call", output_to_operand_aliasing={{1}: (5, {})} | custom-call | tf_op jit(solution)/shard_map/cond/branch_1_fun/pallas_call | solution.py:223
  216.6 5.3 %collective-permute-start.7 = (bf16[32,8192]{1,0:T(8,128)(2,1)}, bf16[32,8192]{1,0:T(8,128)(2,1)S(1)}, u32[]{:S(2)}, u32[]{:S(2)}) collective-permute-start(bf16[32,8192]{1,0:T(8,128)(2,1)} %get-tuple-element.802), channel_id=1, source_target_pairs={{0,8},{8,16},{16,24},{1,9},{9,17},{17,25},{2,10},{10,18},{18,26},{... | collective-permute-start | bytes 1572872 | tf_op jit(solution)/shard_map/ppermute | solution.py:27
  221.9 7.6 %collective-permute-done.15 = bf16[32,8192]{1,0:T(8,128)(2,1)S(1)} collective-permute-done((bf16[32,8192]{1,0:T(8,128)(2,1)}, bf16[32,8192]{1,0:T(8,128)(2,1)S(1)}, u32[]{:S(2)}, u32[]{:S(2)}) %collective-permute-start.15) | collective-permute-done | bytes 524320 | tf_op jit(solution)/shard_map/ppermute | solution.py:27
  229.6 15.3 %conditional.37 = ((bf16[32,8192]{1,0:T(8,128)(2,1)S(1)}, bf16[2,4,32,8192]{3,2,1,0:T(8,128)(2,1)})) conditional(s32[]{:T(128)} %convert_element_type.120, (bf16[32,8192]{1,0:T(8,128)(2,1)S(1)}, bf16[2,4,32,8192]{3,2,1,0:T(8,128)(2,1)}) %tuple.168, (s32[]{:T(128)}, s32[256,3]{0,1:T(4,128)}, s32[]{:T(128)}, bf16[32,8192]{1,0:T(8,128)(2,1)S(1)}, ...), branch_computations={%region_34.35_spmd, %region_35.36_spmd} | conditional | flops 6 | bytes 12350 | solution.py:401
  231.9 5.5 %branch_1_fun.76 = (bf16[32,8192]{1,0:T(8,128)(2,1)}, bf16[2,4,32,8192]{3,2,1,0:T(8,128)(2,1)}) custom-call(s32[2]{0:T(128)} %pad_add_fusion.17.at_ref, s32[768]{0:T(1024)} %reshape.165.idx_ref, bf16[32,8192]{1,0:T(8,128)(2,1)S(1)} %get-tuple-element.696.g_in, f32[2,4,32,8192]{3,2,1,0:T(8,128)} %get-tuple-element.697.sy_hbm, ...), custom_call_target="tpu_custom_call", output_to_operand_aliasing={{1}: (5, {})} | custom-call | tf_op jit(solution)/shard_map/cond/branch_1_fun/pallas_call | solution.py:223
  237.4 7.5 %branch_1_fun.77 = (bf16[32,8192]{1,0:T(8,128)(2,1)S(1)}, bf16[2,4,32,8192]{3,2,1,0:T(8,128)(2,1)}) custom-call(s32[1]{0:T(128)} %bitcast.34.at_ref, s32[768]{0:T(1024)} %reshape.165.idx_ref, bf16[32,8192]{1,0:T(8,128)(2,1)} %get-tuple-element.701.g_in, f32[2,4,32,8192]{3,2,1,0:T(8,128)} %get-tuple-element.697.sy_hbm, ...), custom_call_target="tpu_custom_call", output_to_operand_aliasing={{1}: (5, {})} | custom-call | tf_op jit(solution)/shard_map/cond/branch_1_fun/pallas_call | solution.py:223
  247.0 10.2 %collective-permute-start.8 = (bf16[32,8192]{1,0:T(8,128)(2,1)}, bf16[32,8192]{1,0:T(8,128)(2,1)S(1)}, u32[]{:S(2)}, u32[]{:S(2)}) collective-permute-start(bf16[32,8192]{1,0:T(8,128)(2,1)} %get-tuple-element.807), channel_id=1, source_target_pairs={{0,8},{8,16},{16,24},{1,9},{9,17},{17,25},{2,10},{10,18},{18,26},{... | collective-permute-start | bytes 1572872 | tf_op jit(solution)/shard_map/ppermute | solution.py:27
  257.2 6.1 %collective-permute-done.16 = bf16[32,8192]{1,0:T(8,128)(2,1)} collective-permute-done((bf16[32,8192]{1,0:T(8,128)(2,1)S(1)}, bf16[32,8192]{1,0:T(8,128)(2,1)}, u32[]{:S(2)}, u32[]{:S(2)}) %collective-permute-start.16) | collective-permute-done | bytes 524320 | tf_op jit(solution)/shard_map/ppermute | solution.py:27
  263.3 16.5 %conditional.38 = ((bf16[32,8192]{1,0:T(8,128)(2,1)}, bf16[2,4,32,8192]{3,2,1,0:T(8,128)(2,1)})) conditional(s32[]{:T(128)} %convert_element_type.119, (bf16[32,8192]{1,0:T(8,128)(2,1)}, bf16[2,4,32,8192]{3,2,1,0:T(8,128)(2,1)}) %tuple.170, (s32[]{:T(128)}, s32[256,3]{0,1:T(4,128)}, s32[]{:T(128)}, bf16[32,8192]{1,0:T(8,128)(2,1)}, ...), branch_computations={%region_36.37_spmd.clone, %region_37.38_spmd.clone} | conditional | flops 6 | bytes 12350 | solution.py:401
  265.6 5.9 %branch_1_fun.80 = (bf16[32,8192]{1,0:T(8,128)(2,1)}, bf16[2,4,32,8192]{3,2,1,0:T(8,128)(2,1)}) custom-call(s32[2]{0:T(128)} %pad_add_fusion.19.at_ref, s32[768]{0:T(1024)} %reshape.185.idx_ref, bf16[32,8192]{1,0:T(8,128)(2,1)} %get-tuple-element.837.g_in, f32[2,4,32,8192]{3,2,1,0:T(8,128)} %get-tuple-element.838.sy_hbm, ...), custom_call_target="tpu_custom_call", output_to_operand_aliasing={{1}: (5, {})} | custom-call | tf_op jit(solution)/shard_map/cond/branch_1_fun/pallas_call | solution.py:223
  271.5 8.3 %branch_1_fun.81 = (bf16[32,8192]{1,0:T(8,128)(2,1)}, bf16[2,4,32,8192]{3,2,1,0:T(8,128)(2,1)}) custom-call(s32[1]{0:T(128)} %bitcast.49.at_ref, s32[768]{0:T(1024)} %reshape.185.idx_ref, bf16[32,8192]{1,0:T(8,128)(2,1)} %get-tuple-element.842.g_in, f32[2,4,32,8192]{3,2,1,0:T(8,128)} %get-tuple-element.838.sy_hbm, ...), custom_call_target="tpu_custom_call", output_to_operand_aliasing={{1}: (5, {})} | custom-call | tf_op jit(solution)/shard_map/cond/branch_1_fun/pallas_call | solution.py:223
  282.8 9.7 %collective-permute-done.17 = bf16[32,8192]{1,0:T(8,128)(2,1)S(1)} collective-permute-done((bf16[32,8192]{1,0:T(8,128)(2,1)}, bf16[32,8192]{1,0:T(8,128)(2,1)S(1)}, u32[]{:S(2)}, u32[]{:S(2)}) %collective-permute-start.17) | collective-permute-done | bytes 524320 | tf_op jit(solution)/shard_map/ppermute | solution.py:27
  292.5 15.3 %conditional.39 = (bf16[2,4,32,8192]{3,2,1,0:T(8,128)(2,1)}) conditional(s32[]{:T(128)} %convert_element_type.118, bf16[2,4,32,8192]{3,2,1,0:T(8,128)(2,1)} %get-tuple-element.826, (s32[]{:T(128)}, s32[256,3]{0,1:T(4,128)S(1)}, s32[]{:T(128)}, bf16[32,8192]{1,0:T(8,128)(2,1)S(1)}, f32[2,4,32,8192]{3,2,1,0:T(8,128)}, ...), branch_computations={%region_38.39_spmd, %region_39.40_spmd} | conditional | flops 6 | bytes 12350 | solution.py:401
  294.0 5.5 %branch_1_fun.78 = (bf16[32,8192]{1,0:T(8,128)(2,1)}, bf16[2,4,32,8192]{3,2,1,0:T(8,128)(2,1)}) custom-call(s32[2]{0:T(128)} %pad_add_fusion.18.at_ref, s32[768]{0:T(1024)} %reshape.169.idx_ref, bf16[32,8192]{1,0:T(8,128)(2,1)S(1)} %get-tuple-element.720.g_in, f32[2,4,32,8192]{3,2,1,0:T(8,128)} %get-tuple-element.721.sy_hbm, ...), custom_call_target="tpu_custom_call", output_to_operand_aliasing={{1}: (5, {})} | custom-call | tf_op jit(solution)/shard_map/cond/branch_1_fun/pallas_call | solution.py:223
  299.5 8.3 %branch_1_fun.79 = (bf16[32,8192]{1,0:T(8,128)(2,1)}, bf16[2,4,32,8192]{3,2,1,0:T(8,128)(2,1)}) custom-call(s32[1]{0:T(128)} %bitcast.36.at_ref, s32[768]{0:T(1024)} %reshape.169.idx_ref, bf16[32,8192]{1,0:T(8,128)(2,1)} %get-tuple-element.725.g_in, f32[2,4,32,8192]{3,2,1,0:T(8,128)} %get-tuple-element.721.sy_hbm, ...), custom_call_target="tpu_custom_call", output_to_operand_aliasing={{1}: (5, {})} | custom-call | tf_op jit(solution)/shard_map/cond/branch_1_fun/pallas_call | solution.py:223
  307.8 7.7 %shard_map.48 = bf16[4,32,128,128]{3,2,1,0:T(8,128)(2,1)} custom-call(s32[1]{0:T(128)} %bitcast.42.sel_ref, s32[768]{0:T(1024)} %reshape.178.idx_ref, bf16[2,4,32,8192]{3,2,1,0:T(8,128)(2,1)} %get-tuple-element.808.h_ref, bf16[2,4,32,8192]{3,2,1,0:T(8,128)(2,1)} %get-tuple-element.1118.s_ref), custom_call_target="tpu_custom_call" | custom-call | tf_op jit(solution)/shard_map/pallas_call | solution.py:309
  315.6 9.3 %shard_map.47 = f32[4,32,128,128]{3,2,1,0:T(8,128)} custom-call(s32[1]{0:T(128)} %bitcast.38.sel_ref, s32[768]{0:T(1024)} %reshape.178.idx_ref, bf16[2,4,32,8192]{3,2,1,0:T(8,128)(2,1)} %get-tuple-element.808.h_ref, bf16[2,4,32,8192]{3,2,1,0:T(8,128)(2,1)} %get-tuple-element.1118.s_ref), custom_call_target="tpu_custom_call" | custom-call | tf_op jit(solution)/shard_map/pallas_call | solution.py:309
  324.9 5.0 %fusion = bf16[2,32,128,128]{3,2,1,0:T(8,128)(2,1)} fusion(f32[2,2,32,128,128]{4,3,2,1,0:T(8,128)} %bitcast.80, s32[]{:T(128)S(6)} %select_n.64, bf16[2,2,32,128,128]{4,3,2,1,0:T(8,128)(2,1)} %bitcast.43), kind=kLoop, calls=%fused_computation.21 | loop fusion | flops 3145728 | bytes 8388612 | tf_op jit(solution)/shard_map/convert_element_type | solution.py:319
  329.9 26.2 %collective-permute-done.19 = bf16[2,32,128,128]{3,2,1,0:T(8,128)(2,1)S(1)} collective-permute-done((bf16[2,32,128,128]{3,2,1,0:T(8,128)(2,1)}, bf16[2,32,128,128]{3,2,1,0:T(8,128)(2,1)S(1)}, u32[]{:S(2)}, u32[]{:S(2)}) %collective-permute-start.19) | collective-permute-done | bytes 2097184 | tf_op jit(solution)/shard_map/ppermute | solution.py:319
  361.2 14.8 %collective-permute-done.20 = bf16[32,128,128]{2,1,0:T(8,128)(2,1)S(1)} collective-permute-done((bf16[32,128,128]{2,1,0:T(8,128)(2,1)S(1)}, bf16[32,128,128]{2,1,0:T(8,128)(2,1)S(1)}, u32[]{:S(2)}, u32[]{:S(2)}) %collective-permute-start.20) | collective-permute-done | bytes 1048608 | tf_op jit(solution)/shard_map/ppermute | solution.py:319
  376.0 4.5 %fusion.2 = f32[32,128,128]{2,1,0:T(8,128)} fusion(bf16[32,128,128]{2,1,0:T(8,128)(2,1)S(1)} %collective-permute-done.20, f32[2,32,128,128]{3,2,1,0:T(8,128)} %copy-done.1, s32[]{:T(128)S(6)} %select_n.59, f32[2,2,32,128,128]{4,3,2,1,0:T(8,128)} %bitcast.82, s32[]{:T(128)S(6)} %select_n.60, s32[]{:T(128)S(6)} %select_n.63, ...), kind=kLoop, calls=%fused_computation.25 | loop fusion | flops 2621440 | bytes 8388620 | tf_op jit(solution)/shard_map/add | solution.py:350
  (75 shorter events, 40.8 us)
Async XLA Ops:
  15.7 13.7 %collective-permute-start = (bf16[32,8192]{1,0:T(8,128)(2,1)}, bf16[32,8192]{1,0:T(8,128)(2,1)S(1)}, u32[]{:S(2)}, u32[]{:S(2)}) collective-permute-start(bf16[32,8192]{1,0:T(8,128)(2,1)} %get-tuple-element.781), channel_id=1, source_target_pairs={{0,8},{8,16},{16,24},{1,9},{9,17},{17,25},{2,10},{10,18},{18,26},{... | collective-permute-start | bytes 1572872 | tf_op jit(solution)/shard_map/ppermute | solution.py:27
  17.1 12.3 %copy-start = (bf16[2,64,8192]{2,1,0:T(8,128)(2,1)S(1)}, bf16[2,64,8192]{2,1,0:T(8,128)(2,1)}, u32[]{:S(2)}) copy-start(bf16[2,64,8192]{2,1,0:T(8,128)(2,1)} %param.44) | copy-start | bytes 6291460
  17.9 29.3 %collective-permute-start.9 = (bf16[32,8192]{1,0:T(8,128)(2,1)}, bf16[32,8192]{1,0:T(8,128)(2,1)S(1)}, u32[]{:S(2)}, u32[]{:S(2)}) collective-permute-start(bf16[32,8192]{1,0:T(8,128)(2,1)} %get-tuple-element.810), channel_id=1, source_target_pairs={{8,0},{16,8},{24,16},{9,1},{17,9},{25,17},{10,2},{18,10},{26,18},{... | collective-permute-start | bytes 1572872 | tf_op jit(solution)/shard_map/ppermute | solution.py:27
  42.0 15.5 %collective-permute-start.1 = (bf16[32,8192]{1,0:T(8,128)(2,1)S(1)}, bf16[32,8192]{1,0:T(8,128)(2,1)}, u32[]{:S(2)}, u32[]{:S(2)}) collective-permute-start(bf16[32,8192]{1,0:T(8,128)(2,1)S(1)} %get-tuple-element.784), channel_id=1, source_target_pairs={{0,8},{8,16},{16,24},{1,9},{9,17},{17,25},{2,10},{10,18},{18,26},{... | collective-permute-start | bytes 1572872 | tf_op jit(solution)/shard_map/ppermute | solution.py:27
  47.2 29.5 %collective-permute-start.10 = (bf16[32,8192]{1,0:T(8,128)(2,1)S(1)}, bf16[32,8192]{1,0:T(8,128)(2,1)}, u32[]{:S(2)}, u32[]{:S(2)}) collective-permute-start(bf16[32,8192]{1,0:T(8,128)(2,1)S(1)} %get-tuple-element.812), channel_id=1, source_target_pairs={{8,0},{16,8},{24,16},{9,1},{17,9},{25,17},{10,2},{18,10},{26,18},{... | collective-permute-start | bytes 1572872 | tf_op jit(solution)/shard_map/ppermute | solution.py:27
  71.4 15.1 %collective-permute-start.2 = (bf16[32,8192]{1,0:T(8,128)(2,1)}, bf16[32,8192]{1,0:T(8,128)(2,1)}, u32[]{:S(2)}, u32[]{:S(2)}) collective-permute-start(bf16[32,8192]{1,0:T(8,128)(2,1)} %get-tuple-element.787), channel_id=1, source_target_pairs={{0,8},{8,16},{16,24},{1,9},{9,17},{17,25},{2,10},{10,18},{18,26},{... | collective-permute-start | bytes 1572872 | tf_op jit(solution)/shard_map/ppermute | solution.py:27
  76.7 28.9 %collective-permute-start.11 = (bf16[32,8192]{1,0:T(8,128)(2,1)}, bf16[32,8192]{1,0:T(8,128)(2,1)S(1)}, u32[]{:S(2)}, u32[]{:S(2)}) collective-permute-start(bf16[32,8192]{1,0:T(8,128)(2,1)} %get-tuple-element.814), channel_id=1, source_target_pairs={{8,0},{16,8},{24,16},{9,1},{17,9},{25,17},{10,2},{18,10},{26,18},{... | collective-permute-start | bytes 1572872 | tf_op jit(solution)/shard_map/ppermute | solution.py:27
  100.3 14.2 %collective-permute-start.3 = (bf16[32,8192]{1,0:T(8,128)(2,1)}, bf16[32,8192]{1,0:T(8,128)(2,1)}, u32[]{:S(2)}, u32[]{:S(2)}) collective-permute-start(bf16[32,8192]{1,0:T(8,128)(2,1)} %get-tuple-element.790), channel_id=1, source_target_pairs={{0,8},{8,16},{16,24},{1,9},{9,17},{17,25},{2,10},{10,18},{18,26},{... | collective-permute-start | bytes 1572872 | tf_op jit(solution)/shard_map/ppermute | solution.py:27
  105.5 27.9 %collective-permute-start.12 = (bf16[32,8192]{1,0:T(8,128)(2,1)S(1)}, bf16[32,8192]{1,0:T(8,128)(2,1)S(1)}, u32[]{:S(2)}, u32[]{:S(2)}) collective-permute-start(bf16[32,8192]{1,0:T(8,128)(2,1)S(1)} %get-tuple-element.816), channel_id=1, source_target_pairs={{8,0},{16,8},{24,16},{9,1},{17,9},{25,17},{10,2},{18,10},{26,18},{... | collective-permute-start | bytes 1572872 | tf_op jit(solution)/shard_map/ppermute | solution.py:27
  114.4 27.0 %collective-permute-start.4 = (bf16[32,8192]{1,0:T(8,128)(2,1)}, bf16[32,8192]{1,0:T(8,128)(2,1)}, u32[]{:S(2)}, u32[]{:S(2)}) collective-permute-start(bf16[32,8192]{1,0:T(8,128)(2,1)} %get-tuple-element.793), channel_id=1, source_target_pairs={{0,8},{8,16},{16,24},{1,9},{9,17},{17,25},{2,10},{10,18},{18,26},{... | collective-permute-start | bytes 1572872 | tf_op jit(solution)/shard_map/ppermute | solution.py:27
  133.4 13.2 %collective-permute-start.13 = (bf16[32,8192]{1,0:T(8,128)(2,1)S(1)}, bf16[32,8192]{1,0:T(8,128)(2,1)S(1)}, u32[]{:S(2)}, u32[]{:S(2)}) collective-permute-start(bf16[32,8192]{1,0:T(8,128)(2,1)S(1)} %get-tuple-element.818), channel_id=1, source_target_pairs={{8,0},{16,8},{24,16},{9,1},{17,9},{25,17},{10,2},{18,10},{26,18},{... | collective-permute-start | bytes 1572872 | tf_op jit(solution)/shard_map/ppermute | solution.py:27
  141.4 12.3 %collective-permute-start.5 = (bf16[32,8192]{1,0:T(8,128)(2,1)}, bf16[32,8192]{1,0:T(8,128)(2,1)}, u32[]{:S(2)}, u32[]{:S(2)}) collective-permute-start(bf16[32,8192]{1,0:T(8,128)(2,1)} %get-tuple-element.796), channel_id=1, source_target_pairs={{0,8},{8,16},{16,24},{1,9},{9,17},{17,25},{2,10},{10,18},{18,26},{... | collective-permute-start | bytes 1572872 | tf_op jit(solution)/shard_map/ppermute | solution.py:27
  146.6 51.4 %collective-permute-start.14 = (bf16[32,8192]{1,0:T(8,128)(2,1)S(1)}, bf16[32,8192]{1,0:T(8,128)(2,1)S(1)}, u32[]{:S(2)}, u32[]{:S(2)}) collective-permute-start(bf16[32,8192]{1,0:T(8,128)(2,1)S(1)} %get-tuple-element.820), channel_id=1, source_target_pairs={{8,0},{16,8},{24,16},{9,1},{17,9},{25,17},{10,2},{18,10},{26,18},{... | collective-permute-start | bytes 1572872 | tf_op jit(solution)/shard_map/ppermute | solution.py:27
  153.7 62.9 %collective-permute-start.6 = (bf16[32,8192]{1,0:T(8,128)(2,1)}, bf16[32,8192]{1,0:T(8,128)(2,1)}, u32[]{:S(2)}, u32[]{:S(2)}) collective-permute-start(bf16[32,8192]{1,0:T(8,128)(2,1)} %get-tuple-element.799), channel_id=1, source_target_pairs={{0,8},{8,16},{16,24},{1,9},{9,17},{17,25},{2,10},{10,18},{18,26},{... | collective-permute-start | bytes 1572872 | tf_op jit(solution)/shard_map/ppermute | solution.py:27
  198.1 0.8 copy-start.4
  215.3 14.3 %collective-permute-start.15 = (bf16[32,8192]{1,0:T(8,128)(2,1)}, bf16[32,8192]{1,0:T(8,128)(2,1)S(1)}, u32[]{:S(2)}, u32[]{:S(2)}) collective-permute-start(bf16[32,8192]{1,0:T(8,128)(2,1)} %get-tuple-element.822), channel_id=1, source_target_pairs={{8,0},{16,8},{24,16},{9,1},{17,9},{25,17},{10,2},{18,10},{26,18},{... | collective-permute-start | bytes 1572872 | tf_op jit(solution)/shard_map/ppermute | solution.py:27
  216.6 29.6 %collective-permute-start.7 = (bf16[32,8192]{1,0:T(8,128)(2,1)}, bf16[32,8192]{1,0:T(8,128)(2,1)S(1)}, u32[]{:S(2)}, u32[]{:S(2)}) collective-permute-start(bf16[32,8192]{1,0:T(8,128)(2,1)} %get-tuple-element.802), channel_id=1, source_target_pairs={{0,8},{8,16},{16,24},{1,9},{9,17},{17,25},{2,10},{10,18},{18,26},{... | collective-permute-start | bytes 1572872 | tf_op jit(solution)/shard_map/ppermute | solution.py:27
  244.9 18.4 %collective-permute-start.16 = (bf16[32,8192]{1,0:T(8,128)(2,1)S(1)}, bf16[32,8192]{1,0:T(8,128)(2,1)}, u32[]{:S(2)}, u32[]{:S(2)}) collective-permute-start(bf16[32,8192]{1,0:T(8,128)(2,1)S(1)} %get-tuple-element.824), channel_id=1, source_target_pairs={{8,0},{16,8},{24,16},{9,1},{17,9},{25,17},{10,2},{18,10},{26,18},{... | collective-permute-start | bytes 1572872 | tf_op jit(solution)/shard_map/ppermute | solution.py:27
  246.2 0.8 copy-start.3
  247.0 35.8 %collective-permute-start.8 = (bf16[32,8192]{1,0:T(8,128)(2,1)}, bf16[32,8192]{1,0:T(8,128)(2,1)S(1)}, u32[]{:S(2)}, u32[]{:S(2)}) collective-permute-start(bf16[32,8192]{1,0:T(8,128)(2,1)} %get-tuple-element.807), channel_id=1, source_target_pairs={{0,8},{8,16},{16,24},{1,9},{9,17},{17,25},{2,10},{10,18},{18,26},{... | collective-permute-start | bytes 1572872 | tf_op jit(solution)/shard_map/ppermute | solution.py:27
  263.3 19.5 %copy-start.2 = (s32[256,3]{0,1:T(4,128)S(1)}, s32[256,3]{0,1:T(4,128)}, u32[]{:S(2)}) copy-start(s32[256,3]{0,1:T(4,128)} %param.47) | copy-start | bytes 9220
  279.8 12.6 %collective-permute-start.17 = (bf16[32,8192]{1,0:T(8,128)(2,1)}, bf16[32,8192]{1,0:T(8,128)(2,1)S(1)}, u32[]{:S(2)}, u32[]{:S(2)}) collective-permute-start(bf16[32,8192]{1,0:T(8,128)(2,1)} %get-tuple-element.827), channel_id=1, source_target_pairs={{8,0},{16,8},{24,16},{9,1},{17,9},{25,17},{10,2},{18,10},{26,18},{... | collective-permute-start | bytes 1572872 | tf_op jit(solution)/shard_map/ppermute | solution.py:27
  315.6 9.3 %collective-permute-start.18 = (bf16[4,32,128,128]{3,2,1,0:T(8,128)(2,1)}, bf16[4,32,128,128]{3,2,1,0:T(8,128)(2,1)}, u32[]{:S(2)}, u32[]{:S(2)}) collective-permute-start(bf16[4,32,128,128]{3,2,1,0:T(8,128)(2,1)} %shard_map.48), channel_id=1, source_target_pairs={{0,1},{1,0},{2,3},{3,2},{4,5},{5,4},{6,7},{7,6},{8,9},{9,8},{10,11... | collective-permute-start | bytes 12582920 | tf_op jit(solution)/shard_map/ppermute | solution.py:333
  329.9 26.2 %collective-permute-start.19 = (bf16[2,32,128,128]{3,2,1,0:T(8,128)(2,1)}, bf16[2,32,128,128]{3,2,1,0:T(8,128)(2,1)S(1)}, u32[]{:S(2)}, u32[]{:S(2)}) collective-permute-start(bf16[2,32,128,128]{3,2,1,0:T(8,128)(2,1)} %fusion), channel_id=1, source_target_pairs={{0,2},{1,5},{2,0},{3,7},{4,6},{5,1},{6,4},{7,3},{8,10},{9,13},{10,... | collective-permute-start | bytes 6291464 | tf_op jit(solution)/shard_map/ppermute | solution.py:319
  356.7 2.1 copy-start.1
  361.1 14.9 %collective-permute-start.20 = (bf16[32,128,128]{2,1,0:T(8,128)(2,1)S(1)}, bf16[32,128,128]{2,1,0:T(8,128)(2,1)S(1)}, u32[]{:S(2)}, u32[]{:S(2)}) collective-permute-start(bf16[32,128,128]{2,1,0:T(8,128)(2,1)S(1)} %fusion.1), channel_id=1, source_target_pairs={{0,4},{1,3},{2,6},{3,1},{4,0},{5,7},{6,2},{7,5},{8,12},{9,11},{10,... | collective-permute-start | bytes 3145736 | tf_op jit(solution)/shard_map/ppermute | solution.py:319

commit v4 on v3

--- a/solution.py
+++ b/solution.py
@@ -13,7 +13,7 @@
 CH = 512
 NSUB = 16
 SPLIT = 2
-GROUP = 8
+GROUP = 16
 VMEM_LIMIT = 60 * 1024 * 1024
 
 _SMEM = pl.BlockSpec(memory_space=pltpu.SMEM)

time: 377 us -> 382 us (1.013); the launches traced: 380 us -> 379 us
  no operation moved by 1% of the time
where the time goes in v4:
time: 382 us; the launch traced here: 379 us
  waiting for transfers between devices  120 us (31%)
  Pallas kernels  115 us (30%)
  starting transfers between devices  107 us (28%)
  local copies, waits for them, and re-layouts  19.2 us (5%)
  other arithmetic  17.2 us (5%)
    ppermute x18, starting transfers between devices, shifted(): lax.ppermute(value, axis, [(source, source + steps) for source in range(l...  106 us
    ppermute x18, waiting for transfers between devices, shifted(): lax.ppermute(value, axis, [(source, source + steps) for source in range(l...  79.1 us
    pallas_call x8, Pallas kernels, layer_backward(): pl.pallas_call(functools.partial(_bwd_kernel, layer * KMAX, layer, entry)...  53.6 us
    pallas_call x8, Pallas kernels, layer_forward(): pl.pallas_call(functools.partial(_fwd_kernel, layer * KMAX, layer), out_s...  45.2 us
    ppermute x2, waiting for transfers between devices, _exchange(): lax.ppermute(send.astype(jnp.bfloat16), 'dp', pairs).astype(jnp.float32)  41 us
    pallas_call x2, Pallas kernels, dw_half(): pl.pallas_call(_dw_half_kernel, out_shape=jax.ShapeDtypeStruct((4, per, B...  16.6 us
  transfers between devices with their start and end apart: 21, of which 12 were waited for; matrix products, arithmetic and copies ran while one was open for 4% of the time, Pallas kernels for 22%

profile of v4, /device:TPU:0, one launch (start us, length us, event | category | flops | bytes accessed | tf_op | source)
XLA Modules:
  0.0 379.1 jit_solution(9284362523270717331)
XLA Ops:
  0.0 15.4 %conditional.20 = ((bf16[32,8192]{1,0:T(8,128)(2,1)}, bf16[2,4,32,8192]{3,2,1,0:T(8,128)(2,1)}, f32[2,4,32,8192]{3,2,1,0:T(8,128)})) conditional(s32[]{:T(128)} %convert_element_type.117, (bf16[2,4,32,8192]{3,2,1,0:T(8,128)(2,1)}, f32[2,4,32,8192]{3,2,1,0:T(8,128)}) %tuple.135, (s32[]{:T(128)}, s32[256,3]{0,1:T(4,128)}, s32[]{:T(128)}, ...), branch_computations={%region_0.1_spmd, %region_1.2_spmd} | conditional | flops 6 | bytes 536640 | solution.py:386
  3.0 7.2 %branch_1_fun.42 = (bf16[32,8192]{1,0:T(8,128)(2,1)}, bf16[2,4,32,8192]{3,2,1,0:T(8,128)(2,1)}, f32[2,4,32,8192]{3,2,1,0:T(8,128)}) custom-call(s32[2]{0:T(128)} %pad_add_fusion.at_ref, s32[768]{0:T(1024)} %reshape.123.idx_ref, bf16[32,8192]{1,0:T(8,128)(2,1)} %broadcast_in_dim.9.h_in, ...), custom_call_target="tpu_custom_call", output_to_operand_aliasing={{1}: (4, {}), {2}: (5, {})} | custom-call | tf_op jit(solution)/shard_map/cond/branch_1_fun/pallas_call | solution.py:142
  10.2 5.3 %branch_1_fun.43 = (bf16[32,8192]{1,0:T(8,128)(2,1)}, bf16[2,4,32,8192]{3,2,1,0:T(8,128)(2,1)}, f32[2,4,32,8192]{3,2,1,0:T(8,128)}) custom-call(s32[1]{0:T(128)} %bitcast.at_ref, s32[768]{0:T(1024)} %reshape.123.idx_ref, bf16[32,8192]{1,0:T(8,128)(2,1)} %get-tuple-element.521.h_in, ...), custom_call_target="tpu_custom_call", output_to_operand_aliasing={{1}: (4, {}), {2}: (5, {})} | custom-call | tf_op jit(solution)/shard_map/cond/branch_1_fun/pallas_call | solution.py:142
  18.9 10.2 %collective-permute-done = bf16[32,8192]{1,0:T(8,128)(2,1)S(1)} collective-permute-done((bf16[32,8192]{1,0:T(8,128)(2,1)}, bf16[32,8192]{1,0:T(8,128)(2,1)S(1)}, u32[]{:S(2)}, u32[]{:S(2)}) %collective-permute-start) | collective-permute-done | bytes 524320 | tf_op jit(solution)/shard_map/ppermute | solution.py:27
  29.1 12.4 %conditional.21 = ((bf16[32,8192]{1,0:T(8,128)(2,1)S(1)}, bf16[2,4,32,8192]{3,2,1,0:T(8,128)(2,1)}, f32[2,4,32,8192]{3,2,1,0:T(8,128)})) conditional(s32[]{:T(128)} %convert_element_type.116, (bf16[32,8192]{1,0:T(8,128)(2,1)S(1)}, bf16[2,4,32,8192]{3,2,1,0:T(8,128)(2,1)}, f32[2,4,32,8192]{3,2,1,0:T(8,128)}) %tuple.137, (s32[]{:T(128)}, ...), branch_computations={%region_2.3_spmd, %region_3.4_spmd} | conditional | flops 6 | bytes 12350 | solution.py:386
  31.4 5.7 %branch_1_fun.44 = (bf16[32,8192]{1,0:T(8,128)(2,1)}, bf16[2,4,32,8192]{3,2,1,0:T(8,128)(2,1)}, f32[2,4,32,8192]{3,2,1,0:T(8,128)}) custom-call(s32[2]{0:T(128)} %pad_add_fusion.1.at_ref, s32[768]{0:T(1024)} %reshape.125.idx_ref, bf16[32,8192]{1,0:T(8,128)(2,1)S(1)} %get-tuple-element.527.h_in, ...), custom_call_target="tpu_custom_call", output_to_operand_aliasing={{1}: (4, {}), {2}: (5, {})} | custom-call | tf_op jit(solution)/shard_map/cond/branch_1_fun/pallas_call | solution.py:142
  37.0 4.5 %branch_1_fun.45 = (bf16[32,8192]{1,0:T(8,128)(2,1)S(1)}, bf16[2,4,32,8192]{3,2,1,0:T(8,128)(2,1)}, f32[2,4,32,8192]{3,2,1,0:T(8,128)}) custom-call(s32[1]{0:T(128)} %bitcast.2.at_ref, s32[768]{0:T(1024)} %reshape.125.idx_ref, bf16[32,8192]{1,0:T(8,128)(2,1)} %get-tuple-element.532.h_in, ...), custom_call_target="tpu_custom_call", output_to_operand_aliasing={{1}: (4, {}), {2}: (5, {})} | custom-call | tf_op jit(solution)/shard_map/cond/branch_1_fun/pallas_call | solution.py:142
  41.5 5.4 %collective-permute-start.1 = (bf16[32,8192]{1,0:T(8,128)(2,1)S(1)}, bf16[32,8192]{1,0:T(8,128)(2,1)}, u32[]{:S(2)}, u32[]{:S(2)}) collective-permute-start(bf16[32,8192]{1,0:T(8,128)(2,1)S(1)} %get-tuple-element.784), channel_id=1, source_target_pairs={{0,8},{8,16},{16,24},{1,9},{9,17},{17,25},{2,10},{10,18},{18,26},{... | collective-permute-start | bytes 1572872 | tf_op jit(solution)/shard_map/ppermute | solution.py:27
  48.2 9.1 %collective-permute-done.1 = bf16[32,8192]{1,0:T(8,128)(2,1)} collective-permute-done((bf16[32,8192]{1,0:T(8,128)(2,1)S(1)}, bf16[32,8192]{1,0:T(8,128)(2,1)}, u32[]{:S(2)}, u32[]{:S(2)}) %collective-permute-start.1) | collective-permute-done | bytes 524320 | tf_op jit(solution)/shard_map/ppermute | solution.py:27
  57.3 13.6 %conditional.22 = ((bf16[32,8192]{1,0:T(8,128)(2,1)}, bf16[2,4,32,8192]{3,2,1,0:T(8,128)(2,1)}, f32[2,4,32,8192]{3,2,1,0:T(8,128)})) conditional(s32[]{:T(128)} %convert_element_type.115, (bf16[32,8192]{1,0:T(8,128)(2,1)}, bf16[2,4,32,8192]{3,2,1,0:T(8,128)(2,1)}, f32[2,4,32,8192]{3,2,1,0:T(8,128)}) %tuple.139, (s32[]{:T(128)}, s32[256,3]{0,1:T(4,128)}, ...), branch_computations={%region_4.5_spmd, %region_5.6_spmd} | conditional | flops 6 | bytes 12350 | solution.py:386
  59.5 6.0 %branch_1_fun.46 = (bf16[32,8192]{1,0:T(8,128)(2,1)}, bf16[2,4,32,8192]{3,2,1,0:T(8,128)(2,1)}, f32[2,4,32,8192]{3,2,1,0:T(8,128)}) custom-call(s32[2]{0:T(128)} %pad_add_fusion.2.at_ref, s32[768]{0:T(1024)} %reshape.127.idx_ref, bf16[32,8192]{1,0:T(8,128)(2,1)} %get-tuple-element.538.h_in, ...), custom_call_target="tpu_custom_call", output_to_operand_aliasing={{1}: (4, {}), {2}: (5, {})} | custom-call | tf_op jit(solution)/shard_map/cond/branch_1_fun/pallas_call | solution.py:142
  65.5 5.3 %branch_1_fun.47 = (bf16[32,8192]{1,0:T(8,128)(2,1)}, bf16[2,4,32,8192]{3,2,1,0:T(8,128)(2,1)}, f32[2,4,32,8192]{3,2,1,0:T(8,128)}) custom-call(s32[1]{0:T(128)} %bitcast.4.at_ref, s32[768]{0:T(1024)} %reshape.127.idx_ref, bf16[32,8192]{1,0:T(8,128)(2,1)} %get-tuple-element.543.h_in, ...), custom_call_target="tpu_custom_call", output_to_operand_aliasing={{1}: (4, {}), {2}: (5, {})} | custom-call | tf_op jit(solution)/shard_map/cond/branch_1_fun/pallas_call | solution.py:142
  70.9 5.5 %collective-permute-start.2 = (bf16[32,8192]{1,0:T(8,128)(2,1)}, bf16[32,8192]{1,0:T(8,128)(2,1)}, u32[]{:S(2)}, u32[]{:S(2)}) collective-permute-start(bf16[32,8192]{1,0:T(8,128)(2,1)} %get-tuple-element.787), channel_id=1, source_target_pairs={{0,8},{8,16},{16,24},{1,9},{9,17},{17,25},{2,10},{10,18},{18,26},{... | collective-permute-start | bytes 1572872 | tf_op jit(solution)/shard_map/ppermute | solution.py:27
  77.7 8.5 %collective-permute-done.2 = bf16[32,8192]{1,0:T(8,128)(2,1)} collective-permute-done((bf16[32,8192]{1,0:T(8,128)(2,1)}, bf16[32,8192]{1,0:T(8,128)(2,1)}, u32[]{:S(2)}, u32[]{:S(2)}) %collective-permute-start.2) | collective-permute-done | bytes 524320 | tf_op jit(solution)/shard_map/ppermute | solution.py:27
  86.2 13.5 %conditional.23 = ((bf16[32,8192]{1,0:T(8,128)(2,1)}, bf16[2,4,32,8192]{3,2,1,0:T(8,128)(2,1)}, f32[2,4,32,8192]{3,2,1,0:T(8,128)})) conditional(s32[]{:T(128)} %convert_element_type.114, (bf16[32,8192]{1,0:T(8,128)(2,1)}, bf16[2,4,32,8192]{3,2,1,0:T(8,128)(2,1)}, f32[2,4,32,8192]{3,2,1,0:T(8,128)}) %tuple.141, (s32[]{:T(128)}, s32[256,3]{0,1:T(4,128)}, ...), branch_computations={%region_6.7_spmd, %region_7.8_spmd} | conditional | flops 6 | bytes 12350 | solution.py:386
  88.4 6.0 %branch_1_fun.48 = (bf16[32,8192]{1,0:T(8,128)(2,1)}, bf16[2,4,32,8192]{3,2,1,0:T(8,128)(2,1)}, f32[2,4,32,8192]{3,2,1,0:T(8,128)}) custom-call(s32[2]{0:T(128)} %pad_add_fusion.3.at_ref, s32[768]{0:T(1024)} %reshape.137.idx_ref, bf16[32,8192]{1,0:T(8,128)(2,1)} %get-tuple-element.549.h_in, ...), custom_call_target="tpu_custom_call", output_to_operand_aliasing={{1}: (4, {}), {2}: (5, {})} | custom-call | tf_op jit(solution)/shard_map/cond/branch_1_fun/pallas_call | solution.py:142
  94.4 5.3 %branch_1_fun.49 = (bf16[32,8192]{1,0:T(8,128)(2,1)}, bf16[2,4,32,8192]{3,2,1,0:T(8,128)(2,1)}, f32[2,4,32,8192]{3,2,1,0:T(8,128)}) custom-call(s32[1]{0:T(128)} %bitcast.6.at_ref, s32[768]{0:T(1024)} %reshape.137.idx_ref, bf16[32,8192]{1,0:T(8,128)(2,1)} %get-tuple-element.554.h_in, ...), custom_call_target="tpu_custom_call", output_to_operand_aliasing={{1}: (4, {}), {2}: (5, {})} | custom-call | tf_op jit(solution)/shard_map/cond/branch_1_fun/pallas_call | solution.py:142
  99.7 5.5 %collective-permute-start.3 = (bf16[32,8192]{1,0:T(8,128)(2,1)}, bf16[32,8192]{1,0:T(8,128)(2,1)}, u32[]{:S(2)}, u32[]{:S(2)}) collective-permute-start(bf16[32,8192]{1,0:T(8,128)(2,1)} %get-tuple-element.790), channel_id=1, source_target_pairs={{0,8},{8,16},{16,24},{1,9},{9,17},{17,25},{2,10},{10,18},{18,26},{... | collective-permute-start | bytes 1572872 | tf_op jit(solution)/shard_map/ppermute | solution.py:27
  106.6 7.6 %collective-permute-done.3 = bf16[32,8192]{1,0:T(8,128)(2,1)} collective-permute-done((bf16[32,8192]{1,0:T(8,128)(2,1)}, bf16[32,8192]{1,0:T(8,128)(2,1)}, u32[]{:S(2)}, u32[]{:S(2)}) %collective-permute-start.3) | collective-permute-done | bytes 524320 | tf_op jit(solution)/shard_map/ppermute | solution.py:27
  114.2 19.0 %collective-permute-start.4 = (bf16[32,8192]{1,0:T(8,128)(2,1)}, bf16[32,8192]{1,0:T(8,128)(2,1)}, u32[]{:S(2)}, u32[]{:S(2)}) collective-permute-start(bf16[32,8192]{1,0:T(8,128)(2,1)} %get-tuple-element.793), channel_id=1, source_target_pairs={{0,8},{8,16},{16,24},{1,9},{9,17},{17,25},{2,10},{10,18},{18,26},{... | collective-permute-start | bytes 1572872 | tf_op jit(solution)/shard_map/ppermute | solution.py:27
  134.5 6.7 %collective-permute-done.4 = bf16[32,8192]{1,0:T(8,128)(2,1)} collective-permute-done((bf16[32,8192]{1,0:T(8,128)(2,1)}, bf16[32,8192]{1,0:T(8,128)(2,1)}, u32[]{:S(2)}, u32[]{:S(2)}) %collective-permute-start.4) | collective-permute-done | bytes 524320 | tf_op jit(solution)/shard_map/ppermute | solution.py:27
  141.2 5.2 %collective-permute-start.5 = (bf16[32,8192]{1,0:T(8,128)(2,1)}, bf16[32,8192]{1,0:T(8,128)(2,1)}, u32[]{:S(2)}, u32[]{:S(2)}) collective-permute-start(bf16[32,8192]{1,0:T(8,128)(2,1)} %get-tuple-element.796), channel_id=1, source_target_pairs={{0,8},{8,16},{16,24},{1,9},{9,17},{17,25},{2,10},{10,18},{18,26},{... | collective-permute-start | bytes 1572872 | tf_op jit(solution)/shard_map/ppermute | solution.py:27
  147.7 5.8 %collective-permute-done.5 = bf16[32,8192]{1,0:T(8,128)(2,1)} collective-permute-done((bf16[32,8192]{1,0:T(8,128)(2,1)}, bf16[32,8192]{1,0:T(8,128)(2,1)}, u32[]{:S(2)}, u32[]{:S(2)}) %collective-permute-start.5) | collective-permute-done | bytes 524320 | tf_op jit(solution)/shard_map/ppermute | solution.py:27
  153.4 36.7 %collective-permute-start.6 = (bf16[32,8192]{1,0:T(8,128)(2,1)}, bf16[32,8192]{1,0:T(8,128)(2,1)}, u32[]{:S(2)}, u32[]{:S(2)}) collective-permute-start(bf16[32,8192]{1,0:T(8,128)(2,1)} %get-tuple-element.799), channel_id=1, source_target_pairs={{0,8},{8,16},{16,24},{1,9},{9,17},{17,25},{2,10},{10,18},{18,26},{... | collective-permute-start | bytes 1572872 | tf_op jit(solution)/shard_map/ppermute | solution.py:27
  190.1 7.3 %collective-permute-done.14 = bf16[32,8192]{1,0:T(8,128)(2,1)S(1)} collective-permute-done((bf16[32,8192]{1,0:T(8,128)(2,1)S(1)}, bf16[32,8192]{1,0:T(8,128)(2,1)S(1)}, u32[]{:S(2)}, u32[]{:S(2)}) %collective-permute-start.14) | collective-permute-done | bytes 524320 | tf_op jit(solution)/shard_map/ppermute | solution.py:27
  198.2 16.0 %conditional.36 = ((bf16[32,8192]{1,0:T(8,128)(2,1)}, bf16[2,4,32,8192]{3,2,1,0:T(8,128)(2,1)})) conditional(s32[]{:T(128)} %convert_element_type.121, (bf16[32,8192]{1,0:T(8,128)(2,1)}, bf16[2,4,32,8192]{3,2,1,0:T(8,128)(2,1)}) %tuple.299, (s32[]{:T(128)}, s32[256,3]{0,1:T(4,128)}, bf16[32,8192]{1,0:T(8,128)(2,1)}, f32[2,4,32,8192]{3,2,1,0:T(8,128)}, ...), branch_computations={%region_32.33_spmd, %region_33.34_spmd} | conditional | flops 6 | bytes 12350 | solution.py:401
  200.4 5.8 %branch_1_fun.74 = (bf16[32,8192]{1,0:T(8,128)(2,1)}, bf16[2,4,32,8192]{3,2,1,0:T(8,128)(2,1)}) custom-call(s32[2]{0:T(128)} %pad_add_fusion.16.at_ref, s32[768]{0:T(1024)} %reshape.163.idx_ref, bf16[32,8192]{1,0:T(8,128)(2,1)} %get-tuple-element.686.g_in, f32[2,4,32,8192]{3,2,1,0:T(8,128)} %get-tuple-element.687.sy_hbm, ...), custom_call_target="tpu_custom_call", output_to_operand_aliasing={{1}: (5, {})} | custom-call | tf_op jit(solution)/shard_map/cond/branch_1_fun/pallas_call | solution.py:223
  206.3 7.9 %branch_1_fun.75 = (bf16[32,8192]{1,0:T(8,128)(2,1)}, bf16[2,4,32,8192]{3,2,1,0:T(8,128)(2,1)}) custom-call(s32[1]{0:T(128)} %bitcast.32.at_ref, s32[768]{0:T(1024)} %reshape.163.idx_ref, bf16[32,8192]{1,0:T(8,128)(2,1)} %get-tuple-element.691.g_in, f32[2,4,32,8192]{3,2,1,0:T(8,128)} %get-tuple-element.687.sy_hbm, ...), custom_call_target="tpu_custom_call", output_to_operand_aliasing={{1}: (5, {})} | custom-call | tf_op jit(solution)/shard_map/cond/branch_1_fun/pallas_call | solution.py:223
  215.5 5.7 %collective-permute-start.7 = (bf16[32,8192]{1,0:T(8,128)(2,1)}, bf16[32,8192]{1,0:T(8,128)(2,1)S(1)}, u32[]{:S(2)}, u32[]{:S(2)}) collective-permute-start(bf16[32,8192]{1,0:T(8,128)(2,1)} %get-tuple-element.802), channel_id=1, source_target_pairs={{0,8},{8,16},{16,24},{1,9},{9,17},{17,25},{2,10},{10,18},{18,26},{... | collective-permute-start | bytes 1572872 | tf_op jit(solution)/shard_map/ppermute | solution.py:27
  221.3 7.6 %collective-permute-done.15 = bf16[32,8192]{1,0:T(8,128)(2,1)S(1)} collective-permute-done((bf16[32,8192]{1,0:T(8,128)(2,1)}, bf16[32,8192]{1,0:T(8,128)(2,1)S(1)}, u32[]{:S(2)}, u32[]{:S(2)}) %collective-permute-start.15) | collective-permute-done | bytes 524320 | tf_op jit(solution)/shard_map/ppermute | solution.py:27
  228.9 14.9 %conditional.37 = ((bf16[32,8192]{1,0:T(8,128)(2,1)S(1)}, bf16[2,4,32,8192]{3,2,1,0:T(8,128)(2,1)})) conditional(s32[]{:T(128)} %convert_element_type.120, (bf16[32,8192]{1,0:T(8,128)(2,1)S(1)}, bf16[2,4,32,8192]{3,2,1,0:T(8,128)(2,1)}) %tuple.168, (s32[]{:T(128)}, s32[256,3]{0,1:T(4,128)}, s32[]{:T(128)}, bf16[32,8192]{1,0:T(8,128)(2,1)S(1)}, ...), branch_computations={%region_34.35_spmd, %region_35.36_spmd} | conditional | flops 6 | bytes 12350 | solution.py:401
  231.2 5.5 %branch_1_fun.76 = (bf16[32,8192]{1,0:T(8,128)(2,1)}, bf16[2,4,32,8192]{3,2,1,0:T(8,128)(2,1)}) custom-call(s32[2]{0:T(128)} %pad_add_fusion.17.at_ref, s32[768]{0:T(1024)} %reshape.165.idx_ref, bf16[32,8192]{1,0:T(8,128)(2,1)S(1)} %get-tuple-element.696.g_in, f32[2,4,32,8192]{3,2,1,0:T(8,128)} %get-tuple-element.697.sy_hbm, ...), custom_call_target="tpu_custom_call", output_to_operand_aliasing={{1}: (5, {})} | custom-call | tf_op jit(solution)/shard_map/cond/branch_1_fun/pallas_call | solution.py:223
  236.7 7.1 %branch_1_fun.77 = (bf16[32,8192]{1,0:T(8,128)(2,1)S(1)}, bf16[2,4,32,8192]{3,2,1,0:T(8,128)(2,1)}) custom-call(s32[1]{0:T(128)} %bitcast.34.at_ref, s32[768]{0:T(1024)} %reshape.165.idx_ref, bf16[32,8192]{1,0:T(8,128)(2,1)} %get-tuple-element.701.g_in, f32[2,4,32,8192]{3,2,1,0:T(8,128)} %get-tuple-element.697.sy_hbm, ...), custom_call_target="tpu_custom_call", output_to_operand_aliasing={{1}: (5, {})} | custom-call | tf_op jit(solution)/shard_map/cond/branch_1_fun/pallas_call | solution.py:223
  245.9 10.6 %collective-permute-start.8 = (bf16[32,8192]{1,0:T(8,128)(2,1)}, bf16[32,8192]{1,0:T(8,128)(2,1)S(1)}, u32[]{:S(2)}, u32[]{:S(2)}) collective-permute-start(bf16[32,8192]{1,0:T(8,128)(2,1)} %get-tuple-element.807), channel_id=1, source_target_pairs={{0,8},{8,16},{16,24},{1,9},{9,17},{17,25},{2,10},{10,18},{18,26},{... | collective-permute-start | bytes 1572872 | tf_op jit(solution)/shard_map/ppermute | solution.py:27
  256.6 6.1 %collective-permute-done.16 = bf16[32,8192]{1,0:T(8,128)(2,1)} collective-permute-done((bf16[32,8192]{1,0:T(8,128)(2,1)S(1)}, bf16[32,8192]{1,0:T(8,128)(2,1)}, u32[]{:S(2)}, u32[]{:S(2)}) %collective-permute-start.16) | collective-permute-done | bytes 524320 | tf_op jit(solution)/shard_map/ppermute | solution.py:27
  262.6 16.1 %conditional.38 = ((bf16[32,8192]{1,0:T(8,128)(2,1)}, bf16[2,4,32,8192]{3,2,1,0:T(8,128)(2,1)})) conditional(s32[]{:T(128)} %convert_element_type.119, (bf16[32,8192]{1,0:T(8,128)(2,1)}, bf16[2,4,32,8192]{3,2,1,0:T(8,128)(2,1)}) %tuple.170, (s32[]{:T(128)}, s32[256,3]{0,1:T(4,128)}, s32[]{:T(128)}, bf16[32,8192]{1,0:T(8,128)(2,1)}, ...), branch_computations={%region_36.37_spmd.clone, %region_37.38_spmd.clone} | conditional | flops 6 | bytes 12350 | solution.py:401
  265.0 5.9 %branch_1_fun.80 = (bf16[32,8192]{1,0:T(8,128)(2,1)}, bf16[2,4,32,8192]{3,2,1,0:T(8,128)(2,1)}) custom-call(s32[2]{0:T(128)} %pad_add_fusion.19.at_ref, s32[768]{0:T(1024)} %reshape.185.idx_ref, bf16[32,8192]{1,0:T(8,128)(2,1)} %get-tuple-element.837.g_in, f32[2,4,32,8192]{3,2,1,0:T(8,128)} %get-tuple-element.838.sy_hbm, ...), custom_call_target="tpu_custom_call", output_to_operand_aliasing={{1}: (5, {})} | custom-call | tf_op jit(solution)/shard_map/cond/branch_1_fun/pallas_call | solution.py:223
  270.8 7.9 %branch_1_fun.81 = (bf16[32,8192]{1,0:T(8,128)(2,1)}, bf16[2,4,32,8192]{3,2,1,0:T(8,128)(2,1)}) custom-call(s32[1]{0:T(128)} %bitcast.49.at_ref, s32[768]{0:T(1024)} %reshape.185.idx_ref, bf16[32,8192]{1,0:T(8,128)(2,1)} %get-tuple-element.842.g_in, f32[2,4,32,8192]{3,2,1,0:T(8,128)} %get-tuple-element.838.sy_hbm, ...), custom_call_target="tpu_custom_call", output_to_operand_aliasing={{1}: (5, {})} | custom-call | tf_op jit(solution)/shard_map/cond/branch_1_fun/pallas_call | solution.py:223
  281.7 10.2 %collective-permute-done.17 = bf16[32,8192]{1,0:T(8,128)(2,1)S(1)} collective-permute-done((bf16[32,8192]{1,0:T(8,128)(2,1)}, bf16[32,8192]{1,0:T(8,128)(2,1)S(1)}, u32[]{:S(2)}, u32[]{:S(2)}) %collective-permute-start.17) | collective-permute-done | bytes 524320 | tf_op jit(solution)/shard_map/ppermute | solution.py:27
  291.9 14.9 %conditional.39 = (bf16[2,4,32,8192]{3,2,1,0:T(8,128)(2,1)}) conditional(s32[]{:T(128)} %convert_element_type.118, bf16[2,4,32,8192]{3,2,1,0:T(8,128)(2,1)} %get-tuple-element.826, (s32[]{:T(128)}, s32[256,3]{0,1:T(4,128)S(1)}, s32[]{:T(128)}, bf16[32,8192]{1,0:T(8,128)(2,1)S(1)}, f32[2,4,32,8192]{3,2,1,0:T(8,128)}, ...), branch_computations={%region_38.39_spmd, %region_39.40_spmd} | conditional | flops 6 | bytes 12350 | solution.py:401
  293.4 5.5 %branch_1_fun.78 = (bf16[32,8192]{1,0:T(8,128)(2,1)}, bf16[2,4,32,8192]{3,2,1,0:T(8,128)(2,1)}) custom-call(s32[2]{0:T(128)} %pad_add_fusion.18.at_ref, s32[768]{0:T(1024)} %reshape.169.idx_ref, bf16[32,8192]{1,0:T(8,128)(2,1)S(1)} %get-tuple-element.720.g_in, f32[2,4,32,8192]{3,2,1,0:T(8,128)} %get-tuple-element.721.sy_hbm, ...), custom_call_target="tpu_custom_call", output_to_operand_aliasing={{1}: (5, {})} | custom-call | tf_op jit(solution)/shard_map/cond/branch_1_fun/pallas_call | solution.py:223
  298.9 7.9 %branch_1_fun.79 = (bf16[32,8192]{1,0:T(8,128)(2,1)}, bf16[2,4,32,8192]{3,2,1,0:T(8,128)(2,1)}) custom-call(s32[1]{0:T(128)} %bitcast.36.at_ref, s32[768]{0:T(1024)} %reshape.169.idx_ref, bf16[32,8192]{1,0:T(8,128)(2,1)} %get-tuple-element.725.g_in, f32[2,4,32,8192]{3,2,1,0:T(8,128)} %get-tuple-element.721.sy_hbm, ...), custom_call_target="tpu_custom_call", output_to_operand_aliasing={{1}: (5, {})} | custom-call | tf_op jit(solution)/shard_map/cond/branch_1_fun/pallas_call | solution.py:223
  306.9 7.3 %shard_map.48 = bf16[4,32,128,128]{3,2,1,0:T(8,128)(2,1)} custom-call(s32[1]{0:T(128)} %bitcast.42.sel_ref, s32[768]{0:T(1024)} %reshape.178.idx_ref, bf16[2,4,32,8192]{3,2,1,0:T(8,128)(2,1)} %get-tuple-element.808.h_ref, bf16[2,4,32,8192]{3,2,1,0:T(8,128)(2,1)} %get-tuple-element.1118.s_ref), custom_call_target="tpu_custom_call" | custom-call | tf_op jit(solution)/shard_map/pallas_call | solution.py:309
  314.2 9.3 %shard_map.47 = f32[4,32,128,128]{3,2,1,0:T(8,128)} custom-call(s32[1]{0:T(128)} %bitcast.38.sel_ref, s32[768]{0:T(1024)} %reshape.178.idx_ref, bf16[2,4,32,8192]{3,2,1,0:T(8,128)(2,1)} %get-tuple-element.808.h_ref, bf16[2,4,32,8192]{3,2,1,0:T(8,128)(2,1)} %get-tuple-element.1118.s_ref), custom_call_target="tpu_custom_call" | custom-call | tf_op jit(solution)/shard_map/pallas_call | solution.py:309
  323.5 5.0 %fusion = bf16[2,32,128,128]{3,2,1,0:T(8,128)(2,1)} fusion(f32[2,2,32,128,128]{4,3,2,1,0:T(8,128)} %bitcast.80, s32[]{:T(128)S(6)} %select_n.64, bf16[2,2,32,128,128]{4,3,2,1,0:T(8,128)(2,1)} %bitcast.43), kind=kLoop, calls=%fused_computation.21 | loop fusion | flops 3145728 | bytes 8388612 | tf_op jit(solution)/shard_map/convert_element_type | solution.py:319
  328.5 26.2 %collective-permute-done.19 = bf16[2,32,128,128]{3,2,1,0:T(8,128)(2,1)S(1)} collective-permute-done((bf16[2,32,128,128]{3,2,1,0:T(8,128)(2,1)}, bf16[2,32,128,128]{3,2,1,0:T(8,128)(2,1)S(1)}, u32[]{:S(2)}, u32[]{:S(2)}) %collective-permute-start.19) | collective-permute-done | bytes 2097184 | tf_op jit(solution)/shard_map/ppermute | solution.py:319
  359.8 14.8 %collective-permute-done.20 = bf16[32,128,128]{2,1,0:T(8,128)(2,1)S(1)} collective-permute-done((bf16[32,128,128]{2,1,0:T(8,128)(2,1)S(1)}, bf16[32,128,128]{2,1,0:T(8,128)(2,1)S(1)}, u32[]{:S(2)}, u32[]{:S(2)}) %collective-permute-start.20) | collective-permute-done | bytes 1048608 | tf_op jit(solution)/shard_map/ppermute | solution.py:319
  374.6 4.5 %fusion.2 = f32[32,128,128]{2,1,0:T(8,128)} fusion(bf16[32,128,128]{2,1,0:T(8,128)(2,1)S(1)} %collective-permute-done.20, f32[2,32,128,128]{3,2,1,0:T(8,128)} %copy-done.1, s32[]{:T(128)S(6)} %select_n.59, f32[2,2,32,128,128]{4,3,2,1,0:T(8,128)} %bitcast.82, s32[]{:T(128)S(6)} %select_n.60, s32[]{:T(128)S(6)} %select_n.63, ...), kind=kLoop, calls=%fused_computation.25 | loop fusion | flops 2621440 | bytes 8388620 | tf_op jit(solution)/shard_map/add | solution.py:350
  (75 shorter events, 40.8 us)
Async XLA Ops:
  15.5 13.7 %collective-permute-start = (bf16[32,8192]{1,0:T(8,128)(2,1)}, bf16[32,8192]{1,0:T(8,128)(2,1)S(1)}, u32[]{:S(2)}, u32[]{:S(2)}) collective-permute-start(bf16[32,8192]{1,0:T(8,128)(2,1)} %get-tuple-element.781), channel_id=1, source_target_pairs={{0,8},{8,16},{16,24},{1,9},{9,17},{17,25},{2,10},{10,18},{18,26},{... | collective-permute-start | bytes 1572872 | tf_op jit(solution)/shard_map/ppermute | solution.py:27
  16.8 12.3 %copy-start = (bf16[2,64,8192]{2,1,0:T(8,128)(2,1)S(1)}, bf16[2,64,8192]{2,1,0:T(8,128)(2,1)}, u32[]{:S(2)}) copy-start(bf16[2,64,8192]{2,1,0:T(8,128)(2,1)} %param.44) | copy-start | bytes 6291460
  17.7 29.3 %collective-permute-start.9 = (bf16[32,8192]{1,0:T(8,128)(2,1)}, bf16[32,8192]{1,0:T(8,128)(2,1)S(1)}, u32[]{:S(2)}, u32[]{:S(2)}) collective-permute-start(bf16[32,8192]{1,0:T(8,128)(2,1)} %get-tuple-element.810), channel_id=1, source_target_pairs={{8,0},{16,8},{24,16},{9,1},{17,9},{25,17},{10,2},{18,10},{26,18},{... | collective-permute-start | bytes 1572872 | tf_op jit(solution)/shard_map/ppermute | solution.py:27
  41.5 15.8 %collective-permute-start.1 = (bf16[32,8192]{1,0:T(8,128)(2,1)S(1)}, bf16[32,8192]{1,0:T(8,128)(2,1)}, u32[]{:S(2)}, u32[]{:S(2)}) collective-permute-start(bf16[32,8192]{1,0:T(8,128)(2,1)S(1)} %get-tuple-element.784), channel_id=1, source_target_pairs={{0,8},{8,16},{16,24},{1,9},{9,17},{17,25},{2,10},{10,18},{18,26},{... | collective-permute-start | bytes 1572872 | tf_op jit(solution)/shard_map/ppermute | solution.py:27
  46.9 29.5 %collective-permute-start.10 = (bf16[32,8192]{1,0:T(8,128)(2,1)S(1)}, bf16[32,8192]{1,0:T(8,128)(2,1)}, u32[]{:S(2)}, u32[]{:S(2)}) collective-permute-start(bf16[32,8192]{1,0:T(8,128)(2,1)S(1)} %get-tuple-element.812), channel_id=1, source_target_pairs={{8,0},{16,8},{24,16},{9,1},{17,9},{25,17},{10,2},{18,10},{26,18},{... | collective-permute-start | bytes 1572872 | tf_op jit(solution)/shard_map/ppermute | solution.py:27
  70.9 15.3 %collective-permute-start.2 = (bf16[32,8192]{1,0:T(8,128)(2,1)}, bf16[32,8192]{1,0:T(8,128)(2,1)}, u32[]{:S(2)}, u32[]{:S(2)}) collective-permute-start(bf16[32,8192]{1,0:T(8,128)(2,1)} %get-tuple-element.787), channel_id=1, source_target_pairs={{0,8},{8,16},{16,24},{1,9},{9,17},{17,25},{2,10},{10,18},{18,26},{... | collective-permute-start | bytes 1572872 | tf_op jit(solution)/shard_map/ppermute | solution.py:27
  76.4 28.9 %collective-permute-start.11 = (bf16[32,8192]{1,0:T(8,128)(2,1)}, bf16[32,8192]{1,0:T(8,128)(2,1)S(1)}, u32[]{:S(2)}, u32[]{:S(2)}) collective-permute-start(bf16[32,8192]{1,0:T(8,128)(2,1)} %get-tuple-element.814), channel_id=1, source_target_pairs={{8,0},{16,8},{24,16},{9,1},{17,9},{25,17},{10,2},{18,10},{26,18},{... | collective-permute-start | bytes 1572872 | tf_op jit(solution)/shard_map/ppermute | solution.py:27
  99.7 14.4 %collective-permute-start.3 = (bf16[32,8192]{1,0:T(8,128)(2,1)}, bf16[32,8192]{1,0:T(8,128)(2,1)}, u32[]{:S(2)}, u32[]{:S(2)}) collective-permute-start(bf16[32,8192]{1,0:T(8,128)(2,1)} %get-tuple-element.790), channel_id=1, source_target_pairs={{0,8},{8,16},{16,24},{1,9},{9,17},{17,25},{2,10},{10,18},{18,26},{... | collective-permute-start | bytes 1572872 | tf_op jit(solution)/shard_map/ppermute | solution.py:27
  105.3 27.9 %collective-permute-start.12 = (bf16[32,8192]{1,0:T(8,128)(2,1)S(1)}, bf16[32,8192]{1,0:T(8,128)(2,1)S(1)}, u32[]{:S(2)}, u32[]{:S(2)}) collective-permute-start(bf16[32,8192]{1,0:T(8,128)(2,1)S(1)} %get-tuple-element.816), channel_id=1, source_target_pairs={{8,0},{16,8},{24,16},{9,1},{17,9},{25,17},{10,2},{18,10},{26,18},{... | collective-permute-start | bytes 1572872 | tf_op jit(solution)/shard_map/ppermute | solution.py:27
  114.2 27.0 %collective-permute-start.4 = (bf16[32,8192]{1,0:T(8,128)(2,1)}, bf16[32,8192]{1,0:T(8,128)(2,1)}, u32[]{:S(2)}, u32[]{:S(2)}) collective-permute-start(bf16[32,8192]{1,0:T(8,128)(2,1)} %get-tuple-element.793), channel_id=1, source_target_pairs={{0,8},{8,16},{16,24},{1,9},{9,17},{17,25},{2,10},{10,18},{18,26},{... | collective-permute-start | bytes 1572872 | tf_op jit(solution)/shard_map/ppermute | solution.py:27
  133.2 13.2 %collective-permute-start.13 = (bf16[32,8192]{1,0:T(8,128)(2,1)S(1)}, bf16[32,8192]{1,0:T(8,128)(2,1)S(1)}, u32[]{:S(2)}, u32[]{:S(2)}) collective-permute-start(bf16[32,8192]{1,0:T(8,128)(2,1)S(1)} %get-tuple-element.818), channel_id=1, source_target_pairs={{8,0},{16,8},{24,16},{9,1},{17,9},{25,17},{10,2},{18,10},{26,18},{... | collective-permute-start | bytes 1572872 | tf_op jit(solution)/shard_map/ppermute | solution.py:27
  141.2 12.3 %collective-permute-start.5 = (bf16[32,8192]{1,0:T(8,128)(2,1)}, bf16[32,8192]{1,0:T(8,128)(2,1)}, u32[]{:S(2)}, u32[]{:S(2)}) collective-permute-start(bf16[32,8192]{1,0:T(8,128)(2,1)} %get-tuple-element.796), channel_id=1, source_target_pairs={{0,8},{8,16},{16,24},{1,9},{9,17},{17,25},{2,10},{10,18},{18,26},{... | collective-permute-start | bytes 1572872 | tf_op jit(solution)/shard_map/ppermute | solution.py:27
  146.4 51.0 %collective-permute-start.14 = (bf16[32,8192]{1,0:T(8,128)(2,1)S(1)}, bf16[32,8192]{1,0:T(8,128)(2,1)S(1)}, u32[]{:S(2)}, u32[]{:S(2)}) collective-permute-start(bf16[32,8192]{1,0:T(8,128)(2,1)S(1)} %get-tuple-element.820), channel_id=1, source_target_pairs={{8,0},{16,8},{24,16},{9,1},{17,9},{25,17},{10,2},{18,10},{26,18},{... | collective-permute-start | bytes 1572872 | tf_op jit(solution)/shard_map/ppermute | solution.py:27
  153.4 62.1 %collective-permute-start.6 = (bf16[32,8192]{1,0:T(8,128)(2,1)}, bf16[32,8192]{1,0:T(8,128)(2,1)}, u32[]{:S(2)}, u32[]{:S(2)}) collective-permute-start(bf16[32,8192]{1,0:T(8,128)(2,1)} %get-tuple-element.799), channel_id=1, source_target_pairs={{0,8},{8,16},{16,24},{1,9},{9,17},{17,25},{2,10},{10,18},{18,26},{... | collective-permute-start | bytes 1572872 | tf_op jit(solution)/shard_map/ppermute | solution.py:27
  197.4 0.8 copy-start.4
  214.2 14.7 %collective-permute-start.15 = (bf16[32,8192]{1,0:T(8,128)(2,1)}, bf16[32,8192]{1,0:T(8,128)(2,1)S(1)}, u32[]{:S(2)}, u32[]{:S(2)}) collective-permute-start(bf16[32,8192]{1,0:T(8,128)(2,1)} %get-tuple-element.822), channel_id=1, source_target_pairs={{8,0},{16,8},{24,16},{9,1},{17,9},{25,17},{10,2},{18,10},{26,18},{... | collective-permute-start | bytes 1572872 | tf_op jit(solution)/shard_map/ppermute | solution.py:27
  215.5 29.6 %collective-permute-start.7 = (bf16[32,8192]{1,0:T(8,128)(2,1)}, bf16[32,8192]{1,0:T(8,128)(2,1)S(1)}, u32[]{:S(2)}, u32[]{:S(2)}) collective-permute-start(bf16[32,8192]{1,0:T(8,128)(2,1)} %get-tuple-element.802), channel_id=1, source_target_pairs={{0,8},{8,16},{16,24},{1,9},{9,17},{17,25},{2,10},{10,18},{18,26},{... | collective-permute-start | bytes 1572872 | tf_op jit(solution)/shard_map/ppermute | solution.py:27
  243.8 18.8 %collective-permute-start.16 = (bf16[32,8192]{1,0:T(8,128)(2,1)S(1)}, bf16[32,8192]{1,0:T(8,128)(2,1)}, u32[]{:S(2)}, u32[]{:S(2)}) collective-permute-start(bf16[32,8192]{1,0:T(8,128)(2,1)S(1)} %get-tuple-element.824), channel_id=1, source_target_pairs={{8,0},{16,8},{24,16},{9,1},{17,9},{25,17},{10,2},{18,10},{26,18},{... | collective-permute-start | bytes 1572872 | tf_op jit(solution)/shard_map/ppermute | solution.py:27
  245.1 0.8 copy-start.3
  245.9 35.8 %collective-permute-start.8 = (bf16[32,8192]{1,0:T(8,128)(2,1)}, bf16[32,8192]{1,0:T(8,128)(2,1)S(1)}, u32[]{:S(2)}, u32[]{:S(2)}) collective-permute-start(bf16[32,8192]{1,0:T(8,128)(2,1)} %get-tuple-element.807), channel_id=1, source_target_pairs={{0,8},{8,16},{16,24},{1,9},{9,17},{17,25},{2,10},{10,18},{18,26},{... | collective-permute-start | bytes 1572872 | tf_op jit(solution)/shard_map/ppermute | solution.py:27
  262.6 19.1 %copy-start.2 = (s32[256,3]{0,1:T(4,128)S(1)}, s32[256,3]{0,1:T(4,128)}, u32[]{:S(2)}) copy-start(s32[256,3]{0,1:T(4,128)} %param.47) | copy-start | bytes 9220
  278.8 13.1 %collective-permute-start.17 = (bf16[32,8192]{1,0:T(8,128)(2,1)}, bf16[32,8192]{1,0:T(8,128)(2,1)S(1)}, u32[]{:S(2)}, u32[]{:S(2)}) collective-permute-start(bf16[32,8192]{1,0:T(8,128)(2,1)} %get-tuple-element.827), channel_id=1, source_target_pairs={{8,0},{16,8},{24,16},{9,1},{17,9},{25,17},{10,2},{18,10},{26,18},{... | collective-permute-start | bytes 1572872 | tf_op jit(solution)/shard_map/ppermute | solution.py:27
  314.2 9.3 %collective-permute-start.18 = (bf16[4,32,128,128]{3,2,1,0:T(8,128)(2,1)}, bf16[4,32,128,128]{3,2,1,0:T(8,128)(2,1)}, u32[]{:S(2)}, u32[]{:S(2)}) collective-permute-start(bf16[4,32,128,128]{3,2,1,0:T(8,128)(2,1)} %shard_map.48), channel_id=1, source_target_pairs={{0,1},{1,0},{2,3},{3,2},{4,5},{5,4},{6,7},{7,6},{8,9},{9,8},{10,11... | collective-permute-start | bytes 12582920 | tf_op jit(solution)/shard_map/ppermute | solution.py:333
  328.5 26.2 %collective-permute-start.19 = (bf16[2,32,128,128]{3,2,1,0:T(8,128)(2,1)}, bf16[2,32,128,128]{3,2,1,0:T(8,128)(2,1)S(1)}, u32[]{:S(2)}, u32[]{:S(2)}) collective-permute-start(bf16[2,32,128,128]{3,2,1,0:T(8,128)(2,1)} %fusion), channel_id=1, source_target_pairs={{0,2},{1,5},{2,0},{3,7},{4,6},{5,1},{6,4},{7,3},{8,10},{9,13},{10,... | collective-permute-start | bytes 6291464 | tf_op jit(solution)/shard_map/ppermute | solution.py:319
  355.3 2.1 copy-start.1
  359.7 14.9 %collective-permute-start.20 = (bf16[32,128,128]{2,1,0:T(8,128)(2,1)S(1)}, bf16[32,128,128]{2,1,0:T(8,128)(2,1)S(1)}, u32[]{:S(2)}, u32[]{:S(2)}) collective-permute-start(bf16[32,128,128]{2,1,0:T(8,128)(2,1)S(1)} %fusion.1), channel_id=1, source_target_pairs={{0,4},{1,3},{2,6},{3,1},{4,0},{5,7},{6,2},{7,5},{8,12},{9,11},{10,... | collective-permute-start | bytes 3145736 | tf_op jit(solution)/shard_map/ppermute | solution.py:319

commit v5 on v4

--- a/solution.py
+++ b/solution.py
@@ -11,7 +11,7 @@
 LSLOT = 2
 KMAX = 128
 CH = 512
-NSUB = 16
+NSUB = 32
 SPLIT = 2
 GROUP = 16
 VMEM_LIMIT = 60 * 1024 * 1024

time: 382 us -> 373 us (0.976)
  starting transfers between devices: 107 us -> 93.4 us
  Pallas kernels: 115 us -> 121 us
    ppermute x18, starting transfers between devices: 106 us -> 93.3 us  [shifted(): lax.ppermute(value, axis, [(source, source + steps) for source in range(l...]
  transfers between devices with their start and end apart: 21 -> 21, of which waited for: 12 -> 12; matrix products, arithmetic and copies ran while one was open for 4% -> 4% of each run, Pallas kernels for 22% -> 23%
where the time goes in v5:
time: 373 us; the launch traced here: 370 us
  Pallas kernels  121 us (32%)
  waiting for transfers between devices  119 us (32%)
  starting transfers between devices  93.4 us (25%)
  local copies, waits for them, and re-layouts  19.2 us (5%)
  other arithmetic  17.2 us (5%)
    ppermute x18, starting transfers between devices, shifted(): lax.ppermute(value, axis, [(source, source + steps) for source in range(l...  93.3 us
    ppermute x18, waiting for transfers between devices, shifted(): lax.ppermute(value, axis, [(source, source + steps) for source in range(l...  78 us
    pallas_call x8, Pallas kernels, layer_backward(): pl.pallas_call(functools.partial(_bwd_kernel, layer * KMAX, layer, entry)...  57.1 us
    pallas_call x8, Pallas kernels, layer_forward(): pl.pallas_call(functools.partial(_fwd_kernel, layer * KMAX, layer), out_s...  45.9 us
    ppermute x2, waiting for transfers between devices, _exchange(): lax.ppermute(send.astype(jnp.bfloat16), 'dp', pairs).astype(jnp.float32)  41 us
    pallas_call x2, Pallas kernels, dw_half(): pl.pallas_call(_dw_half_kernel, out_shape=jax.ShapeDtypeStruct((4, per, B...  18.1 us
  transfers between devices with their start and end apart: 21, of which 12 were waited for; matrix products, arithmetic and copies ran while one was open for 4% of the time, Pallas kernels for 23%

profile of v5, /device:TPU:0, one launch (start us, length us, event | category | flops | bytes accessed | tf_op | source)
XLA Modules:
  0.0 370.5 jit_solution(206447550269975829)
XLA Ops:
  0.0 15.5 %conditional.20 = ((bf16[32,8192]{1,0:T(8,128)(2,1)}, bf16[2,4,32,8192]{3,2,1,0:T(8,128)(2,1)}, f32[2,4,32,8192]{3,2,1,0:T(8,128)})) conditional(s32[]{:T(128)} %convert_element_type.117, (bf16[2,4,32,8192]{3,2,1,0:T(8,128)(2,1)}, f32[2,4,32,8192]{3,2,1,0:T(8,128)}) %tuple.135, (s32[]{:T(128)}, s32[256,3]{0,1:T(4,128)}, s32[]{:T(128)}, ...), branch_computations={%region_0.1_spmd, %region_1.2_spmd} | conditional | flops 6 | bytes 536640 | solution.py:386
  3.0 6.9 %branch_1_fun.42 = (bf16[32,8192]{1,0:T(8,128)(2,1)}, bf16[2,4,32,8192]{3,2,1,0:T(8,128)(2,1)}, f32[2,4,32,8192]{3,2,1,0:T(8,128)}) custom-call(s32[2]{0:T(128)} %pad_add_fusion.at_ref, s32[768]{0:T(1024)} %reshape.123.idx_ref, bf16[32,8192]{1,0:T(8,128)(2,1)} %broadcast_in_dim.9.h_in, ...), custom_call_target="tpu_custom_call", output_to_operand_aliasing={{1}: (4, {}), {2}: (5, {})} | custom-call | tf_op jit(solution)/shard_map/cond/branch_1_fun/pallas_call | solution.py:142
  9.9 5.6 %branch_1_fun.43 = (bf16[32,8192]{1,0:T(8,128)(2,1)}, bf16[2,4,32,8192]{3,2,1,0:T(8,128)(2,1)}, f32[2,4,32,8192]{3,2,1,0:T(8,128)}) custom-call(s32[1]{0:T(128)} %bitcast.at_ref, s32[768]{0:T(1024)} %reshape.123.idx_ref, bf16[32,8192]{1,0:T(8,128)(2,1)} %get-tuple-element.521.h_in, ...), custom_call_target="tpu_custom_call", output_to_operand_aliasing={{1}: (4, {}), {2}: (5, {})} | custom-call | tf_op jit(solution)/shard_map/cond/branch_1_fun/pallas_call | solution.py:142
  19.0 10.2 %collective-permute-done = bf16[32,8192]{1,0:T(8,128)(2,1)S(1)} collective-permute-done((bf16[32,8192]{1,0:T(8,128)(2,1)}, bf16[32,8192]{1,0:T(8,128)(2,1)S(1)}, u32[]{:S(2)}, u32[]{:S(2)}) %collective-permute-start) | collective-permute-done | bytes 524320 | tf_op jit(solution)/shard_map/ppermute | solution.py:27
  29.2 12.6 %conditional.21 = ((bf16[32,8192]{1,0:T(8,128)(2,1)S(1)}, bf16[2,4,32,8192]{3,2,1,0:T(8,128)(2,1)}, f32[2,4,32,8192]{3,2,1,0:T(8,128)})) conditional(s32[]{:T(128)} %convert_element_type.116, (bf16[32,8192]{1,0:T(8,128)(2,1)S(1)}, bf16[2,4,32,8192]{3,2,1,0:T(8,128)(2,1)}, f32[2,4,32,8192]{3,2,1,0:T(8,128)}) %tuple.137, (s32[]{:T(128)}, ...), branch_computations={%region_2.3_spmd, %region_3.4_spmd} | conditional | flops 6 | bytes 12350 | solution.py:386
  31.4 5.6 %branch_1_fun.44 = (bf16[32,8192]{1,0:T(8,128)(2,1)}, bf16[2,4,32,8192]{3,2,1,0:T(8,128)(2,1)}, f32[2,4,32,8192]{3,2,1,0:T(8,128)}) custom-call(s32[2]{0:T(128)} %pad_add_fusion.1.at_ref, s32[768]{0:T(1024)} %reshape.125.idx_ref, bf16[32,8192]{1,0:T(8,128)(2,1)S(1)} %get-tuple-element.527.h_in, ...), custom_call_target="tpu_custom_call", output_to_operand_aliasing={{1}: (4, {}), {2}: (5, {})} | custom-call | tf_op jit(solution)/shard_map/cond/branch_1_fun/pallas_call | solution.py:142
  37.0 4.7 %branch_1_fun.45 = (bf16[32,8192]{1,0:T(8,128)(2,1)S(1)}, bf16[2,4,32,8192]{3,2,1,0:T(8,128)(2,1)}, f32[2,4,32,8192]{3,2,1,0:T(8,128)}) custom-call(s32[1]{0:T(128)} %bitcast.2.at_ref, s32[768]{0:T(1024)} %reshape.125.idx_ref, bf16[32,8192]{1,0:T(8,128)(2,1)} %get-tuple-element.532.h_in, ...), custom_call_target="tpu_custom_call", output_to_operand_aliasing={{1}: (4, {}), {2}: (5, {})} | custom-call | tf_op jit(solution)/shard_map/cond/branch_1_fun/pallas_call | solution.py:142
  41.8 4.8 %collective-permute-start.1 = (bf16[32,8192]{1,0:T(8,128)(2,1)S(1)}, bf16[32,8192]{1,0:T(8,128)(2,1)}, u32[]{:S(2)}, u32[]{:S(2)}) collective-permute-start(bf16[32,8192]{1,0:T(8,128)(2,1)S(1)} %get-tuple-element.784), channel_id=1, source_target_pairs={{0,8},{8,16},{16,24},{1,9},{9,17},{17,25},{2,10},{10,18},{18,26},{... | collective-permute-start | bytes 1572872 | tf_op jit(solution)/shard_map/ppermute | solution.py:27
  47.9 9.1 %collective-permute-done.1 = bf16[32,8192]{1,0:T(8,128)(2,1)} collective-permute-done((bf16[32,8192]{1,0:T(8,128)(2,1)S(1)}, bf16[32,8192]{1,0:T(8,128)(2,1)}, u32[]{:S(2)}, u32[]{:S(2)}) %collective-permute-start.1) | collective-permute-done | bytes 524320 | tf_op jit(solution)/shard_map/ppermute | solution.py:27
  57.0 13.8 %conditional.22 = ((bf16[32,8192]{1,0:T(8,128)(2,1)}, bf16[2,4,32,8192]{3,2,1,0:T(8,128)(2,1)}, f32[2,4,32,8192]{3,2,1,0:T(8,128)})) conditional(s32[]{:T(128)} %convert_element_type.115, (bf16[32,8192]{1,0:T(8,128)(2,1)}, bf16[2,4,32,8192]{3,2,1,0:T(8,128)(2,1)}, f32[2,4,32,8192]{3,2,1,0:T(8,128)}) %tuple.139, (s32[]{:T(128)}, s32[256,3]{0,1:T(4,128)}, ...), branch_computations={%region_4.5_spmd, %region_5.6_spmd} | conditional | flops 6 | bytes 12350 | solution.py:386
  59.2 5.9 %branch_1_fun.46 = (bf16[32,8192]{1,0:T(8,128)(2,1)}, bf16[2,4,32,8192]{3,2,1,0:T(8,128)(2,1)}, f32[2,4,32,8192]{3,2,1,0:T(8,128)}) custom-call(s32[2]{0:T(128)} %pad_add_fusion.2.at_ref, s32[768]{0:T(1024)} %reshape.127.idx_ref, bf16[32,8192]{1,0:T(8,128)(2,1)} %get-tuple-element.538.h_in, ...), custom_call_target="tpu_custom_call", output_to_operand_aliasing={{1}: (4, {}), {2}: (5, {})} | custom-call | tf_op jit(solution)/shard_map/cond/branch_1_fun/pallas_call | solution.py:142
  65.1 5.6 %branch_1_fun.47 = (bf16[32,8192]{1,0:T(8,128)(2,1)}, bf16[2,4,32,8192]{3,2,1,0:T(8,128)(2,1)}, f32[2,4,32,8192]{3,2,1,0:T(8,128)}) custom-call(s32[1]{0:T(128)} %bitcast.4.at_ref, s32[768]{0:T(1024)} %reshape.127.idx_ref, bf16[32,8192]{1,0:T(8,128)(2,1)} %get-tuple-element.543.h_in, ...), custom_call_target="tpu_custom_call", output_to_operand_aliasing={{1}: (4, {}), {2}: (5, {})} | custom-call | tf_op jit(solution)/shard_map/cond/branch_1_fun/pallas_call | solution.py:142
  70.8 4.9 %collective-permute-start.2 = (bf16[32,8192]{1,0:T(8,128)(2,1)}, bf16[32,8192]{1,0:T(8,128)(2,1)}, u32[]{:S(2)}, u32[]{:S(2)}) collective-permute-start(bf16[32,8192]{1,0:T(8,128)(2,1)} %get-tuple-element.787), channel_id=1, source_target_pairs={{0,8},{8,16},{16,24},{1,9},{9,17},{17,25},{2,10},{10,18},{18,26},{... | collective-permute-start | bytes 1572872 | tf_op jit(solution)/shard_map/ppermute | solution.py:27
  77.0 8.5 %collective-permute-done.2 = bf16[32,8192]{1,0:T(8,128)(2,1)} collective-permute-done((bf16[32,8192]{1,0:T(8,128)(2,1)}, bf16[32,8192]{1,0:T(8,128)(2,1)}, u32[]{:S(2)}, u32[]{:S(2)}) %collective-permute-start.2) | collective-permute-done | bytes 524320 | tf_op jit(solution)/shard_map/ppermute | solution.py:27
  85.6 13.7 %conditional.23 = ((bf16[32,8192]{1,0:T(8,128)(2,1)}, bf16[2,4,32,8192]{3,2,1,0:T(8,128)(2,1)}, f32[2,4,32,8192]{3,2,1,0:T(8,128)})) conditional(s32[]{:T(128)} %convert_element_type.114, (bf16[32,8192]{1,0:T(8,128)(2,1)}, bf16[2,4,32,8192]{3,2,1,0:T(8,128)(2,1)}, f32[2,4,32,8192]{3,2,1,0:T(8,128)}) %tuple.141, (s32[]{:T(128)}, s32[256,3]{0,1:T(4,128)}, ...), branch_computations={%region_6.7_spmd, %region_7.8_spmd} | conditional | flops 6 | bytes 12350 | solution.py:386
  87.7 6.0 %branch_1_fun.48 = (bf16[32,8192]{1,0:T(8,128)(2,1)}, bf16[2,4,32,8192]{3,2,1,0:T(8,128)(2,1)}, f32[2,4,32,8192]{3,2,1,0:T(8,128)}) custom-call(s32[2]{0:T(128)} %pad_add_fusion.3.at_ref, s32[768]{0:T(1024)} %reshape.137.idx_ref, bf16[32,8192]{1,0:T(8,128)(2,1)} %get-tuple-element.549.h_in, ...), custom_call_target="tpu_custom_call", output_to_operand_aliasing={{1}: (4, {}), {2}: (5, {})} | custom-call | tf_op jit(solution)/shard_map/cond/branch_1_fun/pallas_call | solution.py:142
  93.7 5.6 %branch_1_fun.49 = (bf16[32,8192]{1,0:T(8,128)(2,1)}, bf16[2,4,32,8192]{3,2,1,0:T(8,128)(2,1)}, f32[2,4,32,8192]{3,2,1,0:T(8,128)}) custom-call(s32[1]{0:T(128)} %bitcast.6.at_ref, s32[768]{0:T(1024)} %reshape.137.idx_ref, bf16[32,8192]{1,0:T(8,128)(2,1)} %get-tuple-element.554.h_in, ...), custom_call_target="tpu_custom_call", output_to_operand_aliasing={{1}: (4, {}), {2}: (5, {})} | custom-call | tf_op jit(solution)/shard_map/cond/branch_1_fun/pallas_call | solution.py:142
  99.3 5.0 %collective-permute-start.3 = (bf16[32,8192]{1,0:T(8,128)(2,1)}, bf16[32,8192]{1,0:T(8,128)(2,1)}, u32[]{:S(2)}, u32[]{:S(2)}) collective-permute-start(bf16[32,8192]{1,0:T(8,128)(2,1)} %get-tuple-element.790), channel_id=1, source_target_pairs={{0,8},{8,16},{16,24},{1,9},{9,17},{17,25},{2,10},{10,18},{18,26},{... | collective-permute-start | bytes 1572872 | tf_op jit(solution)/shard_map/ppermute | solution.py:27
  105.5 7.6 %collective-permute-done.3 = bf16[32,8192]{1,0:T(8,128)(2,1)} collective-permute-done((bf16[32,8192]{1,0:T(8,128)(2,1)}, bf16[32,8192]{1,0:T(8,128)(2,1)}, u32[]{:S(2)}, u32[]{:S(2)}) %collective-permute-start.3) | collective-permute-done | bytes 524320 | tf_op jit(solution)/shard_map/ppermute | solution.py:27
  113.2 18.6 %collective-permute-start.4 = (bf16[32,8192]{1,0:T(8,128)(2,1)}, bf16[32,8192]{1,0:T(8,128)(2,1)}, u32[]{:S(2)}, u32[]{:S(2)}) collective-permute-start(bf16[32,8192]{1,0:T(8,128)(2,1)} %get-tuple-element.793), channel_id=1, source_target_pairs={{0,8},{8,16},{16,24},{1,9},{9,17},{17,25},{2,10},{10,18},{18,26},{... | collective-permute-start | bytes 1572872 | tf_op jit(solution)/shard_map/ppermute | solution.py:27
  133.1 6.7 %collective-permute-done.4 = bf16[32,8192]{1,0:T(8,128)(2,1)} collective-permute-done((bf16[32,8192]{1,0:T(8,128)(2,1)}, bf16[32,8192]{1,0:T(8,128)(2,1)}, u32[]{:S(2)}, u32[]{:S(2)}) %collective-permute-start.4) | collective-permute-done | bytes 524320 | tf_op jit(solution)/shard_map/ppermute | solution.py:27
  139.8 5.2 %collective-permute-start.5 = (bf16[32,8192]{1,0:T(8,128)(2,1)}, bf16[32,8192]{1,0:T(8,128)(2,1)}, u32[]{:S(2)}, u32[]{:S(2)}) collective-permute-start(bf16[32,8192]{1,0:T(8,128)(2,1)} %get-tuple-element.796), channel_id=1, source_target_pairs={{0,8},{8,16},{16,24},{1,9},{9,17},{17,25},{2,10},{10,18},{18,26},{... | collective-permute-start | bytes 1572872 | tf_op jit(solution)/shard_map/ppermute | solution.py:27
  146.3 5.8 %collective-permute-done.5 = bf16[32,8192]{1,0:T(8,128)(2,1)} collective-permute-done((bf16[32,8192]{1,0:T(8,128)(2,1)}, bf16[32,8192]{1,0:T(8,128)(2,1)}, u32[]{:S(2)}, u32[]{:S(2)}) %collective-permute-start.5) | collective-permute-done | bytes 524320 | tf_op jit(solution)/shard_map/ppermute | solution.py:27
  152.1 31.3 %collective-permute-start.6 = (bf16[32,8192]{1,0:T(8,128)(2,1)}, bf16[32,8192]{1,0:T(8,128)(2,1)}, u32[]{:S(2)}, u32[]{:S(2)}) collective-permute-start(bf16[32,8192]{1,0:T(8,128)(2,1)} %get-tuple-element.799), channel_id=1, source_target_pairs={{0,8},{8,16},{16,24},{1,9},{9,17},{17,25},{2,10},{10,18},{18,26},{... | collective-permute-start | bytes 1572872 | tf_op jit(solution)/shard_map/ppermute | solution.py:27
  183.4 7.4 %collective-permute-done.14 = bf16[32,8192]{1,0:T(8,128)(2,1)S(1)} collective-permute-done((bf16[32,8192]{1,0:T(8,128)(2,1)S(1)}, bf16[32,8192]{1,0:T(8,128)(2,1)S(1)}, u32[]{:S(2)}, u32[]{:S(2)}) %collective-permute-start.14) | collective-permute-done | bytes 524320 | tf_op jit(solution)/shard_map/ppermute | solution.py:27
  191.6 16.9 %conditional.36 = ((bf16[32,8192]{1,0:T(8,128)(2,1)}, bf16[2,4,32,8192]{3,2,1,0:T(8,128)(2,1)})) conditional(s32[]{:T(128)} %convert_element_type.121, (bf16[32,8192]{1,0:T(8,128)(2,1)}, bf16[2,4,32,8192]{3,2,1,0:T(8,128)(2,1)}) %tuple.299, (s32[]{:T(128)}, s32[256,3]{0,1:T(4,128)}, bf16[32,8192]{1,0:T(8,128)(2,1)}, f32[2,4,32,8192]{3,2,1,0:T(8,128)}, ...), branch_computations={%region_32.33_spmd, %region_33.34_spmd} | conditional | flops 6 | bytes 12350 | solution.py:401
  193.9 7.0 %branch_1_fun.74 = (bf16[32,8192]{1,0:T(8,128)(2,1)}, bf16[2,4,32,8192]{3,2,1,0:T(8,128)(2,1)}) custom-call(s32[2]{0:T(128)} %pad_add_fusion.16.at_ref, s32[768]{0:T(1024)} %reshape.163.idx_ref, bf16[32,8192]{1,0:T(8,128)(2,1)} %get-tuple-element.686.g_in, f32[2,4,32,8192]{3,2,1,0:T(8,128)} %get-tuple-element.687.sy_hbm, ...), custom_call_target="tpu_custom_call", output_to_operand_aliasing={{1}: (5, {})} | custom-call | tf_op jit(solution)/shard_map/cond/branch_1_fun/pallas_call | solution.py:223
  200.9 7.6 %branch_1_fun.75 = (bf16[32,8192]{1,0:T(8,128)(2,1)}, bf16[2,4,32,8192]{3,2,1,0:T(8,128)(2,1)}) custom-call(s32[1]{0:T(128)} %bitcast.32.at_ref, s32[768]{0:T(1024)} %reshape.163.idx_ref, bf16[32,8192]{1,0:T(8,128)(2,1)} %get-tuple-element.691.g_in, f32[2,4,32,8192]{3,2,1,0:T(8,128)} %get-tuple-element.687.sy_hbm, ...), custom_call_target="tpu_custom_call", output_to_operand_aliasing={{1}: (5, {})} | custom-call | tf_op jit(solution)/shard_map/cond/branch_1_fun/pallas_call | solution.py:223
  209.9 4.6 %collective-permute-start.7 = (bf16[32,8192]{1,0:T(8,128)(2,1)}, bf16[32,8192]{1,0:T(8,128)(2,1)S(1)}, u32[]{:S(2)}, u32[]{:S(2)}) collective-permute-start(bf16[32,8192]{1,0:T(8,128)(2,1)} %get-tuple-element.802), channel_id=1, source_target_pairs={{0,8},{8,16},{16,24},{1,9},{9,17},{17,25},{2,10},{10,18},{18,26},{... | collective-permute-start | bytes 1572872 | tf_op jit(solution)/shard_map/ppermute | solution.py:27
  214.5 7.5 %collective-permute-done.15 = bf16[32,8192]{1,0:T(8,128)(2,1)S(1)} collective-permute-done((bf16[32,8192]{1,0:T(8,128)(2,1)}, bf16[32,8192]{1,0:T(8,128)(2,1)S(1)}, u32[]{:S(2)}, u32[]{:S(2)}) %collective-permute-start.15) | collective-permute-done | bytes 524320 | tf_op jit(solution)/shard_map/ppermute | solution.py:27
  222.0 15.8 %conditional.37 = ((bf16[32,8192]{1,0:T(8,128)(2,1)S(1)}, bf16[2,4,32,8192]{3,2,1,0:T(8,128)(2,1)})) conditional(s32[]{:T(128)} %convert_element_type.120, (bf16[32,8192]{1,0:T(8,128)(2,1)S(1)}, bf16[2,4,32,8192]{3,2,1,0:T(8,128)(2,1)}) %tuple.168, (s32[]{:T(128)}, s32[256,3]{0,1:T(4,128)}, s32[]{:T(128)}, bf16[32,8192]{1,0:T(8,128)(2,1)S(1)}, ...), branch_computations={%region_34.35_spmd, %region_35.36_spmd} | conditional | flops 6 | bytes 12350 | solution.py:401
  224.3 6.7 %branch_1_fun.76 = (bf16[32,8192]{1,0:T(8,128)(2,1)}, bf16[2,4,32,8192]{3,2,1,0:T(8,128)(2,1)}) custom-call(s32[2]{0:T(128)} %pad_add_fusion.17.at_ref, s32[768]{0:T(1024)} %reshape.165.idx_ref, bf16[32,8192]{1,0:T(8,128)(2,1)S(1)} %get-tuple-element.696.g_in, f32[2,4,32,8192]{3,2,1,0:T(8,128)} %get-tuple-element.697.sy_hbm, ...), custom_call_target="tpu_custom_call", output_to_operand_aliasing={{1}: (5, {})} | custom-call | tf_op jit(solution)/shard_map/cond/branch_1_fun/pallas_call | solution.py:223
  230.9 6.8 %branch_1_fun.77 = (bf16[32,8192]{1,0:T(8,128)(2,1)S(1)}, bf16[2,4,32,8192]{3,2,1,0:T(8,128)(2,1)}) custom-call(s32[1]{0:T(128)} %bitcast.34.at_ref, s32[768]{0:T(1024)} %reshape.165.idx_ref, bf16[32,8192]{1,0:T(8,128)(2,1)} %get-tuple-element.701.g_in, f32[2,4,32,8192]{3,2,1,0:T(8,128)} %get-tuple-element.697.sy_hbm, ...), custom_call_target="tpu_custom_call", output_to_operand_aliasing={{1}: (5, {})} | custom-call | tf_op jit(solution)/shard_map/cond/branch_1_fun/pallas_call | solution.py:223
  239.9 6.0 %collective-permute-start.8 = (bf16[32,8192]{1,0:T(8,128)(2,1)}, bf16[32,8192]{1,0:T(8,128)(2,1)S(1)}, u32[]{:S(2)}, u32[]{:S(2)}) collective-permute-start(bf16[32,8192]{1,0:T(8,128)(2,1)} %get-tuple-element.807), channel_id=1, source_target_pairs={{0,8},{8,16},{16,24},{1,9},{9,17},{17,25},{2,10},{10,18},{18,26},{... | collective-permute-start | bytes 1572872 | tf_op jit(solution)/shard_map/ppermute | solution.py:27
  245.9 6.1 %collective-permute-done.16 = bf16[32,8192]{1,0:T(8,128)(2,1)} collective-permute-done((bf16[32,8192]{1,0:T(8,128)(2,1)S(1)}, bf16[32,8192]{1,0:T(8,128)(2,1)}, u32[]{:S(2)}, u32[]{:S(2)}) %collective-permute-start.16) | collective-permute-done | bytes 524320 | tf_op jit(solution)/shard_map/ppermute | solution.py:27
  252.0 17.0 %conditional.38 = ((bf16[32,8192]{1,0:T(8,128)(2,1)}, bf16[2,4,32,8192]{3,2,1,0:T(8,128)(2,1)})) conditional(s32[]{:T(128)} %convert_element_type.119, (bf16[32,8192]{1,0:T(8,128)(2,1)}, bf16[2,4,32,8192]{3,2,1,0:T(8,128)(2,1)}) %tuple.170, (s32[]{:T(128)}, s32[256,3]{0,1:T(4,128)}, s32[]{:T(128)}, bf16[32,8192]{1,0:T(8,128)(2,1)}, ...), branch_computations={%region_36.37_spmd.clone, %region_37.38_spmd.clone} | conditional | flops 6 | bytes 12350 | solution.py:401
  254.4 7.0 %branch_1_fun.80 = (bf16[32,8192]{1,0:T(8,128)(2,1)}, bf16[2,4,32,8192]{3,2,1,0:T(8,128)(2,1)}) custom-call(s32[2]{0:T(128)} %pad_add_fusion.19.at_ref, s32[768]{0:T(1024)} %reshape.185.idx_ref, bf16[32,8192]{1,0:T(8,128)(2,1)} %get-tuple-element.837.g_in, f32[2,4,32,8192]{3,2,1,0:T(8,128)} %get-tuple-element.838.sy_hbm, ...), custom_call_target="tpu_custom_call", output_to_operand_aliasing={{1}: (5, {})} | custom-call | tf_op jit(solution)/shard_map/cond/branch_1_fun/pallas_call | solution.py:223
  261.4 7.6 %branch_1_fun.81 = (bf16[32,8192]{1,0:T(8,128)(2,1)}, bf16[2,4,32,8192]{3,2,1,0:T(8,128)(2,1)}) custom-call(s32[1]{0:T(128)} %bitcast.49.at_ref, s32[768]{0:T(1024)} %reshape.185.idx_ref, bf16[32,8192]{1,0:T(8,128)(2,1)} %get-tuple-element.842.g_in, f32[2,4,32,8192]{3,2,1,0:T(8,128)} %get-tuple-element.838.sy_hbm, ...), custom_call_target="tpu_custom_call", output_to_operand_aliasing={{1}: (5, {})} | custom-call | tf_op jit(solution)/shard_map/cond/branch_1_fun/pallas_call | solution.py:223
  272.0 9.0 %collective-permute-done.17 = bf16[32,8192]{1,0:T(8,128)(2,1)S(1)} collective-permute-done((bf16[32,8192]{1,0:T(8,128)(2,1)}, bf16[32,8192]{1,0:T(8,128)(2,1)S(1)}, u32[]{:S(2)}, u32[]{:S(2)}) %collective-permute-start.17) | collective-permute-done | bytes 524320 | tf_op jit(solution)/shard_map/ppermute | solution.py:27
  281.0 15.8 %conditional.39 = (bf16[2,4,32,8192]{3,2,1,0:T(8,128)(2,1)}) conditional(s32[]{:T(128)} %convert_element_type.118, bf16[2,4,32,8192]{3,2,1,0:T(8,128)(2,1)} %get-tuple-element.826, (s32[]{:T(128)}, s32[256,3]{0,1:T(4,128)S(1)}, s32[]{:T(128)}, bf16[32,8192]{1,0:T(8,128)(2,1)S(1)}, f32[2,4,32,8192]{3,2,1,0:T(8,128)}, ...), branch_computations={%region_38.39_spmd, %region_39.40_spmd} | conditional | flops 6 | bytes 12350 | solution.py:401
  282.5 6.7 %branch_1_fun.78 = (bf16[32,8192]{1,0:T(8,128)(2,1)}, bf16[2,4,32,8192]{3,2,1,0:T(8,128)(2,1)}) custom-call(s32[2]{0:T(128)} %pad_add_fusion.18.at_ref, s32[768]{0:T(1024)} %reshape.169.idx_ref, bf16[32,8192]{1,0:T(8,128)(2,1)S(1)} %get-tuple-element.720.g_in, f32[2,4,32,8192]{3,2,1,0:T(8,128)} %get-tuple-element.721.sy_hbm, ...), custom_call_target="tpu_custom_call", output_to_operand_aliasing={{1}: (5, {})} | custom-call | tf_op jit(solution)/shard_map/cond/branch_1_fun/pallas_call | solution.py:223
  289.2 7.6 %branch_1_fun.79 = (bf16[32,8192]{1,0:T(8,128)(2,1)}, bf16[2,4,32,8192]{3,2,1,0:T(8,128)(2,1)}) custom-call(s32[1]{0:T(128)} %bitcast.36.at_ref, s32[768]{0:T(1024)} %reshape.169.idx_ref, bf16[32,8192]{1,0:T(8,128)(2,1)} %get-tuple-element.725.g_in, f32[2,4,32,8192]{3,2,1,0:T(8,128)} %get-tuple-element.721.sy_hbm, ...), custom_call_target="tpu_custom_call", output_to_operand_aliasing={{1}: (5, {})} | custom-call | tf_op jit(solution)/shard_map/cond/branch_1_fun/pallas_call | solution.py:223
  296.8 8.2 %shard_map.48 = bf16[4,32,128,128]{3,2,1,0:T(8,128)(2,1)} custom-call(s32[1]{0:T(128)} %bitcast.42.sel_ref, s32[768]{0:T(1024)} %reshape.178.idx_ref, bf16[2,4,32,8192]{3,2,1,0:T(8,128)(2,1)} %get-tuple-element.808.h_ref, bf16[2,4,32,8192]{3,2,1,0:T(8,128)(2,1)} %get-tuple-element.1118.s_ref), custom_call_target="tpu_custom_call" | custom-call | tf_op jit(solution)/shard_map/pallas_call | solution.py:309
  305.0 9.9 %shard_map.47 = f32[4,32,128,128]{3,2,1,0:T(8,128)} custom-call(s32[1]{0:T(128)} %bitcast.38.sel_ref, s32[768]{0:T(1024)} %reshape.178.idx_ref, bf16[2,4,32,8192]{3,2,1,0:T(8,128)(2,1)} %get-tuple-element.808.h_ref, bf16[2,4,32,8192]{3,2,1,0:T(8,128)(2,1)} %get-tuple-element.1118.s_ref), custom_call_target="tpu_custom_call" | custom-call | tf_op jit(solution)/shard_map/pallas_call | solution.py:309
  314.9 5.0 %fusion = bf16[2,32,128,128]{3,2,1,0:T(8,128)(2,1)} fusion(f32[2,2,32,128,128]{4,3,2,1,0:T(8,128)} %bitcast.80, s32[]{:T(128)S(6)} %select_n.64, bf16[2,2,32,128,128]{4,3,2,1,0:T(8,128)(2,1)} %bitcast.43), kind=kLoop, calls=%fused_computation.21 | loop fusion | flops 3145728 | bytes 8388612 | tf_op jit(solution)/shard_map/convert_element_type | solution.py:319
  319.9 26.2 %collective-permute-done.19 = bf16[2,32,128,128]{3,2,1,0:T(8,128)(2,1)S(1)} collective-permute-done((bf16[2,32,128,128]{3,2,1,0:T(8,128)(2,1)}, bf16[2,32,128,128]{3,2,1,0:T(8,128)(2,1)S(1)}, u32[]{:S(2)}, u32[]{:S(2)}) %collective-permute-start.19) | collective-permute-done | bytes 2097184 | tf_op jit(solution)/shard_map/ppermute | solution.py:319
  351.2 14.8 %collective-permute-done.20 = bf16[32,128,128]{2,1,0:T(8,128)(2,1)S(1)} collective-permute-done((bf16[32,128,128]{2,1,0:T(8,128)(2,1)S(1)}, bf16[32,128,128]{2,1,0:T(8,128)(2,1)S(1)}, u32[]{:S(2)}, u32[]{:S(2)}) %collective-permute-start.20) | collective-permute-done | bytes 1048608 | tf_op jit(solution)/shard_map/ppermute | solution.py:319
  366.0 4.5 %fusion.2 = f32[32,128,128]{2,1,0:T(8,128)} fusion(bf16[32,128,128]{2,1,0:T(8,128)(2,1)S(1)} %collective-permute-done.20, f32[2,32,128,128]{3,2,1,0:T(8,128)} %copy-done.1, s32[]{:T(128)S(6)} %select_n.59, f32[2,2,32,128,128]{4,3,2,1,0:T(8,128)} %bitcast.82, s32[]{:T(128)S(6)} %select_n.60, s32[]{:T(128)S(6)} %select_n.63, ...), kind=kLoop, calls=%fused_computation.25 | loop fusion | flops 2621440 | bytes 8388620 | tf_op jit(solution)/shard_map/add | solution.py:350
  (75 shorter events, 40.8 us)
Async XLA Ops:
  15.5 13.7 %collective-permute-start = (bf16[32,8192]{1,0:T(8,128)(2,1)}, bf16[32,8192]{1,0:T(8,128)(2,1)S(1)}, u32[]{:S(2)}, u32[]{:S(2)}) collective-permute-start(bf16[32,8192]{1,0:T(8,128)(2,1)} %get-tuple-element.781), channel_id=1, source_target_pairs={{0,8},{8,16},{16,24},{1,9},{9,17},{17,25},{2,10},{10,18},{18,26},{... | collective-permute-start | bytes 1572872 | tf_op jit(solution)/shard_map/ppermute | solution.py:27
  16.8 12.3 %copy-start = (bf16[2,64,8192]{2,1,0:T(8,128)(2,1)S(1)}, bf16[2,64,8192]{2,1,0:T(8,128)(2,1)}, u32[]{:S(2)}) copy-start(bf16[2,64,8192]{2,1,0:T(8,128)(2,1)} %param.44) | copy-start | bytes 6291460
  17.7 28.9 %collective-permute-start.9 = (bf16[32,8192]{1,0:T(8,128)(2,1)}, bf16[32,8192]{1,0:T(8,128)(2,1)S(1)}, u32[]{:S(2)}, u32[]{:S(2)}) collective-permute-start(bf16[32,8192]{1,0:T(8,128)(2,1)} %get-tuple-element.810), channel_id=1, source_target_pairs={{8,0},{16,8},{24,16},{9,1},{17,9},{25,17},{10,2},{18,10},{26,18},{... | collective-permute-start | bytes 1572872 | tf_op jit(solution)/shard_map/ppermute | solution.py:27
  41.8 15.2 %collective-permute-start.1 = (bf16[32,8192]{1,0:T(8,128)(2,1)S(1)}, bf16[32,8192]{1,0:T(8,128)(2,1)}, u32[]{:S(2)}, u32[]{:S(2)}) collective-permute-start(bf16[32,8192]{1,0:T(8,128)(2,1)S(1)} %get-tuple-element.784), channel_id=1, source_target_pairs={{0,8},{8,16},{16,24},{1,9},{9,17},{17,25},{2,10},{10,18},{18,26},{... | collective-permute-start | bytes 1572872 | tf_op jit(solution)/shard_map/ppermute | solution.py:27
  46.6 29.1 %collective-permute-start.10 = (bf16[32,8192]{1,0:T(8,128)(2,1)S(1)}, bf16[32,8192]{1,0:T(8,128)(2,1)}, u32[]{:S(2)}, u32[]{:S(2)}) collective-permute-start(bf16[32,8192]{1,0:T(8,128)(2,1)S(1)} %get-tuple-element.812), channel_id=1, source_target_pairs={{8,0},{16,8},{24,16},{9,1},{17,9},{25,17},{10,2},{18,10},{26,18},{... | collective-permute-start | bytes 1572872 | tf_op jit(solution)/shard_map/ppermute | solution.py:27
  70.8 14.8 %collective-permute-start.2 = (bf16[32,8192]{1,0:T(8,128)(2,1)}, bf16[32,8192]{1,0:T(8,128)(2,1)}, u32[]{:S(2)}, u32[]{:S(2)}) collective-permute-start(bf16[32,8192]{1,0:T(8,128)(2,1)} %get-tuple-element.787), channel_id=1, source_target_pairs={{0,8},{8,16},{16,24},{1,9},{9,17},{17,25},{2,10},{10,18},{18,26},{... | collective-permute-start | bytes 1572872 | tf_op jit(solution)/shard_map/ppermute | solution.py:27
  75.7 28.5 %collective-permute-start.11 = (bf16[32,8192]{1,0:T(8,128)(2,1)}, bf16[32,8192]{1,0:T(8,128)(2,1)S(1)}, u32[]{:S(2)}, u32[]{:S(2)}) collective-permute-start(bf16[32,8192]{1,0:T(8,128)(2,1)} %get-tuple-element.814), channel_id=1, source_target_pairs={{8,0},{16,8},{24,16},{9,1},{17,9},{25,17},{10,2},{18,10},{26,18},{... | collective-permute-start | bytes 1572872 | tf_op jit(solution)/shard_map/ppermute | solution.py:27
  99.3 13.9 %collective-permute-start.3 = (bf16[32,8192]{1,0:T(8,128)(2,1)}, bf16[32,8192]{1,0:T(8,128)(2,1)}, u32[]{:S(2)}, u32[]{:S(2)}) collective-permute-start(bf16[32,8192]{1,0:T(8,128)(2,1)} %get-tuple-element.790), channel_id=1, source_target_pairs={{0,8},{8,16},{16,24},{1,9},{9,17},{17,25},{2,10},{10,18},{18,26},{... | collective-permute-start | bytes 1572872 | tf_op jit(solution)/shard_map/ppermute | solution.py:27
  104.2 27.6 %collective-permute-start.12 = (bf16[32,8192]{1,0:T(8,128)(2,1)S(1)}, bf16[32,8192]{1,0:T(8,128)(2,1)S(1)}, u32[]{:S(2)}, u32[]{:S(2)}) collective-permute-start(bf16[32,8192]{1,0:T(8,128)(2,1)S(1)} %get-tuple-element.816), channel_id=1, source_target_pairs={{8,0},{16,8},{24,16},{9,1},{17,9},{25,17},{10,2},{18,10},{26,18},{... | collective-permute-start | bytes 1572872 | tf_op jit(solution)/shard_map/ppermute | solution.py:27
  113.2 26.7 %collective-permute-start.4 = (bf16[32,8192]{1,0:T(8,128)(2,1)}, bf16[32,8192]{1,0:T(8,128)(2,1)}, u32[]{:S(2)}, u32[]{:S(2)}) collective-permute-start(bf16[32,8192]{1,0:T(8,128)(2,1)} %get-tuple-element.793), channel_id=1, source_target_pairs={{0,8},{8,16},{16,24},{1,9},{9,17},{17,25},{2,10},{10,18},{18,26},{... | collective-permute-start | bytes 1572872 | tf_op jit(solution)/shard_map/ppermute | solution.py:27
  131.8 13.2 %collective-permute-start.13 = (bf16[32,8192]{1,0:T(8,128)(2,1)S(1)}, bf16[32,8192]{1,0:T(8,128)(2,1)S(1)}, u32[]{:S(2)}, u32[]{:S(2)}) collective-permute-start(bf16[32,8192]{1,0:T(8,128)(2,1)S(1)} %get-tuple-element.818), channel_id=1, source_target_pairs={{8,0},{16,8},{24,16},{9,1},{17,9},{25,17},{10,2},{18,10},{26,18},{... | collective-permute-start | bytes 1572872 | tf_op jit(solution)/shard_map/ppermute | solution.py:27
  139.8 12.3 %collective-permute-start.5 = (bf16[32,8192]{1,0:T(8,128)(2,1)}, bf16[32,8192]{1,0:T(8,128)(2,1)}, u32[]{:S(2)}, u32[]{:S(2)}) collective-permute-start(bf16[32,8192]{1,0:T(8,128)(2,1)} %get-tuple-element.796), channel_id=1, source_target_pairs={{0,8},{8,16},{16,24},{1,9},{9,17},{17,25},{2,10},{10,18},{18,26},{... | collective-permute-start | bytes 1572872 | tf_op jit(solution)/shard_map/ppermute | solution.py:27
  145.0 45.8 %collective-permute-start.14 = (bf16[32,8192]{1,0:T(8,128)(2,1)S(1)}, bf16[32,8192]{1,0:T(8,128)(2,1)S(1)}, u32[]{:S(2)}, u32[]{:S(2)}) collective-permute-start(bf16[32,8192]{1,0:T(8,128)(2,1)S(1)} %get-tuple-element.820), channel_id=1, source_target_pairs={{8,0},{16,8},{24,16},{9,1},{17,9},{25,17},{10,2},{18,10},{26,18},{... | collective-permute-start | bytes 1572872 | tf_op jit(solution)/shard_map/ppermute | solution.py:27
  152.1 57.8 %collective-permute-start.6 = (bf16[32,8192]{1,0:T(8,128)(2,1)}, bf16[32,8192]{1,0:T(8,128)(2,1)}, u32[]{:S(2)}, u32[]{:S(2)}) collective-permute-start(bf16[32,8192]{1,0:T(8,128)(2,1)} %get-tuple-element.799), channel_id=1, source_target_pairs={{0,8},{8,16},{16,24},{1,9},{9,17},{17,25},{2,10},{10,18},{18,26},{... | collective-permute-start | bytes 1572872 | tf_op jit(solution)/shard_map/ppermute | solution.py:27
  190.8 0.8 copy-start.4
  208.5 13.4 %collective-permute-start.15 = (bf16[32,8192]{1,0:T(8,128)(2,1)}, bf16[32,8192]{1,0:T(8,128)(2,1)S(1)}, u32[]{:S(2)}, u32[]{:S(2)}) collective-permute-start(bf16[32,8192]{1,0:T(8,128)(2,1)} %get-tuple-element.822), channel_id=1, source_target_pairs={{8,0},{16,8},{24,16},{9,1},{17,9},{25,17},{10,2},{18,10},{26,18},{... | collective-permute-start | bytes 1572872 | tf_op jit(solution)/shard_map/ppermute | solution.py:27
  209.9 29.2 %collective-permute-start.7 = (bf16[32,8192]{1,0:T(8,128)(2,1)}, bf16[32,8192]{1,0:T(8,128)(2,1)S(1)}, u32[]{:S(2)}, u32[]{:S(2)}) collective-permute-start(bf16[32,8192]{1,0:T(8,128)(2,1)} %get-tuple-element.802), channel_id=1, source_target_pairs={{0,8},{8,16},{16,24},{1,9},{9,17},{17,25},{2,10},{10,18},{18,26},{... | collective-permute-start | bytes 1572872 | tf_op jit(solution)/shard_map/ppermute | solution.py:27
  237.8 14.2 %collective-permute-start.16 = (bf16[32,8192]{1,0:T(8,128)(2,1)S(1)}, bf16[32,8192]{1,0:T(8,128)(2,1)}, u32[]{:S(2)}, u32[]{:S(2)}) collective-permute-start(bf16[32,8192]{1,0:T(8,128)(2,1)S(1)} %get-tuple-element.824), channel_id=1, source_target_pairs={{8,0},{16,8},{24,16},{9,1},{17,9},{25,17},{10,2},{18,10},{26,18},{... | collective-permute-start | bytes 1572872 | tf_op jit(solution)/shard_map/ppermute | solution.py:27
  239.1 0.8 copy-start.3
  239.9 32.1 %collective-permute-start.8 = (bf16[32,8192]{1,0:T(8,128)(2,1)}, bf16[32,8192]{1,0:T(8,128)(2,1)S(1)}, u32[]{:S(2)}, u32[]{:S(2)}) collective-permute-start(bf16[32,8192]{1,0:T(8,128)(2,1)} %get-tuple-element.807), channel_id=1, source_target_pairs={{0,8},{8,16},{16,24},{1,9},{9,17},{17,25},{2,10},{10,18},{18,26},{... | collective-permute-start | bytes 1572872 | tf_op jit(solution)/shard_map/ppermute | solution.py:27
  252.0 20.0 %copy-start.2 = (s32[256,3]{0,1:T(4,128)S(1)}, s32[256,3]{0,1:T(4,128)}, u32[]{:S(2)}) copy-start(s32[256,3]{0,1:T(4,128)} %param.47) | copy-start | bytes 9220
  269.0 11.9 %collective-permute-start.17 = (bf16[32,8192]{1,0:T(8,128)(2,1)}, bf16[32,8192]{1,0:T(8,128)(2,1)S(1)}, u32[]{:S(2)}, u32[]{:S(2)}) collective-permute-start(bf16[32,8192]{1,0:T(8,128)(2,1)} %get-tuple-element.827), channel_id=1, source_target_pairs={{8,0},{16,8},{24,16},{9,1},{17,9},{25,17},{10,2},{18,10},{26,18},{... | collective-permute-start | bytes 1572872 | tf_op jit(solution)/shard_map/ppermute | solution.py:27
  305.0 9.9 %collective-permute-start.18 = (bf16[4,32,128,128]{3,2,1,0:T(8,128)(2,1)}, bf16[4,32,128,128]{3,2,1,0:T(8,128)(2,1)}, u32[]{:S(2)}, u32[]{:S(2)}) collective-permute-start(bf16[4,32,128,128]{3,2,1,0:T(8,128)(2,1)} %shard_map.48), channel_id=1, source_target_pairs={{0,1},{1,0},{2,3},{3,2},{4,5},{5,4},{6,7},{7,6},{8,9},{9,8},{10,11... | collective-permute-start | bytes 12582920 | tf_op jit(solution)/shard_map/ppermute | solution.py:333
  319.9 26.2 %collective-permute-start.19 = (bf16[2,32,128,128]{3,2,1,0:T(8,128)(2,1)}, bf16[2,32,128,128]{3,2,1,0:T(8,128)(2,1)S(1)}, u32[]{:S(2)}, u32[]{:S(2)}) collective-permute-start(bf16[2,32,128,128]{3,2,1,0:T(8,128)(2,1)} %fusion), channel_id=1, source_target_pairs={{0,2},{1,5},{2,0},{3,7},{4,6},{5,1},{6,4},{7,3},{8,10},{9,13},{10,... | collective-permute-start | bytes 6291464 | tf_op jit(solution)/shard_map/ppermute | solution.py:319
  346.7 2.1 copy-start.1
  351.1 14.9 %collective-permute-start.20 = (bf16[32,128,128]{2,1,0:T(8,128)(2,1)S(1)}, bf16[32,128,128]{2,1,0:T(8,128)(2,1)S(1)}, u32[]{:S(2)}, u32[]{:S(2)}) collective-permute-start(bf16[32,128,128]{2,1,0:T(8,128)(2,1)S(1)} %fusion.1), channel_id=1, source_target_pairs={{0,4},{1,3},{2,6},{3,1},{4,0},{5,7},{6,2},{7,5},{8,12},{9,11},{10,... | collective-permute-start | bytes 3145736 | tf_op jit(solution)/shard_map/ppermute | solution.py:319

commit v6 on v5

--- a/solution.py
+++ b/solution.py
@@ -10,7 +10,7 @@
 BLK = 128
 LSLOT = 2
 KMAX = 128
-CH = 512
+CH = 1024
 NSUB = 32
 SPLIT = 2
 GROUP = 16

time: 373 us -> 369 us (0.989)
  Pallas kernels: 121 us -> 115 us
    pallas_call x8, Pallas kernels: 57.1 us -> 52.9 us  [layer_backward(): pl.pallas_call(functools.partial(_bwd_kernel, layer * KMAX, layer, entry)...]
  transfers between devices with their start and end apart: 21 -> 21, of which waited for: 12 -> 12; matrix products, arithmetic and copies ran while one was open for 4% -> 4% of each run, Pallas kernels for 23% -> 22%
where the time goes in v6:
time: 369 us; the launch traced here: 368 us
  waiting for transfers between devices  119 us (32%)
  Pallas kernels  115 us (31%)
  starting transfers between devices  96.2 us (26%)
  local copies, waits for them, and re-layouts  19.2 us (5%)
  other arithmetic  17.2 us (5%)
    ppermute x18, starting transfers between devices, shifted(): lax.ppermute(value, axis, [(source, source + steps) for source in range(l...  96.1 us
    ppermute x18, waiting for transfers between devices, shifted(): lax.ppermute(value, axis, [(source, source + steps) for source in range(l...  78.4 us
    pallas_call x8, Pallas kernels, layer_backward(): pl.pallas_call(functools.partial(_bwd_kernel, layer * KMAX, layer, entry)...  52.9 us
    pallas_call x8, Pallas kernels, layer_forward(): pl.pallas_call(functools.partial(_fwd_kernel, layer * KMAX, layer), out_s...  44.7 us
    ppermute x2, waiting for transfers between devices, _exchange(): lax.ppermute(send.astype(jnp.bfloat16), 'dp', pairs).astype(jnp.float32)  41 us
    pallas_call x2, Pallas kernels, dw_half(): pl.pallas_call(_dw_half_kernel, out_shape=jax.ShapeDtypeStruct((4, per, B...  17.5 us
  transfers between devices with their start and end apart: 21, of which 12 were waited for; matrix products, arithmetic and copies ran while one was open for 4% of the time, Pallas kernels for 22%

profile of v6, /device:TPU:0, one launch (start us, length us, event | category | flops | bytes accessed | tf_op | source)
XLA Modules:
  0.0 367.7 jit_solution(17803006929081377428)
XLA Ops:
  0.0 15.2 %conditional.20 = ((bf16[32,8192]{1,0:T(8,128)(2,1)}, bf16[2,4,32,8192]{3,2,1,0:T(8,128)(2,1)}, f32[2,4,32,8192]{3,2,1,0:T(8,128)})) conditional(s32[]{:T(128)} %convert_element_type.117, (bf16[2,4,32,8192]{3,2,1,0:T(8,128)(2,1)}, f32[2,4,32,8192]{3,2,1,0:T(8,128)}) %tuple.135, (s32[]{:T(128)}, s32[256,3]{0,1:T(4,128)}, s32[]{:T(128)}, ...), branch_computations={%region_0.1_spmd, %region_1.2_spmd} | conditional | flops 6 | bytes 536640 | solution.py:386
  3.0 6.9 %branch_1_fun.42 = (bf16[32,8192]{1,0:T(8,128)(2,1)}, bf16[2,4,32,8192]{3,2,1,0:T(8,128)(2,1)}, f32[2,4,32,8192]{3,2,1,0:T(8,128)}) custom-call(s32[2]{0:T(128)} %pad_add_fusion.at_ref, s32[768]{0:T(1024)} %reshape.123.idx_ref, bf16[32,8192]{1,0:T(8,128)(2,1)} %broadcast_in_dim.9.h_in, ...), custom_call_target="tpu_custom_call", output_to_operand_aliasing={{1}: (4, {}), {2}: (5, {})} | custom-call | tf_op jit(solution)/shard_map/cond/branch_1_fun/pallas_call | solution.py:142
  9.9 5.3 %branch_1_fun.43 = (bf16[32,8192]{1,0:T(8,128)(2,1)}, bf16[2,4,32,8192]{3,2,1,0:T(8,128)(2,1)}, f32[2,4,32,8192]{3,2,1,0:T(8,128)}) custom-call(s32[1]{0:T(128)} %bitcast.at_ref, s32[768]{0:T(1024)} %reshape.123.idx_ref, bf16[32,8192]{1,0:T(8,128)(2,1)} %get-tuple-element.521.h_in, ...), custom_call_target="tpu_custom_call", output_to_operand_aliasing={{1}: (4, {}), {2}: (5, {})} | custom-call | tf_op jit(solution)/shard_map/cond/branch_1_fun/pallas_call | solution.py:142
  18.7 10.2 %collective-permute-done = bf16[32,8192]{1,0:T(8,128)(2,1)S(1)} collective-permute-done((bf16[32,8192]{1,0:T(8,128)(2,1)}, bf16[32,8192]{1,0:T(8,128)(2,1)S(1)}, u32[]{:S(2)}, u32[]{:S(2)}) %collective-permute-start) | collective-permute-done | bytes 524320 | tf_op jit(solution)/shard_map/ppermute | solution.py:27
  28.9 12.3 %conditional.21 = ((bf16[32,8192]{1,0:T(8,128)(2,1)S(1)}, bf16[2,4,32,8192]{3,2,1,0:T(8,128)(2,1)}, f32[2,4,32,8192]{3,2,1,0:T(8,128)})) conditional(s32[]{:T(128)} %convert_element_type.116, (bf16[32,8192]{1,0:T(8,128)(2,1)S(1)}, bf16[2,4,32,8192]{3,2,1,0:T(8,128)(2,1)}, f32[2,4,32,8192]{3,2,1,0:T(8,128)}) %tuple.137, (s32[]{:T(128)}, ...), branch_computations={%region_2.3_spmd, %region_3.4_spmd} | conditional | flops 6 | bytes 12350 | solution.py:386
  31.1 5.6 %branch_1_fun.44 = (bf16[32,8192]{1,0:T(8,128)(2,1)}, bf16[2,4,32,8192]{3,2,1,0:T(8,128)(2,1)}, f32[2,4,32,8192]{3,2,1,0:T(8,128)}) custom-call(s32[2]{0:T(128)} %pad_add_fusion.1.at_ref, s32[768]{0:T(1024)} %reshape.125.idx_ref, bf16[32,8192]{1,0:T(8,128)(2,1)S(1)} %get-tuple-element.527.h_in, ...), custom_call_target="tpu_custom_call", output_to_operand_aliasing={{1}: (4, {}), {2}: (5, {})} | custom-call | tf_op jit(solution)/shard_map/cond/branch_1_fun/pallas_call | solution.py:142
  36.7 4.5 %branch_1_fun.45 = (bf16[32,8192]{1,0:T(8,128)(2,1)S(1)}, bf16[2,4,32,8192]{3,2,1,0:T(8,128)(2,1)}, f32[2,4,32,8192]{3,2,1,0:T(8,128)}) custom-call(s32[1]{0:T(128)} %bitcast.2.at_ref, s32[768]{0:T(1024)} %reshape.125.idx_ref, bf16[32,8192]{1,0:T(8,128)(2,1)} %get-tuple-element.532.h_in, ...), custom_call_target="tpu_custom_call", output_to_operand_aliasing={{1}: (4, {}), {2}: (5, {})} | custom-call | tf_op jit(solution)/shard_map/cond/branch_1_fun/pallas_call | solution.py:142
  41.2 5.4 %collective-permute-start.1 = (bf16[32,8192]{1,0:T(8,128)(2,1)S(1)}, bf16[32,8192]{1,0:T(8,128)(2,1)}, u32[]{:S(2)}, u32[]{:S(2)}) collective-permute-start(bf16[32,8192]{1,0:T(8,128)(2,1)S(1)} %get-tuple-element.784), channel_id=1, source_target_pairs={{0,8},{8,16},{16,24},{1,9},{9,17},{17,25},{2,10},{10,18},{18,26},{... | collective-permute-start | bytes 1572872 | tf_op jit(solution)/shard_map/ppermute | solution.py:27
  47.9 9.1 %collective-permute-done.1 = bf16[32,8192]{1,0:T(8,128)(2,1)} collective-permute-done((bf16[32,8192]{1,0:T(8,128)(2,1)S(1)}, bf16[32,8192]{1,0:T(8,128)(2,1)}, u32[]{:S(2)}, u32[]{:S(2)}) %collective-permute-start.1) | collective-permute-done | bytes 524320 | tf_op jit(solution)/shard_map/ppermute | solution.py:27
  57.0 13.5 %conditional.22 = ((bf16[32,8192]{1,0:T(8,128)(2,1)}, bf16[2,4,32,8192]{3,2,1,0:T(8,128)(2,1)}, f32[2,4,32,8192]{3,2,1,0:T(8,128)})) conditional(s32[]{:T(128)} %convert_element_type.115, (bf16[32,8192]{1,0:T(8,128)(2,1)}, bf16[2,4,32,8192]{3,2,1,0:T(8,128)(2,1)}, f32[2,4,32,8192]{3,2,1,0:T(8,128)}) %tuple.139, (s32[]{:T(128)}, s32[256,3]{0,1:T(4,128)}, ...), branch_computations={%region_4.5_spmd, %region_5.6_spmd} | conditional | flops 6 | bytes 12350 | solution.py:386
  59.2 5.9 %branch_1_fun.46 = (bf16[32,8192]{1,0:T(8,128)(2,1)}, bf16[2,4,32,8192]{3,2,1,0:T(8,128)(2,1)}, f32[2,4,32,8192]{3,2,1,0:T(8,128)}) custom-call(s32[2]{0:T(128)} %pad_add_fusion.2.at_ref, s32[768]{0:T(1024)} %reshape.127.idx_ref, bf16[32,8192]{1,0:T(8,128)(2,1)} %get-tuple-element.538.h_in, ...), custom_call_target="tpu_custom_call", output_to_operand_aliasing={{1}: (4, {}), {2}: (5, {})} | custom-call | tf_op jit(solution)/shard_map/cond/branch_1_fun/pallas_call | solution.py:142
  65.1 5.3 %branch_1_fun.47 = (bf16[32,8192]{1,0:T(8,128)(2,1)}, bf16[2,4,32,8192]{3,2,1,0:T(8,128)(2,1)}, f32[2,4,32,8192]{3,2,1,0:T(8,128)}) custom-call(s32[1]{0:T(128)} %bitcast.4.at_ref, s32[768]{0:T(1024)} %reshape.127.idx_ref, bf16[32,8192]{1,0:T(8,128)(2,1)} %get-tuple-element.543.h_in, ...), custom_call_target="tpu_custom_call", output_to_operand_aliasing={{1}: (4, {}), {2}: (5, {})} | custom-call | tf_op jit(solution)/shard_map/cond/branch_1_fun/pallas_call | solution.py:142
  70.5 5.5 %collective-permute-start.2 = (bf16[32,8192]{1,0:T(8,128)(2,1)}, bf16[32,8192]{1,0:T(8,128)(2,1)}, u32[]{:S(2)}, u32[]{:S(2)}) collective-permute-start(bf16[32,8192]{1,0:T(8,128)(2,1)} %get-tuple-element.787), channel_id=1, source_target_pairs={{0,8},{8,16},{16,24},{1,9},{9,17},{17,25},{2,10},{10,18},{18,26},{... | collective-permute-start | bytes 1572872 | tf_op jit(solution)/shard_map/ppermute | solution.py:27
  77.3 8.5 %collective-permute-done.2 = bf16[32,8192]{1,0:T(8,128)(2,1)} collective-permute-done((bf16[32,8192]{1,0:T(8,128)(2,1)}, bf16[32,8192]{1,0:T(8,128)(2,1)}, u32[]{:S(2)}, u32[]{:S(2)}) %collective-permute-start.2) | collective-permute-done | bytes 524320 | tf_op jit(solution)/shard_map/ppermute | solution.py:27
  85.9 13.4 %conditional.23 = ((bf16[32,8192]{1,0:T(8,128)(2,1)}, bf16[2,4,32,8192]{3,2,1,0:T(8,128)(2,1)}, f32[2,4,32,8192]{3,2,1,0:T(8,128)})) conditional(s32[]{:T(128)} %convert_element_type.114, (bf16[32,8192]{1,0:T(8,128)(2,1)}, bf16[2,4,32,8192]{3,2,1,0:T(8,128)(2,1)}, f32[2,4,32,8192]{3,2,1,0:T(8,128)}) %tuple.141, (s32[]{:T(128)}, s32[256,3]{0,1:T(4,128)}, ...), branch_computations={%region_6.7_spmd, %region_7.8_spmd} | conditional | flops 6 | bytes 12350 | solution.py:386
  88.0 5.9 %branch_1_fun.48 = (bf16[32,8192]{1,0:T(8,128)(2,1)}, bf16[2,4,32,8192]{3,2,1,0:T(8,128)(2,1)}, f32[2,4,32,8192]{3,2,1,0:T(8,128)}) custom-call(s32[2]{0:T(128)} %pad_add_fusion.3.at_ref, s32[768]{0:T(1024)} %reshape.137.idx_ref, bf16[32,8192]{1,0:T(8,128)(2,1)} %get-tuple-element.549.h_in, ...), custom_call_target="tpu_custom_call", output_to_operand_aliasing={{1}: (4, {}), {2}: (5, {})} | custom-call | tf_op jit(solution)/shard_map/cond/branch_1_fun/pallas_call | solution.py:142
  94.0 5.3 %branch_1_fun.49 = (bf16[32,8192]{1,0:T(8,128)(2,1)}, bf16[2,4,32,8192]{3,2,1,0:T(8,128)(2,1)}, f32[2,4,32,8192]{3,2,1,0:T(8,128)}) custom-call(s32[1]{0:T(128)} %bitcast.6.at_ref, s32[768]{0:T(1024)} %reshape.137.idx_ref, bf16[32,8192]{1,0:T(8,128)(2,1)} %get-tuple-element.554.h_in, ...), custom_call_target="tpu_custom_call", output_to_operand_aliasing={{1}: (4, {}), {2}: (5, {})} | custom-call | tf_op jit(solution)/shard_map/cond/branch_1_fun/pallas_call | solution.py:142
  99.3 5.6 %collective-permute-start.3 = (bf16[32,8192]{1,0:T(8,128)(2,1)}, bf16[32,8192]{1,0:T(8,128)(2,1)}, u32[]{:S(2)}, u32[]{:S(2)}) collective-permute-start(bf16[32,8192]{1,0:T(8,128)(2,1)} %get-tuple-element.790), channel_id=1, source_target_pairs={{0,8},{8,16},{16,24},{1,9},{9,17},{17,25},{2,10},{10,18},{18,26},{... | collective-permute-start | bytes 1572872 | tf_op jit(solution)/shard_map/ppermute | solution.py:27
  106.1 7.6 %collective-permute-done.3 = bf16[32,8192]{1,0:T(8,128)(2,1)} collective-permute-done((bf16[32,8192]{1,0:T(8,128)(2,1)}, bf16[32,8192]{1,0:T(8,128)(2,1)}, u32[]{:S(2)}, u32[]{:S(2)}) %collective-permute-start.3) | collective-permute-done | bytes 524320 | tf_op jit(solution)/shard_map/ppermute | solution.py:27
  113.8 18.9 %collective-permute-start.4 = (bf16[32,8192]{1,0:T(8,128)(2,1)}, bf16[32,8192]{1,0:T(8,128)(2,1)}, u32[]{:S(2)}, u32[]{:S(2)}) collective-permute-start(bf16[32,8192]{1,0:T(8,128)(2,1)} %get-tuple-element.793), channel_id=1, source_target_pairs={{0,8},{8,16},{16,24},{1,9},{9,17},{17,25},{2,10},{10,18},{18,26},{... | collective-permute-start | bytes 1572872 | tf_op jit(solution)/shard_map/ppermute | solution.py:27
  134.0 6.7 %collective-permute-done.4 = bf16[32,8192]{1,0:T(8,128)(2,1)} collective-permute-done((bf16[32,8192]{1,0:T(8,128)(2,1)}, bf16[32,8192]{1,0:T(8,128)(2,1)}, u32[]{:S(2)}, u32[]{:S(2)}) %collective-permute-start.4) | collective-permute-done | bytes 524320 | tf_op jit(solution)/shard_map/ppermute | solution.py:27
  140.7 5.2 %collective-permute-start.5 = (bf16[32,8192]{1,0:T(8,128)(2,1)}, bf16[32,8192]{1,0:T(8,128)(2,1)}, u32[]{:S(2)}, u32[]{:S(2)}) collective-permute-start(bf16[32,8192]{1,0:T(8,128)(2,1)} %get-tuple-element.796), channel_id=1, source_target_pairs={{0,8},{8,16},{16,24},{1,9},{9,17},{17,25},{2,10},{10,18},{18,26},{... | collective-permute-start | bytes 1572872 | tf_op jit(solution)/shard_map/ppermute | solution.py:27
  147.2 5.8 %collective-permute-done.5 = bf16[32,8192]{1,0:T(8,128)(2,1)} collective-permute-done((bf16[32,8192]{1,0:T(8,128)(2,1)}, bf16[32,8192]{1,0:T(8,128)(2,1)}, u32[]{:S(2)}, u32[]{:S(2)}) %collective-permute-start.5) | collective-permute-done | bytes 524320 | tf_op jit(solution)/shard_map/ppermute | solution.py:27
  153.0 31.1 %collective-permute-start.6 = (bf16[32,8192]{1,0:T(8,128)(2,1)}, bf16[32,8192]{1,0:T(8,128)(2,1)}, u32[]{:S(2)}, u32[]{:S(2)}) collective-permute-start(bf16[32,8192]{1,0:T(8,128)(2,1)} %get-tuple-element.799), channel_id=1, source_target_pairs={{0,8},{8,16},{16,24},{1,9},{9,17},{17,25},{2,10},{10,18},{18,26},{... | collective-permute-start | bytes 1572872 | tf_op jit(solution)/shard_map/ppermute | solution.py:27
  184.1 7.4 %collective-permute-done.14 = bf16[32,8192]{1,0:T(8,128)(2,1)S(1)} collective-permute-done((bf16[32,8192]{1,0:T(8,128)(2,1)S(1)}, bf16[32,8192]{1,0:T(8,128)(2,1)S(1)}, u32[]{:S(2)}, u32[]{:S(2)}) %collective-permute-start.14) | collective-permute-done | bytes 524320 | tf_op jit(solution)/shard_map/ppermute | solution.py:27
  192.4 15.9 %conditional.36 = ((bf16[32,8192]{1,0:T(8,128)(2,1)}, bf16[2,4,32,8192]{3,2,1,0:T(8,128)(2,1)})) conditional(s32[]{:T(128)} %convert_element_type.121, (bf16[32,8192]{1,0:T(8,128)(2,1)}, bf16[2,4,32,8192]{3,2,1,0:T(8,128)(2,1)}) %tuple.299, (s32[]{:T(128)}, s32[256,3]{0,1:T(4,128)}, bf16[32,8192]{1,0:T(8,128)(2,1)}, f32[2,4,32,8192]{3,2,1,0:T(8,128)}, ...), branch_computations={%region_32.33_spmd, %region_33.34_spmd} | conditional | flops 6 | bytes 12350 | solution.py:401
  194.6 6.2 %branch_1_fun.74 = (bf16[32,8192]{1,0:T(8,128)(2,1)}, bf16[2,4,32,8192]{3,2,1,0:T(8,128)(2,1)}) custom-call(s32[2]{0:T(128)} %pad_add_fusion.16.at_ref, s32[768]{0:T(1024)} %reshape.163.idx_ref, bf16[32,8192]{1,0:T(8,128)(2,1)} %get-tuple-element.686.g_in, f32[2,4,32,8192]{3,2,1,0:T(8,128)} %get-tuple-element.687.sy_hbm, ...), custom_call_target="tpu_custom_call", output_to_operand_aliasing={{1}: (5, {})} | custom-call | tf_op jit(solution)/shard_map/cond/branch_1_fun/pallas_call | solution.py:223
  200.8 7.4 %branch_1_fun.75 = (bf16[32,8192]{1,0:T(8,128)(2,1)}, bf16[2,4,32,8192]{3,2,1,0:T(8,128)(2,1)}) custom-call(s32[1]{0:T(128)} %bitcast.32.at_ref, s32[768]{0:T(1024)} %reshape.163.idx_ref, bf16[32,8192]{1,0:T(8,128)(2,1)} %get-tuple-element.691.g_in, f32[2,4,32,8192]{3,2,1,0:T(8,128)} %get-tuple-element.687.sy_hbm, ...), custom_call_target="tpu_custom_call", output_to_operand_aliasing={{1}: (5, {})} | custom-call | tf_op jit(solution)/shard_map/cond/branch_1_fun/pallas_call | solution.py:223
  209.6 4.9 %collective-permute-start.7 = (bf16[32,8192]{1,0:T(8,128)(2,1)}, bf16[32,8192]{1,0:T(8,128)(2,1)S(1)}, u32[]{:S(2)}, u32[]{:S(2)}) collective-permute-start(bf16[32,8192]{1,0:T(8,128)(2,1)} %get-tuple-element.802), channel_id=1, source_target_pairs={{0,8},{8,16},{16,24},{1,9},{9,17},{17,25},{2,10},{10,18},{18,26},{... | collective-permute-start | bytes 1572872 | tf_op jit(solution)/shard_map/ppermute | solution.py:27
  214.5 7.6 %collective-permute-done.15 = bf16[32,8192]{1,0:T(8,128)(2,1)S(1)} collective-permute-done((bf16[32,8192]{1,0:T(8,128)(2,1)}, bf16[32,8192]{1,0:T(8,128)(2,1)S(1)}, u32[]{:S(2)}, u32[]{:S(2)}) %collective-permute-start.15) | collective-permute-done | bytes 524320 | tf_op jit(solution)/shard_map/ppermute | solution.py:27
  222.2 14.8 %conditional.37 = ((bf16[32,8192]{1,0:T(8,128)(2,1)S(1)}, bf16[2,4,32,8192]{3,2,1,0:T(8,128)(2,1)})) conditional(s32[]{:T(128)} %convert_element_type.120, (bf16[32,8192]{1,0:T(8,128)(2,1)S(1)}, bf16[2,4,32,8192]{3,2,1,0:T(8,128)(2,1)}) %tuple.168, (s32[]{:T(128)}, s32[256,3]{0,1:T(4,128)}, s32[]{:T(128)}, bf16[32,8192]{1,0:T(8,128)(2,1)S(1)}, ...), branch_computations={%region_34.35_spmd, %region_35.36_spmd} | conditional | flops 6 | bytes 12350 | solution.py:401
  224.4 5.8 %branch_1_fun.76 = (bf16[32,8192]{1,0:T(8,128)(2,1)}, bf16[2,4,32,8192]{3,2,1,0:T(8,128)(2,1)}) custom-call(s32[2]{0:T(128)} %pad_add_fusion.17.at_ref, s32[768]{0:T(1024)} %reshape.165.idx_ref, bf16[32,8192]{1,0:T(8,128)(2,1)S(1)} %get-tuple-element.696.g_in, f32[2,4,32,8192]{3,2,1,0:T(8,128)} %get-tuple-element.697.sy_hbm, ...), custom_call_target="tpu_custom_call", output_to_operand_aliasing={{1}: (5, {})} | custom-call | tf_op jit(solution)/shard_map/cond/branch_1_fun/pallas_call | solution.py:223
  230.3 6.6 %branch_1_fun.77 = (bf16[32,8192]{1,0:T(8,128)(2,1)S(1)}, bf16[2,4,32,8192]{3,2,1,0:T(8,128)(2,1)}) custom-call(s32[1]{0:T(128)} %bitcast.34.at_ref, s32[768]{0:T(1024)} %reshape.165.idx_ref, bf16[32,8192]{1,0:T(8,128)(2,1)} %get-tuple-element.701.g_in, f32[2,4,32,8192]{3,2,1,0:T(8,128)} %get-tuple-element.697.sy_hbm, ...), custom_call_target="tpu_custom_call", output_to_operand_aliasing={{1}: (5, {})} | custom-call | tf_op jit(solution)/shard_map/cond/branch_1_fun/pallas_call | solution.py:223
  239.0 6.5 %collective-permute-start.8 = (bf16[32,8192]{1,0:T(8,128)(2,1)}, bf16[32,8192]{1,0:T(8,128)(2,1)S(1)}, u32[]{:S(2)}, u32[]{:S(2)}) collective-permute-start(bf16[32,8192]{1,0:T(8,128)(2,1)} %get-tuple-element.807), channel_id=1, source_target_pairs={{0,8},{8,16},{16,24},{1,9},{9,17},{17,25},{2,10},{10,18},{18,26},{... | collective-permute-start | bytes 1572872 | tf_op jit(solution)/shard_map/ppermute | solution.py:27
  245.5 6.1 %collective-permute-done.16 = bf16[32,8192]{1,0:T(8,128)(2,1)} collective-permute-done((bf16[32,8192]{1,0:T(8,128)(2,1)S(1)}, bf16[32,8192]{1,0:T(8,128)(2,1)}, u32[]{:S(2)}, u32[]{:S(2)}) %collective-permute-start.16) | collective-permute-done | bytes 524320 | tf_op jit(solution)/shard_map/ppermute | solution.py:27
  251.6 16.0 %conditional.38 = ((bf16[32,8192]{1,0:T(8,128)(2,1)}, bf16[2,4,32,8192]{3,2,1,0:T(8,128)(2,1)})) conditional(s32[]{:T(128)} %convert_element_type.119, (bf16[32,8192]{1,0:T(8,128)(2,1)}, bf16[2,4,32,8192]{3,2,1,0:T(8,128)(2,1)}) %tuple.170, (s32[]{:T(128)}, s32[256,3]{0,1:T(4,128)}, s32[]{:T(128)}, bf16[32,8192]{1,0:T(8,128)(2,1)}, ...), branch_computations={%region_36.37_spmd.clone, %region_37.38_spmd.clone} | conditional | flops 6 | bytes 12350 | solution.py:401
  254.0 6.2 %branch_1_fun.80 = (bf16[32,8192]{1,0:T(8,128)(2,1)}, bf16[2,4,32,8192]{3,2,1,0:T(8,128)(2,1)}) custom-call(s32[2]{0:T(128)} %pad_add_fusion.19.at_ref, s32[768]{0:T(1024)} %reshape.185.idx_ref, bf16[32,8192]{1,0:T(8,128)(2,1)} %get-tuple-element.837.g_in, f32[2,4,32,8192]{3,2,1,0:T(8,128)} %get-tuple-element.838.sy_hbm, ...), custom_call_target="tpu_custom_call", output_to_operand_aliasing={{1}: (5, {})} | custom-call | tf_op jit(solution)/shard_map/cond/branch_1_fun/pallas_call | solution.py:223
  260.1 7.4 %branch_1_fun.81 = (bf16[32,8192]{1,0:T(8,128)(2,1)}, bf16[2,4,32,8192]{3,2,1,0:T(8,128)(2,1)}) custom-call(s32[1]{0:T(128)} %bitcast.49.at_ref, s32[768]{0:T(1024)} %reshape.185.idx_ref, bf16[32,8192]{1,0:T(8,128)(2,1)} %get-tuple-element.842.g_in, f32[2,4,32,8192]{3,2,1,0:T(8,128)} %get-tuple-element.838.sy_hbm, ...), custom_call_target="tpu_custom_call", output_to_operand_aliasing={{1}: (5, {})} | custom-call | tf_op jit(solution)/shard_map/cond/branch_1_fun/pallas_call | solution.py:223
  270.5 9.4 %collective-permute-done.17 = bf16[32,8192]{1,0:T(8,128)(2,1)S(1)} collective-permute-done((bf16[32,8192]{1,0:T(8,128)(2,1)}, bf16[32,8192]{1,0:T(8,128)(2,1)S(1)}, u32[]{:S(2)}, u32[]{:S(2)}) %collective-permute-start.17) | collective-permute-done | bytes 524320 | tf_op jit(solution)/shard_map/ppermute | solution.py:27
  279.9 14.8 %conditional.39 = (bf16[2,4,32,8192]{3,2,1,0:T(8,128)(2,1)}) conditional(s32[]{:T(128)} %convert_element_type.118, bf16[2,4,32,8192]{3,2,1,0:T(8,128)(2,1)} %get-tuple-element.826, (s32[]{:T(128)}, s32[256,3]{0,1:T(4,128)S(1)}, s32[]{:T(128)}, bf16[32,8192]{1,0:T(8,128)(2,1)S(1)}, f32[2,4,32,8192]{3,2,1,0:T(8,128)}, ...), branch_computations={%region_38.39_spmd, %region_39.40_spmd} | conditional | flops 6 | bytes 12350 | solution.py:401
  281.4 5.8 %branch_1_fun.78 = (bf16[32,8192]{1,0:T(8,128)(2,1)}, bf16[2,4,32,8192]{3,2,1,0:T(8,128)(2,1)}) custom-call(s32[2]{0:T(128)} %pad_add_fusion.18.at_ref, s32[768]{0:T(1024)} %reshape.169.idx_ref, bf16[32,8192]{1,0:T(8,128)(2,1)S(1)} %get-tuple-element.720.g_in, f32[2,4,32,8192]{3,2,1,0:T(8,128)} %get-tuple-element.721.sy_hbm, ...), custom_call_target="tpu_custom_call", output_to_operand_aliasing={{1}: (5, {})} | custom-call | tf_op jit(solution)/shard_map/cond/branch_1_fun/pallas_call | solution.py:223
  287.2 7.4 %branch_1_fun.79 = (bf16[32,8192]{1,0:T(8,128)(2,1)}, bf16[2,4,32,8192]{3,2,1,0:T(8,128)(2,1)}) custom-call(s32[1]{0:T(128)} %bitcast.36.at_ref, s32[768]{0:T(1024)} %reshape.169.idx_ref, bf16[32,8192]{1,0:T(8,128)(2,1)} %get-tuple-element.725.g_in, f32[2,4,32,8192]{3,2,1,0:T(8,128)} %get-tuple-element.721.sy_hbm, ...), custom_call_target="tpu_custom_call", output_to_operand_aliasing={{1}: (5, {})} | custom-call | tf_op jit(solution)/shard_map/cond/branch_1_fun/pallas_call | solution.py:223
  294.7 8.2 %shard_map.48 = bf16[4,32,128,128]{3,2,1,0:T(8,128)(2,1)} custom-call(s32[1]{0:T(128)} %bitcast.42.sel_ref, s32[768]{0:T(1024)} %reshape.178.idx_ref, bf16[2,4,32,8192]{3,2,1,0:T(8,128)(2,1)} %get-tuple-element.808.h_ref, bf16[2,4,32,8192]{3,2,1,0:T(8,128)(2,1)} %get-tuple-element.1118.s_ref), custom_call_target="tpu_custom_call" | custom-call | tf_op jit(solution)/shard_map/pallas_call | solution.py:309
  302.9 9.3 %shard_map.47 = f32[4,32,128,128]{3,2,1,0:T(8,128)} custom-call(s32[1]{0:T(128)} %bitcast.38.sel_ref, s32[768]{0:T(1024)} %reshape.178.idx_ref, bf16[2,4,32,8192]{3,2,1,0:T(8,128)(2,1)} %get-tuple-element.808.h_ref, bf16[2,4,32,8192]{3,2,1,0:T(8,128)(2,1)} %get-tuple-element.1118.s_ref), custom_call_target="tpu_custom_call" | custom-call | tf_op jit(solution)/shard_map/pallas_call | solution.py:309
  312.2 5.0 %fusion = bf16[2,32,128,128]{3,2,1,0:T(8,128)(2,1)} fusion(f32[2,2,32,128,128]{4,3,2,1,0:T(8,128)} %bitcast.80, s32[]{:T(128)S(6)} %select_n.64, bf16[2,2,32,128,128]{4,3,2,1,0:T(8,128)(2,1)} %bitcast.43), kind=kLoop, calls=%fused_computation.21 | loop fusion | flops 3145728 | bytes 8388612 | tf_op jit(solution)/shard_map/convert_element_type | solution.py:319
  317.2 26.2 %collective-permute-done.19 = bf16[2,32,128,128]{3,2,1,0:T(8,128)(2,1)S(1)} collective-permute-done((bf16[2,32,128,128]{3,2,1,0:T(8,128)(2,1)}, bf16[2,32,128,128]{3,2,1,0:T(8,128)(2,1)S(1)}, u32[]{:S(2)}, u32[]{:S(2)}) %collective-permute-start.19) | collective-permute-done | bytes 2097184 | tf_op jit(solution)/shard_map/ppermute | solution.py:319
  348.5 14.8 %collective-permute-done.20 = bf16[32,128,128]{2,1,0:T(8,128)(2,1)S(1)} collective-permute-done((bf16[32,128,128]{2,1,0:T(8,128)(2,1)S(1)}, bf16[32,128,128]{2,1,0:T(8,128)(2,1)S(1)}, u32[]{:S(2)}, u32[]{:S(2)}) %collective-permute-start.20) | collective-permute-done | bytes 1048608 | tf_op jit(solution)/shard_map/ppermute | solution.py:319
  363.2 4.5 %fusion.2 = f32[32,128,128]{2,1,0:T(8,128)} fusion(bf16[32,128,128]{2,1,0:T(8,128)(2,1)S(1)} %collective-permute-done.20, f32[2,32,128,128]{3,2,1,0:T(8,128)} %copy-done.1, s32[]{:T(128)S(6)} %select_n.59, f32[2,2,32,128,128]{4,3,2,1,0:T(8,128)} %bitcast.82, s32[]{:T(128)S(6)} %select_n.60, s32[]{:T(128)S(6)} %select_n.63, ...), kind=kLoop, calls=%fused_computation.25 | loop fusion | flops 2621440 | bytes 8388620 | tf_op jit(solution)/shard_map/add | solution.py:350
  (75 shorter events, 40.8 us)
Async XLA Ops:
  15.2 13.7 %collective-permute-start = (bf16[32,8192]{1,0:T(8,128)(2,1)}, bf16[32,8192]{1,0:T(8,128)(2,1)S(1)}, u32[]{:S(2)}, u32[]{:S(2)}) collective-permute-start(bf16[32,8192]{1,0:T(8,128)(2,1)} %get-tuple-element.781), channel_id=1, source_target_pairs={{0,8},{8,16},{16,24},{1,9},{9,17},{17,25},{2,10},{10,18},{18,26},{... | collective-permute-start | bytes 1572872 | tf_op jit(solution)/shard_map/ppermute | solution.py:27
  16.5 12.3 %copy-start = (bf16[2,64,8192]{2,1,0:T(8,128)(2,1)S(1)}, bf16[2,64,8192]{2,1,0:T(8,128)(2,1)}, u32[]{:S(2)}) copy-start(bf16[2,64,8192]{2,1,0:T(8,128)(2,1)} %param.44) | copy-start | bytes 6291460
  17.4 29.2 %collective-permute-start.9 = (bf16[32,8192]{1,0:T(8,128)(2,1)}, bf16[32,8192]{1,0:T(8,128)(2,1)S(1)}, u32[]{:S(2)}, u32[]{:S(2)}) collective-permute-start(bf16[32,8192]{1,0:T(8,128)(2,1)} %get-tuple-element.810), channel_id=1, source_target_pairs={{8,0},{16,8},{24,16},{9,1},{17,9},{25,17},{10,2},{18,10},{26,18},{... | collective-permute-start | bytes 1572872 | tf_op jit(solution)/shard_map/ppermute | solution.py:27
  41.2 15.8 %collective-permute-start.1 = (bf16[32,8192]{1,0:T(8,128)(2,1)S(1)}, bf16[32,8192]{1,0:T(8,128)(2,1)}, u32[]{:S(2)}, u32[]{:S(2)}) collective-permute-start(bf16[32,8192]{1,0:T(8,128)(2,1)S(1)} %get-tuple-element.784), channel_id=1, source_target_pairs={{0,8},{8,16},{16,24},{1,9},{9,17},{17,25},{2,10},{10,18},{18,26},{... | collective-permute-start | bytes 1572872 | tf_op jit(solution)/shard_map/ppermute | solution.py:27
  46.6 29.4 %collective-permute-start.10 = (bf16[32,8192]{1,0:T(8,128)(2,1)S(1)}, bf16[32,8192]{1,0:T(8,128)(2,1)}, u32[]{:S(2)}, u32[]{:S(2)}) collective-permute-start(bf16[32,8192]{1,0:T(8,128)(2,1)S(1)} %get-tuple-element.812), channel_id=1, source_target_pairs={{8,0},{16,8},{24,16},{9,1},{17,9},{25,17},{10,2},{18,10},{26,18},{... | collective-permute-start | bytes 1572872 | tf_op jit(solution)/shard_map/ppermute | solution.py:27
  70.5 15.4 %collective-permute-start.2 = (bf16[32,8192]{1,0:T(8,128)(2,1)}, bf16[32,8192]{1,0:T(8,128)(2,1)}, u32[]{:S(2)}, u32[]{:S(2)}) collective-permute-start(bf16[32,8192]{1,0:T(8,128)(2,1)} %get-tuple-element.787), channel_id=1, source_target_pairs={{0,8},{8,16},{16,24},{1,9},{9,17},{17,25},{2,10},{10,18},{18,26},{... | collective-permute-start | bytes 1572872 | tf_op jit(solution)/shard_map/ppermute | solution.py:27
  76.0 28.8 %collective-permute-start.11 = (bf16[32,8192]{1,0:T(8,128)(2,1)}, bf16[32,8192]{1,0:T(8,128)(2,1)S(1)}, u32[]{:S(2)}, u32[]{:S(2)}) collective-permute-start(bf16[32,8192]{1,0:T(8,128)(2,1)} %get-tuple-element.814), channel_id=1, source_target_pairs={{8,0},{16,8},{24,16},{9,1},{17,9},{25,17},{10,2},{18,10},{26,18},{... | collective-permute-start | bytes 1572872 | tf_op jit(solution)/shard_map/ppermute | solution.py:27
  99.3 14.5 %collective-permute-start.3 = (bf16[32,8192]{1,0:T(8,128)(2,1)}, bf16[32,8192]{1,0:T(8,128)(2,1)}, u32[]{:S(2)}, u32[]{:S(2)}) collective-permute-start(bf16[32,8192]{1,0:T(8,128)(2,1)} %get-tuple-element.790), channel_id=1, source_target_pairs={{0,8},{8,16},{16,24},{1,9},{9,17},{17,25},{2,10},{10,18},{18,26},{... | collective-permute-start | bytes 1572872 | tf_op jit(solution)/shard_map/ppermute | solution.py:27
  104.8 27.9 %collective-permute-start.12 = (bf16[32,8192]{1,0:T(8,128)(2,1)S(1)}, bf16[32,8192]{1,0:T(8,128)(2,1)S(1)}, u32[]{:S(2)}, u32[]{:S(2)}) collective-permute-start(bf16[32,8192]{1,0:T(8,128)(2,1)S(1)} %get-tuple-element.816), channel_id=1, source_target_pairs={{8,0},{16,8},{24,16},{9,1},{17,9},{25,17},{10,2},{18,10},{26,18},{... | collective-permute-start | bytes 1572872 | tf_op jit(solution)/shard_map/ppermute | solution.py:27
  113.8 27.0 %collective-permute-start.4 = (bf16[32,8192]{1,0:T(8,128)(2,1)}, bf16[32,8192]{1,0:T(8,128)(2,1)}, u32[]{:S(2)}, u32[]{:S(2)}) collective-permute-start(bf16[32,8192]{1,0:T(8,128)(2,1)} %get-tuple-element.793), channel_id=1, source_target_pairs={{0,8},{8,16},{16,24},{1,9},{9,17},{17,25},{2,10},{10,18},{18,26},{... | collective-permute-start | bytes 1572872 | tf_op jit(solution)/shard_map/ppermute | solution.py:27
  132.7 13.2 %collective-permute-start.13 = (bf16[32,8192]{1,0:T(8,128)(2,1)S(1)}, bf16[32,8192]{1,0:T(8,128)(2,1)S(1)}, u32[]{:S(2)}, u32[]{:S(2)}) collective-permute-start(bf16[32,8192]{1,0:T(8,128)(2,1)S(1)} %get-tuple-element.818), channel_id=1, source_target_pairs={{8,0},{16,8},{24,16},{9,1},{17,9},{25,17},{10,2},{18,10},{26,18},{... | collective-permute-start | bytes 1572872 | tf_op jit(solution)/shard_map/ppermute | solution.py:27
  140.7 12.3 %collective-permute-start.5 = (bf16[32,8192]{1,0:T(8,128)(2,1)}, bf16[32,8192]{1,0:T(8,128)(2,1)}, u32[]{:S(2)}, u32[]{:S(2)}) collective-permute-start(bf16[32,8192]{1,0:T(8,128)(2,1)} %get-tuple-element.796), channel_id=1, source_target_pairs={{0,8},{8,16},{16,24},{1,9},{9,17},{17,25},{2,10},{10,18},{18,26},{... | collective-permute-start | bytes 1572872 | tf_op jit(solution)/shard_map/ppermute | solution.py:27
  145.9 45.7 %collective-permute-start.14 = (bf16[32,8192]{1,0:T(8,128)(2,1)S(1)}, bf16[32,8192]{1,0:T(8,128)(2,1)S(1)}, u32[]{:S(2)}, u32[]{:S(2)}) collective-permute-start(bf16[32,8192]{1,0:T(8,128)(2,1)S(1)} %get-tuple-element.820), channel_id=1, source_target_pairs={{8,0},{16,8},{24,16},{9,1},{17,9},{25,17},{10,2},{18,10},{26,18},{... | collective-permute-start | bytes 1572872 | tf_op jit(solution)/shard_map/ppermute | solution.py:27
  153.0 56.6 %collective-permute-start.6 = (bf16[32,8192]{1,0:T(8,128)(2,1)}, bf16[32,8192]{1,0:T(8,128)(2,1)}, u32[]{:S(2)}, u32[]{:S(2)}) collective-permute-start(bf16[32,8192]{1,0:T(8,128)(2,1)} %get-tuple-element.799), channel_id=1, source_target_pairs={{0,8},{8,16},{16,24},{1,9},{9,17},{17,25},{2,10},{10,18},{18,26},{... | collective-permute-start | bytes 1572872 | tf_op jit(solution)/shard_map/ppermute | solution.py:27
  191.6 0.8 copy-start.4
  208.3 13.9 %collective-permute-start.15 = (bf16[32,8192]{1,0:T(8,128)(2,1)}, bf16[32,8192]{1,0:T(8,128)(2,1)S(1)}, u32[]{:S(2)}, u32[]{:S(2)}) collective-permute-start(bf16[32,8192]{1,0:T(8,128)(2,1)} %get-tuple-element.822), channel_id=1, source_target_pairs={{8,0},{16,8},{24,16},{9,1},{17,9},{25,17},{10,2},{18,10},{26,18},{... | collective-permute-start | bytes 1572872 | tf_op jit(solution)/shard_map/ppermute | solution.py:27
  209.6 28.6 %collective-permute-start.7 = (bf16[32,8192]{1,0:T(8,128)(2,1)}, bf16[32,8192]{1,0:T(8,128)(2,1)S(1)}, u32[]{:S(2)}, u32[]{:S(2)}) collective-permute-start(bf16[32,8192]{1,0:T(8,128)(2,1)} %get-tuple-element.802), channel_id=1, source_target_pairs={{0,8},{8,16},{16,24},{1,9},{9,17},{17,25},{2,10},{10,18},{18,26},{... | collective-permute-start | bytes 1572872 | tf_op jit(solution)/shard_map/ppermute | solution.py:27
  236.9 14.7 %collective-permute-start.16 = (bf16[32,8192]{1,0:T(8,128)(2,1)S(1)}, bf16[32,8192]{1,0:T(8,128)(2,1)}, u32[]{:S(2)}, u32[]{:S(2)}) collective-permute-start(bf16[32,8192]{1,0:T(8,128)(2,1)S(1)} %get-tuple-element.824), channel_id=1, source_target_pairs={{8,0},{16,8},{24,16},{9,1},{17,9},{25,17},{10,2},{18,10},{26,18},{... | collective-permute-start | bytes 1572872 | tf_op jit(solution)/shard_map/ppermute | solution.py:27
  238.2 0.8 copy-start.3
  239.0 31.5 %collective-permute-start.8 = (bf16[32,8192]{1,0:T(8,128)(2,1)}, bf16[32,8192]{1,0:T(8,128)(2,1)S(1)}, u32[]{:S(2)}, u32[]{:S(2)}) collective-permute-start(bf16[32,8192]{1,0:T(8,128)(2,1)} %get-tuple-element.807), channel_id=1, source_target_pairs={{0,8},{8,16},{16,24},{1,9},{9,17},{17,25},{2,10},{10,18},{18,26},{... | collective-permute-start | bytes 1572872 | tf_op jit(solution)/shard_map/ppermute | solution.py:27
  251.6 18.9 %copy-start.2 = (s32[256,3]{0,1:T(4,128)S(1)}, s32[256,3]{0,1:T(4,128)}, u32[]{:S(2)}) copy-start(s32[256,3]{0,1:T(4,128)} %param.47) | copy-start | bytes 9220
  267.6 12.3 %collective-permute-start.17 = (bf16[32,8192]{1,0:T(8,128)(2,1)}, bf16[32,8192]{1,0:T(8,128)(2,1)S(1)}, u32[]{:S(2)}, u32[]{:S(2)}) collective-permute-start(bf16[32,8192]{1,0:T(8,128)(2,1)} %get-tuple-element.827), channel_id=1, source_target_pairs={{8,0},{16,8},{24,16},{9,1},{17,9},{25,17},{10,2},{18,10},{26,18},{... | collective-permute-start | bytes 1572872 | tf_op jit(solution)/shard_map/ppermute | solution.py:27
  302.8 9.3 %collective-permute-start.18 = (bf16[4,32,128,128]{3,2,1,0:T(8,128)(2,1)}, bf16[4,32,128,128]{3,2,1,0:T(8,128)(2,1)}, u32[]{:S(2)}, u32[]{:S(2)}) collective-permute-start(bf16[4,32,128,128]{3,2,1,0:T(8,128)(2,1)} %shard_map.48), channel_id=1, source_target_pairs={{0,1},{1,0},{2,3},{3,2},{4,5},{5,4},{6,7},{7,6},{8,9},{9,8},{10,11... | collective-permute-start | bytes 12582920 | tf_op jit(solution)/shard_map/ppermute | solution.py:333
  317.2 26.2 %collective-permute-start.19 = (bf16[2,32,128,128]{3,2,1,0:T(8,128)(2,1)}, bf16[2,32,128,128]{3,2,1,0:T(8,128)(2,1)S(1)}, u32[]{:S(2)}, u32[]{:S(2)}) collective-permute-start(bf16[2,32,128,128]{3,2,1,0:T(8,128)(2,1)} %fusion), channel_id=1, source_target_pairs={{0,2},{1,5},{2,0},{3,7},{4,6},{5,1},{6,4},{7,3},{8,10},{9,13},{10,... | collective-permute-start | bytes 6291464 | tf_op jit(solution)/shard_map/ppermute | solution.py:319
  343.9 2.1 copy-start.1
  348.4 14.9 %collective-permute-start.20 = (bf16[32,128,128]{2,1,0:T(8,128)(2,1)S(1)}, bf16[32,128,128]{2,1,0:T(8,128)(2,1)S(1)}, u32[]{:S(2)}, u32[]{:S(2)}) collective-permute-start(bf16[32,128,128]{2,1,0:T(8,128)(2,1)S(1)} %fusion.1), channel_id=1, source_target_pairs={{0,4},{1,3},{2,6},{3,1},{4,0},{5,7},{6,2},{7,5},{8,12},{9,11},{10,... | collective-permute-start | bytes 3145736 | tf_op jit(solution)/shard_map/ppermute | solution.py:319

commit v7 on v6

--- a/solution.py
+++ b/solution.py
@@ -13,7 +13,7 @@
 CH = 1024
 NSUB = 32
 SPLIT = 2
-GROUP = 16
+GROUP = 32
 VMEM_LIMIT = 60 * 1024 * 1024
 
 _SMEM = pl.BlockSpec(memory_space=pltpu.SMEM)

time: 369 us -> 374 us (1.014)
  starting transfers between devices: 96.2 us -> 111 us
  Pallas kernels: 115 us -> 106 us
    ppermute x18, starting transfers between devices: 96.1 us -> 111 us  [shifted(): lax.ppermute(value, axis, [(source, source + steps) for source in range(l...]
    pallas_call x8, Pallas kernels: 52.9 us -> 47.6 us  [layer_backward(): pl.pallas_call(functools.partial(_bwd_kernel, layer * KMAX, layer, entry)...]
  transfers between devices with their start and end apart: 21 -> 21, of which waited for: 12 -> 12; matrix products, arithmetic and copies ran while one was open for 4% -> 4% of each run, Pallas kernels for 22% -> 20%
where the time goes in v7:
time: 374 us; the launch traced here: 375 us
  waiting for transfers between devices  122 us (33%)
  starting transfers between devices  111 us (30%)
  Pallas kernels  106 us (28%)
  local copies, waits for them, and re-layouts  19.2 us (5%)
  other arithmetic  17.2 us (5%)
    ppermute x18, starting transfers between devices, shifted(): lax.ppermute(value, axis, [(source, source + steps) for source in range(l...  111 us
    ppermute x18, waiting for transfers between devices, shifted(): lax.ppermute(value, axis, [(source, source + steps) for source in range(l...  80.6 us
    pallas_call x8, Pallas kernels, layer_backward(): pl.pallas_call(functools.partial(_bwd_kernel, layer * KMAX, layer, entry)...  47.6 us
    pallas_call x8, Pallas kernels, layer_forward(): pl.pallas_call(functools.partial(_fwd_kernel, layer * KMAX, layer), out_s...  41.9 us
    ppermute x2, waiting for transfers between devices, _exchange(): lax.ppermute(send.astype(jnp.bfloat16), 'dp', pairs).astype(jnp.float32)  41 us
    pallas_call x2, Pallas kernels, dw_half(): pl.pallas_call(_dw_half_kernel, out_shape=jax.ShapeDtypeStruct((4, per, B...  16.2 us
  transfers between devices with their start and end apart: 21, of which 12 were waited for; matrix products, arithmetic and copies ran while one was open for 4% of the time, Pallas kernels for 20%

profile of v7, /device:TPU:0, one launch (start us, length us, event | category | flops | bytes accessed | tf_op | source)
XLA Modules:
  0.0 375.1 jit_solution(17803006929081377428)
XLA Ops:
  0.0 14.4 %conditional.20 = ((bf16[32,8192]{1,0:T(8,128)(2,1)}, bf16[2,4,32,8192]{3,2,1,0:T(8,128)(2,1)}, f32[2,4,32,8192]{3,2,1,0:T(8,128)})) conditional(s32[]{:T(128)} %convert_element_type.117, (bf16[2,4,32,8192]{3,2,1,0:T(8,128)(2,1)}, f32[2,4,32,8192]{3,2,1,0:T(8,128)}) %tuple.135, (s32[]{:T(128)}, s32[256,3]{0,1:T(4,128)}, s32[]{:T(128)}, ...), branch_computations={%region_0.1_spmd, %region_1.2_spmd} | conditional | flops 6 | bytes 536640 | solution.py:386
  3.0 6.1 %branch_1_fun.42 = (bf16[32,8192]{1,0:T(8,128)(2,1)}, bf16[2,4,32,8192]{3,2,1,0:T(8,128)(2,1)}, f32[2,4,32,8192]{3,2,1,0:T(8,128)}) custom-call(s32[2]{0:T(128)} %pad_add_fusion.at_ref, s32[768]{0:T(1024)} %reshape.123.idx_ref, bf16[32,8192]{1,0:T(8,128)(2,1)} %broadcast_in_dim.9.h_in, ...), custom_call_target="tpu_custom_call", output_to_operand_aliasing={{1}: (4, {}), {2}: (5, {})} | custom-call | tf_op jit(solution)/shard_map/cond/branch_1_fun/pallas_call | solution.py:142
  9.1 5.3 %branch_1_fun.43 = (bf16[32,8192]{1,0:T(8,128)(2,1)}, bf16[2,4,32,8192]{3,2,1,0:T(8,128)(2,1)}, f32[2,4,32,8192]{3,2,1,0:T(8,128)}) custom-call(s32[1]{0:T(128)} %bitcast.at_ref, s32[768]{0:T(1024)} %reshape.123.idx_ref, bf16[32,8192]{1,0:T(8,128)(2,1)} %get-tuple-element.521.h_in, ...), custom_call_target="tpu_custom_call", output_to_operand_aliasing={{1}: (4, {}), {2}: (5, {})} | custom-call | tf_op jit(solution)/shard_map/cond/branch_1_fun/pallas_call | solution.py:142
  17.9 10.2 %collective-permute-done = bf16[32,8192]{1,0:T(8,128)(2,1)S(1)} collective-permute-done((bf16[32,8192]{1,0:T(8,128)(2,1)}, bf16[32,8192]{1,0:T(8,128)(2,1)S(1)}, u32[]{:S(2)}, u32[]{:S(2)}) %collective-permute-start) | collective-permute-done | bytes 524320 | tf_op jit(solution)/shard_map/ppermute | solution.py:27
  28.1 11.6 %conditional.21 = ((bf16[32,8192]{1,0:T(8,128)(2,1)S(1)}, bf16[2,4,32,8192]{3,2,1,0:T(8,128)(2,1)}, f32[2,4,32,8192]{3,2,1,0:T(8,128)})) conditional(s32[]{:T(128)} %convert_element_type.116, (bf16[32,8192]{1,0:T(8,128)(2,1)S(1)}, bf16[2,4,32,8192]{3,2,1,0:T(8,128)(2,1)}, f32[2,4,32,8192]{3,2,1,0:T(8,128)}) %tuple.137, (s32[]{:T(128)}, ...), branch_computations={%region_2.3_spmd, %region_3.4_spmd} | conditional | flops 6 | bytes 12350 | solution.py:386
  30.3 4.9 %branch_1_fun.44 = (bf16[32,8192]{1,0:T(8,128)(2,1)}, bf16[2,4,32,8192]{3,2,1,0:T(8,128)(2,1)}, f32[2,4,32,8192]{3,2,1,0:T(8,128)}) custom-call(s32[2]{0:T(128)} %pad_add_fusion.1.at_ref, s32[768]{0:T(1024)} %reshape.125.idx_ref, bf16[32,8192]{1,0:T(8,128)(2,1)S(1)} %get-tuple-element.527.h_in, ...), custom_call_target="tpu_custom_call", output_to_operand_aliasing={{1}: (4, {}), {2}: (5, {})} | custom-call | tf_op jit(solution)/shard_map/cond/branch_1_fun/pallas_call | solution.py:142
  35.2 4.5 %branch_1_fun.45 = (bf16[32,8192]{1,0:T(8,128)(2,1)S(1)}, bf16[2,4,32,8192]{3,2,1,0:T(8,128)(2,1)}, f32[2,4,32,8192]{3,2,1,0:T(8,128)}) custom-call(s32[1]{0:T(128)} %bitcast.2.at_ref, s32[768]{0:T(1024)} %reshape.125.idx_ref, bf16[32,8192]{1,0:T(8,128)(2,1)} %get-tuple-element.532.h_in, ...), custom_call_target="tpu_custom_call", output_to_operand_aliasing={{1}: (4, {}), {2}: (5, {})} | custom-call | tf_op jit(solution)/shard_map/cond/branch_1_fun/pallas_call | solution.py:142
  39.7 5.8 %collective-permute-start.1 = (bf16[32,8192]{1,0:T(8,128)(2,1)S(1)}, bf16[32,8192]{1,0:T(8,128)(2,1)}, u32[]{:S(2)}, u32[]{:S(2)}) collective-permute-start(bf16[32,8192]{1,0:T(8,128)(2,1)S(1)} %get-tuple-element.784), channel_id=1, source_target_pairs={{0,8},{8,16},{16,24},{1,9},{9,17},{17,25},{2,10},{10,18},{18,26},{... | collective-permute-start | bytes 1572872 | tf_op jit(solution)/shard_map/ppermute | solution.py:27
  46.8 9.1 %collective-permute-done.1 = bf16[32,8192]{1,0:T(8,128)(2,1)} collective-permute-done((bf16[32,8192]{1,0:T(8,128)(2,1)S(1)}, bf16[32,8192]{1,0:T(8,128)(2,1)}, u32[]{:S(2)}, u32[]{:S(2)}) %collective-permute-start.1) | collective-permute-done | bytes 524320 | tf_op jit(solution)/shard_map/ppermute | solution.py:27
  55.9 12.8 %conditional.22 = ((bf16[32,8192]{1,0:T(8,128)(2,1)}, bf16[2,4,32,8192]{3,2,1,0:T(8,128)(2,1)}, f32[2,4,32,8192]{3,2,1,0:T(8,128)})) conditional(s32[]{:T(128)} %convert_element_type.115, (bf16[32,8192]{1,0:T(8,128)(2,1)}, bf16[2,4,32,8192]{3,2,1,0:T(8,128)(2,1)}, f32[2,4,32,8192]{3,2,1,0:T(8,128)}) %tuple.139, (s32[]{:T(128)}, s32[256,3]{0,1:T(4,128)}, ...), branch_computations={%region_4.5_spmd, %region_5.6_spmd} | conditional | flops 6 | bytes 12350 | solution.py:386
  58.1 5.2 %branch_1_fun.46 = (bf16[32,8192]{1,0:T(8,128)(2,1)}, bf16[2,4,32,8192]{3,2,1,0:T(8,128)(2,1)}, f32[2,4,32,8192]{3,2,1,0:T(8,128)}) custom-call(s32[2]{0:T(128)} %pad_add_fusion.2.at_ref, s32[768]{0:T(1024)} %reshape.127.idx_ref, bf16[32,8192]{1,0:T(8,128)(2,1)} %get-tuple-element.538.h_in, ...), custom_call_target="tpu_custom_call", output_to_operand_aliasing={{1}: (4, {}), {2}: (5, {})} | custom-call | tf_op jit(solution)/shard_map/cond/branch_1_fun/pallas_call | solution.py:142
  63.4 5.3 %branch_1_fun.47 = (bf16[32,8192]{1,0:T(8,128)(2,1)}, bf16[2,4,32,8192]{3,2,1,0:T(8,128)(2,1)}, f32[2,4,32,8192]{3,2,1,0:T(8,128)}) custom-call(s32[1]{0:T(128)} %bitcast.4.at_ref, s32[768]{0:T(1024)} %reshape.127.idx_ref, bf16[32,8192]{1,0:T(8,128)(2,1)} %get-tuple-element.543.h_in, ...), custom_call_target="tpu_custom_call", output_to_operand_aliasing={{1}: (4, {}), {2}: (5, {})} | custom-call | tf_op jit(solution)/shard_map/cond/branch_1_fun/pallas_call | solution.py:142
  68.7 5.9 %collective-permute-start.2 = (bf16[32,8192]{1,0:T(8,128)(2,1)}, bf16[32,8192]{1,0:T(8,128)(2,1)}, u32[]{:S(2)}, u32[]{:S(2)}) collective-permute-start(bf16[32,8192]{1,0:T(8,128)(2,1)} %get-tuple-element.787), channel_id=1, source_target_pairs={{0,8},{8,16},{16,24},{1,9},{9,17},{17,25},{2,10},{10,18},{18,26},{... | collective-permute-start | bytes 1572872 | tf_op jit(solution)/shard_map/ppermute | solution.py:27
  75.9 8.5 %collective-permute-done.2 = bf16[32,8192]{1,0:T(8,128)(2,1)} collective-permute-done((bf16[32,8192]{1,0:T(8,128)(2,1)}, bf16[32,8192]{1,0:T(8,128)(2,1)}, u32[]{:S(2)}, u32[]{:S(2)}) %collective-permute-start.2) | collective-permute-done | bytes 524320 | tf_op jit(solution)/shard_map/ppermute | solution.py:27
  84.5 12.7 %conditional.23 = ((bf16[32,8192]{1,0:T(8,128)(2,1)}, bf16[2,4,32,8192]{3,2,1,0:T(8,128)(2,1)}, f32[2,4,32,8192]{3,2,1,0:T(8,128)})) conditional(s32[]{:T(128)} %convert_element_type.114, (bf16[32,8192]{1,0:T(8,128)(2,1)}, bf16[2,4,32,8192]{3,2,1,0:T(8,128)(2,1)}, f32[2,4,32,8192]{3,2,1,0:T(8,128)}) %tuple.141, (s32[]{:T(128)}, s32[256,3]{0,1:T(4,128)}, ...), branch_computations={%region_6.7_spmd, %region_7.8_spmd} | conditional | flops 6 | bytes 12350 | solution.py:386
  86.7 5.3 %branch_1_fun.48 = (bf16[32,8192]{1,0:T(8,128)(2,1)}, bf16[2,4,32,8192]{3,2,1,0:T(8,128)(2,1)}, f32[2,4,32,8192]{3,2,1,0:T(8,128)}) custom-call(s32[2]{0:T(128)} %pad_add_fusion.3.at_ref, s32[768]{0:T(1024)} %reshape.137.idx_ref, bf16[32,8192]{1,0:T(8,128)(2,1)} %get-tuple-element.549.h_in, ...), custom_call_target="tpu_custom_call", output_to_operand_aliasing={{1}: (4, {}), {2}: (5, {})} | custom-call | tf_op jit(solution)/shard_map/cond/branch_1_fun/pallas_call | solution.py:142
  91.9 5.3 %branch_1_fun.49 = (bf16[32,8192]{1,0:T(8,128)(2,1)}, bf16[2,4,32,8192]{3,2,1,0:T(8,128)(2,1)}, f32[2,4,32,8192]{3,2,1,0:T(8,128)}) custom-call(s32[1]{0:T(128)} %bitcast.6.at_ref, s32[768]{0:T(1024)} %reshape.137.idx_ref, bf16[32,8192]{1,0:T(8,128)(2,1)} %get-tuple-element.554.h_in, ...), custom_call_target="tpu_custom_call", output_to_operand_aliasing={{1}: (4, {}), {2}: (5, {})} | custom-call | tf_op jit(solution)/shard_map/cond/branch_1_fun/pallas_call | solution.py:142
  97.2 5.9 %collective-permute-start.3 = (bf16[32,8192]{1,0:T(8,128)(2,1)}, bf16[32,8192]{1,0:T(8,128)(2,1)}, u32[]{:S(2)}, u32[]{:S(2)}) collective-permute-start(bf16[32,8192]{1,0:T(8,128)(2,1)} %get-tuple-element.790), channel_id=1, source_target_pairs={{0,8},{8,16},{16,24},{1,9},{9,17},{17,25},{2,10},{10,18},{18,26},{... | collective-permute-start | bytes 1572872 | tf_op jit(solution)/shard_map/ppermute | solution.py:27
  104.4 7.6 %collective-permute-done.3 = bf16[32,8192]{1,0:T(8,128)(2,1)} collective-permute-done((bf16[32,8192]{1,0:T(8,128)(2,1)}, bf16[32,8192]{1,0:T(8,128)(2,1)}, u32[]{:S(2)}, u32[]{:S(2)}) %collective-permute-start.3) | collective-permute-done | bytes 524320 | tf_op jit(solution)/shard_map/ppermute | solution.py:27
  112.1 18.6 %collective-permute-start.4 = (bf16[32,8192]{1,0:T(8,128)(2,1)}, bf16[32,8192]{1,0:T(8,128)(2,1)}, u32[]{:S(2)}, u32[]{:S(2)}) collective-permute-start(bf16[32,8192]{1,0:T(8,128)(2,1)} %get-tuple-element.793), channel_id=1, source_target_pairs={{0,8},{8,16},{16,24},{1,9},{9,17},{17,25},{2,10},{10,18},{18,26},{... | collective-permute-start | bytes 1572872 | tf_op jit(solution)/shard_map/ppermute | solution.py:27
  132.0 6.8 %collective-permute-done.4 = bf16[32,8192]{1,0:T(8,128)(2,1)} collective-permute-done((bf16[32,8192]{1,0:T(8,128)(2,1)}, bf16[32,8192]{1,0:T(8,128)(2,1)}, u32[]{:S(2)}, u32[]{:S(2)}) %collective-permute-start.4) | collective-permute-done | bytes 524320 | tf_op jit(solution)/shard_map/ppermute | solution.py:27
  138.8 5.9 %collective-permute-start.5 = (bf16[32,8192]{1,0:T(8,128)(2,1)}, bf16[32,8192]{1,0:T(8,128)(2,1)}, u32[]{:S(2)}, u32[]{:S(2)}) collective-permute-start(bf16[32,8192]{1,0:T(8,128)(2,1)} %get-tuple-element.796), channel_id=1, source_target_pairs={{0,8},{8,16},{16,24},{1,9},{9,17},{17,25},{2,10},{10,18},{18,26},{... | collective-permute-start | bytes 1572872 | tf_op jit(solution)/shard_map/ppermute | solution.py:27
  146.0 6.1 %collective-permute-done.5 = bf16[32,8192]{1,0:T(8,128)(2,1)} collective-permute-done((bf16[32,8192]{1,0:T(8,128)(2,1)}, bf16[32,8192]{1,0:T(8,128)(2,1)}, u32[]{:S(2)}, u32[]{:S(2)}) %collective-permute-start.5) | collective-permute-done | bytes 524320 | tf_op jit(solution)/shard_map/ppermute | solution.py:27
  152.1 36.5 %collective-permute-start.6 = (bf16[32,8192]{1,0:T(8,128)(2,1)}, bf16[32,8192]{1,0:T(8,128)(2,1)}, u32[]{:S(2)}, u32[]{:S(2)}) collective-permute-start(bf16[32,8192]{1,0:T(8,128)(2,1)} %get-tuple-element.799), channel_id=1, source_target_pairs={{0,8},{8,16},{16,24},{1,9},{9,17},{17,25},{2,10},{10,18},{18,26},{... | collective-permute-start | bytes 1572872 | tf_op jit(solution)/shard_map/ppermute | solution.py:27
  188.7 7.4 %collective-permute-done.14 = bf16[32,8192]{1,0:T(8,128)(2,1)S(1)} collective-permute-done((bf16[32,8192]{1,0:T(8,128)(2,1)S(1)}, bf16[32,8192]{1,0:T(8,128)(2,1)S(1)}, u32[]{:S(2)}, u32[]{:S(2)}) %collective-permute-start.14) | collective-permute-done | bytes 524320 | tf_op jit(solution)/shard_map/ppermute | solution.py:27
  196.9 14.5 %conditional.36 = ((bf16[32,8192]{1,0:T(8,128)(2,1)}, bf16[2,4,32,8192]{3,2,1,0:T(8,128)(2,1)})) conditional(s32[]{:T(128)} %convert_element_type.121, (bf16[32,8192]{1,0:T(8,128)(2,1)}, bf16[2,4,32,8192]{3,2,1,0:T(8,128)(2,1)}) %tuple.299, (s32[]{:T(128)}, s32[256,3]{0,1:T(4,128)}, bf16[32,8192]{1,0:T(8,128)(2,1)}, f32[2,4,32,8192]{3,2,1,0:T(8,128)}, ...), branch_computations={%region_32.33_spmd, %region_33.34_spmd} | conditional | flops 6 | bytes 12350 | solution.py:401
  199.2 6.1 %branch_1_fun.74 = (bf16[32,8192]{1,0:T(8,128)(2,1)}, bf16[2,4,32,8192]{3,2,1,0:T(8,128)(2,1)}) custom-call(s32[2]{0:T(128)} %pad_add_fusion.16.at_ref, s32[768]{0:T(1024)} %reshape.163.idx_ref, bf16[32,8192]{1,0:T(8,128)(2,1)} %get-tuple-element.686.g_in, f32[2,4,32,8192]{3,2,1,0:T(8,128)} %get-tuple-element.687.sy_hbm, ...), custom_call_target="tpu_custom_call", output_to_operand_aliasing={{1}: (5, {})} | custom-call | tf_op jit(solution)/shard_map/cond/branch_1_fun/pallas_call | solution.py:223
  205.3 6.1 %branch_1_fun.75 = (bf16[32,8192]{1,0:T(8,128)(2,1)}, bf16[2,4,32,8192]{3,2,1,0:T(8,128)(2,1)}) custom-call(s32[1]{0:T(128)} %bitcast.32.at_ref, s32[768]{0:T(1024)} %reshape.163.idx_ref, bf16[32,8192]{1,0:T(8,128)(2,1)} %get-tuple-element.691.g_in, f32[2,4,32,8192]{3,2,1,0:T(8,128)} %get-tuple-element.687.sy_hbm, ...), custom_call_target="tpu_custom_call", output_to_operand_aliasing={{1}: (5, {})} | custom-call | tf_op jit(solution)/shard_map/cond/branch_1_fun/pallas_call | solution.py:223
  212.8 6.3 %collective-permute-start.7 = (bf16[32,8192]{1,0:T(8,128)(2,1)}, bf16[32,8192]{1,0:T(8,128)(2,1)S(1)}, u32[]{:S(2)}, u32[]{:S(2)}) collective-permute-start(bf16[32,8192]{1,0:T(8,128)(2,1)} %get-tuple-element.802), channel_id=1, source_target_pairs={{0,8},{8,16},{16,24},{1,9},{9,17},{17,25},{2,10},{10,18},{18,26},{... | collective-permute-start | bytes 1572872 | tf_op jit(solution)/shard_map/ppermute | solution.py:27
  219.1 7.6 %collective-permute-done.15 = bf16[32,8192]{1,0:T(8,128)(2,1)S(1)} collective-permute-done((bf16[32,8192]{1,0:T(8,128)(2,1)}, bf16[32,8192]{1,0:T(8,128)(2,1)S(1)}, u32[]{:S(2)}, u32[]{:S(2)}) %collective-permute-start.15) | collective-permute-done | bytes 524320 | tf_op jit(solution)/shard_map/ppermute | solution.py:27
  226.8 13.4 %conditional.37 = ((bf16[32,8192]{1,0:T(8,128)(2,1)S(1)}, bf16[2,4,32,8192]{3,2,1,0:T(8,128)(2,1)})) conditional(s32[]{:T(128)} %convert_element_type.120, (bf16[32,8192]{1,0:T(8,128)(2,1)S(1)}, bf16[2,4,32,8192]{3,2,1,0:T(8,128)(2,1)}) %tuple.168, (s32[]{:T(128)}, s32[256,3]{0,1:T(4,128)}, s32[]{:T(128)}, bf16[32,8192]{1,0:T(8,128)(2,1)S(1)}, ...), branch_computations={%region_34.35_spmd, %region_35.36_spmd} | conditional | flops 6 | bytes 12350 | solution.py:401
  229.0 5.8 %branch_1_fun.76 = (bf16[32,8192]{1,0:T(8,128)(2,1)}, bf16[2,4,32,8192]{3,2,1,0:T(8,128)(2,1)}) custom-call(s32[2]{0:T(128)} %pad_add_fusion.17.at_ref, s32[768]{0:T(1024)} %reshape.165.idx_ref, bf16[32,8192]{1,0:T(8,128)(2,1)S(1)} %get-tuple-element.696.g_in, f32[2,4,32,8192]{3,2,1,0:T(8,128)} %get-tuple-element.697.sy_hbm, ...), custom_call_target="tpu_custom_call", output_to_operand_aliasing={{1}: (5, {})} | custom-call | tf_op jit(solution)/shard_map/cond/branch_1_fun/pallas_call | solution.py:223
  234.9 5.3 %branch_1_fun.77 = (bf16[32,8192]{1,0:T(8,128)(2,1)S(1)}, bf16[2,4,32,8192]{3,2,1,0:T(8,128)(2,1)}) custom-call(s32[1]{0:T(128)} %bitcast.34.at_ref, s32[768]{0:T(1024)} %reshape.165.idx_ref, bf16[32,8192]{1,0:T(8,128)(2,1)} %get-tuple-element.701.g_in, f32[2,4,32,8192]{3,2,1,0:T(8,128)} %get-tuple-element.697.sy_hbm, ...), custom_call_target="tpu_custom_call", output_to_operand_aliasing={{1}: (5, {})} | custom-call | tf_op jit(solution)/shard_map/cond/branch_1_fun/pallas_call | solution.py:223
  242.3 12.8 %collective-permute-start.8 = (bf16[32,8192]{1,0:T(8,128)(2,1)}, bf16[32,8192]{1,0:T(8,128)(2,1)S(1)}, u32[]{:S(2)}, u32[]{:S(2)}) collective-permute-start(bf16[32,8192]{1,0:T(8,128)(2,1)} %get-tuple-element.807), channel_id=1, source_target_pairs={{0,8},{8,16},{16,24},{1,9},{9,17},{17,25},{2,10},{10,18},{18,26},{... | collective-permute-start | bytes 1572872 | tf_op jit(solution)/shard_map/ppermute | solution.py:27
  255.1 6.1 %collective-permute-done.16 = bf16[32,8192]{1,0:T(8,128)(2,1)} collective-permute-done((bf16[32,8192]{1,0:T(8,128)(2,1)S(1)}, bf16[32,8192]{1,0:T(8,128)(2,1)}, u32[]{:S(2)}, u32[]{:S(2)}) %collective-permute-start.16) | collective-permute-done | bytes 524320 | tf_op jit(solution)/shard_map/ppermute | solution.py:27
  261.2 14.6 %conditional.38 = ((bf16[32,8192]{1,0:T(8,128)(2,1)}, bf16[2,4,32,8192]{3,2,1,0:T(8,128)(2,1)})) conditional(s32[]{:T(128)} %convert_element_type.119, (bf16[32,8192]{1,0:T(8,128)(2,1)}, bf16[2,4,32,8192]{3,2,1,0:T(8,128)(2,1)}) %tuple.170, (s32[]{:T(128)}, s32[256,3]{0,1:T(4,128)}, s32[]{:T(128)}, bf16[32,8192]{1,0:T(8,128)(2,1)}, ...), branch_computations={%region_36.37_spmd.clone, %region_37.38_spmd.clone} | conditional | flops 6 | bytes 12350 | solution.py:401
  263.5 6.2 %branch_1_fun.80 = (bf16[32,8192]{1,0:T(8,128)(2,1)}, bf16[2,4,32,8192]{3,2,1,0:T(8,128)(2,1)}) custom-call(s32[2]{0:T(128)} %pad_add_fusion.19.at_ref, s32[768]{0:T(1024)} %reshape.185.idx_ref, bf16[32,8192]{1,0:T(8,128)(2,1)} %get-tuple-element.837.g_in, f32[2,4,32,8192]{3,2,1,0:T(8,128)} %get-tuple-element.838.sy_hbm, ...), custom_call_target="tpu_custom_call", output_to_operand_aliasing={{1}: (5, {})} | custom-call | tf_op jit(solution)/shard_map/cond/branch_1_fun/pallas_call | solution.py:223
  269.7 6.1 %branch_1_fun.81 = (bf16[32,8192]{1,0:T(8,128)(2,1)}, bf16[2,4,32,8192]{3,2,1,0:T(8,128)(2,1)}) custom-call(s32[1]{0:T(128)} %bitcast.49.at_ref, s32[768]{0:T(1024)} %reshape.185.idx_ref, bf16[32,8192]{1,0:T(8,128)(2,1)} %get-tuple-element.842.g_in, f32[2,4,32,8192]{3,2,1,0:T(8,128)} %get-tuple-element.838.sy_hbm, ...), custom_call_target="tpu_custom_call", output_to_operand_aliasing={{1}: (5, {})} | custom-call | tf_op jit(solution)/shard_map/cond/branch_1_fun/pallas_call | solution.py:223
  278.7 11.1 %collective-permute-done.17 = bf16[32,8192]{1,0:T(8,128)(2,1)S(1)} collective-permute-done((bf16[32,8192]{1,0:T(8,128)(2,1)}, bf16[32,8192]{1,0:T(8,128)(2,1)S(1)}, u32[]{:S(2)}, u32[]{:S(2)}) %collective-permute-start.17) | collective-permute-done | bytes 524320 | tf_op jit(solution)/shard_map/ppermute | solution.py:27
  289.8 13.4 %conditional.39 = (bf16[2,4,32,8192]{3,2,1,0:T(8,128)(2,1)}) conditional(s32[]{:T(128)} %convert_element_type.118, bf16[2,4,32,8192]{3,2,1,0:T(8,128)(2,1)} %get-tuple-element.826, (s32[]{:T(128)}, s32[256,3]{0,1:T(4,128)S(1)}, s32[]{:T(128)}, bf16[32,8192]{1,0:T(8,128)(2,1)S(1)}, f32[2,4,32,8192]{3,2,1,0:T(8,128)}, ...), branch_computations={%region_38.39_spmd, %region_39.40_spmd} | conditional | flops 6 | bytes 12350 | solution.py:401
  291.3 5.8 %branch_1_fun.78 = (bf16[32,8192]{1,0:T(8,128)(2,1)}, bf16[2,4,32,8192]{3,2,1,0:T(8,128)(2,1)}) custom-call(s32[2]{0:T(128)} %pad_add_fusion.18.at_ref, s32[768]{0:T(1024)} %reshape.169.idx_ref, bf16[32,8192]{1,0:T(8,128)(2,1)S(1)} %get-tuple-element.720.g_in, f32[2,4,32,8192]{3,2,1,0:T(8,128)} %get-tuple-element.721.sy_hbm, ...), custom_call_target="tpu_custom_call", output_to_operand_aliasing={{1}: (5, {})} | custom-call | tf_op jit(solution)/shard_map/cond/branch_1_fun/pallas_call | solution.py:223
  297.2 6.1 %branch_1_fun.79 = (bf16[32,8192]{1,0:T(8,128)(2,1)}, bf16[2,4,32,8192]{3,2,1,0:T(8,128)(2,1)}) custom-call(s32[1]{0:T(128)} %bitcast.36.at_ref, s32[768]{0:T(1024)} %reshape.169.idx_ref, bf16[32,8192]{1,0:T(8,128)(2,1)} %get-tuple-element.725.g_in, f32[2,4,32,8192]{3,2,1,0:T(8,128)} %get-tuple-element.721.sy_hbm, ...), custom_call_target="tpu_custom_call", output_to_operand_aliasing={{1}: (5, {})} | custom-call | tf_op jit(solution)/shard_map/cond/branch_1_fun/pallas_call | solution.py:223
  303.3 7.6 %shard_map.48 = bf16[4,32,128,128]{3,2,1,0:T(8,128)(2,1)} custom-call(s32[1]{0:T(128)} %bitcast.42.sel_ref, s32[768]{0:T(1024)} %reshape.178.idx_ref, bf16[2,4,32,8192]{3,2,1,0:T(8,128)(2,1)} %get-tuple-element.808.h_ref, bf16[2,4,32,8192]{3,2,1,0:T(8,128)(2,1)} %get-tuple-element.1118.s_ref), custom_call_target="tpu_custom_call" | custom-call | tf_op jit(solution)/shard_map/pallas_call | solution.py:309
  310.8 8.7 %shard_map.47 = f32[4,32,128,128]{3,2,1,0:T(8,128)} custom-call(s32[1]{0:T(128)} %bitcast.38.sel_ref, s32[768]{0:T(1024)} %reshape.178.idx_ref, bf16[2,4,32,8192]{3,2,1,0:T(8,128)(2,1)} %get-tuple-element.808.h_ref, bf16[2,4,32,8192]{3,2,1,0:T(8,128)(2,1)} %get-tuple-element.1118.s_ref), custom_call_target="tpu_custom_call" | custom-call | tf_op jit(solution)/shard_map/pallas_call | solution.py:309
  319.5 5.0 %fusion = bf16[2,32,128,128]{3,2,1,0:T(8,128)(2,1)} fusion(f32[2,2,32,128,128]{4,3,2,1,0:T(8,128)} %bitcast.80, s32[]{:T(128)S(6)} %select_n.64, bf16[2,2,32,128,128]{4,3,2,1,0:T(8,128)(2,1)} %bitcast.43), kind=kLoop, calls=%fused_computation.21 | loop fusion | flops 3145728 | bytes 8388612 | tf_op jit(solution)/shard_map/convert_element_type | solution.py:319
  324.5 26.2 %collective-permute-done.19 = bf16[2,32,128,128]{3,2,1,0:T(8,128)(2,1)S(1)} collective-permute-done((bf16[2,32,128,128]{3,2,1,0:T(8,128)(2,1)}, bf16[2,32,128,128]{3,2,1,0:T(8,128)(2,1)S(1)}, u32[]{:S(2)}, u32[]{:S(2)}) %collective-permute-start.19) | collective-permute-done | bytes 2097184 | tf_op jit(solution)/shard_map/ppermute | solution.py:319
  355.8 14.8 %collective-permute-done.20 = bf16[32,128,128]{2,1,0:T(8,128)(2,1)S(1)} collective-permute-done((bf16[32,128,128]{2,1,0:T(8,128)(2,1)S(1)}, bf16[32,128,128]{2,1,0:T(8,128)(2,1)S(1)}, u32[]{:S(2)}, u32[]{:S(2)}) %collective-permute-start.20) | collective-permute-done | bytes 1048608 | tf_op jit(solution)/shard_map/ppermute | solution.py:319
  370.6 4.5 %fusion.2 = f32[32,128,128]{2,1,0:T(8,128)} fusion(bf16[32,128,128]{2,1,0:T(8,128)(2,1)S(1)} %collective-permute-done.20, f32[2,32,128,128]{3,2,1,0:T(8,128)} %copy-done.1, s32[]{:T(128)S(6)} %select_n.59, f32[2,2,32,128,128]{4,3,2,1,0:T(8,128)} %bitcast.82, s32[]{:T(128)S(6)} %select_n.60, s32[]{:T(128)S(6)} %select_n.63, ...), kind=kLoop, calls=%fused_computation.25 | loop fusion | flops 2621440 | bytes 8388620 | tf_op jit(solution)/shard_map/add | solution.py:350
  (75 shorter events, 40.8 us)
Async XLA Ops:
  14.4 13.7 %collective-permute-start = (bf16[32,8192]{1,0:T(8,128)(2,1)}, bf16[32,8192]{1,0:T(8,128)(2,1)S(1)}, u32[]{:S(2)}, u32[]{:S(2)}) collective-permute-start(bf16[32,8192]{1,0:T(8,128)(2,1)} %get-tuple-element.781), channel_id=1, source_target_pairs={{0,8},{8,16},{16,24},{1,9},{9,17},{17,25},{2,10},{10,18},{18,26},{... | collective-permute-start | bytes 1572872 | tf_op jit(solution)/shard_map/ppermute | solution.py:27
  15.7 12.3 %copy-start = (bf16[2,64,8192]{2,1,0:T(8,128)(2,1)S(1)}, bf16[2,64,8192]{2,1,0:T(8,128)(2,1)}, u32[]{:S(2)}) copy-start(bf16[2,64,8192]{2,1,0:T(8,128)(2,1)} %param.44) | copy-start | bytes 6291460
  16.6 28.9 %collective-permute-start.9 = (bf16[32,8192]{1,0:T(8,128)(2,1)}, bf16[32,8192]{1,0:T(8,128)(2,1)S(1)}, u32[]{:S(2)}, u32[]{:S(2)}) collective-permute-start(bf16[32,8192]{1,0:T(8,128)(2,1)} %get-tuple-element.810), channel_id=1, source_target_pairs={{8,0},{16,8},{24,16},{9,1},{17,9},{25,17},{10,2},{18,10},{26,18},{... | collective-permute-start | bytes 1572872 | tf_op jit(solution)/shard_map/ppermute | solution.py:27
  39.7 16.2 %collective-permute-start.1 = (bf16[32,8192]{1,0:T(8,128)(2,1)S(1)}, bf16[32,8192]{1,0:T(8,128)(2,1)}, u32[]{:S(2)}, u32[]{:S(2)}) collective-permute-start(bf16[32,8192]{1,0:T(8,128)(2,1)S(1)} %get-tuple-element.784), channel_id=1, source_target_pairs={{0,8},{8,16},{16,24},{1,9},{9,17},{17,25},{2,10},{10,18},{18,26},{... | collective-permute-start | bytes 1572872 | tf_op jit(solution)/shard_map/ppermute | solution.py:27
  45.5 29.1 %collective-permute-start.10 = (bf16[32,8192]{1,0:T(8,128)(2,1)S(1)}, bf16[32,8192]{1,0:T(8,128)(2,1)}, u32[]{:S(2)}, u32[]{:S(2)}) collective-permute-start(bf16[32,8192]{1,0:T(8,128)(2,1)S(1)} %get-tuple-element.812), channel_id=1, source_target_pairs={{8,0},{16,8},{24,16},{9,1},{17,9},{25,17},{10,2},{18,10},{26,18},{... | collective-permute-start | bytes 1572872 | tf_op jit(solution)/shard_map/ppermute | solution.py:27
  68.7 15.8 %collective-permute-start.2 = (bf16[32,8192]{1,0:T(8,128)(2,1)}, bf16[32,8192]{1,0:T(8,128)(2,1)}, u32[]{:S(2)}, u32[]{:S(2)}) collective-permute-start(bf16[32,8192]{1,0:T(8,128)(2,1)} %get-tuple-element.787), channel_id=1, source_target_pairs={{0,8},{8,16},{16,24},{1,9},{9,17},{17,25},{2,10},{10,18},{18,26},{... | collective-permute-start | bytes 1572872 | tf_op jit(solution)/shard_map/ppermute | solution.py:27
  74.6 28.5 %collective-permute-start.11 = (bf16[32,8192]{1,0:T(8,128)(2,1)}, bf16[32,8192]{1,0:T(8,128)(2,1)S(1)}, u32[]{:S(2)}, u32[]{:S(2)}) collective-permute-start(bf16[32,8192]{1,0:T(8,128)(2,1)} %get-tuple-element.814), channel_id=1, source_target_pairs={{8,0},{16,8},{24,16},{9,1},{17,9},{25,17},{10,2},{18,10},{26,18},{... | collective-permute-start | bytes 1572872 | tf_op jit(solution)/shard_map/ppermute | solution.py:27
  97.2 14.9 %collective-permute-start.3 = (bf16[32,8192]{1,0:T(8,128)(2,1)}, bf16[32,8192]{1,0:T(8,128)(2,1)}, u32[]{:S(2)}, u32[]{:S(2)}) collective-permute-start(bf16[32,8192]{1,0:T(8,128)(2,1)} %get-tuple-element.790), channel_id=1, source_target_pairs={{0,8},{8,16},{16,24},{1,9},{9,17},{17,25},{2,10},{10,18},{18,26},{... | collective-permute-start | bytes 1572872 | tf_op jit(solution)/shard_map/ppermute | solution.py:27
  103.1 27.6 %collective-permute-start.12 = (bf16[32,8192]{1,0:T(8,128)(2,1)S(1)}, bf16[32,8192]{1,0:T(8,128)(2,1)S(1)}, u32[]{:S(2)}, u32[]{:S(2)}) collective-permute-start(bf16[32,8192]{1,0:T(8,128)(2,1)S(1)} %get-tuple-element.816), channel_id=1, source_target_pairs={{8,0},{16,8},{24,16},{9,1},{17,9},{25,17},{10,2},{18,10},{26,18},{... | collective-permute-start | bytes 1572872 | tf_op jit(solution)/shard_map/ppermute | solution.py:27
  112.1 26.7 %collective-permute-start.4 = (bf16[32,8192]{1,0:T(8,128)(2,1)}, bf16[32,8192]{1,0:T(8,128)(2,1)}, u32[]{:S(2)}, u32[]{:S(2)}) collective-permute-start(bf16[32,8192]{1,0:T(8,128)(2,1)} %get-tuple-element.793), channel_id=1, source_target_pairs={{0,8},{8,16},{16,24},{1,9},{9,17},{17,25},{2,10},{10,18},{18,26},{... | collective-permute-start | bytes 1572872 | tf_op jit(solution)/shard_map/ppermute | solution.py:27
  130.7 14.0 %collective-permute-start.13 = (bf16[32,8192]{1,0:T(8,128)(2,1)S(1)}, bf16[32,8192]{1,0:T(8,128)(2,1)S(1)}, u32[]{:S(2)}, u32[]{:S(2)}) collective-permute-start(bf16[32,8192]{1,0:T(8,128)(2,1)S(1)} %get-tuple-element.818), channel_id=1, source_target_pairs={{8,0},{16,8},{24,16},{9,1},{17,9},{25,17},{10,2},{18,10},{26,18},{... | collective-permute-start | bytes 1572872 | tf_op jit(solution)/shard_map/ppermute | solution.py:27
  138.8 13.3 %collective-permute-start.5 = (bf16[32,8192]{1,0:T(8,128)(2,1)}, bf16[32,8192]{1,0:T(8,128)(2,1)}, u32[]{:S(2)}, u32[]{:S(2)}) collective-permute-start(bf16[32,8192]{1,0:T(8,128)(2,1)} %get-tuple-element.796), channel_id=1, source_target_pairs={{0,8},{8,16},{16,24},{1,9},{9,17},{17,25},{2,10},{10,18},{18,26},{... | collective-permute-start | bytes 1572872 | tf_op jit(solution)/shard_map/ppermute | solution.py:27
  144.7 51.4 %collective-permute-start.14 = (bf16[32,8192]{1,0:T(8,128)(2,1)S(1)}, bf16[32,8192]{1,0:T(8,128)(2,1)S(1)}, u32[]{:S(2)}, u32[]{:S(2)}) collective-permute-start(bf16[32,8192]{1,0:T(8,128)(2,1)S(1)} %get-tuple-element.820), channel_id=1, source_target_pairs={{8,0},{16,8},{24,16},{9,1},{17,9},{25,17},{10,2},{18,10},{26,18},{... | collective-permute-start | bytes 1572872 | tf_op jit(solution)/shard_map/ppermute | solution.py:27
  152.1 60.6 %collective-permute-start.6 = (bf16[32,8192]{1,0:T(8,128)(2,1)}, bf16[32,8192]{1,0:T(8,128)(2,1)}, u32[]{:S(2)}, u32[]{:S(2)}) collective-permute-start(bf16[32,8192]{1,0:T(8,128)(2,1)} %get-tuple-element.799), channel_id=1, source_target_pairs={{0,8},{8,16},{16,24},{1,9},{9,17},{17,25},{2,10},{10,18},{18,26},{... | collective-permute-start | bytes 1572872 | tf_op jit(solution)/shard_map/ppermute | solution.py:27
  196.1 0.8 copy-start.4
  211.5 15.3 %collective-permute-start.15 = (bf16[32,8192]{1,0:T(8,128)(2,1)}, bf16[32,8192]{1,0:T(8,128)(2,1)S(1)}, u32[]{:S(2)}, u32[]{:S(2)}) collective-permute-start(bf16[32,8192]{1,0:T(8,128)(2,1)} %get-tuple-element.822), channel_id=1, source_target_pairs={{8,0},{16,8},{24,16},{9,1},{17,9},{25,17},{10,2},{18,10},{26,18},{... | collective-permute-start | bytes 1572872 | tf_op jit(solution)/shard_map/ppermute | solution.py:27
  212.8 28.7 %collective-permute-start.7 = (bf16[32,8192]{1,0:T(8,128)(2,1)}, bf16[32,8192]{1,0:T(8,128)(2,1)S(1)}, u32[]{:S(2)}, u32[]{:S(2)}) collective-permute-start(bf16[32,8192]{1,0:T(8,128)(2,1)} %get-tuple-element.802), channel_id=1, source_target_pairs={{0,8},{8,16},{16,24},{1,9},{9,17},{17,25},{2,10},{10,18},{18,26},{... | collective-permute-start | bytes 1572872 | tf_op jit(solution)/shard_map/ppermute | solution.py:27
  240.2 21.0 %collective-permute-start.16 = (bf16[32,8192]{1,0:T(8,128)(2,1)S(1)}, bf16[32,8192]{1,0:T(8,128)(2,1)}, u32[]{:S(2)}, u32[]{:S(2)}) collective-permute-start(bf16[32,8192]{1,0:T(8,128)(2,1)S(1)} %get-tuple-element.824), channel_id=1, source_target_pairs={{8,0},{16,8},{24,16},{9,1},{17,9},{25,17},{10,2},{18,10},{26,18},{... | collective-permute-start | bytes 1572872 | tf_op jit(solution)/shard_map/ppermute | solution.py:27
  241.5 0.8 copy-start.3
  242.3 36.4 %collective-permute-start.8 = (bf16[32,8192]{1,0:T(8,128)(2,1)}, bf16[32,8192]{1,0:T(8,128)(2,1)S(1)}, u32[]{:S(2)}, u32[]{:S(2)}) collective-permute-start(bf16[32,8192]{1,0:T(8,128)(2,1)} %get-tuple-element.807), channel_id=1, source_target_pairs={{0,8},{8,16},{16,24},{1,9},{9,17},{17,25},{2,10},{10,18},{18,26},{... | collective-permute-start | bytes 1572872 | tf_op jit(solution)/shard_map/ppermute | solution.py:27
  261.2 17.6 %copy-start.2 = (s32[256,3]{0,1:T(4,128)S(1)}, s32[256,3]{0,1:T(4,128)}, u32[]{:S(2)}) copy-start(s32[256,3]{0,1:T(4,128)} %param.47) | copy-start | bytes 9220
  275.8 14.0 %collective-permute-start.17 = (bf16[32,8192]{1,0:T(8,128)(2,1)}, bf16[32,8192]{1,0:T(8,128)(2,1)S(1)}, u32[]{:S(2)}, u32[]{:S(2)}) collective-permute-start(bf16[32,8192]{1,0:T(8,128)(2,1)} %get-tuple-element.827), channel_id=1, source_target_pairs={{8,0},{16,8},{24,16},{9,1},{17,9},{25,17},{10,2},{18,10},{26,18},{... | collective-permute-start | bytes 1572872 | tf_op jit(solution)/shard_map/ppermute | solution.py:27
  310.8 8.7 %collective-permute-start.18 = (bf16[4,32,128,128]{3,2,1,0:T(8,128)(2,1)}, bf16[4,32,128,128]{3,2,1,0:T(8,128)(2,1)}, u32[]{:S(2)}, u32[]{:S(2)}) collective-permute-start(bf16[4,32,128,128]{3,2,1,0:T(8,128)(2,1)} %shard_map.48), channel_id=1, source_target_pairs={{0,1},{1,0},{2,3},{3,2},{4,5},{5,4},{6,7},{7,6},{8,9},{9,8},{10,11... | collective-permute-start | bytes 12582920 | tf_op jit(solution)/shard_map/ppermute | solution.py:333
  324.5 26.2 %collective-permute-start.19 = (bf16[2,32,128,128]{3,2,1,0:T(8,128)(2,1)}, bf16[2,32,128,128]{3,2,1,0:T(8,128)(2,1)S(1)}, u32[]{:S(2)}, u32[]{:S(2)}) collective-permute-start(bf16[2,32,128,128]{3,2,1,0:T(8,128)(2,1)} %fusion), channel_id=1, source_target_pairs={{0,2},{1,5},{2,0},{3,7},{4,6},{5,1},{6,4},{7,3},{8,10},{9,13},{10,... | collective-permute-start | bytes 6291464 | tf_op jit(solution)/shard_map/ppermute | solution.py:319
  351.3 2.1 copy-start.1
  355.7 14.9 %collective-permute-start.20 = (bf16[32,128,128]{2,1,0:T(8,128)(2,1)S(1)}, bf16[32,128,128]{2,1,0:T(8,128)(2,1)S(1)}, u32[]{:S(2)}, u32[]{:S(2)}) collective-permute-start(bf16[32,128,128]{2,1,0:T(8,128)(2,1)S(1)} %fusion.1), channel_id=1, source_target_pairs={{0,4},{1,3},{2,6},{3,1},{4,0},{5,7},{6,2},{7,5},{8,12},{9,11},{10,... | collective-permute-start | bytes 3145736 | tf_op jit(solution)/shard_map/ppermute | solution.py:319

commit v8 on v6

--- a/solution.py
+++ b/solution.py
@@ -10,7 +10,7 @@
 BLK = 128
 LSLOT = 2
 KMAX = 128
-CH = 1024
+CH = 2048
 NSUB = 32
 SPLIT = 2
 GROUP = 16

time: 369 us -> 372 us (level)
  starting transfers between devices: 96.2 us -> 102 us
    ppermute x18, starting transfers between devices: 96.1 us -> 102 us  [shifted(): lax.ppermute(value, axis, [(source, source + steps) for source in range(l...]
where the time goes in v8:
time: 372 us; the launch traced here: 373 us
  waiting for transfers between devices  120 us (32%)
  Pallas kernels  114 us (31%)
  starting transfers between devices  102 us (27%)
  local copies, waits for them, and re-layouts  19.2 us (5%)
  other arithmetic  17.2 us (5%)
    ppermute x18, starting transfers between devices, shifted(): lax.ppermute(value, axis, [(source, source + steps) for source in range(l...  102 us
    ppermute x18, waiting for transfers between devices, shifted(): lax.ppermute(value, axis, [(source, source + steps) for source in range(l...  78.5 us
    pallas_call x8, Pallas kernels, layer_backward(): pl.pallas_call(functools.partial(_bwd_kernel, layer * KMAX, layer, entry)...  52.3 us
    pallas_call x8, Pallas kernels, layer_forward(): pl.pallas_call(functools.partial(_fwd_kernel, layer * KMAX, layer), out_s...  44.7 us
    ppermute x2, waiting for transfers between devices, _exchange(): lax.ppermute(send.astype(jnp.bfloat16), 'dp', pairs).astype(jnp.float32)  41 us
    pallas_call x2, Pallas kernels, dw_half(): pl.pallas_call(_dw_half_kernel, out_shape=jax.ShapeDtypeStruct((4, per, B...  17.5 us
  transfers between devices with their start and end apart: 21, of which 12 were waited for; matrix products, arithmetic and copies ran while one was open for 4% of the time, Pallas kernels for 22%

profile of v8, /device:TPU:0, one launch (start us, length us, event | category | flops | bytes accessed | tf_op | source)
XLA Modules:
  0.0 372.7 jit_solution(13216592425715191632)
XLA Ops:
  0.0 15.2 %conditional.20 = ((bf16[32,8192]{1,0:T(8,128)(2,1)}, bf16[2,4,32,8192]{3,2,1,0:T(8,128)(2,1)}, f32[2,4,32,8192]{3,2,1,0:T(8,128)})) conditional(s32[]{:T(128)} %convert_element_type.117, (bf16[2,4,32,8192]{3,2,1,0:T(8,128)(2,1)}, f32[2,4,32,8192]{3,2,1,0:T(8,128)}) %tuple.135, (s32[]{:T(128)}, s32[256,3]{0,1:T(4,128)}, s32[]{:T(128)}, ...), branch_computations={%region_0.1_spmd, %region_1.2_spmd} | conditional | flops 6 | bytes 536640 | solution.py:386
  3.0 6.9 %branch_1_fun.42 = (bf16[32,8192]{1,0:T(8,128)(2,1)}, bf16[2,4,32,8192]{3,2,1,0:T(8,128)(2,1)}, f32[2,4,32,8192]{3,2,1,0:T(8,128)}) custom-call(s32[2]{0:T(128)} %pad_add_fusion.at_ref, s32[768]{0:T(1024)} %reshape.123.idx_ref, bf16[32,8192]{1,0:T(8,128)(2,1)} %broadcast_in_dim.9.h_in, ...), custom_call_target="tpu_custom_call", output_to_operand_aliasing={{1}: (4, {}), {2}: (5, {})} | custom-call | tf_op jit(solution)/shard_map/cond/branch_1_fun/pallas_call | solution.py:142
  9.9 5.3 %branch_1_fun.43 = (bf16[32,8192]{1,0:T(8,128)(2,1)}, bf16[2,4,32,8192]{3,2,1,0:T(8,128)(2,1)}, f32[2,4,32,8192]{3,2,1,0:T(8,128)}) custom-call(s32[1]{0:T(128)} %bitcast.at_ref, s32[768]{0:T(1024)} %reshape.123.idx_ref, bf16[32,8192]{1,0:T(8,128)(2,1)} %get-tuple-element.521.h_in, ...), custom_call_target="tpu_custom_call", output_to_operand_aliasing={{1}: (4, {}), {2}: (5, {})} | custom-call | tf_op jit(solution)/shard_map/cond/branch_1_fun/pallas_call | solution.py:142
  18.7 10.2 %collective-permute-done = bf16[32,8192]{1,0:T(8,128)(2,1)S(1)} collective-permute-done((bf16[32,8192]{1,0:T(8,128)(2,1)}, bf16[32,8192]{1,0:T(8,128)(2,1)S(1)}, u32[]{:S(2)}, u32[]{:S(2)}) %collective-permute-start) | collective-permute-done | bytes 524320 | tf_op jit(solution)/shard_map/ppermute | solution.py:27
  28.9 12.3 %conditional.21 = ((bf16[32,8192]{1,0:T(8,128)(2,1)S(1)}, bf16[2,4,32,8192]{3,2,1,0:T(8,128)(2,1)}, f32[2,4,32,8192]{3,2,1,0:T(8,128)})) conditional(s32[]{:T(128)} %convert_element_type.116, (bf16[32,8192]{1,0:T(8,128)(2,1)S(1)}, bf16[2,4,32,8192]{3,2,1,0:T(8,128)(2,1)}, f32[2,4,32,8192]{3,2,1,0:T(8,128)}) %tuple.137, (s32[]{:T(128)}, ...), branch_computations={%region_2.3_spmd, %region_3.4_spmd} | conditional | flops 6 | bytes 12350 | solution.py:386
  31.1 5.6 %branch_1_fun.44 = (bf16[32,8192]{1,0:T(8,128)(2,1)}, bf16[2,4,32,8192]{3,2,1,0:T(8,128)(2,1)}, f32[2,4,32,8192]{3,2,1,0:T(8,128)}) custom-call(s32[2]{0:T(128)} %pad_add_fusion.1.at_ref, s32[768]{0:T(1024)} %reshape.125.idx_ref, bf16[32,8192]{1,0:T(8,128)(2,1)S(1)} %get-tuple-element.527.h_in, ...), custom_call_target="tpu_custom_call", output_to_operand_aliasing={{1}: (4, {}), {2}: (5, {})} | custom-call | tf_op jit(solution)/shard_map/cond/branch_1_fun/pallas_call | solution.py:142
  36.7 4.5 %branch_1_fun.45 = (bf16[32,8192]{1,0:T(8,128)(2,1)S(1)}, bf16[2,4,32,8192]{3,2,1,0:T(8,128)(2,1)}, f32[2,4,32,8192]{3,2,1,0:T(8,128)}) custom-call(s32[1]{0:T(128)} %bitcast.2.at_ref, s32[768]{0:T(1024)} %reshape.125.idx_ref, bf16[32,8192]{1,0:T(8,128)(2,1)} %get-tuple-element.532.h_in, ...), custom_call_target="tpu_custom_call", output_to_operand_aliasing={{1}: (4, {}), {2}: (5, {})} | custom-call | tf_op jit(solution)/shard_map/cond/branch_1_fun/pallas_call | solution.py:142
  41.2 4.7 %collective-permute-start.1 = (bf16[32,8192]{1,0:T(8,128)(2,1)S(1)}, bf16[32,8192]{1,0:T(8,128)(2,1)}, u32[]{:S(2)}, u32[]{:S(2)}) collective-permute-start(bf16[32,8192]{1,0:T(8,128)(2,1)S(1)} %get-tuple-element.784), channel_id=1, source_target_pairs={{0,8},{8,16},{16,24},{1,9},{9,17},{17,25},{2,10},{10,18},{18,26},{... | collective-permute-start | bytes 1572872 | tf_op jit(solution)/shard_map/ppermute | solution.py:27
  47.2 9.1 %collective-permute-done.1 = bf16[32,8192]{1,0:T(8,128)(2,1)} collective-permute-done((bf16[32,8192]{1,0:T(8,128)(2,1)S(1)}, bf16[32,8192]{1,0:T(8,128)(2,1)}, u32[]{:S(2)}, u32[]{:S(2)}) %collective-permute-start.1) | collective-permute-done | bytes 524320 | tf_op jit(solution)/shard_map/ppermute | solution.py:27
  56.3 13.5 %conditional.22 = ((bf16[32,8192]{1,0:T(8,128)(2,1)}, bf16[2,4,32,8192]{3,2,1,0:T(8,128)(2,1)}, f32[2,4,32,8192]{3,2,1,0:T(8,128)})) conditional(s32[]{:T(128)} %convert_element_type.115, (bf16[32,8192]{1,0:T(8,128)(2,1)}, bf16[2,4,32,8192]{3,2,1,0:T(8,128)(2,1)}, f32[2,4,32,8192]{3,2,1,0:T(8,128)}) %tuple.139, (s32[]{:T(128)}, s32[256,3]{0,1:T(4,128)}, ...), branch_computations={%region_4.5_spmd, %region_5.6_spmd} | conditional | flops 6 | bytes 12350 | solution.py:386
  58.5 5.9 %branch_1_fun.46 = (bf16[32,8192]{1,0:T(8,128)(2,1)}, bf16[2,4,32,8192]{3,2,1,0:T(8,128)(2,1)}, f32[2,4,32,8192]{3,2,1,0:T(8,128)}) custom-call(s32[2]{0:T(128)} %pad_add_fusion.2.at_ref, s32[768]{0:T(1024)} %reshape.127.idx_ref, bf16[32,8192]{1,0:T(8,128)(2,1)} %get-tuple-element.538.h_in, ...), custom_call_target="tpu_custom_call", output_to_operand_aliasing={{1}: (4, {}), {2}: (5, {})} | custom-call | tf_op jit(solution)/shard_map/cond/branch_1_fun/pallas_call | solution.py:142
  64.4 5.3 %branch_1_fun.47 = (bf16[32,8192]{1,0:T(8,128)(2,1)}, bf16[2,4,32,8192]{3,2,1,0:T(8,128)(2,1)}, f32[2,4,32,8192]{3,2,1,0:T(8,128)}) custom-call(s32[1]{0:T(128)} %bitcast.4.at_ref, s32[768]{0:T(1024)} %reshape.127.idx_ref, bf16[32,8192]{1,0:T(8,128)(2,1)} %get-tuple-element.543.h_in, ...), custom_call_target="tpu_custom_call", output_to_operand_aliasing={{1}: (4, {}), {2}: (5, {})} | custom-call | tf_op jit(solution)/shard_map/cond/branch_1_fun/pallas_call | solution.py:142
  69.8 4.8 %collective-permute-start.2 = (bf16[32,8192]{1,0:T(8,128)(2,1)}, bf16[32,8192]{1,0:T(8,128)(2,1)}, u32[]{:S(2)}, u32[]{:S(2)}) collective-permute-start(bf16[32,8192]{1,0:T(8,128)(2,1)} %get-tuple-element.787), channel_id=1, source_target_pairs={{0,8},{8,16},{16,24},{1,9},{9,17},{17,25},{2,10},{10,18},{18,26},{... | collective-permute-start | bytes 1572872 | tf_op jit(solution)/shard_map/ppermute | solution.py:27
  75.9 8.5 %collective-permute-done.2 = bf16[32,8192]{1,0:T(8,128)(2,1)} collective-permute-done((bf16[32,8192]{1,0:T(8,128)(2,1)}, bf16[32,8192]{1,0:T(8,128)(2,1)}, u32[]{:S(2)}, u32[]{:S(2)}) %collective-permute-start.2) | collective-permute-done | bytes 524320 | tf_op jit(solution)/shard_map/ppermute | solution.py:27
  84.5 13.4 %conditional.23 = ((bf16[32,8192]{1,0:T(8,128)(2,1)}, bf16[2,4,32,8192]{3,2,1,0:T(8,128)(2,1)}, f32[2,4,32,8192]{3,2,1,0:T(8,128)})) conditional(s32[]{:T(128)} %convert_element_type.114, (bf16[32,8192]{1,0:T(8,128)(2,1)}, bf16[2,4,32,8192]{3,2,1,0:T(8,128)(2,1)}, f32[2,4,32,8192]{3,2,1,0:T(8,128)}) %tuple.141, (s32[]{:T(128)}, s32[256,3]{0,1:T(4,128)}, ...), branch_computations={%region_6.7_spmd, %region_7.8_spmd} | conditional | flops 6 | bytes 12350 | solution.py:386
  86.7 5.9 %branch_1_fun.48 = (bf16[32,8192]{1,0:T(8,128)(2,1)}, bf16[2,4,32,8192]{3,2,1,0:T(8,128)(2,1)}, f32[2,4,32,8192]{3,2,1,0:T(8,128)}) custom-call(s32[2]{0:T(128)} %pad_add_fusion.3.at_ref, s32[768]{0:T(1024)} %reshape.137.idx_ref, bf16[32,8192]{1,0:T(8,128)(2,1)} %get-tuple-element.549.h_in, ...), custom_call_target="tpu_custom_call", output_to_operand_aliasing={{1}: (4, {}), {2}: (5, {})} | custom-call | tf_op jit(solution)/shard_map/cond/branch_1_fun/pallas_call | solution.py:142
  92.6 5.3 %branch_1_fun.49 = (bf16[32,8192]{1,0:T(8,128)(2,1)}, bf16[2,4,32,8192]{3,2,1,0:T(8,128)(2,1)}, f32[2,4,32,8192]{3,2,1,0:T(8,128)}) custom-call(s32[1]{0:T(128)} %bitcast.6.at_ref, s32[768]{0:T(1024)} %reshape.137.idx_ref, bf16[32,8192]{1,0:T(8,128)(2,1)} %get-tuple-element.554.h_in, ...), custom_call_target="tpu_custom_call", output_to_operand_aliasing={{1}: (4, {}), {2}: (5, {})} | custom-call | tf_op jit(solution)/shard_map/cond/branch_1_fun/pallas_call | solution.py:142
  97.9 4.9 %collective-permute-start.3 = (bf16[32,8192]{1,0:T(8,128)(2,1)}, bf16[32,8192]{1,0:T(8,128)(2,1)}, u32[]{:S(2)}, u32[]{:S(2)}) collective-permute-start(bf16[32,8192]{1,0:T(8,128)(2,1)} %get-tuple-element.790), channel_id=1, source_target_pairs={{0,8},{8,16},{16,24},{1,9},{9,17},{17,25},{2,10},{10,18},{18,26},{... | collective-permute-start | bytes 1572872 | tf_op jit(solution)/shard_map/ppermute | solution.py:27
  104.1 7.6 %collective-permute-done.3 = bf16[32,8192]{1,0:T(8,128)(2,1)} collective-permute-done((bf16[32,8192]{1,0:T(8,128)(2,1)}, bf16[32,8192]{1,0:T(8,128)(2,1)}, u32[]{:S(2)}, u32[]{:S(2)}) %collective-permute-start.3) | collective-permute-done | bytes 524320 | tf_op jit(solution)/shard_map/ppermute | solution.py:27
  111.7 18.2 %collective-permute-start.4 = (bf16[32,8192]{1,0:T(8,128)(2,1)}, bf16[32,8192]{1,0:T(8,128)(2,1)}, u32[]{:S(2)}, u32[]{:S(2)}) collective-permute-start(bf16[32,8192]{1,0:T(8,128)(2,1)} %get-tuple-element.793), channel_id=1, source_target_pairs={{0,8},{8,16},{16,24},{1,9},{9,17},{17,25},{2,10},{10,18},{18,26},{... | collective-permute-start | bytes 1572872 | tf_op jit(solution)/shard_map/ppermute | solution.py:27
  131.2 6.8 %collective-permute-done.4 = bf16[32,8192]{1,0:T(8,128)(2,1)} collective-permute-done((bf16[32,8192]{1,0:T(8,128)(2,1)}, bf16[32,8192]{1,0:T(8,128)(2,1)}, u32[]{:S(2)}, u32[]{:S(2)}) %collective-permute-start.4) | collective-permute-done | bytes 524320 | tf_op jit(solution)/shard_map/ppermute | solution.py:27
  138.0 5.9 %collective-permute-start.5 = (bf16[32,8192]{1,0:T(8,128)(2,1)}, bf16[32,8192]{1,0:T(8,128)(2,1)}, u32[]{:S(2)}, u32[]{:S(2)}) collective-permute-start(bf16[32,8192]{1,0:T(8,128)(2,1)} %get-tuple-element.796), channel_id=1, source_target_pairs={{0,8},{8,16},{16,24},{1,9},{9,17},{17,25},{2,10},{10,18},{18,26},{... | collective-permute-start | bytes 1572872 | tf_op jit(solution)/shard_map/ppermute | solution.py:27
  145.3 6.1 %collective-permute-done.5 = bf16[32,8192]{1,0:T(8,128)(2,1)} collective-permute-done((bf16[32,8192]{1,0:T(8,128)(2,1)}, bf16[32,8192]{1,0:T(8,128)(2,1)}, u32[]{:S(2)}, u32[]{:S(2)}) %collective-permute-start.5) | collective-permute-done | bytes 524320 | tf_op jit(solution)/shard_map/ppermute | solution.py:27
  151.4 34.5 %collective-permute-start.6 = (bf16[32,8192]{1,0:T(8,128)(2,1)}, bf16[32,8192]{1,0:T(8,128)(2,1)}, u32[]{:S(2)}, u32[]{:S(2)}) collective-permute-start(bf16[32,8192]{1,0:T(8,128)(2,1)} %get-tuple-element.799), channel_id=1, source_target_pairs={{0,8},{8,16},{16,24},{1,9},{9,17},{17,25},{2,10},{10,18},{18,26},{... | collective-permute-start | bytes 1572872 | tf_op jit(solution)/shard_map/ppermute | solution.py:27
  185.9 7.4 %collective-permute-done.14 = bf16[32,8192]{1,0:T(8,128)(2,1)S(1)} collective-permute-done((bf16[32,8192]{1,0:T(8,128)(2,1)S(1)}, bf16[32,8192]{1,0:T(8,128)(2,1)S(1)}, u32[]{:S(2)}, u32[]{:S(2)}) %collective-permute-start.14) | collective-permute-done | bytes 524320 | tf_op jit(solution)/shard_map/ppermute | solution.py:27
  194.1 15.7 %conditional.36 = ((bf16[32,8192]{1,0:T(8,128)(2,1)}, bf16[2,4,32,8192]{3,2,1,0:T(8,128)(2,1)})) conditional(s32[]{:T(128)} %convert_element_type.121, (bf16[32,8192]{1,0:T(8,128)(2,1)}, bf16[2,4,32,8192]{3,2,1,0:T(8,128)(2,1)}) %tuple.299, (s32[]{:T(128)}, s32[256,3]{0,1:T(4,128)}, bf16[32,8192]{1,0:T(8,128)(2,1)}, f32[2,4,32,8192]{3,2,1,0:T(8,128)}, ...), branch_computations={%region_32.33_spmd, %region_33.34_spmd} | conditional | flops 6 | bytes 12350 | solution.py:401
  196.4 6.1 %branch_1_fun.74 = (bf16[32,8192]{1,0:T(8,128)(2,1)}, bf16[2,4,32,8192]{3,2,1,0:T(8,128)(2,1)}) custom-call(s32[2]{0:T(128)} %pad_add_fusion.16.at_ref, s32[768]{0:T(1024)} %reshape.163.idx_ref, bf16[32,8192]{1,0:T(8,128)(2,1)} %get-tuple-element.686.g_in, f32[2,4,32,8192]{3,2,1,0:T(8,128)} %get-tuple-element.687.sy_hbm, ...), custom_call_target="tpu_custom_call", output_to_operand_aliasing={{1}: (5, {})} | custom-call | tf_op jit(solution)/shard_map/cond/branch_1_fun/pallas_call | solution.py:223
  202.5 7.4 %branch_1_fun.75 = (bf16[32,8192]{1,0:T(8,128)(2,1)}, bf16[2,4,32,8192]{3,2,1,0:T(8,128)(2,1)}) custom-call(s32[1]{0:T(128)} %bitcast.32.at_ref, s32[768]{0:T(1024)} %reshape.163.idx_ref, bf16[32,8192]{1,0:T(8,128)(2,1)} %get-tuple-element.691.g_in, f32[2,4,32,8192]{3,2,1,0:T(8,128)} %get-tuple-element.687.sy_hbm, ...), custom_call_target="tpu_custom_call", output_to_operand_aliasing={{1}: (5, {})} | custom-call | tf_op jit(solution)/shard_map/cond/branch_1_fun/pallas_call | solution.py:223
  211.2 4.8 %collective-permute-start.7 = (bf16[32,8192]{1,0:T(8,128)(2,1)}, bf16[32,8192]{1,0:T(8,128)(2,1)S(1)}, u32[]{:S(2)}, u32[]{:S(2)}) collective-permute-start(bf16[32,8192]{1,0:T(8,128)(2,1)} %get-tuple-element.802), channel_id=1, source_target_pairs={{0,8},{8,16},{16,24},{1,9},{9,17},{17,25},{2,10},{10,18},{18,26},{... | collective-permute-start | bytes 1572872 | tf_op jit(solution)/shard_map/ppermute | solution.py:27
  216.0 7.6 %collective-permute-done.15 = bf16[32,8192]{1,0:T(8,128)(2,1)S(1)} collective-permute-done((bf16[32,8192]{1,0:T(8,128)(2,1)}, bf16[32,8192]{1,0:T(8,128)(2,1)S(1)}, u32[]{:S(2)}, u32[]{:S(2)}) %collective-permute-start.15) | collective-permute-done | bytes 524320 | tf_op jit(solution)/shard_map/ppermute | solution.py:27
  223.6 14.6 %conditional.37 = ((bf16[32,8192]{1,0:T(8,128)(2,1)S(1)}, bf16[2,4,32,8192]{3,2,1,0:T(8,128)(2,1)})) conditional(s32[]{:T(128)} %convert_element_type.120, (bf16[32,8192]{1,0:T(8,128)(2,1)S(1)}, bf16[2,4,32,8192]{3,2,1,0:T(8,128)(2,1)}) %tuple.168, (s32[]{:T(128)}, s32[256,3]{0,1:T(4,128)}, s32[]{:T(128)}, bf16[32,8192]{1,0:T(8,128)(2,1)S(1)}, ...), branch_computations={%region_34.35_spmd, %region_35.36_spmd} | conditional | flops 6 | bytes 12350 | solution.py:401
  225.9 5.7 %branch_1_fun.76 = (bf16[32,8192]{1,0:T(8,128)(2,1)}, bf16[2,4,32,8192]{3,2,1,0:T(8,128)(2,1)}) custom-call(s32[2]{0:T(128)} %pad_add_fusion.17.at_ref, s32[768]{0:T(1024)} %reshape.165.idx_ref, bf16[32,8192]{1,0:T(8,128)(2,1)S(1)} %get-tuple-element.696.g_in, f32[2,4,32,8192]{3,2,1,0:T(8,128)} %get-tuple-element.697.sy_hbm, ...), custom_call_target="tpu_custom_call", output_to_operand_aliasing={{1}: (5, {})} | custom-call | tf_op jit(solution)/shard_map/cond/branch_1_fun/pallas_call | solution.py:223
  231.6 6.6 %branch_1_fun.77 = (bf16[32,8192]{1,0:T(8,128)(2,1)S(1)}, bf16[2,4,32,8192]{3,2,1,0:T(8,128)(2,1)}) custom-call(s32[1]{0:T(128)} %bitcast.34.at_ref, s32[768]{0:T(1024)} %reshape.165.idx_ref, bf16[32,8192]{1,0:T(8,128)(2,1)} %get-tuple-element.701.g_in, f32[2,4,32,8192]{3,2,1,0:T(8,128)} %get-tuple-element.697.sy_hbm, ...), custom_call_target="tpu_custom_call", output_to_operand_aliasing={{1}: (5, {})} | custom-call | tf_op jit(solution)/shard_map/cond/branch_1_fun/pallas_call | solution.py:223
  240.3 10.8 %collective-permute-start.8 = (bf16[32,8192]{1,0:T(8,128)(2,1)}, bf16[32,8192]{1,0:T(8,128)(2,1)S(1)}, u32[]{:S(2)}, u32[]{:S(2)}) collective-permute-start(bf16[32,8192]{1,0:T(8,128)(2,1)} %get-tuple-element.807), channel_id=1, source_target_pairs={{0,8},{8,16},{16,24},{1,9},{9,17},{17,25},{2,10},{10,18},{18,26},{... | collective-permute-start | bytes 1572872 | tf_op jit(solution)/shard_map/ppermute | solution.py:27
  251.1 6.1 %collective-permute-done.16 = bf16[32,8192]{1,0:T(8,128)(2,1)} collective-permute-done((bf16[32,8192]{1,0:T(8,128)(2,1)S(1)}, bf16[32,8192]{1,0:T(8,128)(2,1)}, u32[]{:S(2)}, u32[]{:S(2)}) %collective-permute-start.16) | collective-permute-done | bytes 524320 | tf_op jit(solution)/shard_map/ppermute | solution.py:27
  257.2 15.8 %conditional.38 = ((bf16[32,8192]{1,0:T(8,128)(2,1)}, bf16[2,4,32,8192]{3,2,1,0:T(8,128)(2,1)})) conditional(s32[]{:T(128)} %convert_element_type.119, (bf16[32,8192]{1,0:T(8,128)(2,1)}, bf16[2,4,32,8192]{3,2,1,0:T(8,128)(2,1)}) %tuple.170, (s32[]{:T(128)}, s32[256,3]{0,1:T(4,128)}, s32[]{:T(128)}, bf16[32,8192]{1,0:T(8,128)(2,1)}, ...), branch_computations={%region_36.37_spmd.clone, %region_37.38_spmd.clone} | conditional | flops 6 | bytes 12350 | solution.py:401
  259.5 6.1 %branch_1_fun.80 = (bf16[32,8192]{1,0:T(8,128)(2,1)}, bf16[2,4,32,8192]{3,2,1,0:T(8,128)(2,1)}) custom-call(s32[2]{0:T(128)} %pad_add_fusion.19.at_ref, s32[768]{0:T(1024)} %reshape.185.idx_ref, bf16[32,8192]{1,0:T(8,128)(2,1)} %get-tuple-element.837.g_in, f32[2,4,32,8192]{3,2,1,0:T(8,128)} %get-tuple-element.838.sy_hbm, ...), custom_call_target="tpu_custom_call", output_to_operand_aliasing={{1}: (5, {})} | custom-call | tf_op jit(solution)/shard_map/cond/branch_1_fun/pallas_call | solution.py:223
  265.6 7.4 %branch_1_fun.81 = (bf16[32,8192]{1,0:T(8,128)(2,1)}, bf16[2,4,32,8192]{3,2,1,0:T(8,128)(2,1)}) custom-call(s32[1]{0:T(128)} %bitcast.49.at_ref, s32[768]{0:T(1024)} %reshape.185.idx_ref, bf16[32,8192]{1,0:T(8,128)(2,1)} %get-tuple-element.842.g_in, f32[2,4,32,8192]{3,2,1,0:T(8,128)} %get-tuple-element.838.sy_hbm, ...), custom_call_target="tpu_custom_call", output_to_operand_aliasing={{1}: (5, {})} | custom-call | tf_op jit(solution)/shard_map/cond/branch_1_fun/pallas_call | solution.py:223
  276.0 9.1 %collective-permute-done.17 = bf16[32,8192]{1,0:T(8,128)(2,1)S(1)} collective-permute-done((bf16[32,8192]{1,0:T(8,128)(2,1)}, bf16[32,8192]{1,0:T(8,128)(2,1)S(1)}, u32[]{:S(2)}, u32[]{:S(2)}) %collective-permute-start.17) | collective-permute-done | bytes 524320 | tf_op jit(solution)/shard_map/ppermute | solution.py:27
  285.0 14.6 %conditional.39 = (bf16[2,4,32,8192]{3,2,1,0:T(8,128)(2,1)}) conditional(s32[]{:T(128)} %convert_element_type.118, bf16[2,4,32,8192]{3,2,1,0:T(8,128)(2,1)} %get-tuple-element.826, (s32[]{:T(128)}, s32[256,3]{0,1:T(4,128)S(1)}, s32[]{:T(128)}, bf16[32,8192]{1,0:T(8,128)(2,1)S(1)}, f32[2,4,32,8192]{3,2,1,0:T(8,128)}, ...), branch_computations={%region_38.39_spmd, %region_39.40_spmd} | conditional | flops 6 | bytes 12350 | solution.py:401
  286.5 5.7 %branch_1_fun.78 = (bf16[32,8192]{1,0:T(8,128)(2,1)}, bf16[2,4,32,8192]{3,2,1,0:T(8,128)(2,1)}) custom-call(s32[2]{0:T(128)} %pad_add_fusion.18.at_ref, s32[768]{0:T(1024)} %reshape.169.idx_ref, bf16[32,8192]{1,0:T(8,128)(2,1)S(1)} %get-tuple-element.720.g_in, f32[2,4,32,8192]{3,2,1,0:T(8,128)} %get-tuple-element.721.sy_hbm, ...), custom_call_target="tpu_custom_call", output_to_operand_aliasing={{1}: (5, {})} | custom-call | tf_op jit(solution)/shard_map/cond/branch_1_fun/pallas_call | solution.py:223
  292.3 7.4 %branch_1_fun.79 = (bf16[32,8192]{1,0:T(8,128)(2,1)}, bf16[2,4,32,8192]{3,2,1,0:T(8,128)(2,1)}) custom-call(s32[1]{0:T(128)} %bitcast.36.at_ref, s32[768]{0:T(1024)} %reshape.169.idx_ref, bf16[32,8192]{1,0:T(8,128)(2,1)} %get-tuple-element.725.g_in, f32[2,4,32,8192]{3,2,1,0:T(8,128)} %get-tuple-element.721.sy_hbm, ...), custom_call_target="tpu_custom_call", output_to_operand_aliasing={{1}: (5, {})} | custom-call | tf_op jit(solution)/shard_map/cond/branch_1_fun/pallas_call | solution.py:223
  299.7 8.2 %shard_map.48 = bf16[4,32,128,128]{3,2,1,0:T(8,128)(2,1)} custom-call(s32[1]{0:T(128)} %bitcast.42.sel_ref, s32[768]{0:T(1024)} %reshape.178.idx_ref, bf16[2,4,32,8192]{3,2,1,0:T(8,128)(2,1)} %get-tuple-element.808.h_ref, bf16[2,4,32,8192]{3,2,1,0:T(8,128)(2,1)} %get-tuple-element.1118.s_ref), custom_call_target="tpu_custom_call" | custom-call | tf_op jit(solution)/shard_map/pallas_call | solution.py:309
  307.8 9.3 %shard_map.47 = f32[4,32,128,128]{3,2,1,0:T(8,128)} custom-call(s32[1]{0:T(128)} %bitcast.38.sel_ref, s32[768]{0:T(1024)} %reshape.178.idx_ref, bf16[2,4,32,8192]{3,2,1,0:T(8,128)(2,1)} %get-tuple-element.808.h_ref, bf16[2,4,32,8192]{3,2,1,0:T(8,128)(2,1)} %get-tuple-element.1118.s_ref), custom_call_target="tpu_custom_call" | custom-call | tf_op jit(solution)/shard_map/pallas_call | solution.py:309
  317.1 5.0 %fusion = bf16[2,32,128,128]{3,2,1,0:T(8,128)(2,1)} fusion(f32[2,2,32,128,128]{4,3,2,1,0:T(8,128)} %bitcast.80, s32[]{:T(128)S(6)} %select_n.64, bf16[2,2,32,128,128]{4,3,2,1,0:T(8,128)(2,1)} %bitcast.43), kind=kLoop, calls=%fused_computation.21 | loop fusion | flops 3145728 | bytes 8388612 | tf_op jit(solution)/shard_map/convert_element_type | solution.py:319
  322.2 26.2 %collective-permute-done.19 = bf16[2,32,128,128]{3,2,1,0:T(8,128)(2,1)S(1)} collective-permute-done((bf16[2,32,128,128]{3,2,1,0:T(8,128)(2,1)}, bf16[2,32,128,128]{3,2,1,0:T(8,128)(2,1)S(1)}, u32[]{:S(2)}, u32[]{:S(2)}) %collective-permute-start.19) | collective-permute-done | bytes 2097184 | tf_op jit(solution)/shard_map/ppermute | solution.py:319
  353.4 14.8 %collective-permute-done.20 = bf16[32,128,128]{2,1,0:T(8,128)(2,1)S(1)} collective-permute-done((bf16[32,128,128]{2,1,0:T(8,128)(2,1)S(1)}, bf16[32,128,128]{2,1,0:T(8,128)(2,1)S(1)}, u32[]{:S(2)}, u32[]{:S(2)}) %collective-permute-start.20) | collective-permute-done | bytes 1048608 | tf_op jit(solution)/shard_map/ppermute | solution.py:319
  368.2 4.5 %fusion.2 = f32[32,128,128]{2,1,0:T(8,128)} fusion(bf16[32,128,128]{2,1,0:T(8,128)(2,1)S(1)} %collective-permute-done.20, f32[2,32,128,128]{3,2,1,0:T(8,128)} %copy-done.1, s32[]{:T(128)S(6)} %select_n.59, f32[2,2,32,128,128]{4,3,2,1,0:T(8,128)} %bitcast.82, s32[]{:T(128)S(6)} %select_n.60, s32[]{:T(128)S(6)} %select_n.63, ...), kind=kLoop, calls=%fused_computation.25 | loop fusion | flops 2621440 | bytes 8388620 | tf_op jit(solution)/shard_map/add | solution.py:350
  (75 shorter events, 40.8 us)
Async XLA Ops:
  15.2 13.7 %collective-permute-start = (bf16[32,8192]{1,0:T(8,128)(2,1)}, bf16[32,8192]{1,0:T(8,128)(2,1)S(1)}, u32[]{:S(2)}, u32[]{:S(2)}) collective-permute-start(bf16[32,8192]{1,0:T(8,128)(2,1)} %get-tuple-element.781), channel_id=1, source_target_pairs={{0,8},{8,16},{16,24},{1,9},{9,17},{17,25},{2,10},{10,18},{18,26},{... | collective-permute-start | bytes 1572872 | tf_op jit(solution)/shard_map/ppermute | solution.py:27
  16.5 12.3 %copy-start = (bf16[2,64,8192]{2,1,0:T(8,128)(2,1)S(1)}, bf16[2,64,8192]{2,1,0:T(8,128)(2,1)}, u32[]{:S(2)}) copy-start(bf16[2,64,8192]{2,1,0:T(8,128)(2,1)} %param.44) | copy-start | bytes 6291460
  17.4 28.5 %collective-permute-start.9 = (bf16[32,8192]{1,0:T(8,128)(2,1)}, bf16[32,8192]{1,0:T(8,128)(2,1)S(1)}, u32[]{:S(2)}, u32[]{:S(2)}) collective-permute-start(bf16[32,8192]{1,0:T(8,128)(2,1)} %get-tuple-element.810), channel_id=1, source_target_pairs={{8,0},{16,8},{24,16},{9,1},{17,9},{25,17},{10,2},{18,10},{26,18},{... | collective-permute-start | bytes 1572872 | tf_op jit(solution)/shard_map/ppermute | solution.py:27
  41.2 15.1 %collective-permute-start.1 = (bf16[32,8192]{1,0:T(8,128)(2,1)S(1)}, bf16[32,8192]{1,0:T(8,128)(2,1)}, u32[]{:S(2)}, u32[]{:S(2)}) collective-permute-start(bf16[32,8192]{1,0:T(8,128)(2,1)S(1)} %get-tuple-element.784), channel_id=1, source_target_pairs={{0,8},{8,16},{16,24},{1,9},{9,17},{17,25},{2,10},{10,18},{18,26},{... | collective-permute-start | bytes 1572872 | tf_op jit(solution)/shard_map/ppermute | solution.py:27
  45.9 28.7 %collective-permute-start.10 = (bf16[32,8192]{1,0:T(8,128)(2,1)S(1)}, bf16[32,8192]{1,0:T(8,128)(2,1)}, u32[]{:S(2)}, u32[]{:S(2)}) collective-permute-start(bf16[32,8192]{1,0:T(8,128)(2,1)S(1)} %get-tuple-element.812), channel_id=1, source_target_pairs={{8,0},{16,8},{24,16},{9,1},{17,9},{25,17},{10,2},{18,10},{26,18},{... | collective-permute-start | bytes 1572872 | tf_op jit(solution)/shard_map/ppermute | solution.py:27
  69.8 14.7 %collective-permute-start.2 = (bf16[32,8192]{1,0:T(8,128)(2,1)}, bf16[32,8192]{1,0:T(8,128)(2,1)}, u32[]{:S(2)}, u32[]{:S(2)}) collective-permute-start(bf16[32,8192]{1,0:T(8,128)(2,1)} %get-tuple-element.787), channel_id=1, source_target_pairs={{0,8},{8,16},{16,24},{1,9},{9,17},{17,25},{2,10},{10,18},{18,26},{... | collective-permute-start | bytes 1572872 | tf_op jit(solution)/shard_map/ppermute | solution.py:27
  74.6 28.1 %collective-permute-start.11 = (bf16[32,8192]{1,0:T(8,128)(2,1)}, bf16[32,8192]{1,0:T(8,128)(2,1)S(1)}, u32[]{:S(2)}, u32[]{:S(2)}) collective-permute-start(bf16[32,8192]{1,0:T(8,128)(2,1)} %get-tuple-element.814), channel_id=1, source_target_pairs={{8,0},{16,8},{24,16},{9,1},{17,9},{25,17},{10,2},{18,10},{26,18},{... | collective-permute-start | bytes 1572872 | tf_op jit(solution)/shard_map/ppermute | solution.py:27
  97.9 13.8 %collective-permute-start.3 = (bf16[32,8192]{1,0:T(8,128)(2,1)}, bf16[32,8192]{1,0:T(8,128)(2,1)}, u32[]{:S(2)}, u32[]{:S(2)}) collective-permute-start(bf16[32,8192]{1,0:T(8,128)(2,1)} %get-tuple-element.790), channel_id=1, source_target_pairs={{0,8},{8,16},{16,24},{1,9},{9,17},{17,25},{2,10},{10,18},{18,26},{... | collective-permute-start | bytes 1572872 | tf_op jit(solution)/shard_map/ppermute | solution.py:27
  102.8 27.2 %collective-permute-start.12 = (bf16[32,8192]{1,0:T(8,128)(2,1)S(1)}, bf16[32,8192]{1,0:T(8,128)(2,1)S(1)}, u32[]{:S(2)}, u32[]{:S(2)}) collective-permute-start(bf16[32,8192]{1,0:T(8,128)(2,1)S(1)} %get-tuple-element.816), channel_id=1, source_target_pairs={{8,0},{16,8},{24,16},{9,1},{17,9},{25,17},{10,2},{18,10},{26,18},{... | collective-permute-start | bytes 1572872 | tf_op jit(solution)/shard_map/ppermute | solution.py:27
  111.7 26.3 %collective-permute-start.4 = (bf16[32,8192]{1,0:T(8,128)(2,1)}, bf16[32,8192]{1,0:T(8,128)(2,1)}, u32[]{:S(2)}, u32[]{:S(2)}) collective-permute-start(bf16[32,8192]{1,0:T(8,128)(2,1)} %get-tuple-element.793), channel_id=1, source_target_pairs={{0,8},{8,16},{16,24},{1,9},{9,17},{17,25},{2,10},{10,18},{18,26},{... | collective-permute-start | bytes 1572872 | tf_op jit(solution)/shard_map/ppermute | solution.py:27
  129.9 14.0 %collective-permute-start.13 = (bf16[32,8192]{1,0:T(8,128)(2,1)S(1)}, bf16[32,8192]{1,0:T(8,128)(2,1)S(1)}, u32[]{:S(2)}, u32[]{:S(2)}) collective-permute-start(bf16[32,8192]{1,0:T(8,128)(2,1)S(1)} %get-tuple-element.818), channel_id=1, source_target_pairs={{8,0},{16,8},{24,16},{9,1},{17,9},{25,17},{10,2},{18,10},{26,18},{... | collective-permute-start | bytes 1572872 | tf_op jit(solution)/shard_map/ppermute | solution.py:27
  138.0 13.3 %collective-permute-start.5 = (bf16[32,8192]{1,0:T(8,128)(2,1)}, bf16[32,8192]{1,0:T(8,128)(2,1)}, u32[]{:S(2)}, u32[]{:S(2)}) collective-permute-start(bf16[32,8192]{1,0:T(8,128)(2,1)} %get-tuple-element.796), channel_id=1, source_target_pairs={{0,8},{8,16},{16,24},{1,9},{9,17},{17,25},{2,10},{10,18},{18,26},{... | collective-permute-start | bytes 1572872 | tf_op jit(solution)/shard_map/ppermute | solution.py:27
  144.0 49.4 %collective-permute-start.14 = (bf16[32,8192]{1,0:T(8,128)(2,1)S(1)}, bf16[32,8192]{1,0:T(8,128)(2,1)S(1)}, u32[]{:S(2)}, u32[]{:S(2)}) collective-permute-start(bf16[32,8192]{1,0:T(8,128)(2,1)S(1)} %get-tuple-element.820), channel_id=1, source_target_pairs={{8,0},{16,8},{24,16},{9,1},{17,9},{25,17},{10,2},{18,10},{26,18},{... | collective-permute-start | bytes 1572872 | tf_op jit(solution)/shard_map/ppermute | solution.py:27
  151.4 59.8 %collective-permute-start.6 = (bf16[32,8192]{1,0:T(8,128)(2,1)}, bf16[32,8192]{1,0:T(8,128)(2,1)}, u32[]{:S(2)}, u32[]{:S(2)}) collective-permute-start(bf16[32,8192]{1,0:T(8,128)(2,1)} %get-tuple-element.799), channel_id=1, source_target_pairs={{0,8},{8,16},{16,24},{1,9},{9,17},{17,25},{2,10},{10,18},{18,26},{... | collective-permute-start | bytes 1572872 | tf_op jit(solution)/shard_map/ppermute | solution.py:27
  193.3 0.8 copy-start.4
  209.9 13.7 %collective-permute-start.15 = (bf16[32,8192]{1,0:T(8,128)(2,1)}, bf16[32,8192]{1,0:T(8,128)(2,1)S(1)}, u32[]{:S(2)}, u32[]{:S(2)}) collective-permute-start(bf16[32,8192]{1,0:T(8,128)(2,1)} %get-tuple-element.822), channel_id=1, source_target_pairs={{8,0},{16,8},{24,16},{9,1},{17,9},{25,17},{10,2},{18,10},{26,18},{... | collective-permute-start | bytes 1572872 | tf_op jit(solution)/shard_map/ppermute | solution.py:27
  211.2 28.3 %collective-permute-start.7 = (bf16[32,8192]{1,0:T(8,128)(2,1)}, bf16[32,8192]{1,0:T(8,128)(2,1)S(1)}, u32[]{:S(2)}, u32[]{:S(2)}) collective-permute-start(bf16[32,8192]{1,0:T(8,128)(2,1)} %get-tuple-element.802), channel_id=1, source_target_pairs={{0,8},{8,16},{16,24},{1,9},{9,17},{17,25},{2,10},{10,18},{18,26},{... | collective-permute-start | bytes 1572872 | tf_op jit(solution)/shard_map/ppermute | solution.py:27
  238.2 19.0 %collective-permute-start.16 = (bf16[32,8192]{1,0:T(8,128)(2,1)S(1)}, bf16[32,8192]{1,0:T(8,128)(2,1)}, u32[]{:S(2)}, u32[]{:S(2)}) collective-permute-start(bf16[32,8192]{1,0:T(8,128)(2,1)S(1)} %get-tuple-element.824), channel_id=1, source_target_pairs={{8,0},{16,8},{24,16},{9,1},{17,9},{25,17},{10,2},{18,10},{26,18},{... | collective-permute-start | bytes 1572872 | tf_op jit(solution)/shard_map/ppermute | solution.py:27
  239.5 0.8 copy-start.3
  240.3 35.6 %collective-permute-start.8 = (bf16[32,8192]{1,0:T(8,128)(2,1)}, bf16[32,8192]{1,0:T(8,128)(2,1)S(1)}, u32[]{:S(2)}, u32[]{:S(2)}) collective-permute-start(bf16[32,8192]{1,0:T(8,128)(2,1)} %get-tuple-element.807), channel_id=1, source_target_pairs={{0,8},{8,16},{16,24},{1,9},{9,17},{17,25},{2,10},{10,18},{18,26},{... | collective-permute-start | bytes 1572872 | tf_op jit(solution)/shard_map/ppermute | solution.py:27
  257.2 18.8 %copy-start.2 = (s32[256,3]{0,1:T(4,128)S(1)}, s32[256,3]{0,1:T(4,128)}, u32[]{:S(2)}) copy-start(s32[256,3]{0,1:T(4,128)} %param.47) | copy-start | bytes 9220
  273.0 12.0 %collective-permute-start.17 = (bf16[32,8192]{1,0:T(8,128)(2,1)}, bf16[32,8192]{1,0:T(8,128)(2,1)S(1)}, u32[]{:S(2)}, u32[]{:S(2)}) collective-permute-start(bf16[32,8192]{1,0:T(8,128)(2,1)} %get-tuple-element.827), channel_id=1, source_target_pairs={{8,0},{16,8},{24,16},{9,1},{17,9},{25,17},{10,2},{18,10},{26,18},{... | collective-permute-start | bytes 1572872 | tf_op jit(solution)/shard_map/ppermute | solution.py:27
  307.8 9.3 %collective-permute-start.18 = (bf16[4,32,128,128]{3,2,1,0:T(8,128)(2,1)}, bf16[4,32,128,128]{3,2,1,0:T(8,128)(2,1)}, u32[]{:S(2)}, u32[]{:S(2)}) collective-permute-start(bf16[4,32,128,128]{3,2,1,0:T(8,128)(2,1)} %shard_map.48), channel_id=1, source_target_pairs={{0,1},{1,0},{2,3},{3,2},{4,5},{5,4},{6,7},{7,6},{8,9},{9,8},{10,11... | collective-permute-start | bytes 12582920 | tf_op jit(solution)/shard_map/ppermute | solution.py:333
  322.2 26.2 %collective-permute-start.19 = (bf16[2,32,128,128]{3,2,1,0:T(8,128)(2,1)}, bf16[2,32,128,128]{3,2,1,0:T(8,128)(2,1)S(1)}, u32[]{:S(2)}, u32[]{:S(2)}) collective-permute-start(bf16[2,32,128,128]{3,2,1,0:T(8,128)(2,1)} %fusion), channel_id=1, source_target_pairs={{0,2},{1,5},{2,0},{3,7},{4,6},{5,1},{6,4},{7,3},{8,10},{9,13},{10,... | collective-permute-start | bytes 6291464 | tf_op jit(solution)/shard_map/ppermute | solution.py:319
  348.9 2.1 copy-start.1
  353.4 14.9 %collective-permute-start.20 = (bf16[32,128,128]{2,1,0:T(8,128)(2,1)S(1)}, bf16[32,128,128]{2,1,0:T(8,128)(2,1)S(1)}, u32[]{:S(2)}, u32[]{:S(2)}) collective-permute-start(bf16[32,128,128]{2,1,0:T(8,128)(2,1)S(1)} %fusion.1), channel_id=1, source_target_pairs={{0,4},{1,3},{2,6},{3,1},{4,0},{5,7},{6,2},{7,5},{8,12},{9,11},{10,... | collective-permute-start | bytes 3145736 | tf_op jit(solution)/shard_map/ppermute | solution.py:319
